TPU v7x, 32 devices: a whole 2x2x4 slice. The times are simulated.
32 devices in a mesh: seq: 16 (over z, y, core), dp: 2 (over x).
Axes of the slice: x: 2, y: 2, z: 4, core: 2. Of those that a mesh axis runs over, the one named last changes fastest.
Arguments:
- queries: bfloat16 [2, 3072, 1536], P('dp', 'seq'), may hold values from -100 to 100
- key_vectors: bfloat16 [2, 3072, 1536], P('dp', 'seq'), may hold values from -6 to 6
- value_vectors: bfloat16 [2, 3072, 1536], P('dp', 'seq'), may hold values from -48 to 48
- w_out: bfloat16 [1536, 1536], P(('seq', 'dp')), may hold values from -0.15625 to 0.15625
- cotangent: bfloat16 [2, 3072, 1536], P('dp', 'seq'), may hold values from -0.119628906 to 0.119628906
Outputs:
- projected: bfloat16 [2, 3072, 1536], P('dp', 'seq')
- grad_w_out: float32 [1536, 1536], P(('seq', 'dp'))
All inputs are finite; a program needn't handle non-finite values.
Results may differ from a plain program's by a relative error of at most 0.0055.
Values may be sent and summed in bfloat16 or wider, within the bound.
No kernel may reach another device: no remote copies, remote signals or barrier semaphores. Data moves between devices by JAX's collectives and lax.ppermute only.
A program may use at most 128 MiB of HBM per device.

v0:
```python
import jax
import jax.numpy as jnp
from jax import lax
from jax.sharding import PartitionSpec as P

HEADS = 8
HEAD_DIM = 192


def attend(query_here, key_all, value_all):
    query_count = query_here.shape[0]
    head_width = query_here.shape[1]
    block_size = min(512, query_count)
    score_scale = HEAD_DIM ** (-0.5)

    def one_block(query_block):
        scores = jnp.dot(query_block, key_all.T, preferred_element_type=jnp.float32) * score_scale
        largest = jnp.max(scores, axis=1, keepdims=True)
        raised = jnp.exp(scores - largest)
        denominator = jnp.sum(raised, axis=1, keepdims=True)
        weights = raised.astype(jnp.bfloat16)
        mixed = jnp.dot(weights, value_all, preferred_element_type=jnp.float32)
        return (mixed / denominator).astype(jnp.bfloat16)

    blocks = lax.map(
        one_block, query_here.reshape(query_count // block_size, block_size, head_width)
    )
    return blocks.reshape(query_count, head_width)


def local(queries, key_vectors, value_vectors, w_out, cotangent):
    head_count = HEADS
    head_width = HEAD_DIM
    seq_count = lax.axis_size("seq")
    dp_count = lax.axis_size("dp")
    per_head = seq_count // head_count
    row_count = queries.shape[1]
    sub = row_count // per_head
    width = queries.shape[2]

    w_full = lax.all_gather(w_out, ("seq", "dp"), axis=0, tiled=True)

    def a2a(tensor):
        return lax.all_to_all(tensor, "seq", split_axis=0, concat_axis=0, tiled=True)

    query_slots = (
        queries[0]
        .reshape(per_head, sub, head_count, head_width)
        .transpose(2, 0, 1, 3)
        .reshape(seq_count, sub, head_width)
    )

    def head_slots(tensor):
        tensor = tensor[0].reshape(row_count, head_count, head_width).transpose(1, 0, 2)
        tensor = jnp.broadcast_to(
            tensor[:, None], (head_count, per_head, row_count, head_width)
        )
        return tensor.reshape(seq_count, row_count, head_width)

    cot_slots = jnp.broadcast_to(
        cotangent[0].reshape(1, per_head, sub, width), (head_count, per_head, sub, width)
    ).reshape(seq_count, sub, width)

    got_query = a2a(query_slots)
    got_key = a2a(head_slots(key_vectors))
    got_value = a2a(head_slots(value_vectors))
    got_cot = a2a(cot_slots)

    query_here = got_query.reshape(seq_count * sub, head_width)
    key_all = got_key.reshape(seq_count * row_count, head_width)
    value_all = got_value.reshape(seq_count * row_count, head_width)
    cot_here = got_cot.reshape(seq_count * sub, width)

    attended_here = attend(query_here, key_all, value_all)

    partial = lax.dot_general(
        attended_here, cot_here, (((0,), (0,)), ((), ())), preferred_element_type=jnp.float32
    )

    returned = a2a(attended_here.reshape(seq_count, sub, head_width))
    attended = (
        returned.reshape(head_count, per_head, sub, head_width)
        .transpose(1, 2, 0, 3)
        .reshape(row_count, width)
    )
    projected = jnp.dot(attended, w_full, preferred_element_type=jnp.float32).astype(
        jnp.bfloat16
    )

    seq_index = lax.axis_index("seq")
    group = seq_index % per_head
    chunk = head_width // per_head
    pieces = partial.reshape(per_head, chunk, width)
    summed = lax.dynamic_index_in_dim(pieces, group, axis=0, keepdims=False)
    if per_head > 1:
        for step in range(1, per_head):
            target = (group + step) % per_head
            outgoing = lax.dynamic_index_in_dim(pieces, target, axis=0, keepdims=False)
            perm = [
                (s, (s // per_head) * per_head + (s % per_head + step) % per_head)
                for s in range(seq_count)
            ]
            summed = summed + lax.ppermute(outgoing, "seq", perm)
    grad_w_out = lax.psum_scatter(summed, "dp", scatter_dimension=0, tiled=True)
    return (projected.reshape(1, row_count, width), grad_w_out)


def solution(mesh):
    placed = (
        P("dp", "seq", None),
        P("dp", "seq", None),
        P("dp", "seq", None),
        P(("seq", "dp"), None),
        P("dp", "seq", None),
    )
    return jax.shard_map(
        local,
        mesh=mesh,
        in_specs=placed,
        out_specs=(P("dp", "seq", None), P(("seq", "dp"), None)),
        check_vma=False,
    )
```

profile of v0, /device:TPU:1, one launch (start us, length us, event | category | flops | bytes accessed | tf_op | source)
XLA Modules:
  0.0 296.1 jit_solution(9150849071924576565)
XLA Ops:
  8.0 0.0 copy-start.1
  8.0 1.8 reshape_squeeze.10
  9.8 1.1 copy.10
  10.9 0.0 copy-start.2
  10.9 7.5 %all-to-all-start = ((bf16[16,96,192]{2,1,0:T(8,128)(2,1)}), bf16[16,96,192]{2,1,0:T(8,128)(2,1)S(1)}, u32[]{:S(2)}, u32[]{:S(2)}) async-start(bf16[16,96,192]{2,1,0:T(8,128)(2,1)} %bitcast.3), calls=%async_computation | async-start | bytes 1572864 | tf_op jit(solution)/shard_map/all_to_all | solution.py:44
  18.3 0.0 copy-done.1
  18.4 0.6 reshape_squeeze.11
  19.0 0.2 copy.11
  19.1 17.8 %all-to-all-done = bf16[16,96,192]{2,1,0:T(8,128)(2,1)S(1)} async-done(((bf16[16,96,192]{2,1,0:T(8,128)(2,1)}), bf16[16,96,192]{2,1,0:T(8,128)(2,1)S(1)}, u32[]{:S(2)}, u32[]{:S(2)}) %all-to-all-start) | async-done | bytes 589856 | tf_op jit(solution)/shard_map/all_to_all | solution.py:44
  36.9 1.4 broadcast_in_dim.14
  38.2 5.6 %all-to-all-start.1 = ((bf16[16,192,192]{2,1,0:T(8,128)(2,1)}), bf16[16,192,192]{2,1,0:T(8,128)(2,1)S(1)}, u32[]{:S(2)}, u32[]{:S(2)}) async-start(bf16[16,192,192]{2,1,0:T(8,128)(2,1)} %bitcast.6), calls=%async_computation.1 | async-start | bytes 3145728 | tf_op jit(solution)/shard_map/all_to_all | solution.py:44
  43.9 0.0 copy-done.2
  43.9 1.5 reshape_squeeze.12
  45.4 1.3 copy.12
  46.7 29.6 %all-to-all-done.1 = bf16[16,192,192]{2,1,0:T(8,128)(2,1)S(1)} async-done(((bf16[16,192,192]{2,1,0:T(8,128)(2,1)}), bf16[16,192,192]{2,1,0:T(8,128)(2,1)S(1)}, u32[]{:S(2)}, u32[]{:S(2)}) %all-to-all-start.1) | async-done | bytes 1179680 | tf_op jit(solution)/shard_map/all_to_all | solution.py:44
  76.2 0.0 copy-start.3
  76.2 0.1 broadcast_in_dim.30
  76.4 45.2 %all_to_all.25 = bf16[16,192,192]{2,1,0:T(8,128)(2,1)} all-to-all(bf16[16,192,192]{2,1,0:T(8,128)(2,1)S(1)} %bitcast.58), channel_id=1, replica_groups=mesh['seq'=16,'dp'=2] {'seq'}, dimensions={0} | all-to-all | bytes 2359296 | tf_op jit(solution)/shard_map/all_to_all | solution.py:44
  121.6 0.0 copy-done.3
  121.6 2.7 broadcast_in_dim.32
  124.3 4.7 %all-to-all-start.4 = ((bf16[16,96,1536]{2,1,0:T(8,128)(2,1)}), bf16[16,96,1536]{2,1,0:T(8,128)(2,1)}, u32[]{:S(2)}, u32[]{:S(2)}) async-start(bf16[16,96,1536]{2,1,0:T(8,128)(2,1)} %bitcast.57), calls=%async_computation.4 | async-start | bytes 9437184 | tf_op jit(solution)/shard_map/all_to_all | solution.py:44
  129.0 0.0 all-gather.2.cloned.1.call-start
  129.0 0.7 all-gather.2.cloned.1.call-update
  129.7 12.1 %while.10 = (s32[]{:T(128)}, bf16[3,512,192]{1,2,0:T(8,128)(2,1)S(1)}, bf16[3,512,192]{2,1,0:T(8,128)(2,1)S(1)}, bf16[3072,192]{1,0:T(8,128)(2,1)S(1)}, bf16[3072,192]{1,0:T(8,128)(2,1)}, /*index=5*/s32[]{:T(128)}) while((s32[]{:T(128)}, bf16[3,512,192]{1,2,0:T(8,128)(2,1)S(1)}, bf16[3,512,192]{2,1,0:T(8,128)(2,1)S(1)}, ...), condition=%wide.region_3.4_spmd, body=%wide.region_0.3_spmd.sunk | while | flops 1220738048 | bytes 27207792 | solution.py:25
  129.8 1.1 multiply_reduce_fusion.2
  130.9 0.0 copy-start
  130.9 1.2 fusion.39
  132.0 0.2 copy-done
  132.3 1.5 fusion.40
  133.8 1.1 multiply_reduce_fusion.2
  134.9 0.0 copy-start
  134.9 1.2 fusion.39
  136.1 0.2 copy-done
  136.3 1.5 fusion.40
  137.8 1.1 multiply_reduce_fusion.2
  138.9 0.0 copy-start
  138.9 1.2 fusion.39
  140.1 0.2 copy-done
  140.3 1.5 fusion.40
  141.9 83.8 %all-to-all-done.4 = bf16[16,96,1536]{2,1,0:T(8,128)(2,1)} async-done(((bf16[16,96,1536]{2,1,0:T(8,128)(2,1)}), bf16[16,96,1536]{2,1,0:T(8,128)(2,1)}, u32[]{:S(2)}, u32[]{:S(2)}) %all-to-all-start.4) | async-done | bytes 4718624 | tf_op jit(solution)/shard_map/all_to_all | solution.py:44
  225.7 3.6 %fusion.24 = f32[2,96,1536]{2,1,0:T(8,128)S(1)} fusion(bf16[2,96,1536]{2,1,0:T(8,128)(2,1)S(1)} %bitcast.65, bf16[1536,1536,1]{1,0,2:T(8,128)(2,1)} %bitcast.20), kind=kOutput, calls=%fused_computation.21 | convolution fusion | flops 905969664 | bytes 6488064 | tf_op jit(solution)/shard_map/dot_general | solution.py:76
  229.3 0.2 collective-permute-start
  229.6 1.2 copy.13
  230.8 34.0 %all-to-all-start.3 = ((bf16[16,96,192]{2,1,0:T(8,128)(2,1)}), bf16[16,96,192]{2,1,0:T(8,128)(2,1)S(1)}, u32[]{:S(2)}, u32[]{:S(2)}) async-start(bf16[16,96,192]{2,1,0:T(8,128)(2,1)} %bitcast.11), calls=%async_computation.3 | async-start | bytes 1572864 | tf_op jit(solution)/shard_map/all_to_all | solution.py:44
  264.7 0.0 reduce-scatter.2.cloned.1.call-start
  264.8 0.0 collective-permute-done
  264.8 2.0 bitcast_add_fusion
  266.8 0.0 reduce-scatter.2.cloned.1.call-update
  266.8 16.5 %all-to-all-done.3 = bf16[16,96,192]{2,1,0:T(8,128)(2,1)S(1)} async-done(((bf16[16,96,192]{2,1,0:T(8,128)(2,1)}), bf16[16,96,192]{2,1,0:T(8,128)(2,1)S(1)}, u32[]{:S(2)}, u32[]{:S(2)}) %all-to-all-start.3) | async-done | bytes 589856 | tf_op jit(solution)/shard_map/all_to_all | solution.py:44
  283.3 0.4 copy.18
  283.7 0.7 reshape.50
  284.4 0.0 all-gather.2.cloned.1.call-done
  284.5 4.2 %fusion.23 = bf16[1,192,1536]{2,1,0:T(8,128)(2,1)} fusion(bf16[192,1536]{1,0:T(8,128)(2,1)S(1)} %reshape.50, bf16[1536,1536]{1,0:T(8,128)(2,1)} %all-gather.2.cloned.1.call-done), kind=kOutput, calls=%fused_computation.17 | convolution fusion | flops 906264576 | bytes 5898240 | tf_op jit(solution)/shard_map/dot_general | solution.py:86
  288.7 0.0 reduce-scatter.2.cloned.1.call-done
  (3 shorter events, 0.1 us)
Async XLA Ops:
  8.0 10.4 %copy-start.1 = (bf16[1,192,1536]{2,1,0:T(8,128)(2,1)S(1)}, bf16[1,192,1536]{2,1,0:T(8,128)(2,1)}, u32[]{:S(2)}) copy-start(bf16[1,192,1536]{2,1,0:T(8,128)(2,1)} %param.8) | copy-start | bytes 1769476
  10.9 33.0 %copy-start.2 = (bf16[1,192,1536]{2,1,0:T(8,128)(2,1)S(1)}, bf16[1,192,1536]{2,1,0:T(8,128)(2,1)}, u32[]{:S(2)}) copy-start(bf16[1,192,1536]{2,1,0:T(8,128)(2,1)} %param.9) | copy-start | bytes 1769476
  10.9 26.0 %all-to-all-start = ((bf16[16,96,192]{2,1,0:T(8,128)(2,1)}), bf16[16,96,192]{2,1,0:T(8,128)(2,1)S(1)}, u32[]{:S(2)}, u32[]{:S(2)}) async-start(bf16[16,96,192]{2,1,0:T(8,128)(2,1)} %bitcast.3), calls=%async_computation | async-start | bytes 1572864 | tf_op jit(solution)/shard_map/all_to_all | solution.py:44
  38.2 38.0 %all-to-all-start.1 = ((bf16[16,192,192]{2,1,0:T(8,128)(2,1)}), bf16[16,192,192]{2,1,0:T(8,128)(2,1)S(1)}, u32[]{:S(2)}, u32[]{:S(2)}) async-start(bf16[16,192,192]{2,1,0:T(8,128)(2,1)} %bitcast.6), calls=%async_computation.1 | async-start | bytes 3145728 | tf_op jit(solution)/shard_map/all_to_all | solution.py:44
  76.2 45.4 %copy-start.3 = (bf16[1,192,1536]{2,1,0:T(8,128)(2,1)S(1)}, bf16[1,192,1536]{2,1,0:T(8,128)(2,1)}, u32[]{:S(2)}) copy-start(bf16[1,192,1536]{2,1,0:T(8,128)(2,1)} %param.11) | copy-start | bytes 1769476
  124.3 101.4 %all-to-all-start.4 = ((bf16[16,96,1536]{2,1,0:T(8,128)(2,1)}), bf16[16,96,1536]{2,1,0:T(8,128)(2,1)}, u32[]{:S(2)}, u32[]{:S(2)}) async-start(bf16[16,96,1536]{2,1,0:T(8,128)(2,1)} %bitcast.57), calls=%async_computation.4 | async-start | bytes 9437184 | tf_op jit(solution)/shard_map/all_to_all | solution.py:44
  129.0 155.5 %all-gather.2.cloned.1.call-start = ((), (), s32[]{:S(2)}) async-start(), calls=%async_computation.6 | async-start | bytes 4866048 | tf_op jit(solution)/shard_map/all_gather | solution.py:41
  130.9 1.4 copy-start
  134.9 1.4 copy-start
  138.9 1.4 copy-start
  229.3 35.5 %collective-permute-start = (f32[96,1536]{1,0:T(8,128)S(1)}, f32[96,1536]{1,0:T(8,128)}, u32[]{:S(2)}, u32[]{:S(2)}) collective-permute-start(f32[96,1536]{1,0:T(8,128)S(1)} %dynamic-slice_bitcast_fusion), channel_id=1, source_target_pairs={{0,2},{2,0},{4,6},{6,4},{8,10},{10,8},{12,14},{14,12},{16,18},{18,... | collective-permute-start | bytes 1769480 | tf_op jit(solution)/shard_map/ppermute | solution.py:103
  230.8 52.5 %all-to-all-start.3 = ((bf16[16,96,192]{2,1,0:T(8,128)(2,1)}), bf16[16,96,192]{2,1,0:T(8,128)(2,1)S(1)}, u32[]{:S(2)}, u32[]{:S(2)}) async-start(bf16[16,96,192]{2,1,0:T(8,128)(2,1)} %bitcast.11), calls=%async_computation.3 | async-start | bytes 1572864 | tf_op jit(solution)/shard_map/all_to_all | solution.py:44
  264.7 23.9 %reduce-scatter.2.cloned.1.call-start = ((), (), s32[]{:S(2)}) async-start(), calls=%async_computation.7 | async-start | bytes 884736 | tf_op jit(solution)/shard_map/reduce_scatter | solution.py:104
Sparse Core Ops, SparseCore 0:
  132.7 117.1 all-gather.1
Sparse Core Ops, SparseCore 1:
  268.0 15.8 reduce-scatter.1
where the time goes:
time: 297 us; the launch traced here: 296 us
  waiting for transfers between devices  148 us (50%)
  starting transfers between devices  52.1 us (18%)
  blocking collectives  45.2 us (15%)
  matrix products  15.6 us (5%)
  between operations  15.6 us (5%)
  local copies, waits for them, and re-layouts  13.7 us (5%)
  other arithmetic  5.45 us (2%)
    all_to_all x4, waiting for transfers between devices, a2a(): lax.all_to_all(tensor, 'seq', split_axis=0, concat_axis=0, tiled=True)  148 us
    all_to_all x4, starting transfers between devices, a2a(): lax.all_to_all(tensor, 'seq', split_axis=0, concat_axis=0, tiled=True)  51.8 us
    all_to_all x1, blocking collectives, a2a(): lax.all_to_all(tensor, 'seq', split_axis=0, concat_axis=0, tiled=True)  45.2 us
  transfers between devices with their start and end apart: 7, of which 4 were waited for; matrix products, arithmetic and copies ran while one was open for 9% of the time, Pallas kernels for 0%

commit v1 on v0

v1 whole, which is shorter than its diff:
```python
import jax
import jax.numpy as jnp
from jax import lax
from jax.sharding import Mesh
from jax.sharding import PartitionSpec as P

HEADS = 8
HEAD_DIM = 192


def attend(query_here, key_all, value_all):
    query_count = query_here.shape[0]
    head_width = query_here.shape[1]
    block_size = min(512, query_count)
    score_scale = HEAD_DIM ** (-0.5)

    def one_block(query_block):
        scores = jnp.dot(query_block, key_all.T, preferred_element_type=jnp.float32) * score_scale
        largest = jnp.max(scores, axis=1, keepdims=True)
        raised = jnp.exp(scores - largest)
        denominator = jnp.sum(raised, axis=1, keepdims=True)
        weights = raised.astype(jnp.bfloat16)
        mixed = jnp.dot(weights, value_all, preferred_element_type=jnp.float32)
        return (mixed / denominator).astype(jnp.bfloat16)

    blocks = lax.map(
        one_block, query_here.reshape(query_count // block_size, block_size, head_width)
    )
    return blocks.reshape(query_count, head_width)


ALL = ("side", "inner", "dp")


def local(queries, key_vectors, value_vectors, w_out, cotangent):
    head_count = HEADS
    head_width = HEAD_DIM
    side_count = lax.axis_size("side")
    dp_count = lax.axis_size("dp")
    row_count = queries.shape[1]
    width = queries.shape[2]

    w_full = lax.all_gather(w_out, ALL, axis=0, tiled=True)
    cot_side = lax.all_gather(cotangent[0], "inner", axis=0, tiled=True)

    def a2a(tensor):
        return lax.all_to_all(tensor, "inner", split_axis=0, concat_axis=0, tiled=True)

    def by_head(tensor):
        return tensor[0].reshape(row_count, head_count, head_width).transpose(1, 0, 2)

    query_here = a2a(by_head(queries)).reshape(head_count * row_count, head_width)
    key_side = a2a(by_head(key_vectors)).reshape(head_count * row_count, head_width)
    value_side = a2a(by_head(value_vectors)).reshape(head_count * row_count, head_width)
    key_all = lax.all_gather(key_side, "side", axis=0, tiled=True)
    value_all = lax.all_gather(value_side, "side", axis=0, tiled=True)

    attended_here = attend(query_here, key_all, value_all)

    partial = lax.dot_general(
        attended_here, cot_side, (((0,), (0,)), ((), ())), preferred_element_type=jnp.float32
    )

    returned = a2a(attended_here.reshape(head_count, row_count, head_width))
    attended = returned.transpose(1, 0, 2).reshape(row_count, width)
    projected = jnp.dot(attended, w_full, preferred_element_type=jnp.float32).astype(
        jnp.bfloat16
    )

    seq_count = side_count * head_count
    if side_count == dp_count:
        reduced = lax.psum_scatter(partial, "dp", scatter_dimension=0, tiled=True)
        reduced = lax.psum_scatter(reduced, "side", scatter_dimension=0, tiled=True)
        perm = []
        for g in range(side_count):
            for h in range(head_count):
                for p in range(dp_count):
                    source = (g * head_count + h) * dp_count + p
                    target = (side_count * h + p) * dp_count + g
                    perm.append((source, target))
        grad_w_out = lax.ppermute(reduced, ALL, perm)
    else:
        reduced = lax.psum_scatter(partial, "side", scatter_dimension=0, tiled=True)
        reduced = lax.psum_scatter(reduced, "dp", scatter_dimension=0, tiled=True)
        perm = [
            (g * head_count + h, side_count * h + g)
            for g in range(side_count)
            for h in range(head_count)
        ]
        grad_w_out = lax.ppermute(reduced, ("side", "inner"), perm)
    del seq_count
    return (projected.reshape(1, row_count, width), grad_w_out)


def solution(mesh):
    seq_count = mesh.shape["seq"]
    dp_count = mesh.shape["dp"]
    fine = Mesh(
        mesh.devices.reshape(seq_count // HEADS, HEADS, dp_count), ("side", "inner", "dp")
    )
    seq = ("side", "inner")
    placed = (
        P("dp", seq, None),
        P("dp", seq, None),
        P("dp", seq, None),
        P(ALL, None),
        P("dp", seq, None),
    )
    return jax.shard_map(
        local,
        mesh=fine,
        in_specs=placed,
        out_specs=(P("dp", seq, None), P(ALL, None)),
        check_vma=False,
    )
```

time: 297 us -> 270 us (0.909)
  starting transfers between devices: 52.1 us -> 9.13 us
  blocking collectives: 45.2 us -> 57.6 us
  waiting for transfers between devices: 148 us -> 156 us
  local copies, waits for them, and re-layouts: 13.7 us -> 7.43 us
  matrix products: 15.6 us -> 20.6 us
    all_to_all x4 -> x1, waiting for transfers between devices: 148 us -> 21.6 us  [a2a(): lax.all_to_all(tensor, 'inner', split_axis=0, concat_axis=0, tiled=True)]
    all_gather x1 -> x4, waiting for transfers between devices: 0.02 us -> 112 us  [the longest x1 53.5 us: local(): w_full = lax.all_gather(w_out, ALL, axis=0, tiled=True)]
    all_to_all x4 -> x1, starting transfers between devices: 51.8 us -> 4.54 us  [a2a(): lax.all_to_all(tensor, 'inner', split_axis=0, concat_axis=0, tiled=True)]
    reduce_scatter x1 -> x2, waiting for transfers between devices: 0.01 us -> 21.5 us  [the longest x1 21.4 us: local(): reduced = lax.psum_scatter(partial, 'dp', scatter_dimension=0, tiled=True)]
    all_to_all x1 -> x3, blocking collectives: 45.2 us -> 57.6 us  [a2a(): lax.all_to_all(tensor, 'inner', split_axis=0, concat_axis=0, tiled=True)]
    dot_general x3, matrix products: 3.34 us -> 7.52 us  [one_block(): jnp.dot(query_block, key_all.T, preferred_element_type=jnp.float32)]
    broadcast_in_dim x3 -> x0, local copies, waits for them, and re-layouts: 4.18 us -> none  [the longest x1 2.68 us: local(): jnp.broadcast_to(cotangent[0].reshape(1, per_head, sub, width), (head_cou...]
    ppermute x1, starting transfers between devices: 0.24 us -> 4.38 us  [local(): grad_w_out = lax.ppermute(reduced, ALL, perm)]
  transfers between devices with their start and end apart: 7 -> 8, of which waited for: 4 -> 5; matrix products, arithmetic and copies ran while one was open for 9% -> 9% of each run, Pallas kernels for 0% -> 0%
where the time goes in v1:
time: 270 us
  waiting for transfers between devices  156 us (58%)
  blocking collectives  57.6 us (21%)
  matrix products  20.6 us (8%)
  between operations  15.3 us (6%)
  starting transfers between devices  9.13 us (3%)
  local copies, waits for them, and re-layouts  7.43 us (3%)
  other arithmetic  3.48 us (1%)
    all_to_all x3, blocking collectives, a2a(): lax.all_to_all(tensor, 'inner', split_axis=0, concat_axis=0, tiled=True)  57.6 us
    all_gather x1, waiting for transfers between devices, local(): w_full = lax.all_gather(w_out, ALL, axis=0, tiled=True)  53.5 us
    all_gather x1, waiting for transfers between devices, local(): value_all = lax.all_gather(value_side, 'side', axis=0, tiled=True)  42.1 us
    all_to_all x1, waiting for transfers between devices, a2a(): lax.all_to_all(tensor, 'inner', split_axis=0, concat_axis=0, tiled=True)  21.6 us
    reduce_scatter x1, waiting for transfers between devices, local(): reduced = lax.psum_scatter(partial, 'dp', scatter_dimension=0, tiled=True)  21.4 us
    all_gather x1, waiting for transfers between devices, local(): cot_side = lax.all_gather(cotangent[0], 'inner', axis=0, tiled=True)  16 us
    dot_general x3, matrix products, one_block(): jnp.dot(query_block, key_all.T, preferred_element_type=jnp.float32)  7.52 us
  transfers between devices with their start and end apart: 8, of which 5 were waited for; matrix products, arithmetic and copies ran while one was open for 9% of the time, Pallas kernels for 0%

profile of v1, /device:TPU:1, one launch (start us, length us, event | category | flops | bytes accessed | tf_op | source)
XLA Modules:
  0.0 269.5 jit_solution(4268551076854050702)
XLA Ops:
  8.0 0.0 copy-start
  8.0 0.0 all-gather.6.cloned.1.call-start
  8.1 1.8 reshape_squeeze.10
  9.8 0.0 copy-start.1
  9.9 0.2 copy.21
  10.0 16.2 %all_to_all.20 = bf16[8,192,192]{2,1,0:T(8,128)(2,1)} all-to-all(bf16[8,192,192]{2,1,0:T(8,128)(2,1)S(1)} %bitcast.46), channel_id=1, replica_groups=mesh['side'=2,'inner'=8,'dp'=2] {'inner'}, dimensions={0} | all-to-all | bytes 1179648 | tf_op jit(solution)/shard_map/all_to_all | solution.py:47
  26.2 0.0 all-gather.6.cloned.1.call-update
  26.3 0.0 all-gather.8.cloned.1.call-start
  26.3 0.0 copy-done
  26.3 0.6 reshape_squeeze.11
  26.9 0.2 copy.20
  27.1 19.6 %all_to_all.21 = bf16[8,192,192]{2,1,0:T(8,128)(2,1)} all-to-all(bf16[8,192,192]{2,1,0:T(8,128)(2,1)S(1)} %bitcast.47), channel_id=1, replica_groups=mesh['side'=2,'inner'=8,'dp'=2] {'inner'}, dimensions={0} | all-to-all | bytes 1179648 | tf_op jit(solution)/shard_map/all_to_all | solution.py:47
  46.7 0.0 all-gather.8.cloned.1.call-update
  46.7 0.0 all-gather.12.cloned.1.call-start
  46.8 0.7 all-gather.12.cloned.1.call-update
  47.5 0.0 copy-done.1
  47.5 0.6 reshape_squeeze.9
  48.1 1.1 copy.22
  49.1 4.5 %all-to-all-start = ((bf16[8,192,192]{2,1,0:T(8,128)(2,1)}), bf16[8,192,192]{2,1,0:T(8,128)(2,1)S(1)}, u32[]{:S(2)}, u32[]{:S(2)}) async-start(bf16[8,192,192]{2,1,0:T(8,128)(2,1)} %bitcast.34), calls=%async_computation | async-start | bytes 1572864 | tf_op jit(solution)/shard_map/all_to_all | solution.py:47
  53.7 0.0 reduce-scatter.3.cloned.1.call-start
  53.7 21.6 %all-to-all-done = bf16[8,192,192]{2,1,0:T(8,128)(2,1)S(1)} async-done(((bf16[8,192,192]{2,1,0:T(8,128)(2,1)}), bf16[8,192,192]{2,1,0:T(8,128)(2,1)S(1)}, u32[]{:S(2)}, u32[]{:S(2)}) %all-to-all-start) | async-done | bytes 589856 | tf_op jit(solution)/shard_map/all_to_all | solution.py:47
  75.2 0.0 all-gather.6.cloned.1.call-done
  75.2 42.1 %all-gather.8.cloned.1.call-done = bf16[3072,192]{1,0:T(8,128)(2,1)} async-done(((bf16[1536,192]{1,0:T(8,128)(2,1)}), bf16[3072,192]{1,0:T(8,128)(2,1)}) %all-gather.8.cloned.1.call-update) | async-done | bytes 1179664 | tf_op jit(solution)/shard_map/all_gather | solution.py:56
  117.3 16.4 %while.10 = (s32[]{:T(128)}, bf16[3,512,192]{1,2,0:T(8,128)(2,1)S(1)}, bf16[3,512,192]{2,1,0:T(8,128)(2,1)S(1)}, bf16[3072,192]{1,0:T(8,128)(2,1)}, bf16[3072,192]{1,0:T(8,128)(2,1)}, /*index=5*/s32[]{:T(128)}) while((s32[]{:T(128)}, bf16[3,512,192]{1,2,0:T(8,128)(2,1)S(1)}, bf16[3,512,192]{2,1,0:T(8,128)(2,1)S(1)}, ...), condition=%wide.region_3.4_spmd, body=%wide.region_0.3_spmd.sunk | while | flops 1220738048 | bytes 26814568 | solution.py:26
  117.3 2.5 multiply_reduce_fusion.2
  119.8 0.0 copy-start.2
  119.8 1.2 fusion.39
  121.0 0.2 copy-done.2
  121.2 1.5 fusion.40
  122.7 2.5 multiply_reduce_fusion.2
  125.2 0.0 copy-start.2
  125.2 1.2 fusion.39
  126.4 0.4 copy-done.2
  126.8 1.5 fusion.40
  128.3 2.5 multiply_reduce_fusion.2
  130.8 0.0 copy-start.2
  130.8 1.2 fusion.39
  131.9 0.3 copy-done.2
  132.2 1.5 fusion.40
  133.8 16.0 %all-gather.12.cloned.1.call-done = bf16[1,1536,1536]{2,1,0:T(8,128)(2,1)} async-done(((bf16[1,192,1536]{2,1,0:T(8,128)(2,1)}), bf16[1,1536,1536]{2,1,0:T(8,128)(2,1)}) %all-gather.12.cloned.1.call-update) | async-done | bytes 4718608 | tf_op jit(solution)/shard_map/all_gather | solution.py:44
  149.8 4.5 %fusion.23 = f32[192,1536]{1,0:T(8,128)} fusion(bf16[1536,192]{0,1:T(8,128)(2,1)S(1)} %bitcast.50, bf16[1,1536,1536]{2,1,0:T(8,128)(2,1)} %all-gather.12.cloned.1.call-done), kind=kOutput, calls=%fused_computation.16 | convolution fusion | flops 905969664 | bytes 6488064 | tf_op jit(solution)/shard_map/dot_general | solution.py:60
  154.2 0.0 reduce-scatter.3.cloned.1.call-update
  154.3 0.0 reduce-scatter.5.cloned.1.call-start
  154.3 21.4 %reduce-scatter.3.cloned.1.call-done = f32[96,1536]{1,0:T(8,128)} async-done(((f32[192,1536]{1,0:T(8,128)}), f32[96,1536]{1,0:T(8,128)}) %reduce-scatter.3.cloned.1.call-update) | async-done | bytes 589840 | tf_op jit(solution)/shard_map/reduce_scatter | solution.py:72
  175.7 0.0 reduce-scatter.5.cloned.1.call-update
  175.8 0.0 all-gather.10.cloned.1.call-start
  175.8 0.5 all-gather.10.cloned.1.call-update
  176.4 0.3 copy.13
  176.6 21.8 %all_to_all.22 = bf16[8,192,192]{2,1,0:T(8,128)(2,1)S(1)} all-to-all(bf16[8,192,192]{2,1,0:T(8,128)(2,1)S(1)} %bitcast.49), channel_id=1, replica_groups=mesh['side'=2,'inner'=8,'dp'=2] {'inner'}, dimensions={0} | all-to-all | bytes 1179648 | tf_op jit(solution)/shard_map/all_to_all | solution.py:47
  198.4 0.4 copy.14
  198.9 0.7 reshape.23
  199.5 0.0 reduce-scatter.5.cloned.1.call-done
  199.6 4.4 %collective-permute-start = (f32[48,1536]{1,0:T(8,128)}, f32[48,1536]{1,0:T(8,128)S(1)}, u32[]{:S(2)}, u32[]{:S(2)}) collective-permute-start(f32[48,1536]{1,0:T(8,128)} %reduce-scatter.5.cloned.1.call-done), channel_id=1, source_target_pairs={{0,0},{1,2},{2,4},{3,6},{4,8},{5,10},{6,12},{7,14},{8,16},{9,18},{... | collective-permute-start | bytes 884744 | tf_op jit(solution)/shard_map/ppermute | solution.py:81
  204.0 53.5 %all-gather.10.cloned.1.call-done = bf16[1536,1536]{1,0:T(8,128)(2,1)} async-done(((bf16[48,1536]{1,0:T(8,128)(2,1)}), bf16[1536,1536]{1,0:T(8,128)(2,1)}) %all-gather.10.cloned.1.call-update) | async-done | bytes 4718608 | tf_op jit(solution)/shard_map/all_gather | solution.py:43
  257.4 4.2 %fusion.25 = bf16[1,192,1536]{2,1,0:T(8,128)(2,1)} fusion(bf16[192,1536]{1,0:T(8,128)(2,1)S(1)} %reshape.23, bf16[1536,1536]{1,0:T(8,128)(2,1)} %all-gather.10.cloned.1.call-done), kind=kOutput, calls=%fused_computation.19 | convolution fusion | flops 906264576 | bytes 5898240 | tf_op jit(solution)/shard_map/dot_general | solution.py:66
  261.7 0.0 collective-permute-done
  261.7 0.7 copy.33
  (2 shorter events, 0.0 us)
Async XLA Ops:
  8.0 18.3 %copy-start = (bf16[1,192,1536]{2,1,0:T(8,128)(2,1)S(1)}, bf16[1,192,1536]{2,1,0:T(8,128)(2,1)}, u32[]{:S(2)}) copy-start(bf16[1,192,1536]{2,1,0:T(8,128)(2,1)} %param.9) | copy-start | bytes 1769476
  8.0 67.2 %all-gather.6.cloned.1.call-start = ((), (), s32[]{:S(2)}) async-start(), calls=%async_computation.6 | async-start | bytes 2359296 | tf_op jit(solution)/shard_map/all_gather | solution.py:55
  9.8 37.6 %copy-start.1 = (bf16[1,192,1536]{2,1,0:T(8,128)(2,1)S(1)}, bf16[1,192,1536]{2,1,0:T(8,128)(2,1)}, u32[]{:S(2)}) copy-start(bf16[1,192,1536]{2,1,0:T(8,128)(2,1)} %param.7) | copy-start | bytes 1769476
  26.3 91.0 %all-gather.8.cloned.1.call-start = ((), (), s32[]{:S(2)}) async-start(), calls=%async_computation.7 | async-start | bytes 2359296 | tf_op jit(solution)/shard_map/all_gather | solution.py:56
  46.7 103.1 %all-gather.12.cloned.1.call-start = ((), (), s32[]{:S(2)}) async-start(), calls=%async_computation.11 | async-start | bytes 5308416 | tf_op jit(solution)/shard_map/all_gather | solution.py:44
  49.1 26.1 %all-to-all-start = ((bf16[8,192,192]{2,1,0:T(8,128)(2,1)}), bf16[8,192,192]{2,1,0:T(8,128)(2,1)S(1)}, u32[]{:S(2)}, u32[]{:S(2)}) async-start(bf16[8,192,192]{2,1,0:T(8,128)(2,1)} %bitcast.34), calls=%async_computation | async-start | bytes 1572864 | tf_op jit(solution)/shard_map/all_to_all | solution.py:47
  53.7 122.1 %reduce-scatter.3.cloned.1.call-start = ((), (), s32[]{:S(2)}) async-start(), calls=%async_computation.9 | async-start | bytes 1769472 | tf_op jit(solution)/shard_map/reduce_scatter | solution.py:72
  119.8 1.4 copy-start.2
  125.2 1.5 copy-start.2
  130.8 1.5 copy-start.2
  154.3 45.3 %reduce-scatter.5.cloned.1.call-start = ((), (), s32[]{:S(2)}) async-start(), calls=%async_computation.10 | async-start | bytes 884736 | tf_op jit(solution)/shard_map/reduce_scatter | solution.py:73
  175.8 81.7 %all-gather.10.cloned.1.call-start = ((), (), s32[]{:S(2)}) async-start(), calls=%async_computation.8 | async-start | bytes 4866048 | tf_op jit(solution)/shard_map/all_gather | solution.py:43
  199.6 62.1 %collective-permute-start = (f32[48,1536]{1,0:T(8,128)}, f32[48,1536]{1,0:T(8,128)S(1)}, u32[]{:S(2)}, u32[]{:S(2)}) collective-permute-start(f32[48,1536]{1,0:T(8,128)} %reduce-scatter.5.cloned.1.call-done), channel_id=1, source_target_pairs={{0,0},{1,2},{2,4},{3,6},{4,8},{5,10},{6,12},{7,14},{8,16},{9,18},{... | collective-permute-start | bytes 884744 | tf_op jit(solution)/shard_map/ppermute | solution.py:81
Sparse Core Ops, SparseCore 0:
  26.4 45.3 all-gather.5
  73.3 43.9 all-gather.7
  118.9 30.7 all-gather.11
  154.4 21.3 reduce-scatter.2
  177.9 21.3 reduce-scatter.4
Sparse Core Ops, SparseCore 1:
  179.2 78.2 all-gather.9

commit v2 on v1

--- a/solution.py
+++ b/solution.py
@@ -49,11 +49,21 @@
     def by_head(tensor):
         return tensor[0].reshape(row_count, head_count, head_width).transpose(1, 0, 2)
 
-    query_here = a2a(by_head(queries)).reshape(head_count * row_count, head_width)
-    key_side = a2a(by_head(key_vectors)).reshape(head_count * row_count, head_width)
-    value_side = a2a(by_head(value_vectors)).reshape(head_count * row_count, head_width)
-    key_all = lax.all_gather(key_side, "side", axis=0, tiled=True)
-    value_all = lax.all_gather(value_side, "side", axis=0, tiled=True)
+    side_index = lax.axis_index("side")
+    stacked = jnp.concatenate(
+        [by_head(queries), by_head(key_vectors), by_head(value_vectors)], axis=2
+    )
+    got = a2a(stacked).reshape(head_count * row_count, 3 * head_width)
+    query_here = got[:, :head_width]
+    kv_side = got[:, head_width:]
+    kv_parts = [kv_side]
+    for step in range(1, side_count):
+        perm = [(g, (g + step) % side_count) for g in range(side_count)]
+        kv_parts.append(lax.ppermute(kv_side, "side", perm))
+    kv_all = jnp.concatenate(kv_parts, axis=0)
+    key_all = kv_all[:, :head_width]
+    value_all = kv_all[:, head_width:]
+    del side_index
 
     attended_here = attend(query_here, key_all, value_all)
 
@@ -67,28 +77,27 @@
         jnp.bfloat16
     )
 
-    seq_count = side_count * head_count
-    if side_count == dp_count:
-        reduced = lax.psum_scatter(partial, "dp", scatter_dimension=0, tiled=True)
-        reduced = lax.psum_scatter(reduced, "side", scatter_dimension=0, tiled=True)
+    chunk_count = side_count * dp_count
+    chunk = head_width // chunk_count
+    pieces = partial.reshape(chunk_count, chunk, width)
+    side_index = lax.axis_index("side")
+    dp_index = lax.axis_index("dp")
+    holder = side_index * dp_count + dp_index
+    grad_w_out = None
+    for step in range(chunk_count):
         perm = []
         for g in range(side_count):
             for h in range(head_count):
                 for p in range(dp_count):
+                    c = (g * dp_count + p + step) % chunk_count
                     source = (g * head_count + h) * dp_count + p
-                    target = (side_count * h + p) * dp_count + g
+                    target = (side_count * h + c // dp_count) * dp_count + c % dp_count
                     perm.append((source, target))
-        grad_w_out = lax.ppermute(reduced, ALL, perm)
-    else:
-        reduced = lax.psum_scatter(partial, "side", scatter_dimension=0, tiled=True)
-        reduced = lax.psum_scatter(reduced, "dp", scatter_dimension=0, tiled=True)
-        perm = [
-            (g * head_count + h, side_count * h + g)
-            for g in range(side_count)
-            for h in range(head_count)
-        ]
-        grad_w_out = lax.ppermute(reduced, ("side", "inner"), perm)
-    del seq_count
+        outgoing = lax.dynamic_index_in_dim(
+            pieces, (holder + step) % chunk_count, axis=0, keepdims=False
+        )
+        arrived = lax.ppermute(outgoing, ALL, perm)
+        grad_w_out = arrived if grad_w_out is None else grad_w_out + arrived
     return (projected.reshape(1, row_count, width), grad_w_out)
 
 

time: 270 us -> 205 us (0.76)
  blocking collectives: 57.6 us -> 0 us
  waiting for transfers between devices: 156 us -> 132 us
  starting transfers between devices: 9.13 us -> 20.4 us
  other arithmetic: 3.48 us -> 11.3 us
  matrix products: 20.6 us -> 15.4 us
    all_to_all x3 -> x0, blocking collectives: 57.6 us -> none  [a2a(): lax.all_to_all(tensor, 'inner', split_axis=0, concat_axis=0, tiled=True)]
    ppermute x1 -> x5, waiting for transfers between devices: 0.01 us -> 54.9 us  [the longest x1 54.9 us: local(): kv_parts.append(lax.ppermute(kv_side, 'side', perm))]
    all_to_all x1 -> x2, waiting for transfers between devices: 21.6 us -> 74.5 us  [a2a(): lax.all_to_all(tensor, 'inner', split_axis=0, concat_axis=0, tiled=True)]
    all_gather x1, waiting for transfers between devices: 53.5 us -> 1.39 us  [local(): w_full = lax.all_gather(w_out, ALL, axis=0, tiled=True)]
    all_gather x2 -> x0, waiting for transfers between devices: 42.1 us -> none  [the longest x1 42.1 us: local(): value_all = lax.all_gather(value_side, 'side', axis=0, tiled=True)]
    reduce_scatter x2 -> x0, waiting for transfers between devices: 21.5 us -> none  [the longest x1 21.4 us: local(): reduced = lax.psum_scatter(partial, 'dp', scatter_dimension=0, tiled=True)]
    all_gather x1, waiting for transfers between devices: 16 us -> 0.02 us  [local(): cot_side = lax.all_gather(cotangent[0], 'inner', axis=0, tiled=True)]
    ppermute x1 -> x5, starting transfers between devices: 4.38 us -> 10.6 us  [the longest x4 8.35 us: local(): arrived = lax.ppermute(outgoing, ALL, perm)]
  transfers between devices with their start and end apart: 8 -> 9, of which waited for: 5 -> 4; matrix products, arithmetic and copies ran while one was open for 9% -> 16% of each run, Pallas kernels for 0% -> 0%
where the time goes in v2:
time: 205 us; the launch traced here: 204 us
  waiting for transfers between devices  132 us (64%)
  starting transfers between devices  20.4 us (10%)
  matrix products  15.4 us (8%)
  between operations  14.2 us (7%)
  other arithmetic  11.3 us (6%)
  local copies, waits for them, and re-layouts  10 us (5%)
    all_to_all x2, waiting for transfers between devices, a2a(): lax.all_to_all(tensor, 'inner', split_axis=0, concat_axis=0, tiled=True)  74.5 us
    ppermute x1, waiting for transfers between devices, local(): kv_parts.append(lax.ppermute(kv_side, 'side', perm))  54.9 us
    all_to_all x2, starting transfers between devices, a2a(): lax.all_to_all(tensor, 'inner', split_axis=0, concat_axis=0, tiled=True)  9.74 us
    ppermute x4, starting transfers between devices, local(): arrived = lax.ppermute(outgoing, ALL, perm)  8.35 us
    dot_general x3, matrix products, one_block(): mixed = jnp.dot(weights, value_all, preferred_element_type=jnp.float32)  4.42 us
    dot_general x1, matrix products, local(): jnp.dot(attended, w_full, preferred_element_type=jnp.float32)  4.23 us
    another operation x4, local copies, waits for them, and re-layouts, by_head(): tensor[0].reshape(row_count, head_count, head_width).transpose(1, 0, 2)  4.22 us
  transfers between devices with their start and end apart: 9, of which 4 were waited for; matrix products, arithmetic and copies ran while one was open for 16% of the time, Pallas kernels for 0%

profile of v2, /device:TPU:1, one launch (start us, length us, event | category | flops | bytes accessed | tf_op | source)
XLA Modules:
  0.0 203.6 jit_solution(10312639095172951542)
XLA Ops:
  7.2 0.0 copy-start.1
  7.2 0.0 all-gather.6.cloned.1.call-start
  7.2 0.7 all-gather.6.cloned.1.call-update
  7.9 1.7 reshape_squeeze.11
  9.6 1.7 reshape_squeeze.10
  11.4 0.0 copy-done.1
  11.4 0.6 reshape_squeeze.9
  12.0 0.2 copy.20
  12.2 0.3 copy_bitcast_fusion
  12.5 2.1 %pad_maximum_fusion = bf16[8,192,576]{2,1,0:T(8,128)(2,1)} fusion(bf16[8,192,192]{2,1,0:T(8,128)(2,1)S(1)} %get-tuple-element.48, bf16[8,192,192]{2,1,0:T(8,128)(2,1)S(1)} %get-tuple-element.49, bf16[8,192,192]{2,1,0:T(8,128)(2,1)S(1)} %bitcast.57), kind=kLoop, calls=%fused_computation.22 | loop fusion | flops 5308416 | bytes 3538944 | tf_op jit(solution)/shard_map/concatenate | solution.py:53
  14.6 5.3 %all-to-all-start = ((bf16[8,192,576]{2,1,0:T(8,128)(2,1)}), bf16[8,192,576]{2,1,0:T(8,128)(2,1)S(1)}, u32[]{:S(2)}, u32[]{:S(2)}) async-start(bf16[8,192,576]{2,1,0:T(8,128)(2,1)} %pad_maximum_fusion), calls=%async_computation | async-start | bytes 3932160 | tf_op jit(solution)/shard_map/all_to_all | solution.py:47
  19.9 0.0 all-gather.4.cloned.1.call-start
  19.9 0.7 all-gather.4.cloned.1.call-update
  20.6 40.4 %all-to-all-done = bf16[8,192,576]{2,1,0:T(8,128)(2,1)S(1)} async-done(((bf16[8,192,576]{2,1,0:T(8,128)(2,1)}), bf16[8,192,576]{2,1,0:T(8,128)(2,1)S(1)}, u32[]{:S(2)}, u32[]{:S(2)}) %all-to-all-start) | async-done | bytes 1769504 | tf_op jit(solution)/shard_map/all_to_all | solution.py:47
  61.0 1.5 slice.17
  62.5 2.3 %collective-permute-start = (bf16[1536,384]{1,0:T(8,128)(2,1)}, bf16[1536,384]{1,0:T(8,128)(2,1)}, u32[]{:S(2)}, u32[]{:S(2)}) collective-permute-start(bf16[1536,384]{1,0:T(8,128)(2,1)} %slice.17), channel_id=1, source_target_pairs={{0,16},{16,0},{1,17},{17,1},{2,18},{18,2},{3,19},{19,3},{4,20},{20... | collective-permute-start | bytes 3538952 | tf_op jit(solution)/shard_map/ppermute | solution.py:62
  64.8 0.1 slice.16
  64.9 54.9 %collective-permute-done = bf16[1536,384]{1,0:T(8,128)(2,1)} collective-permute-done((bf16[1536,384]{1,0:T(8,128)(2,1)}, bf16[1536,384]{1,0:T(8,128)(2,1)}, u32[]{:S(2)}, u32[]{:S(2)}) %collective-permute-start) | collective-permute-done | bytes 1179680 | tf_op jit(solution)/shard_map/ppermute | solution.py:62
  119.8 3.8 %pad_maximum_fusion.1 = (bf16[3072,192]{1,0:T(8,128)(2,1)}, bf16[3072,192]{1,0:T(8,128)(2,1)S(1)}) fusion(bf16[1536,384]{1,0:T(8,128)(2,1)} %collective-permute-done, bf16[1536,384]{1,0:T(8,128)(2,1)} %slice.17), kind=kLoop, calls=%fused_computation.24 | loop fusion | flops 4718592 | bytes 4718592 | tf_op jit(solution)/shard_map/concatenate | solution.py:63
  123.6 12.0 %while.10 = (s32[]{:T(128)}, bf16[3,512,192]{1,2,0:T(8,128)(2,1)S(1)}, bf16[3,512,192]{2,1,0:T(8,128)(2,1)S(1)}, bf16[3072,192]{1,0:T(8,128)(2,1)S(1)}, bf16[3072,192]{1,0:T(8,128)(2,1)}, /*index=5*/s32[]{:T(128)}) while((s32[]{:T(128)}, bf16[3,512,192]{1,2,0:T(8,128)(2,1)S(1)}, bf16[3,512,192]{2,1,0:T(8,128)(2,1)S(1)}, ...), condition=%wide.region_3.4_spmd, body=%wide.region_0.3_spmd.sunk | while | flops 1220738048 | bytes 27207792 | solution.py:26
  123.6 1.1 multiply_reduce_fusion.2
  124.7 0.0 copy-start
  124.7 1.2 fusion.40
  125.9 0.2 copy-done
  126.1 1.5 fusion.41
  127.6 1.1 multiply_reduce_fusion.2
  128.7 0.0 copy-start
  128.7 1.2 fusion.40
  129.9 0.2 copy-done
  130.2 1.5 fusion.41
  131.6 1.1 multiply_reduce_fusion.2
  132.8 0.0 copy-start
  132.8 1.2 fusion.40
  133.9 0.2 copy-done
  134.2 1.5 fusion.41
  135.7 1.2 copy.13
  136.8 4.4 %all-to-all-start.1 = ((bf16[8,192,192]{2,1,0:T(8,128)(2,1)}), bf16[8,192,192]{2,1,0:T(8,128)(2,1)S(1)}, u32[]{:S(2)}, u32[]{:S(2)}) async-start(bf16[8,192,192]{2,1,0:T(8,128)(2,1)} %bitcast.7), calls=%async_computation.1 | async-start | bytes 1572864 | tf_op jit(solution)/shard_map/all_to_all | solution.py:47
  141.3 0.0 all-gather.6.cloned.1.call-done
  141.3 3.4 %fusion.23 = f32[4,48,1536]{2,1,0:T(8,128)S(1)} fusion(bf16[4,48,1536]{2,1,0:T(8,128)(2,1)S(1)} %bitcast.58, bf16[1,1536,1536]{2,1,0:T(8,128)(2,1)} %all-gather.6.cloned.1.call-done), kind=kOutput, calls=%fused_computation.16 | convolution fusion | flops 905969664 | bytes 6488064 | tf_op jit(solution)/shard_map/dot_general | solution.py:70
  144.8 0.8 dynamic-slice_bitcast_fusion.2
  145.6 2.4 %collective-permute-start.4 = (f32[48,1536]{1,0:T(8,128)}, f32[48,1536]{1,0:T(8,128)S(1)}, u32[]{:S(2)}, u32[]{:S(2)}) collective-permute-start(f32[48,1536]{1,0:T(8,128)} %get-tuple-element.45), channel_id=1, source_target_pairs={{0,3},{1,0},{2,7},{3,4},{4,11},{5,8},{6,15},{7,12},{8,19},{9,16},{... | collective-permute-start | bytes 884744 | tf_op jit(solution)/shard_map/ppermute | solution.py:99
  147.9 1.1 collective-permute-start.3
  149.0 4.4 %collective-permute-start.1 = (f32[48,1536]{1,0:T(8,128)S(1)}, f32[48,1536]{1,0:T(8,128)}, u32[]{:S(2)}, u32[]{:S(2)}) collective-permute-start(f32[48,1536]{1,0:T(8,128)S(1)} %get-tuple-element.47), channel_id=1, source_target_pairs={{0,0},{1,1},{2,4},{3,5},{4,8},{5,9},{6,12},{7,13},{8,16},{9,17},{1... | collective-permute-start | bytes 884744 | tf_op jit(solution)/shard_map/ppermute | solution.py:99
  153.5 0.5 collective-permute-start.2
  153.9 34.1 %all-to-all-done.1 = bf16[8,192,192]{2,1,0:T(8,128)(2,1)S(1)} async-done(((bf16[8,192,192]{2,1,0:T(8,128)(2,1)}), bf16[8,192,192]{2,1,0:T(8,128)(2,1)S(1)}, u32[]{:S(2)}, u32[]{:S(2)}) %all-to-all-start.1) | async-done | bytes 589856 | tf_op jit(solution)/shard_map/all_to_all | solution.py:47
  188.0 0.4 copy.14
  188.4 0.7 reshape.25
  189.1 0.0 collective-permute-done.4
  189.1 0.0 collective-permute-done.3
  189.2 0.0 collective-permute-done.1
  189.2 0.0 collective-permute-done.2
  189.2 1.9 add_add_fusion
  191.1 1.4 all-gather.4.cloned.1.call-done
  192.5 4.2 %fusion.25 = bf16[1,192,1536]{2,1,0:T(8,128)(2,1)} fusion(bf16[192,1536]{1,0:T(8,128)(2,1)S(1)} %reshape.25, bf16[1536,1536]{1,0:T(8,128)(2,1)} %all-gather.4.cloned.1.call-done), kind=kOutput, calls=%fused_computation.19 | convolution fusion | flops 906264576 | bytes 5898240 | tf_op jit(solution)/shard_map/dot_general | solution.py:76
  (2 shorter events, 0.0 us)
Async XLA Ops:
  7.2 4.2 %copy-start.1 = (bf16[1,192,1536]{2,1,0:T(8,128)(2,1)S(1)}, bf16[1,192,1536]{2,1,0:T(8,128)(2,1)}, u32[]{:S(2)}) copy-start(bf16[1,192,1536]{2,1,0:T(8,128)(2,1)} %param.7) | copy-start | bytes 1769476
  7.2 134.2 %all-gather.6.cloned.1.call-start = ((), (), s32[]{:S(2)}) async-start(), calls=%async_computation.3 | async-start | bytes 5308416 | tf_op jit(solution)/shard_map/all_gather | solution.py:44
  14.6 46.4 %all-to-all-start = ((bf16[8,192,576]{2,1,0:T(8,128)(2,1)}), bf16[8,192,576]{2,1,0:T(8,128)(2,1)S(1)}, u32[]{:S(2)}, u32[]{:S(2)}) async-start(bf16[8,192,576]{2,1,0:T(8,128)(2,1)} %pad_maximum_fusion), calls=%async_computation | async-start | bytes 3932160 | tf_op jit(solution)/shard_map/all_to_all | solution.py:47
  19.9 172.6 %all-gather.4.cloned.1.call-start = ((), (), s32[]{:S(2)}) async-start(), calls=%async_computation.2 | async-start | bytes 4866048 | tf_op jit(solution)/shard_map/all_gather | solution.py:43
  62.5 57.2 %collective-permute-start = (bf16[1536,384]{1,0:T(8,128)(2,1)}, bf16[1536,384]{1,0:T(8,128)(2,1)}, u32[]{:S(2)}, u32[]{:S(2)}) collective-permute-start(bf16[1536,384]{1,0:T(8,128)(2,1)} %slice.17), channel_id=1, source_target_pairs={{0,16},{16,0},{1,17},{17,1},{2,18},{18,2},{3,19},{19,3},{4,20},{20... | collective-permute-start | bytes 3538952 | tf_op jit(solution)/shard_map/ppermute | solution.py:62
  124.7 1.4 copy-start
  128.7 1.4 copy-start
  132.8 1.4 copy-start
  136.8 51.2 %all-to-all-start.1 = ((bf16[8,192,192]{2,1,0:T(8,128)(2,1)}), bf16[8,192,192]{2,1,0:T(8,128)(2,1)S(1)}, u32[]{:S(2)}, u32[]{:S(2)}) async-start(bf16[8,192,192]{2,1,0:T(8,128)(2,1)} %bitcast.7), calls=%async_computation.1 | async-start | bytes 1572864 | tf_op jit(solution)/shard_map/all_to_all | solution.py:47
  145.6 43.6 %collective-permute-start.4 = (f32[48,1536]{1,0:T(8,128)}, f32[48,1536]{1,0:T(8,128)S(1)}, u32[]{:S(2)}, u32[]{:S(2)}) collective-permute-start(f32[48,1536]{1,0:T(8,128)} %get-tuple-element.45), channel_id=1, source_target_pairs={{0,3},{1,0},{2,7},{3,4},{4,11},{5,8},{6,15},{7,12},{8,19},{9,16},{... | collective-permute-start | bytes 884744 | tf_op jit(solution)/shard_map/ppermute | solution.py:99
  147.9 41.2 %collective-permute-start.3 = (f32[48,1536]{1,0:T(8,128)S(1)}, f32[48,1536]{1,0:T(8,128)}, u32[]{:S(2)}, u32[]{:S(2)}) collective-permute-start(f32[48,1536]{1,0:T(8,128)S(1)} %get-tuple-element.46), channel_id=1, source_target_pairs={{0,2},{1,3},{2,6},{3,7},{4,10},{5,11},{6,14},{7,15},{8,18},{9,19},... | collective-permute-start | bytes 884744 | tf_op jit(solution)/shard_map/ppermute | solution.py:99
  149.0 40.1 %collective-permute-start.1 = (f32[48,1536]{1,0:T(8,128)S(1)}, f32[48,1536]{1,0:T(8,128)}, u32[]{:S(2)}, u32[]{:S(2)}) collective-permute-start(f32[48,1536]{1,0:T(8,128)S(1)} %get-tuple-element.47), channel_id=1, source_target_pairs={{0,0},{1,1},{2,4},{3,5},{4,8},{5,9},{6,12},{7,13},{8,16},{9,17},{1... | collective-permute-start | bytes 884744 | tf_op jit(solution)/shard_map/ppermute | solution.py:99
  153.5 35.7 %collective-permute-start.2 = (f32[48,1536]{1,0:T(8,128)S(1)}, f32[48,1536]{1,0:T(8,128)}, u32[]{:S(2)}, u32[]{:S(2)}) collective-permute-start(f32[48,1536]{1,0:T(8,128)S(1)} %get-tuple-element.44), channel_id=1, source_target_pairs={{0,1},{1,2},{2,5},{3,6},{4,9},{5,10},{6,13},{7,14},{8,17},{9,18},{... | collective-permute-start | bytes 884744 | tf_op jit(solution)/shard_map/ppermute | solution.py:99
Sparse Core Ops, SparseCore 0:
  9.6 54.7 all-gather.5
  67.4 125.0 all-gather.3

commit v3 on v2

--- a/solution.py
+++ b/solution.py
@@ -29,7 +29,8 @@
     return blocks.reshape(query_count, head_width)
 
 
-ALL = ("side", "inner", "dp")
+ALL = ("side", "chip", "core", "dp")
+INNER = ("chip", "core")
 
 
 def local(queries, key_vectors, value_vectors, w_out, cotangent):
@@ -40,16 +41,32 @@
     row_count = queries.shape[1]
     width = queries.shape[2]
 
-    w_full = lax.all_gather(w_out, ALL, axis=0, tiled=True)
-    cot_side = lax.all_gather(cotangent[0], "inner", axis=0, tiled=True)
+    chip_count = lax.axis_size("chip")
+    core_count = lax.axis_size("core")
+
+    def with_partner(tensor):
+        core_index = lax.axis_index("core")
+        other = lax.ppermute(tensor, "core", [(0, 1), (1, 0)])
+        first = jnp.where(core_index == 0, tensor, other)
+        second = jnp.where(core_index == 0, other, tensor)
+        return jnp.stack([first, second])
+
+    w_core = lax.all_gather(w_out, ("side", "chip", "dp"), axis=0, tiled=True)
+    w_full = (
+        with_partner(w_core)
+        .reshape(core_count, side_count, chip_count, dp_count, w_out.shape[0], width)
+        .transpose(1, 2, 0, 3, 4, 5)
+        .reshape(w_out.shape[0] * side_count * chip_count * core_count * dp_count, width)
+    )
+    cot_core = lax.all_gather(cotangent[0], "chip", axis=0, tiled=True)
+    cot_side = with_partner(cot_core).reshape(core_count * chip_count * row_count, width)
 
     def a2a(tensor):
-        return lax.all_to_all(tensor, "inner", split_axis=0, concat_axis=0, tiled=True)
+        return lax.all_to_all(tensor, INNER, split_axis=0, concat_axis=0, tiled=True)
 
     def by_head(tensor):
         return tensor[0].reshape(row_count, head_count, head_width).transpose(1, 0, 2)
 
-    side_index = lax.axis_index("side")
     stacked = jnp.concatenate(
         [by_head(queries), by_head(key_vectors), by_head(value_vectors)], axis=2
     )
@@ -63,12 +80,16 @@
     kv_all = jnp.concatenate(kv_parts, axis=0)
     key_all = kv_all[:, :head_width]
     value_all = kv_all[:, head_width:]
-    del side_index
 
     attended_here = attend(query_here, key_all, value_all)
 
+    attended_rows = (
+        attended_here.reshape(chip_count, core_count, row_count, head_width)
+        .transpose(1, 0, 2, 3)
+        .reshape(core_count * chip_count * row_count, head_width)
+    )
     partial = lax.dot_general(
-        attended_here, cot_side, (((0,), (0,)), ((), ())), preferred_element_type=jnp.float32
+        attended_rows, cot_side, (((0,), (0,)), ((), ())), preferred_element_type=jnp.float32
     )
 
     returned = a2a(attended_here.reshape(head_count, row_count, head_width))
@@ -105,9 +126,9 @@
     seq_count = mesh.shape["seq"]
     dp_count = mesh.shape["dp"]
     fine = Mesh(
-        mesh.devices.reshape(seq_count // HEADS, HEADS, dp_count), ("side", "inner", "dp")
+        mesh.devices.reshape(seq_count // HEADS, HEADS // 2, 2, dp_count), ALL
     )
-    seq = ("side", "inner")
+    seq = ("side", "chip", "core")
     placed = (
         P("dp", seq, None),
         P("dp", seq, None),

time: 205 us -> 215 us (1.049)
  the two profiles are of different devices: /device:TPU:1 before, /device:TPU:18 now
where the time goes in v3:
time: 215 us
  waiting for transfers between devices  139 us (65%)
  starting transfers between devices  21.3 us (10%)
  other arithmetic  17.3 us (8%)
  between operations  14.3 us (7%)
  local copies, waits for them, and re-layouts  11.9 us (6%)
  matrix products  10.8 us (5%)
    all_to_all x2, waiting for transfers between devices, a2a(): lax.all_to_all(tensor, INNER, split_axis=0, concat_axis=0, tiled=True)  43.4 us
    ppermute x4, waiting for transfers between devices, local(): arrived = lax.ppermute(outgoing, ALL, perm)  35.1 us
    ppermute x1, waiting for transfers between devices, local(): kv_parts.append(lax.ppermute(kv_side, 'side', perm))  31.2 us
    all_gather x1, waiting for transfers between devices, local(): cot_core = lax.all_gather(cotangent[0], 'chip', axis=0, tiled=True)  16.3 us
    all_to_all x2, starting transfers between devices, a2a(): lax.all_to_all(tensor, INNER, split_axis=0, concat_axis=0, tiled=True)  16 us
    all_gather x1, waiting for transfers between devices, local(): w_core = lax.all_gather(w_out, ('side', 'chip', 'dp'), axis=0, tiled=True)  12.4 us
    ppermute x4, starting transfers between devices, local(): arrived = lax.ppermute(outgoing, ALL, perm)  4.8 us
    dot_general x3, matrix products, one_block(): mixed = jnp.dot(weights, value_all, preferred_element_type=jnp.float32)  4.42 us
  transfers between devices with their start and end apart: 11, of which 8 were waited for; matrix products, arithmetic and copies ran while one was open for 13% of the time, Pallas kernels for 0%

profile of v3, /device:TPU:18, one launch (start us, length us, event | category | flops | bytes accessed | tf_op | source)
XLA Modules:
  0.0 214.8 jit_solution(10913653145344018132)
XLA Ops:
  7.2 0.0 copy-start.1
  7.2 1.8 reshape_squeeze.11
  9.0 1.7 reshape_squeeze.10
  10.7 0.0 copy-done.1
  10.7 0.6 reshape_squeeze.9
  11.3 0.2 copy.26
  11.5 0.3 copy_bitcast_fusion
  11.8 2.1 pad_maximum_fusion.2
  13.9 3.8 %all-to-all-start = ((bf16[8,192,576]{2,1,0:T(8,128)(2,1)}), bf16[8,192,576]{2,1,0:T(8,128)(2,1)S(1)}, u32[]{:S(2)}, u32[]{:S(2)}) async-start(bf16[8,192,576]{2,1,0:T(8,128)(2,1)} %pad_maximum_fusion.2), calls=%async_computation | async-start | bytes 3932160 | tf_op jit(solution)/shard_map/all_to_all | solution.py:65
  17.7 0.0 all-gather.6.cloned.1.call-start
  17.8 0.7 all-gather.6.cloned.1.call-update
  18.5 0.0 all-gather.4.cloned.1.call-start
  18.5 43.4 %all-to-all-done = bf16[8,192,576]{2,1,0:T(8,128)(2,1)S(1)} async-done(((bf16[8,192,576]{2,1,0:T(8,128)(2,1)}), bf16[8,192,576]{2,1,0:T(8,128)(2,1)S(1)}, u32[]{:S(2)}, u32[]{:S(2)}) %all-to-all-start) | async-done | bytes 1769504 | tf_op jit(solution)/shard_map/all_to_all | solution.py:65
  62.0 1.6 slice.17
  63.5 0.3 collective-permute-start
  63.9 0.0 all-gather.4.cloned.1.call-update
  63.9 0.1 slice.16
  64.0 16.3 %all-gather.6.cloned.1.call-done = bf16[1,768,1536]{2,1,0:T(8,128)(2,1)} async-done(((bf16[1,192,1536]{2,1,0:T(8,128)(2,1)}), bf16[1,768,1536]{2,1,0:T(8,128)(2,1)}) %all-gather.6.cloned.1.call-update) | async-done | bytes 2359312 | tf_op jit(solution)/shard_map/all_gather | solution.py:61
  80.3 0.1 collective-permute-start.2
  80.4 31.2 %collective-permute-done = bf16[1536,384]{1,0:T(8,128)(2,1)} collective-permute-done((bf16[1536,384]{1,0:T(8,128)(2,1)}, bf16[1536,384]{1,0:T(8,128)(2,1)}, u32[]{:S(2)}, u32[]{:S(2)}) %collective-permute-start) | collective-permute-done | bytes 1179680 | tf_op jit(solution)/shard_map/ppermute | solution.py:79
  111.6 3.7 %pad_maximum_fusion.3 = (bf16[3072,192]{1,0:T(8,128)(2,1)}, bf16[3072,192]{1,0:T(8,128)(2,1)S(1)}) fusion(bf16[1536,384]{1,0:T(8,128)(2,1)} %collective-permute-done, bf16[1536,384]{1,0:T(8,128)(2,1)} %slice.17), kind=kLoop, calls=%fused_computation.28 | loop fusion | flops 4718592 | bytes 4718592 | tf_op jit(solution)/shard_map/concatenate | solution.py:80
  115.3 12.1 %while.10 = (s32[]{:T(128)}, bf16[3,512,192]{1,2,0:T(8,128)(2,1)S(1)}, bf16[3,512,192]{2,1,0:T(8,128)(2,1)S(1)}, bf16[3072,192]{1,0:T(8,128)(2,1)S(1)}, bf16[3072,192]{1,0:T(8,128)(2,1)}, /*index=5*/s32[]{:T(128)}) while((s32[]{:T(128)}, bf16[3,512,192]{1,2,0:T(8,128)(2,1)S(1)}, bf16[3,512,192]{2,1,0:T(8,128)(2,1)S(1)}, ...), condition=%wide.region_3.4_spmd, body=%wide.region_0.3_spmd.sunk | while | flops 1220738048 | bytes 27207792 | solution.py:26
  115.3 1.1 multiply_reduce_fusion.2
  116.4 0.0 copy-start
  116.4 1.2 fusion.40
  117.6 0.3 copy-done
  117.8 1.5 fusion.41
  119.3 1.1 multiply_reduce_fusion.2
  120.4 0.0 copy-start
  120.4 1.2 fusion.40
  121.6 0.3 copy-done
  121.8 1.5 fusion.41
  123.3 1.1 multiply_reduce_fusion.2
  124.4 0.0 copy-start
  124.5 1.2 fusion.40
  125.6 0.2 copy-done
  125.9 1.5 fusion.41
  127.3 1.1 copy.19
  128.5 12.2 %all-to-all-start.1 = ((bf16[8,192,192]{2,1,0:T(8,128)(2,1)}), bf16[8,192,192]{2,1,0:T(8,128)(2,1)S(1)}, u32[]{:S(2)}, u32[]{:S(2)}) async-start(bf16[8,192,192]{2,1,0:T(8,128)(2,1)} %bitcast.7), calls=%async_computation.1 | async-start | bytes 1572864 | tf_op jit(solution)/shard_map/all_to_all | solution.py:65
  140.7 1.7 copy.22
  142.4 0.9 reshape.39
  143.3 12.4 %all-gather.4.cloned.1.call-done = bf16[768,1536]{1,0:T(8,128)(2,1)} async-done(((bf16[48,1536]{1,0:T(8,128)(2,1)}), bf16[768,1536]{1,0:T(8,128)(2,1)}) %all-gather.4.cloned.1.call-update) | async-done | bytes 2359312 | tf_op jit(solution)/shard_map/all_gather | solution.py:54
  155.6 0.0 collective-permute-start.1
  155.6 0.0 collective-permute-done.2
  155.6 2.7 %select_bitcast_fusion.1 = (bf16[1,768,1536]{2,1,0:T(8,128)(2,1)S(1)}, bf16[1,768,1536]{2,1,0:T(8,128)(2,1)S(1)}) fusion(bf16[768,1536]{1,0:T(8,128)(2,1)} %collective-permute-done.2, pred[]{:T(512)S(6)} %eq.11, bf16[1,768,1536]{2,1,0:T(8,128)(2,1)} %all-gather.6.cloned.1.call-done), kind=kLoop, calls=%fused_computation.23 | loop fusion | flops 2359296 | bytes 9437185 | tf_op jit(solution)/shard_map/stack | solution.py:52
  158.3 0.4 pad_maximum_fusion.1
  158.8 1.1 fusion.25
  159.8 0.1 dynamic-slice_bitcast_fusion.2
  159.9 0.1 collective-permute-start.6
  160.0 0.6 collective-permute-start.5
  160.6 4.1 %collective-permute-start.3 = (f32[48,1536]{1,0:T(8,128)S(1)}, f32[48,1536]{1,0:T(8,128)}, u32[]{:S(2)}, u32[]{:S(2)}) collective-permute-start(f32[48,1536]{1,0:T(8,128)S(1)} %get-tuple-element.51), channel_id=1, source_target_pairs={{0,0},{1,1},{2,4},{3,5},{4,8},{5,9},{6,12},{7,13},{8,16},{9,17},{1... | collective-permute-start | bytes 884744 | tf_op jit(solution)/shard_map/ppermute | solution.py:120
  164.7 0.1 collective-permute-start.4
  164.8 0.0 all-to-all-done.1
  164.8 0.4 copy.20
  165.2 0.7 reshape.36
  165.9 10.9 %collective-permute-done.6 = f32[48,1536]{1,0:T(8,128)S(1)} collective-permute-done((f32[48,1536]{1,0:T(8,128)S(1)}, f32[48,1536]{1,0:T(8,128)S(1)}, u32[]{:S(2)}, u32[]{:S(2)}) %collective-permute-start.6) | collective-permute-done | bytes 294944 | tf_op jit(solution)/shard_map/ppermute | solution.py:120
  176.8 4.3 %collective-permute-done.5 = f32[48,1536]{1,0:T(8,128)S(1)} collective-permute-done((f32[48,1536]{1,0:T(8,128)S(1)}, f32[48,1536]{1,0:T(8,128)S(1)}, u32[]{:S(2)}, u32[]{:S(2)}) %collective-permute-start.5) | collective-permute-done | bytes 294944 | tf_op jit(solution)/shard_map/ppermute | solution.py:120
  181.2 6.2 %collective-permute-done.3 = f32[48,1536]{1,0:T(8,128)} collective-permute-done((f32[48,1536]{1,0:T(8,128)S(1)}, f32[48,1536]{1,0:T(8,128)}, u32[]{:S(2)}, u32[]{:S(2)}) %collective-permute-start.3) | collective-permute-done | bytes 294944 | tf_op jit(solution)/shard_map/ppermute | solution.py:120
  187.3 13.7 %collective-permute-done.4 = f32[48,1536]{1,0:T(8,128)} collective-permute-done((f32[48,1536]{1,0:T(8,128)S(1)}, f32[48,1536]{1,0:T(8,128)}, u32[]{:S(2)}, u32[]{:S(2)}) %collective-permute-start.4) | collective-permute-done | bytes 294944 | tf_op jit(solution)/shard_map/ppermute | solution.py:120
  201.0 1.8 add_add_fusion
  202.9 0.0 collective-permute-done.1
  202.9 2.7 %broadcast_select_fusion.1 = (bf16[768,1536]{1,0:T(8,128)(2,1)S(1)}, bf16[768,1536]{1,0:T(8,128)(2,1)S(1)}) fusion(bf16[768,1536]{1,0:T(8,128)(2,1)} %all-gather.4.cloned.1.call-done, bf16[768,1536]{1,0:T(8,128)(2,1)} %collective-permute-done.1, pred[]{:T(512)S(6)} %eq.11), kind=kLoop, calls=%fused_computation.25 | loop fusion | flops 2359296 | bytes 9437185 | tf_op jit(solution)/shard_map/jit(_where)/select_n | solution.py:50
  205.5 0.4 pad_maximum_fusion
  206.0 1.9 fusion.23
  (1 shorter events, 0.0 us)
Async XLA Ops:
  7.2 3.6 %copy-start.1 = (bf16[1,192,1536]{2,1,0:T(8,128)(2,1)S(1)}, bf16[1,192,1536]{2,1,0:T(8,128)(2,1)}, u32[]{:S(2)}) copy-start(bf16[1,192,1536]{2,1,0:T(8,128)(2,1)} %param.7) | copy-start | bytes 1769476
  13.9 48.0 %all-to-all-start = ((bf16[8,192,576]{2,1,0:T(8,128)(2,1)}), bf16[8,192,576]{2,1,0:T(8,128)(2,1)S(1)}, u32[]{:S(2)}, u32[]{:S(2)}) async-start(bf16[8,192,576]{2,1,0:T(8,128)(2,1)} %pad_maximum_fusion.2), calls=%async_computation | async-start | bytes 3932160 | tf_op jit(solution)/shard_map/all_to_all | solution.py:65
  17.7 62.6 %all-gather.6.cloned.1.call-start = ((), (), s32[]{:S(2)}) async-start(), calls=%async_computation.3 | async-start | bytes 2949120 | tf_op jit(solution)/shard_map/all_gather | solution.py:61
  18.5 137.2 %all-gather.4.cloned.1.call-start = ((), (), s32[]{:S(2)}) async-start(), calls=%async_computation.2 | async-start | bytes 2506752 | tf_op jit(solution)/shard_map/all_gather | solution.py:54
  63.5 48.0 %collective-permute-start = (bf16[1536,384]{1,0:T(8,128)(2,1)}, bf16[1536,384]{1,0:T(8,128)(2,1)}, u32[]{:S(2)}, u32[]{:S(2)}) collective-permute-start(bf16[1536,384]{1,0:T(8,128)(2,1)} %slice.17), channel_id=1, source_target_pairs={{0,16},{16,0},{1,17},{17,1},{2,18},{18,2},{3,19},{19,3},{4,20},{20... | collective-permute-start | bytes 3538952 | tf_op jit(solution)/shard_map/ppermute | solution.py:79
  80.3 75.3 %collective-permute-start.2 = (bf16[768,1536]{1,0:T(8,128)(2,1)}, bf16[768,1536]{1,0:T(8,128)(2,1)}, u32[]{:S(2)}, u32[]{:S(2)}) collective-permute-start(bf16[768,1536]{1,0:T(8,128)(2,1)} %bitcast.77), channel_id=1, source_target_pairs={{0,2},{2,0},{1,3},{3,1},{4,6},{6,4},{5,7},{7,5},{8,10},{10,8},{9,1... | collective-permute-start | bytes 7077896 | tf_op jit(solution)/shard_map/ppermute | solution.py:49
  116.4 1.4 copy-start
  120.4 1.4 copy-start
  124.4 1.4 copy-start
  128.5 36.3 %all-to-all-start.1 = ((bf16[8,192,192]{2,1,0:T(8,128)(2,1)}), bf16[8,192,192]{2,1,0:T(8,128)(2,1)S(1)}, u32[]{:S(2)}, u32[]{:S(2)}) async-start(bf16[8,192,192]{2,1,0:T(8,128)(2,1)} %bitcast.7), calls=%async_computation.1 | async-start | bytes 1572864 | tf_op jit(solution)/shard_map/all_to_all | solution.py:65
  155.6 47.2 %collective-permute-start.1 = (bf16[768,1536]{1,0:T(8,128)(2,1)}, bf16[768,1536]{1,0:T(8,128)(2,1)}, u32[]{:S(2)}, u32[]{:S(2)}) collective-permute-start(bf16[768,1536]{1,0:T(8,128)(2,1)} %all-gather.4.cloned.1.call-done), channel_id=1, source_target_pairs={{0,2},{2,0},{1,3},{3,1},{4,6},{6,4},{5,7},{7,5},{8,10},{10,8},{9,1... | collective-permute-start | bytes 7077896 | tf_op jit(solution)/shard_map/ppermute | solution.py:49
  159.9 16.9 %collective-permute-start.6 = (f32[48,1536]{1,0:T(8,128)S(1)}, f32[48,1536]{1,0:T(8,128)S(1)}, u32[]{:S(2)}, u32[]{:S(2)}) collective-permute-start(f32[48,1536]{1,0:T(8,128)S(1)} %get-tuple-element.49), channel_id=1, source_target_pairs={{0,3},{1,0},{2,7},{3,4},{4,11},{5,8},{6,15},{7,12},{8,19},{9,16},{... | collective-permute-start | bytes 884744 | tf_op jit(solution)/shard_map/ppermute | solution.py:120
  160.0 21.1 %collective-permute-start.5 = (f32[48,1536]{1,0:T(8,128)S(1)}, f32[48,1536]{1,0:T(8,128)S(1)}, u32[]{:S(2)}, u32[]{:S(2)}) collective-permute-start(f32[48,1536]{1,0:T(8,128)S(1)} %get-tuple-element.50), channel_id=1, source_target_pairs={{0,2},{1,3},{2,6},{3,7},{4,10},{5,11},{6,14},{7,15},{8,18},{9,19},... | collective-permute-start | bytes 884744 | tf_op jit(solution)/shard_map/ppermute | solution.py:120
  160.6 26.7 %collective-permute-start.3 = (f32[48,1536]{1,0:T(8,128)S(1)}, f32[48,1536]{1,0:T(8,128)}, u32[]{:S(2)}, u32[]{:S(2)}) collective-permute-start(f32[48,1536]{1,0:T(8,128)S(1)} %get-tuple-element.51), channel_id=1, source_target_pairs={{0,0},{1,1},{2,4},{3,5},{4,8},{5,9},{6,12},{7,13},{8,16},{9,17},{1... | collective-permute-start | bytes 884744 | tf_op jit(solution)/shard_map/ppermute | solution.py:120
  164.7 36.3 %collective-permute-start.4 = (f32[48,1536]{1,0:T(8,128)S(1)}, f32[48,1536]{1,0:T(8,128)}, u32[]{:S(2)}, u32[]{:S(2)}) collective-permute-start(f32[48,1536]{1,0:T(8,128)S(1)} %get-tuple-element.48), channel_id=1, source_target_pairs={{0,1},{1,2},{2,5},{3,6},{4,9},{5,10},{6,13},{7,14},{8,17},{9,18},{... | collective-permute-start | bytes 884744 | tf_op jit(solution)/shard_map/ppermute | solution.py:120
Sparse Core Ops, SparseCore 0:
  20.1 60.1 all-gather.5
  83.1 72.4 all-gather.3

commit v4 on v3

--- a/solution.py
+++ b/solution.py
@@ -52,12 +52,6 @@
         return jnp.stack([first, second])
 
     w_core = lax.all_gather(w_out, ("side", "chip", "dp"), axis=0, tiled=True)
-    w_full = (
-        with_partner(w_core)
-        .reshape(core_count, side_count, chip_count, dp_count, w_out.shape[0], width)
-        .transpose(1, 2, 0, 3, 4, 5)
-        .reshape(w_out.shape[0] * side_count * chip_count * core_count * dp_count, width)
-    )
     cot_core = lax.all_gather(cotangent[0], "chip", axis=0, tiled=True)
     cot_side = with_partner(cot_core).reshape(core_count * chip_count * row_count, width)
 
@@ -67,16 +61,17 @@
     def by_head(tensor):
         return tensor[0].reshape(row_count, head_count, head_width).transpose(1, 0, 2)
 
-    stacked = jnp.concatenate(
-        [by_head(queries), by_head(key_vectors), by_head(value_vectors)], axis=2
-    )
+    kv_raw = jnp.concatenate([by_head(key_vectors), by_head(value_vectors)], axis=2)
+    kv_crossed = [
+        lax.ppermute(kv_raw, "side", [(g, (g + step) % side_count) for g in range(side_count)])
+        for step in range(1, side_count)
+    ]
+    stacked = jnp.concatenate([by_head(queries), kv_raw], axis=2)
     got = a2a(stacked).reshape(head_count * row_count, 3 * head_width)
     query_here = got[:, :head_width]
-    kv_side = got[:, head_width:]
-    kv_parts = [kv_side]
-    for step in range(1, side_count):
-        perm = [(g, (g + step) % side_count) for g in range(side_count)]
-        kv_parts.append(lax.ppermute(kv_side, "side", perm))
+    kv_parts = [got[:, head_width:]]
+    for crossed in kv_crossed:
+        kv_parts.append(a2a(crossed).reshape(head_count * row_count, 2 * head_width))
     kv_all = jnp.concatenate(kv_parts, axis=0)
     key_all = kv_all[:, :head_width]
     value_all = kv_all[:, head_width:]
@@ -94,9 +89,17 @@
 
     returned = a2a(attended_here.reshape(head_count, row_count, head_width))
     attended = returned.transpose(1, 0, 2).reshape(row_count, width)
-    projected = jnp.dot(attended, w_full, preferred_element_type=jnp.float32).astype(
-        jnp.bfloat16
+    core_index = lax.axis_index("core")
+    by_core = attended.reshape(
+        row_count, side_count, chip_count, core_count, dp_count, w_out.shape[0]
     )
+    mine = lax.dynamic_index_in_dim(by_core, core_index, axis=3, keepdims=False)
+    theirs = lax.dynamic_index_in_dim(by_core, 1 - core_index, axis=3, keepdims=False)
+    w_partner = lax.ppermute(w_core, "core", [(0, 1), (1, 0)])
+    projected = (
+        jnp.dot(mine.reshape(row_count, -1), w_core, preferred_element_type=jnp.float32)
+        + jnp.dot(theirs.reshape(row_count, -1), w_partner, preferred_element_type=jnp.float32)
+    ).astype(jnp.bfloat16)
 
     chunk_count = side_count * dp_count
     chunk = head_width // chunk_count

time: 215 us -> 212 us (0.986)
  the two profiles are of different devices: /device:TPU:18 before, /device:TPU:8 now
where the time goes in v4:
time: 212 us
  waiting for transfers between devices  137 us (65%)
  starting transfers between devices  23.9 us (11%)
  between operations  14.2 us (7%)
  other arithmetic  13.8 us (7%)
  local copies, waits for them, and re-layouts  11.2 us (5%)
  matrix products  11 us (5%)
    ppermute x1, waiting for transfers between devices, local(): lax.ppermute(kv_raw, 'side', [(g, (g + step) % side_count) for g in range...  63.9 us
    ppermute x4, waiting for transfers between devices, local(): arrived = lax.ppermute(outgoing, ALL, perm)  32.8 us
    all_to_all x3, waiting for transfers between devices, a2a(): lax.all_to_all(tensor, INNER, split_axis=0, concat_axis=0, tiled=True)  22.7 us
    all_gather x1, waiting for transfers between devices, local(): w_core = lax.all_gather(w_out, ('side', 'chip', 'dp'), axis=0, tiled=True)  16.6 us
    all_to_all x3, starting transfers between devices, a2a(): lax.all_to_all(tensor, INNER, split_axis=0, concat_axis=0, tiled=True)  14 us
    ppermute x4, starting transfers between devices, local(): arrived = lax.ppermute(outgoing, ALL, perm)  7.32 us
    dot_general x3, matrix products, one_block(): mixed = jnp.dot(weights, value_all, preferred_element_type=jnp.float32)  4.41 us
    another operation x4, local copies, waits for them, and re-layouts, by_head(): tensor[0].reshape(row_count, head_count, head_width).transpose(1, 0, 2)  4.28 us
  transfers between devices with their start and end apart: 12, of which 8 were waited for; matrix products, arithmetic and copies ran while one was open for 13% of the time, Pallas kernels for 0%

profile of v4, /device:TPU:8, one launch (start us, length us, event | category | flops | bytes accessed | tf_op | source)
XLA Modules:
  0.0 211.5 jit_solution(15641789123049269678)
XLA Ops:
  7.2 0.0 copy-start.2
  7.2 1.8 reshape_squeeze.11
  9.0 1.7 reshape_squeeze.10
  10.7 0.0 copy-done.2
  10.7 0.6 reshape_squeeze.9
  11.3 0.2 copy.26
  11.5 0.3 copy_bitcast_fusion
  11.8 2.1 pad_maximum_fusion.1
  13.9 4.3 %all-to-all-start = ((bf16[8,192,576]{2,1,0:T(8,128)(2,1)}), bf16[8,192,576]{2,1,0:T(8,128)(2,1)S(1)}, u32[]{:S(2)}, u32[]{:S(2)}) async-start(bf16[8,192,576]{2,1,0:T(8,128)(2,1)} %pad_maximum_fusion.1), calls=%async_computation | async-start | bytes 3932160 | tf_op jit(solution)/shard_map/all_to_all | solution.py:59
  18.2 0.0 all-gather.6.cloned.1.call-start
  18.2 0.7 all-gather.6.cloned.1.call-update
  18.9 0.4 pad_maximum_fusion.3
  19.3 2.7 %collective-permute-start = (bf16[8,192,384]{2,1,0:T(8,128)(2,1)S(1)}, bf16[8,192,384]{2,1,0:T(8,128)(2,1)}, u32[]{:S(2)}, u32[]{:S(2)}) collective-permute-start(bf16[8,192,384]{2,1,0:T(8,128)(2,1)S(1)} %pad_maximum_fusion.3), channel_id=1, source_target_pairs={{0,16},{16,0},{1,17},{17,1},{2,18},{18,2},{3,19},{19,3},{4,20},{20... | collective-permute-start | bytes 3538952 | tf_op jit(solution)/shard_map/ppermute | solution.py:66
  22.0 63.9 %collective-permute-done = bf16[8,192,384]{2,1,0:T(8,128)(2,1)} collective-permute-done((bf16[8,192,384]{2,1,0:T(8,128)(2,1)S(1)}, bf16[8,192,384]{2,1,0:T(8,128)(2,1)}, u32[]{:S(2)}, u32[]{:S(2)}) %collective-permute-start) | collective-permute-done | bytes 1179680 | tf_op jit(solution)/shard_map/ppermute | solution.py:66
  85.9 0.0 all-to-all-done
  85.9 5.7 %all-to-all-start.1 = ((bf16[8,192,384]{2,1,0:T(8,128)(2,1)}), bf16[8,192,384]{2,1,0:T(8,128)(2,1)}, u32[]{:S(2)}, u32[]{:S(2)}) async-start(bf16[8,192,384]{2,1,0:T(8,128)(2,1)} %collective-permute-done), calls=%async_computation.1 | async-start | bytes 2359296 | tf_op jit(solution)/shard_map/all_to_all | solution.py:59
  91.6 0.0 all-gather.4.cloned.1.call-start
  91.6 0.7 all-gather.4.cloned.1.call-update
  92.3 0.1 slice.16
  92.4 1.5 slice.17
  93.9 14.1 %all-to-all-done.1 = bf16[8,192,384]{2,1,0:T(8,128)(2,1)} async-done(((bf16[8,192,384]{2,1,0:T(8,128)(2,1)}), bf16[8,192,384]{2,1,0:T(8,128)(2,1)}, u32[]{:S(2)}, u32[]{:S(2)}) %all-to-all-start.1) | async-done | bytes 1179680 | tf_op jit(solution)/shard_map/all_to_all | solution.py:59
  108.0 3.9 %pad_maximum_fusion.2 = (bf16[3072,192]{1,0:T(8,128)(2,1)}, bf16[3072,192]{1,0:T(8,128)(2,1)S(1)}) fusion(bf16[1536,384]{1,0:T(8,128)(2,1)} %bitcast.7, bf16[1536,384]{1,0:T(8,128)(2,1)} %slice.17), kind=kLoop, calls=%fused_computation.26 | loop fusion | flops 4718592 | bytes 4718592 | tf_op jit(solution)/shard_map/concatenate | solution.py:75
  111.9 0.0 collective-permute-start.2
  111.9 12.0 %while.10 = (s32[]{:T(128)}, bf16[3,512,192]{1,2,0:T(8,128)(2,1)S(1)}, bf16[3,512,192]{2,1,0:T(8,128)(2,1)S(1)}, bf16[3072,192]{1,0:T(8,128)(2,1)S(1)}, bf16[3072,192]{1,0:T(8,128)(2,1)}, /*index=5*/s32[]{:T(128)}) while((s32[]{:T(128)}, bf16[3,512,192]{1,2,0:T(8,128)(2,1)S(1)}, bf16[3,512,192]{2,1,0:T(8,128)(2,1)S(1)}, ...), condition=%wide.region_3.4_spmd, body=%wide.region_0.3_spmd.sunk | while | flops 1220738048 | bytes 27207792 | solution.py:26
  111.9 1.1 multiply_reduce_fusion.2
  113.1 1.2 fusion.44
  114.2 0.2 copy-done.1
  114.5 1.5 fusion.45
  116.0 1.1 multiply_reduce_fusion.2
  117.1 1.2 fusion.44
  118.2 0.2 copy-done.1
  118.5 1.5 fusion.45
  120.0 1.1 multiply_reduce_fusion.2
  121.1 1.2 fusion.44
  122.3 0.2 copy-done.1
  122.5 1.5 fusion.45
  124.0 1.2 copy.19
  125.1 4.0 %all-to-all-start.2 = ((bf16[8,192,192]{2,1,0:T(8,128)(2,1)}), bf16[8,192,192]{2,1,0:T(8,128)(2,1)S(1)}, u32[]{:S(2)}, u32[]{:S(2)}) async-start(bf16[8,192,192]{2,1,0:T(8,128)(2,1)} %bitcast.8), calls=%async_computation.2 | async-start | bytes 1572864 | tf_op jit(solution)/shard_map/all_to_all | solution.py:59
  129.2 1.7 copy.22
  130.9 0.9 reshape.40
  131.7 8.6 %all-to-all-done.2 = bf16[8,192,192]{2,1,0:T(8,128)(2,1)S(1)} async-done(((bf16[8,192,192]{2,1,0:T(8,128)(2,1)}), bf16[8,192,192]{2,1,0:T(8,128)(2,1)S(1)}, u32[]{:S(2)}, u32[]{:S(2)}) %all-to-all-start.2) | async-done | bytes 589856 | tf_op jit(solution)/shard_map/all_to_all | solution.py:59
  140.3 0.3 copy.20
  140.6 0.1 constant_dynamic-slice_fusion
  140.7 16.6 %all-gather.4.cloned.1.call-done = bf16[768,1536]{1,0:T(8,128)(2,1)} async-done(((bf16[48,1536]{1,0:T(8,128)(2,1)}), bf16[768,1536]{1,0:T(8,128)(2,1)}) %all-gather.4.cloned.1.call-update) | async-done | bytes 2359312 | tf_op jit(solution)/shard_map/all_gather | solution.py:54
  157.3 0.0 collective-permute-start.1
  157.3 0.0 collective-permute-done.2
  157.3 2.7 %select_bitcast_fusion.1 = (bf16[1,768,1536]{2,1,0:T(8,128)(2,1)S(1)}, bf16[1,768,1536]{2,1,0:T(8,128)(2,1)S(1)}) fusion(bf16[768,1536]{1,0:T(8,128)(2,1)} %collective-permute-done.2, pred[]{:T(512)S(6)} %eq.9, bf16[1,768,1536]{2,1,0:T(8,128)(2,1)} %all-gather.6.cloned.1.call-done), kind=kLoop, calls=%fused_computation.23 | loop fusion | flops 2359296 | bytes 9437185 | tf_op jit(solution)/shard_map/stack | solution.py:52
  160.0 0.4 pad_maximum_fusion
  160.5 1.1 fusion.27
  161.5 0.0 copy-start
  161.6 0.1 dynamic-slice_bitcast_fusion.2
  161.7 1.9 collective-permute-start.6
  163.5 0.4 collective-permute-start.5
  163.9 2.8 %collective-permute-start.3 = (f32[48,1536]{1,0:T(8,128)S(1)}, f32[48,1536]{1,0:T(8,128)S(1)}, u32[]{:S(2)}, u32[]{:S(2)}) collective-permute-start(f32[48,1536]{1,0:T(8,128)S(1)} %get-tuple-element.49), channel_id=1, source_target_pairs={{0,0},{1,1},{2,4},{3,5},{4,8},{5,9},{6,12},{7,13},{8,16},{9,17},{1... | collective-permute-start | bytes 884744 | tf_op jit(solution)/shard_map/ppermute | solution.py:123
  166.8 2.2 %collective-permute-start.4 = (f32[48,1536]{1,0:T(8,128)S(1)}, f32[48,1536]{1,0:T(8,128)S(1)}, u32[]{:S(2)}, u32[]{:S(2)}) collective-permute-start(f32[48,1536]{1,0:T(8,128)S(1)} %get-tuple-element.46), channel_id=1, source_target_pairs={{0,1},{1,2},{2,5},{3,6},{4,9},{5,10},{6,13},{7,14},{8,17},{9,18},{... | collective-permute-start | bytes 884744 | tf_op jit(solution)/shard_map/ppermute | solution.py:123
  169.0 0.0 copy-done
  169.0 0.7 fusion.26
  169.7 10.2 %collective-permute-done.6 = f32[48,1536]{1,0:T(8,128)S(1)} collective-permute-done((f32[48,1536]{1,0:T(8,128)S(1)}, f32[48,1536]{1,0:T(8,128)S(1)}, u32[]{:S(2)}, u32[]{:S(2)}) %collective-permute-start.6) | collective-permute-done | bytes 294944 | tf_op jit(solution)/shard_map/ppermute | solution.py:123
  179.8 5.0 %collective-permute-done.5 = f32[48,1536]{1,0:T(8,128)S(1)} collective-permute-done((f32[48,1536]{1,0:T(8,128)S(1)}, f32[48,1536]{1,0:T(8,128)S(1)}, u32[]{:S(2)}, u32[]{:S(2)}) %collective-permute-start.5) | collective-permute-done | bytes 294944 | tf_op jit(solution)/shard_map/ppermute | solution.py:123
  184.8 6.4 %collective-permute-done.3 = f32[48,1536]{1,0:T(8,128)S(1)} collective-permute-done((f32[48,1536]{1,0:T(8,128)S(1)}, f32[48,1536]{1,0:T(8,128)S(1)}, u32[]{:S(2)}, u32[]{:S(2)}) %collective-permute-start.3) | collective-permute-done | bytes 294944 | tf_op jit(solution)/shard_map/ppermute | solution.py:123
  191.3 11.1 %collective-permute-done.4 = f32[48,1536]{1,0:T(8,128)S(1)} collective-permute-done((f32[48,1536]{1,0:T(8,128)S(1)}, f32[48,1536]{1,0:T(8,128)S(1)}, u32[]{:S(2)}, u32[]{:S(2)}) %collective-permute-start.4) | collective-permute-done | bytes 294944 | tf_op jit(solution)/shard_map/ppermute | solution.py:123
  202.4 0.8 add_add_fusion
  203.2 0.0 collective-permute-done.1
  203.2 1.5 fusion.24
  (5 shorter events, 0.0 us)
Async XLA Ops:
  7.2 3.6 %copy-start.2 = (bf16[1,192,1536]{2,1,0:T(8,128)(2,1)S(1)}, bf16[1,192,1536]{2,1,0:T(8,128)(2,1)}, u32[]{:S(2)}) copy-start(bf16[1,192,1536]{2,1,0:T(8,128)(2,1)} %param.7) | copy-start | bytes 1769476
  13.9 72.0 %all-to-all-start = ((bf16[8,192,576]{2,1,0:T(8,128)(2,1)}), bf16[8,192,576]{2,1,0:T(8,128)(2,1)S(1)}, u32[]{:S(2)}, u32[]{:S(2)}) async-start(bf16[8,192,576]{2,1,0:T(8,128)(2,1)} %pad_maximum_fusion.1), calls=%async_computation | async-start | bytes 3932160 | tf_op jit(solution)/shard_map/all_to_all | solution.py:59
  18.2 93.8 %all-gather.6.cloned.1.call-start = ((), (), s32[]{:S(2)}) async-start(), calls=%async_computation.4 | async-start | bytes 2949120 | tf_op jit(solution)/shard_map/all_gather | solution.py:55
  19.3 66.6 %collective-permute-start = (bf16[8,192,384]{2,1,0:T(8,128)(2,1)S(1)}, bf16[8,192,384]{2,1,0:T(8,128)(2,1)}, u32[]{:S(2)}, u32[]{:S(2)}) collective-permute-start(bf16[8,192,384]{2,1,0:T(8,128)(2,1)S(1)} %pad_maximum_fusion.3), channel_id=1, source_target_pairs={{0,16},{16,0},{1,17},{17,1},{2,18},{18,2},{3,19},{19,3},{4,20},{20... | collective-permute-start | bytes 3538952 | tf_op jit(solution)/shard_map/ppermute | solution.py:66
  85.9 22.1 %all-to-all-start.1 = ((bf16[8,192,384]{2,1,0:T(8,128)(2,1)}), bf16[8,192,384]{2,1,0:T(8,128)(2,1)}, u32[]{:S(2)}, u32[]{:S(2)}) async-start(bf16[8,192,384]{2,1,0:T(8,128)(2,1)} %collective-permute-done), calls=%async_computation.1 | async-start | bytes 2359296 | tf_op jit(solution)/shard_map/all_to_all | solution.py:59
  91.6 65.8 %all-gather.4.cloned.1.call-start = ((), (), s32[]{:S(2)}) async-start(), calls=%async_computation.3 | async-start | bytes 2506752 | tf_op jit(solution)/shard_map/all_gather | solution.py:54
  111.9 45.4 %collective-permute-start.2 = (bf16[768,1536]{1,0:T(8,128)(2,1)}, bf16[768,1536]{1,0:T(8,128)(2,1)}, u32[]{:S(2)}, u32[]{:S(2)}) collective-permute-start(bf16[768,1536]{1,0:T(8,128)(2,1)} %bitcast.76), channel_id=1, source_target_pairs={{0,2},{2,0},{1,3},{3,1},{4,6},{6,4},{5,7},{7,5},{8,10},{10,8},{9,1... | collective-permute-start | bytes 7077896 | tf_op jit(solution)/shard_map/ppermute | solution.py:49
  113.1 1.4 copy-start.1
  117.1 1.4 copy-start.1
  121.1 1.4 copy-start.1
  125.1 15.1 %all-to-all-start.2 = ((bf16[8,192,192]{2,1,0:T(8,128)(2,1)}), bf16[8,192,192]{2,1,0:T(8,128)(2,1)S(1)}, u32[]{:S(2)}, u32[]{:S(2)}) async-start(bf16[8,192,192]{2,1,0:T(8,128)(2,1)} %bitcast.8), calls=%async_computation.2 | async-start | bytes 1572864 | tf_op jit(solution)/shard_map/all_to_all | solution.py:59
  157.3 45.9 %collective-permute-start.1 = (bf16[768,1536]{1,0:T(8,128)(2,1)}, bf16[768,1536]{1,0:T(8,128)(2,1)S(1)}, u32[]{:S(2)}, u32[]{:S(2)}) collective-permute-start(bf16[768,1536]{1,0:T(8,128)(2,1)} %all-gather.4.cloned.1.call-done), channel_id=1, source_target_pairs={{0,2},{2,0},{1,3},{3,1},{4,6},{6,4},{5,7},{7,5},{8,10},{10,8},{9,1... | collective-permute-start | bytes 7077896 | tf_op jit(solution)/shard_map/ppermute | solution.py:98
  161.5 7.4 %copy-start = (bf16[768,1536]{1,0:T(8,128)(2,1)S(1)}, bf16[768,1536]{1,0:T(8,128)(2,1)}, u32[]{:S(2)}) copy-start(bf16[768,1536]{1,0:T(8,128)(2,1)} %all-gather.4.cloned.1.call-done) | copy-start | bytes 7077892
  161.7 18.2 %collective-permute-start.6 = (f32[48,1536]{1,0:T(8,128)S(1)}, f32[48,1536]{1,0:T(8,128)S(1)}, u32[]{:S(2)}, u32[]{:S(2)}) collective-permute-start(f32[48,1536]{1,0:T(8,128)S(1)} %get-tuple-element.47), channel_id=1, source_target_pairs={{0,3},{1,0},{2,7},{3,4},{4,11},{5,8},{6,15},{7,12},{8,19},{9,16},{... | collective-permute-start | bytes 884744 | tf_op jit(solution)/shard_map/ppermute | solution.py:123
  163.5 21.3 %collective-permute-start.5 = (f32[48,1536]{1,0:T(8,128)S(1)}, f32[48,1536]{1,0:T(8,128)S(1)}, u32[]{:S(2)}, u32[]{:S(2)}) collective-permute-start(f32[48,1536]{1,0:T(8,128)S(1)} %get-tuple-element.48), channel_id=1, source_target_pairs={{0,2},{1,3},{2,6},{3,7},{4,10},{5,11},{6,14},{7,15},{8,18},{9,19},... | collective-permute-start | bytes 884744 | tf_op jit(solution)/shard_map/ppermute | solution.py:123
  163.9 27.3 %collective-permute-start.3 = (f32[48,1536]{1,0:T(8,128)S(1)}, f32[48,1536]{1,0:T(8,128)S(1)}, u32[]{:S(2)}, u32[]{:S(2)}) collective-permute-start(f32[48,1536]{1,0:T(8,128)S(1)} %get-tuple-element.49), channel_id=1, source_target_pairs={{0,0},{1,1},{2,4},{3,5},{4,8},{5,9},{6,12},{7,13},{8,16},{9,17},{1... | collective-permute-start | bytes 884744 | tf_op jit(solution)/shard_map/ppermute | solution.py:123
  166.8 35.6 %collective-permute-start.4 = (f32[48,1536]{1,0:T(8,128)S(1)}, f32[48,1536]{1,0:T(8,128)S(1)}, u32[]{:S(2)}, u32[]{:S(2)}) collective-permute-start(f32[48,1536]{1,0:T(8,128)S(1)} %get-tuple-element.46), channel_id=1, source_target_pairs={{0,1},{1,2},{2,5},{3,6},{4,9},{5,10},{6,13},{7,14},{8,17},{9,18},{... | collective-permute-start | bytes 884744 | tf_op jit(solution)/shard_map/ppermute | solution.py:123
Sparse Core Ops, SparseCore 0:
  20.5 66.9 all-gather.5
  95.2 62.0 all-gather.3

commit v5 on v2

--- a/solution.py
+++ b/solution.py
@@ -40,7 +40,15 @@
     row_count = queries.shape[1]
     width = queries.shape[2]
 
-    w_full = lax.all_gather(w_out, ALL, axis=0, tiled=True)
+    dp_index = lax.axis_index("dp")
+    w_other = lax.ppermute(w_out, "dp", [(p, (p + 1) % dp_count) for p in range(dp_count)])
+    if dp_count == 2:
+        w_pair = jnp.stack(
+            [jnp.where(dp_index == 0, w_out, w_other), jnp.where(dp_index == 0, w_other, w_out)]
+        )
+        w_full = lax.all_gather(w_pair, ("side", "inner"), axis=0, tiled=True).reshape(-1, width)
+    else:
+        w_full = lax.all_gather(w_out, ALL, axis=0, tiled=True)
     cot_side = lax.all_gather(cotangent[0], "inner", axis=0, tiled=True)
 
     def a2a(tensor):
@@ -79,25 +87,45 @@
 
     chunk_count = side_count * dp_count
     chunk = head_width // chunk_count
-    pieces = partial.reshape(chunk_count, chunk, width)
     side_index = lax.axis_index("side")
-    dp_index = lax.axis_index("dp")
-    holder = side_index * dp_count + dp_index
-    grad_w_out = None
-    for step in range(chunk_count):
-        perm = []
-        for g in range(side_count):
-            for h in range(head_count):
-                for p in range(dp_count):
-                    c = (g * dp_count + p + step) % chunk_count
-                    source = (g * head_count + h) * dp_count + p
-                    target = (side_count * h + c // dp_count) * dp_count + c % dp_count
-                    perm.append((source, target))
-        outgoing = lax.dynamic_index_in_dim(
-            pieces, (holder + step) % chunk_count, axis=0, keepdims=False
-        )
-        arrived = lax.ppermute(outgoing, ALL, perm)
-        grad_w_out = arrived if grad_w_out is None else grad_w_out + arrived
+    if dp_count == 2:
+        pieces = partial.reshape(side_count, dp_count, chunk, width)
+        kept = lax.dynamic_index_in_dim(pieces, dp_index, axis=1, keepdims=False)
+        sent = lax.dynamic_index_in_dim(pieces, 1 - dp_index, axis=1, keepdims=False)
+        kept = kept + lax.ppermute(sent, "dp", [(0, 1), (1, 0)])
+        grad_w_out = None
+        for step in range(side_count):
+            perm = []
+            for g in range(side_count):
+                for h in range(head_count):
+                    for p in range(dp_count):
+                        owner_side = (g + step) % side_count
+                        source = (g * head_count + h) * dp_count + p
+                        target = (side_count * h + owner_side) * dp_count + p
+                        perm.append((source, target))
+            outgoing = lax.dynamic_index_in_dim(
+                kept, (side_index + step) % side_count, axis=0, keepdims=False
+            )
+            arrived = lax.ppermute(outgoing, ALL, perm)
+            grad_w_out = arrived if grad_w_out is None else grad_w_out + arrived
+    else:
+        pieces = partial.reshape(chunk_count, chunk, width)
+        holder = side_index * dp_count + dp_index
+        grad_w_out = None
+        for step in range(chunk_count):
+            perm = []
+            for g in range(side_count):
+                for h in range(head_count):
+                    for p in range(dp_count):
+                        c = (g * dp_count + p + step) % chunk_count
+                        source = (g * head_count + h) * dp_count + p
+                        target = (side_count * h + c // dp_count) * dp_count + c % dp_count
+                        perm.append((source, target))
+            outgoing = lax.dynamic_index_in_dim(
+                pieces, (holder + step) % chunk_count, axis=0, keepdims=False
+            )
+            arrived = lax.ppermute(outgoing, ALL, perm)
+            grad_w_out = arrived if grad_w_out is None else grad_w_out + arrived
     return (projected.reshape(1, row_count, width), grad_w_out)
 
 

time: 205 us -> 194 us (0.946)
  waiting for transfers between devices: 132 us -> 121 us
    all_to_all x2, waiting for transfers between devices: 74.5 us -> 47.2 us  [a2a(): lax.all_to_all(tensor, 'inner', split_axis=0, concat_axis=0, tiled=True)]
    ppermute x4 -> x2, waiting for transfers between devices: 0.01 us -> 7.49 us  [local(): arrived = lax.ppermute(outgoing, ALL, perm)]
    ppermute x1, waiting for transfers between devices: 54.9 us -> 61.2 us  [local(): kv_parts.append(lax.ppermute(kv_side, 'side', perm))]
    ppermute x0 -> x2, waiting for transfers between devices: none -> 4.68 us  [the longest x1 4.32 us: local(): lax.ppermute(w_out, 'dp', [(p, (p + 1) % dp_count) for p in range(dp_coun...]
    ppermute x4 -> x2, starting transfers between devices: 8.35 us -> 5.03 us  [local(): arrived = lax.ppermute(outgoing, ALL, perm)]
    ppermute x0 -> x2, starting transfers between devices: none -> 2.53 us  [the longest x1 1.28 us: local(): lax.ppermute(w_out, 'dp', [(p, (p + 1) % dp_count) for p in range(dp_coun...]
  transfers between devices with their start and end apart: 9 -> 9, of which waited for: 4 -> 7; matrix products, arithmetic and copies ran while one was open for 16% -> 18% of each run, Pallas kernels for 0% -> 0%
where the time goes in v5:
time: 194 us; the launch traced here: 192 us
  waiting for transfers between devices  121 us (62%)
  starting transfers between devices  19.5 us (10%)
  matrix products  15.6 us (8%)
  between operations  14.2 us (7%)
  other arithmetic  12.1 us (6%)
  local copies, waits for them, and re-layouts  9.29 us (5%)
    ppermute x1, waiting for transfers between devices, local(): kv_parts.append(lax.ppermute(kv_side, 'side', perm))  61.2 us
    all_to_all x2, waiting for transfers between devices, a2a(): lax.all_to_all(tensor, 'inner', split_axis=0, concat_axis=0, tiled=True)  47.2 us
    all_to_all x2, starting transfers between devices, a2a(): lax.all_to_all(tensor, 'inner', split_axis=0, concat_axis=0, tiled=True)  9.65 us
    ppermute x2, waiting for transfers between devices, local(): arrived = lax.ppermute(outgoing, ALL, perm)  7.49 us
    ppermute x2, starting transfers between devices, local(): arrived = lax.ppermute(outgoing, ALL, perm)  5.03 us
    dot_general x3, matrix products, one_block(): mixed = jnp.dot(weights, value_all, preferred_element_type=jnp.float32)  4.42 us
    ppermute x1, waiting for transfers between devices, local(): lax.ppermute(w_out, 'dp', [(p, (p + 1) % dp_count) for p in range(dp_coun...  4.32 us
    dot_general x1, matrix products, local(): jnp.dot(attended, w_full, preferred_element_type=jnp.float32)  4.23 us
  transfers between devices with their start and end apart: 9, of which 7 were waited for; matrix products, arithmetic and copies ran while one was open for 18% of the time, Pallas kernels for 0%

profile of v5, /device:TPU:1, one launch (start us, length us, event | category | flops | bytes accessed | tf_op | source)
XLA Modules:
  0.0 192.0 jit_solution(12647580551118494300)
XLA Ops:
  7.2 0.0 copy-start.1
  7.2 0.0 all-gather.6.cloned.1.call-start
  7.2 0.7 all-gather.6.cloned.1.call-update
  7.9 1.7 reshape_squeeze.11
  9.6 1.7 reshape_squeeze.10
  11.4 0.0 copy-done.1
  11.4 0.6 reshape_squeeze.9
  12.0 0.2 copy.27
  12.2 0.3 copy_bitcast_fusion
  12.5 0.0 copy-start.2
  12.5 2.0 %pad_maximum_fusion = bf16[8,192,576]{2,1,0:T(8,128)(2,1)} fusion(bf16[8,192,192]{2,1,0:T(8,128)(2,1)S(1)} %get-tuple-element.48, bf16[8,192,192]{2,1,0:T(8,128)(2,1)S(1)} %get-tuple-element.49, bf16[8,192,192]{2,1,0:T(8,128)(2,1)S(1)} %bitcast.65), kind=kLoop, calls=%fused_computation.22 | loop fusion | flops 5308416 | bytes 3538944 | tf_op jit(solution)/shard_map/concatenate | solution.py:61
  14.6 5.3 %all-to-all-start = ((bf16[8,192,576]{2,1,0:T(8,128)(2,1)}), bf16[8,192,576]{2,1,0:T(8,128)(2,1)S(1)}, u32[]{:S(2)}, u32[]{:S(2)}) async-start(bf16[8,192,576]{2,1,0:T(8,128)(2,1)} %pad_maximum_fusion), calls=%async_computation | async-start | bytes 3932160 | tf_op jit(solution)/shard_map/all_to_all | solution.py:55
  19.9 0.0 all-gather.4.cloned.1.call-start
  19.9 0.0 copy-done.2
  19.9 1.3 collective-permute-start.1
  21.2 4.3 %collective-permute-done.1 = bf16[48,1536]{1,0:T(8,128)(2,1)S(1)} collective-permute-done((bf16[48,1536]{1,0:T(8,128)(2,1)S(1)}, bf16[48,1536]{1,0:T(8,128)(2,1)S(1)}, u32[]{:S(2)}, u32[]{:S(2)}) %collective-permute-start.1) | collective-permute-done | bytes 147488 | tf_op jit(solution)/shard_map/ppermute | solution.py:44
  25.5 0.7 pad_maximum_fusion.2
  26.3 0.0 all-gather.4.cloned.1.call-update
  26.3 34.7 %all-to-all-done = bf16[8,192,576]{2,1,0:T(8,128)(2,1)S(1)} async-done(((bf16[8,192,576]{2,1,0:T(8,128)(2,1)}), bf16[8,192,576]{2,1,0:T(8,128)(2,1)S(1)}, u32[]{:S(2)}, u32[]{:S(2)}) %all-to-all-start) | async-done | bytes 1769504 | tf_op jit(solution)/shard_map/all_to_all | solution.py:55
  61.0 1.5 slice.17
  62.5 2.3 %collective-permute-start = (bf16[1536,384]{1,0:T(8,128)(2,1)}, bf16[1536,384]{1,0:T(8,128)(2,1)}, u32[]{:S(2)}, u32[]{:S(2)}) collective-permute-start(bf16[1536,384]{1,0:T(8,128)(2,1)} %slice.17), channel_id=1, source_target_pairs={{0,16},{16,0},{1,17},{17,1},{2,18},{18,2},{3,19},{19,3},{4,20},{20... | collective-permute-start | bytes 3538952 | tf_op jit(solution)/shard_map/ppermute | solution.py:70
  64.8 0.1 slice.16
  64.9 61.2 %collective-permute-done = bf16[1536,384]{1,0:T(8,128)(2,1)} collective-permute-done((bf16[1536,384]{1,0:T(8,128)(2,1)}, bf16[1536,384]{1,0:T(8,128)(2,1)}, u32[]{:S(2)}, u32[]{:S(2)}) %collective-permute-start) | collective-permute-done | bytes 1179680 | tf_op jit(solution)/shard_map/ppermute | solution.py:70
  126.1 3.9 %pad_maximum_fusion.1 = (bf16[3072,192]{1,0:T(8,128)(2,1)}, bf16[3072,192]{1,0:T(8,128)(2,1)S(1)}) fusion(bf16[1536,384]{1,0:T(8,128)(2,1)} %collective-permute-done, bf16[1536,384]{1,0:T(8,128)(2,1)} %slice.17), kind=kLoop, calls=%fused_computation.24 | loop fusion | flops 4718592 | bytes 4718592 | tf_op jit(solution)/shard_map/concatenate | solution.py:71
  130.0 12.0 %while.10 = (s32[]{:T(128)}, bf16[3,512,192]{1,2,0:T(8,128)(2,1)S(1)}, bf16[3,512,192]{2,1,0:T(8,128)(2,1)S(1)}, bf16[3072,192]{1,0:T(8,128)(2,1)S(1)}, bf16[3072,192]{1,0:T(8,128)(2,1)}, /*index=5*/s32[]{:T(128)}) while((s32[]{:T(128)}, bf16[3,512,192]{1,2,0:T(8,128)(2,1)S(1)}, bf16[3,512,192]{2,1,0:T(8,128)(2,1)S(1)}, ...), condition=%wide.region_3.4_spmd, body=%wide.region_0.3_spmd.sunk | while | flops 1220738048 | bytes 27207792 | solution.py:26
  130.0 1.1 multiply_reduce_fusion.2
  131.1 0.0 copy-start
  131.1 1.2 fusion.40
  132.2 0.2 copy-done
  132.5 1.5 fusion.41
  134.0 1.1 multiply_reduce_fusion.2
  135.1 0.0 copy-start
  135.1 1.2 fusion.40
  136.3 0.2 copy-done
  136.5 1.5 fusion.41
  138.0 1.1 multiply_reduce_fusion.2
  139.1 0.0 copy-start
  139.1 1.2 fusion.40
  140.3 0.3 copy-done
  140.5 1.5 fusion.41
  142.0 1.1 copy.19
  143.2 4.3 %all-to-all-start.1 = ((bf16[8,192,192]{2,1,0:T(8,128)(2,1)}), bf16[8,192,192]{2,1,0:T(8,128)(2,1)S(1)}, u32[]{:S(2)}, u32[]{:S(2)}) async-start(bf16[8,192,192]{2,1,0:T(8,128)(2,1)} %bitcast.7), calls=%async_computation.1 | async-start | bytes 1572864 | tf_op jit(solution)/shard_map/all_to_all | solution.py:55
  147.5 0.0 all-gather.6.cloned.1.call-done
  147.6 3.6 %fusion.23 = f32[2,2,48,1536]{3,2,1,0:T(8,128)S(1)} fusion(bf16[2,2,48,1536]{3,2,1,0:T(8,128)(2,1)S(1)} %bitcast.66, bf16[1,1536,1536]{2,1,0:T(8,128)(2,1)} %all-gather.6.cloned.1.call-done), kind=kOutput, calls=%fused_computation.16 | convolution fusion | flops 905969664 | bytes 6488064 | tf_op jit(solution)/shard_map/dot_general | solution.py:78
  151.2 1.3 collective-permute-start.2
  152.5 12.4 %all-to-all-done.1 = bf16[8,192,192]{2,1,0:T(8,128)(2,1)S(1)} async-done(((bf16[8,192,192]{2,1,0:T(8,128)(2,1)}), bf16[8,192,192]{2,1,0:T(8,128)(2,1)S(1)}, u32[]{:S(2)}, u32[]{:S(2)}) %all-to-all-start.1) | async-done | bytes 589856 | tf_op jit(solution)/shard_map/all_to_all | solution.py:55
  164.9 0.4 copy.20
  165.4 0.7 reshape.28
  166.1 0.4 collective-permute-done.2
  166.4 1.1 bitcast_add_fusion
  167.6 3.8 %collective-permute-start.3 = (f32[48,1536]{1,0:T(8,128)S(1)}, f32[48,1536]{1,0:T(8,128)S(1)}, u32[]{:S(2)}, u32[]{:S(2)}) collective-permute-start(f32[48,1536]{1,0:T(8,128)S(1)} %get-tuple-element.45), channel_id=1, source_target_pairs={{0,0},{1,1},{2,4},{3,5},{4,8},{5,9},{6,12},{7,13},{8,16},{9,17},{1... | collective-permute-start | bytes 884744 | tf_op jit(solution)/shard_map/ppermute | solution.py:109
  171.4 1.3 collective-permute-start.4
  172.6 0.0 all-gather.4.cloned.1.call-done
  172.6 4.2 %fusion.25 = bf16[1,192,1536]{2,1,0:T(8,128)(2,1)} fusion(bf16[192,1536]{1,0:T(8,128)(2,1)S(1)} %reshape.28, bf16[1536,1536]{1,0:T(8,128)(2,1)} %bitcast.68), kind=kOutput, calls=%fused_computation.19 | convolution fusion | flops 906264576 | bytes 5898240 | tf_op jit(solution)/shard_map/dot_general | solution.py:84
  176.9 3.0 %collective-permute-done.3 = f32[48,1536]{1,0:T(8,128)S(1)} collective-permute-done((f32[48,1536]{1,0:T(8,128)S(1)}, f32[48,1536]{1,0:T(8,128)S(1)}, u32[]{:S(2)}, u32[]{:S(2)}) %collective-permute-start.3) | collective-permute-done | bytes 294944 | tf_op jit(solution)/shard_map/ppermute | solution.py:109
  179.9 4.5 %collective-permute-done.4 = f32[48,1536]{1,0:T(8,128)S(1)} collective-permute-done((f32[48,1536]{1,0:T(8,128)S(1)}, f32[48,1536]{1,0:T(8,128)S(1)}, u32[]{:S(2)}, u32[]{:S(2)}) %collective-permute-start.4) | collective-permute-done | bytes 294944 | tf_op jit(solution)/shard_map/ppermute | solution.py:109
  184.4 0.7 add.42
  (5 shorter events, 0.2 us)
Async XLA Ops:
  7.2 4.2 %copy-start.1 = (bf16[1,192,1536]{2,1,0:T(8,128)(2,1)S(1)}, bf16[1,192,1536]{2,1,0:T(8,128)(2,1)}, u32[]{:S(2)}) copy-start(bf16[1,192,1536]{2,1,0:T(8,128)(2,1)} %param.7) | copy-start | bytes 1769476
  7.2 140.4 %all-gather.6.cloned.1.call-start = ((), (), s32[]{:S(2)}) async-start(), calls=%async_computation.3 | async-start | bytes 5308416 | tf_op jit(solution)/shard_map/all_gather | solution.py:52
  12.5 7.4 %copy-start.2 = (bf16[48,1536]{1,0:T(8,128)(2,1)S(1)}, bf16[48,1536]{1,0:T(8,128)(2,1)}, u32[]{:S(2)}) copy-start(bf16[48,1536]{1,0:T(8,128)(2,1)} %param.10) | copy-start | bytes 442372
  14.6 46.4 %all-to-all-start = ((bf16[8,192,576]{2,1,0:T(8,128)(2,1)}), bf16[8,192,576]{2,1,0:T(8,128)(2,1)S(1)}, u32[]{:S(2)}, u32[]{:S(2)}) async-start(bf16[8,192,576]{2,1,0:T(8,128)(2,1)} %pad_maximum_fusion), calls=%async_computation | async-start | bytes 3932160 | tf_op jit(solution)/shard_map/all_to_all | solution.py:55
  19.9 152.8 %all-gather.4.cloned.1.call-start = ((), (), s32[]{:S(2)}) async-start(), calls=%async_computation.2 | async-start | bytes 5013504 | tf_op jit(solution)/shard_map/all_gather | solution.py:49
  19.9 5.6 %collective-permute-start.1 = (bf16[48,1536]{1,0:T(8,128)(2,1)S(1)}, bf16[48,1536]{1,0:T(8,128)(2,1)S(1)}, u32[]{:S(2)}, u32[]{:S(2)}) collective-permute-start(bf16[48,1536]{1,0:T(8,128)(2,1)S(1)} %copy-done.2), channel_id=1, source_target_pairs={{0,1},{1,0},{2,3},{3,2},{4,5},{5,4},{6,7},{7,6},{8,9},{9,8},{10,11... | collective-permute-start | bytes 442376 | tf_op jit(solution)/shard_map/ppermute | solution.py:44
  62.5 63.5 %collective-permute-start = (bf16[1536,384]{1,0:T(8,128)(2,1)}, bf16[1536,384]{1,0:T(8,128)(2,1)}, u32[]{:S(2)}, u32[]{:S(2)}) collective-permute-start(bf16[1536,384]{1,0:T(8,128)(2,1)} %slice.17), channel_id=1, source_target_pairs={{0,16},{16,0},{1,17},{17,1},{2,18},{18,2},{3,19},{19,3},{4,20},{20... | collective-permute-start | bytes 3538952 | tf_op jit(solution)/shard_map/ppermute | solution.py:70
  131.1 1.4 copy-start
  135.1 1.4 copy-start
  139.1 1.4 copy-start
  143.2 21.8 %all-to-all-start.1 = ((bf16[8,192,192]{2,1,0:T(8,128)(2,1)}), bf16[8,192,192]{2,1,0:T(8,128)(2,1)S(1)}, u32[]{:S(2)}, u32[]{:S(2)}) async-start(bf16[8,192,192]{2,1,0:T(8,128)(2,1)} %bitcast.7), calls=%async_computation.1 | async-start | bytes 1572864 | tf_op jit(solution)/shard_map/all_to_all | solution.py:55
  151.2 15.2 %collective-permute-start.2 = (f32[2,48,1536]{2,1,0:T(8,128)S(1)}, f32[2,48,1536]{2,1,0:T(8,128)}, u32[]{:S(2)}, u32[]{:S(2)}) collective-permute-start(f32[2,48,1536]{2,1,0:T(8,128)S(1)} %dynamic-slice_bitcast_fusion), channel_id=1, source_target_pairs={{0,1},{1,0},{2,3},{3,2},{4,5},{5,4},{6,7},{7,6},{8,9},{9,8},{10,11... | collective-permute-start | bytes 1769480 | tf_op jit(solution)/shard_map/ppermute | solution.py:95
  167.6 12.3 %collective-permute-start.3 = (f32[48,1536]{1,0:T(8,128)S(1)}, f32[48,1536]{1,0:T(8,128)S(1)}, u32[]{:S(2)}, u32[]{:S(2)}) collective-permute-start(f32[48,1536]{1,0:T(8,128)S(1)} %get-tuple-element.45), channel_id=1, source_target_pairs={{0,0},{1,1},{2,4},{3,5},{4,8},{5,9},{6,12},{7,13},{8,16},{9,17},{1... | collective-permute-start | bytes 884744 | tf_op jit(solution)/shard_map/ppermute | solution.py:109
  171.4 13.0 %collective-permute-start.4 = (f32[48,1536]{1,0:T(8,128)S(1)}, f32[48,1536]{1,0:T(8,128)S(1)}, u32[]{:S(2)}, u32[]{:S(2)}) collective-permute-start(f32[48,1536]{1,0:T(8,128)S(1)} %get-tuple-element.44), channel_id=1, source_target_pairs={{0,2},{1,3},{2,6},{3,7},{4,10},{5,11},{6,14},{7,15},{8,18},{9,19},... | collective-permute-start | bytes 884744 | tf_op jit(solution)/shard_map/ppermute | solution.py:109
Sparse Core Ops, SparseCore 0:
  9.6 54.7 all-gather.5
  67.3 94.8 all-gather.3

commit v6 on v5

--- a/solution.py
+++ b/solution.py
@@ -29,7 +29,8 @@
     return blocks.reshape(query_count, head_width)
 
 
-ALL = ("side", "inner", "dp")
+ALL = ("side", "chip", "core", "dp")
+INNER = ("chip", "core")
 
 
 def local(queries, key_vectors, value_vectors, w_out, cotangent):
@@ -46,13 +47,24 @@
         w_pair = jnp.stack(
             [jnp.where(dp_index == 0, w_out, w_other), jnp.where(dp_index == 0, w_other, w_out)]
         )
-        w_full = lax.all_gather(w_pair, ("side", "inner"), axis=0, tiled=True).reshape(-1, width)
+        w_full = lax.all_gather(w_pair, ("side", "chip", "core"), axis=0, tiled=True).reshape(-1, width)
     else:
         w_full = lax.all_gather(w_out, ALL, axis=0, tiled=True)
-    cot_side = lax.all_gather(cotangent[0], "inner", axis=0, tiled=True)
+    chip_count = lax.axis_size("chip")
+    core_count = lax.axis_size("core")
+    core_index = lax.axis_index("core")
+    cot_core = lax.all_gather(cotangent[0], "chip", axis=0, tiled=True)
+    cot_other = lax.ppermute(cot_core, "core", [(0, 1), (1, 0)])
+    cot_side = jnp.concatenate(
+        [
+            jnp.where(core_index == 0, cot_core, cot_other),
+            jnp.where(core_index == 0, cot_other, cot_core),
+        ],
+        axis=0,
+    )
 
     def a2a(tensor):
-        return lax.all_to_all(tensor, "inner", split_axis=0, concat_axis=0, tiled=True)
+        return lax.all_to_all(tensor, INNER, split_axis=0, concat_axis=0, tiled=True)
 
     def by_head(tensor):
         return tensor[0].reshape(row_count, head_count, head_width).transpose(1, 0, 2)
@@ -75,8 +87,13 @@
 
     attended_here = attend(query_here, key_all, value_all)
 
+    attended_rows = (
+        attended_here.reshape(chip_count, core_count, row_count, head_width)
+        .transpose(1, 0, 2, 3)
+        .reshape(core_count * chip_count * row_count, head_width)
+    )
     partial = lax.dot_general(
-        attended_here, cot_side, (((0,), (0,)), ((), ())), preferred_element_type=jnp.float32
+        attended_rows, cot_side, (((0,), (0,)), ((), ())), preferred_element_type=jnp.float32
     )
 
     returned = a2a(attended_here.reshape(head_count, row_count, head_width))
@@ -132,10 +149,8 @@
 def solution(mesh):
     seq_count = mesh.shape["seq"]
     dp_count = mesh.shape["dp"]
-    fine = Mesh(
-        mesh.devices.reshape(seq_count // HEADS, HEADS, dp_count), ("side", "inner", "dp")
-    )
-    seq = ("side", "inner")
+    fine = Mesh(mesh.devices.reshape(seq_count // HEADS, HEADS // 2, 2, dp_count), ALL)
+    seq = ("side", "chip", "core")
     placed = (
         P("dp", seq, None),
         P("dp", seq, None),

time: 194 us -> 199 us (1.026)
  starting transfers between devices: 19.5 us -> 25.5 us
  matrix products: 15.6 us -> 13.3 us
  local copies, waits for them, and re-layouts: 9.29 us -> 11.5 us
  waiting for transfers between devices: 121 us -> 119 us
    ppermute x1, waiting for transfers between devices: 61.2 us -> 46.5 us  [local(): kv_parts.append(lax.ppermute(kv_side, 'side', perm))]
    all_gather x2, waiting for transfers between devices: 0.02 us -> 12.3 us  [the longest x1 12.3 us: local(): cot_core = lax.all_gather(cotangent[0], 'chip', axis=0, tiled=True)]
    ppermute x2, waiting for transfers between devices: 7.49 us -> 0.01 us  [local(): arrived = lax.ppermute(outgoing, ALL, perm)]
    ppermute x1, waiting for transfers between devices: 0.37 us -> 6.72 us  [local(): kept = kept + lax.ppermute(sent, 'dp', [(0, 1), (1, 0)])]
    dot_general x1, matrix products: 3.61 us -> 1.33 us  [local(): lax.dot_general(attended_rows, cot_side, (((0,), (0,)), ((), ())), prefer...]
    select_n x0 -> x1, other arithmetic: none -> 2.03 us  [local(): jnp.where(core_index == 0, cot_core, cot_other)]
  transfers between devices with their start and end apart: 9 -> 10, of which waited for: 7 -> 6; matrix products, arithmetic and copies ran while one was open for 18% -> 17% of each run, Pallas kernels for 0% -> 0%
where the time goes in v6:
time: 199 us; the launch traced here: 197 us
  waiting for transfers between devices  119 us (60%)
  starting transfers between devices  25.5 us (13%)
  between operations  14.2 us (7%)
  matrix products  13.3 us (7%)
  other arithmetic  13 us (7%)
  local copies, waits for them, and re-layouts  11.5 us (6%)
    all_to_all x2, waiting for transfers between devices, a2a(): lax.all_to_all(tensor, INNER, split_axis=0, concat_axis=0, tiled=True)  48.5 us
    ppermute x1, waiting for transfers between devices, local(): kv_parts.append(lax.ppermute(kv_side, 'side', perm))  46.5 us
    all_gather x1, waiting for transfers between devices, local(): cot_core = lax.all_gather(cotangent[0], 'chip', axis=0, tiled=True)  12.3 us
    all_to_all x2, starting transfers between devices, a2a(): lax.all_to_all(tensor, INNER, split_axis=0, concat_axis=0, tiled=True)  10.7 us
    ppermute x2, starting transfers between devices, local(): arrived = lax.ppermute(outgoing, ALL, perm)  6.76 us
    ppermute x1, waiting for transfers between devices, local(): kept = kept + lax.ppermute(sent, 'dp', [(0, 1), (1, 0)])  6.72 us
    dot_general x3, matrix products, one_block(): mixed = jnp.dot(weights, value_all, preferred_element_type=jnp.float32)  4.41 us
    ppermute x1, waiting for transfers between devices, local(): lax.ppermute(w_out, 'dp', [(p, (p + 1) % dp_count) for p in range(dp_coun...  4.32 us
  transfers between devices with their start and end apart: 10, of which 6 were waited for; matrix products, arithmetic and copies ran while one was open for 17% of the time, Pallas kernels for 0%

profile of v6, /device:TPU:1, one launch (start us, length us, event | category | flops | bytes accessed | tf_op | source)
XLA Modules:
  0.0 196.7 jit_solution(3980846909686388413)
XLA Ops:
  7.2 0.0 copy-start.2
  7.2 0.0 copy-start.3
  7.2 0.0 all-gather.6.cloned.1.call-start
  7.2 0.7 all-gather.6.cloned.1.call-update
  7.9 1.7 reshape_squeeze.11
  9.7 0.0 copy-done.2
  9.7 0.6 reshape_squeeze.10
  10.3 0.0 copy-done.3
  10.3 0.6 reshape_squeeze.9
  10.9 0.2 copy.34
  11.1 0.3 copy_bitcast_fusion
  11.4 2.1 %pad_maximum_fusion = bf16[8,192,576]{2,1,0:T(8,128)(2,1)} fusion(bf16[8,192,192]{2,1,0:T(8,128)(2,1)S(1)} %get-tuple-element.50, bf16[8,192,192]{2,1,0:T(8,128)(2,1)S(1)} %get-tuple-element.51, bf16[8,192,192]{2,1,0:T(8,128)(2,1)S(1)} %bitcast.68), kind=kLoop, calls=%fused_computation.26 | loop fusion | flops 5308416 | bytes 3538944 | tf_op jit(solution)/shard_map/concatenate | solution.py:73
  13.5 0.0 copy-start.5
  13.5 5.4 %all-to-all-start = ((bf16[8,192,576]{2,1,0:T(8,128)(2,1)}), bf16[8,192,576]{2,1,0:T(8,128)(2,1)S(1)}, u32[]{:S(2)}, u32[]{:S(2)}) async-start(bf16[8,192,576]{2,1,0:T(8,128)(2,1)} %pad_maximum_fusion), calls=%async_computation | async-start | bytes 3932160 | tf_op jit(solution)/shard_map/all_to_all | solution.py:67
  19.0 0.0 all-gather.4.cloned.1.call-start
  19.0 0.0 copy-done.5
  19.0 1.3 collective-permute-start.1
  20.3 4.3 %collective-permute-done.1 = bf16[48,1536]{1,0:T(8,128)(2,1)S(1)} collective-permute-done((bf16[48,1536]{1,0:T(8,128)(2,1)S(1)}, bf16[48,1536]{1,0:T(8,128)(2,1)S(1)}, u32[]{:S(2)}, u32[]{:S(2)}) %collective-permute-start.1) | collective-permute-done | bytes 147488 | tf_op jit(solution)/shard_map/ppermute | solution.py:45
  24.6 0.7 pad_maximum_fusion.2
  25.4 0.0 all-gather.4.cloned.1.call-update
  25.4 38.6 %all-to-all-done = bf16[8,192,576]{2,1,0:T(8,128)(2,1)S(1)} async-done(((bf16[8,192,576]{2,1,0:T(8,128)(2,1)}), bf16[8,192,576]{2,1,0:T(8,128)(2,1)S(1)}, u32[]{:S(2)}, u32[]{:S(2)}) %all-to-all-start) | async-done | bytes 1769504 | tf_op jit(solution)/shard_map/all_to_all | solution.py:67
  64.0 1.5 slice.17
  65.5 3.3 %collective-permute-start = (bf16[1536,384]{1,0:T(8,128)(2,1)}, bf16[1536,384]{1,0:T(8,128)(2,1)}, u32[]{:S(2)}, u32[]{:S(2)}) collective-permute-start(bf16[1536,384]{1,0:T(8,128)(2,1)} %slice.17), channel_id=1, source_target_pairs={{0,16},{16,0},{1,17},{17,1},{2,18},{18,2},{3,19},{19,3},{4,20},{20... | collective-permute-start | bytes 3538952 | tf_op jit(solution)/shard_map/ppermute | solution.py:82
  68.8 0.1 slice.16
  68.9 12.3 %all-gather.6.cloned.1.call-done = bf16[1,768,1536]{2,1,0:T(8,128)(2,1)} async-done(((bf16[1,192,1536]{2,1,0:T(8,128)(2,1)}), bf16[1,768,1536]{2,1,0:T(8,128)(2,1)}) %all-gather.6.cloned.1.call-update) | async-done | bytes 2359312 | tf_op jit(solution)/shard_map/all_gather | solution.py:56
  81.1 0.5 collective-permute-start.2
  81.6 46.5 %collective-permute-done = bf16[1536,384]{1,0:T(8,128)(2,1)} collective-permute-done((bf16[1536,384]{1,0:T(8,128)(2,1)}, bf16[1536,384]{1,0:T(8,128)(2,1)}, u32[]{:S(2)}, u32[]{:S(2)}) %collective-permute-start) | collective-permute-done | bytes 1179680 | tf_op jit(solution)/shard_map/ppermute | solution.py:82
  128.1 3.8 %pad_maximum_fusion.1 = (bf16[3072,192]{1,0:T(8,128)(2,1)}, bf16[3072,192]{1,0:T(8,128)(2,1)S(1)}) fusion(bf16[1536,384]{1,0:T(8,128)(2,1)} %collective-permute-done, bf16[1536,384]{1,0:T(8,128)(2,1)} %slice.17), kind=kLoop, calls=%fused_computation.28 | loop fusion | flops 4718592 | bytes 4718592 | tf_op jit(solution)/shard_map/concatenate | solution.py:83
  131.9 12.1 %while.10 = (s32[]{:T(128)}, bf16[3,512,192]{1,2,0:T(8,128)(2,1)S(1)}, bf16[3,512,192]{2,1,0:T(8,128)(2,1)S(1)}, bf16[3072,192]{1,0:T(8,128)(2,1)S(1)}, bf16[3072,192]{1,0:T(8,128)(2,1)}, /*index=5*/s32[]{:T(128)}) while((s32[]{:T(128)}, bf16[3,512,192]{1,2,0:T(8,128)(2,1)S(1)}, bf16[3,512,192]{2,1,0:T(8,128)(2,1)S(1)}, ...), condition=%wide.region_3.4_spmd, body=%wide.region_0.3_spmd.sunk | while | flops 1220738048 | bytes 27207792 | solution.py:26
  131.9 1.1 multiply_reduce_fusion.2
  133.0 0.0 copy-start.1
  133.1 1.2 fusion.42
  134.2 0.2 copy-done.1
  134.5 1.5 fusion.43
  136.0 1.1 multiply_reduce_fusion.2
  137.1 1.2 fusion.42
  138.2 0.3 copy-done.1
  138.5 1.5 fusion.43
  140.0 1.1 multiply_reduce_fusion.2
  141.1 1.2 fusion.42
  142.3 0.2 copy-done.1
  142.5 1.5 fusion.43
  144.0 0.0 copy-start
  144.0 1.1 copy.26
  145.2 1.6 copy.29
  146.8 1.7 reshape.31
  148.5 0.0 collective-permute-done.2
  148.5 0.0 copy-done
  148.5 2.0 %broadcast_select_fusion.1 = (bf16[768,1536]{1,0:T(8,128)(2,1)S(1)}, bf16[768,1536]{1,0:T(8,128)(2,1)S(1)}) fusion(bf16[768,1536]{1,0:T(8,128)(2,1)} %collective-permute-done.2, pred[]{:T(512)S(6)} %eq.12, bf16[1,768,1536]{2,1,0:T(8,128)(2,1)S(1)} %copy-done), kind=kLoop, calls=%fused_computation.25 | loop fusion | flops 2359296 | bytes 9437185 | tf_op jit(solution)/shard_map/jit(_where)/select_n | solution.py:60
  150.6 0.0 copy-done.4
  150.6 1.3 fusion.23
  152.0 3.0 %collective-permute-start.3 = (f32[2,48,1536]{2,1,0:T(8,128)S(1)}, f32[2,48,1536]{2,1,0:T(8,128)S(1)}, u32[]{:S(2)}, u32[]{:S(2)}) collective-permute-start(f32[2,48,1536]{2,1,0:T(8,128)S(1)} %dynamic-slice_bitcast_fusion), channel_id=1, source_target_pairs={{0,1},{1,0},{2,3},{3,2},{4,5},{5,4},{6,7},{7,6},{8,9},{9,8},{10,11... | collective-permute-start | bytes 1769480 | tf_op jit(solution)/shard_map/ppermute | solution.py:112
  154.9 5.3 %all-to-all-start.1 = ((bf16[8,192,192]{2,1,0:T(8,128)(2,1)}), bf16[8,192,192]{2,1,0:T(8,128)(2,1)S(1)}, u32[]{:S(2)}, u32[]{:S(2)}) async-start(bf16[8,192,192]{2,1,0:T(8,128)(2,1)} %bitcast.7), calls=%async_computation.1 | async-start | bytes 1572864 | tf_op jit(solution)/shard_map/all_to_all | solution.py:67
  160.2 6.7 %collective-permute-done.3 = f32[2,48,1536]{2,1,0:T(8,128)S(1)} collective-permute-done((f32[2,48,1536]{2,1,0:T(8,128)S(1)}, f32[2,48,1536]{2,1,0:T(8,128)S(1)}, u32[]{:S(2)}, u32[]{:S(2)}) %collective-permute-start.3) | collective-permute-done | bytes 589856 | tf_op jit(solution)/shard_map/ppermute | solution.py:112
  167.0 0.1 bitcast_add_fusion
  167.1 3.7 %collective-permute-start.4 = (f32[48,1536]{1,0:T(8,128)S(1)}, f32[48,1536]{1,0:T(8,128)S(1)}, u32[]{:S(2)}, u32[]{:S(2)}) collective-permute-start(f32[48,1536]{1,0:T(8,128)S(1)} %get-tuple-element.47), channel_id=1, source_target_pairs={{0,0},{1,1},{2,4},{3,5},{4,8},{5,9},{6,12},{7,13},{8,16},{9,17},{1... | collective-permute-start | bytes 884744 | tf_op jit(solution)/shard_map/ppermute | solution.py:126
  170.8 3.1 %collective-permute-start.5 = (f32[48,1536]{1,0:T(8,128)S(1)}, f32[48,1536]{1,0:T(8,128)S(1)}, u32[]{:S(2)}, u32[]{:S(2)}) collective-permute-start(f32[48,1536]{1,0:T(8,128)S(1)} %get-tuple-element.46), channel_id=1, source_target_pairs={{0,2},{1,3},{2,6},{3,7},{4,10},{5,11},{6,14},{7,15},{8,18},{9,19},... | collective-permute-start | bytes 884744 | tf_op jit(solution)/shard_map/ppermute | solution.py:126
  173.9 9.8 %all-to-all-done.1 = bf16[8,192,192]{2,1,0:T(8,128)(2,1)S(1)} async-done(((bf16[8,192,192]{2,1,0:T(8,128)(2,1)}), bf16[8,192,192]{2,1,0:T(8,128)(2,1)S(1)}, u32[]{:S(2)}, u32[]{:S(2)}) %all-to-all-start.1) | async-done | bytes 589856 | tf_op jit(solution)/shard_map/all_to_all | solution.py:67
  183.7 0.4 copy.27
  184.1 0.7 reshape.28
  184.8 0.0 collective-permute-done.4
  184.8 0.0 collective-permute-done.5
  184.8 0.7 add.42
  185.6 4.2 %fusion.26 = bf16[1,192,1536]{2,1,0:T(8,128)(2,1)} fusion(bf16[192,1536]{1,0:T(8,128)(2,1)S(1)} %reshape.28, bf16[1536,1536]{1,0:T(8,128)(2,1)} %bitcast.71), kind=kOutput, calls=%fused_computation.21 | convolution fusion | flops 906264576 | bytes 5898240 | tf_op jit(solution)/shard_map/dot_general | solution.py:101
  (8 shorter events, 0.1 us)
Async XLA Ops:
  7.2 2.5 %copy-start.2 = (bf16[1,192,1536]{2,1,0:T(8,128)(2,1)S(1)}, bf16[1,192,1536]{2,1,0:T(8,128)(2,1)}, u32[]{:S(2)}) copy-start(bf16[1,192,1536]{2,1,0:T(8,128)(2,1)} %param.8) | copy-start | bytes 1769476
  7.2 3.1 %copy-start.3 = (bf16[1,192,1536]{2,1,0:T(8,128)(2,1)S(1)}, bf16[1,192,1536]{2,1,0:T(8,128)(2,1)}, u32[]{:S(2)}) copy-start(bf16[1,192,1536]{2,1,0:T(8,128)(2,1)} %param.7) | copy-start | bytes 1769476
  7.2 73.9 %all-gather.6.cloned.1.call-start = ((), (), s32[]{:S(2)}) async-start(), calls=%async_computation.3 | async-start | bytes 2949120 | tf_op jit(solution)/shard_map/all_gather | solution.py:56
  13.5 5.4 %copy-start.5 = (bf16[48,1536]{1,0:T(8,128)(2,1)S(1)}, bf16[48,1536]{1,0:T(8,128)(2,1)}, u32[]{:S(2)}) copy-start(bf16[48,1536]{1,0:T(8,128)(2,1)} %param.10) | copy-start | bytes 442372
  13.5 50.5 %all-to-all-start = ((bf16[8,192,576]{2,1,0:T(8,128)(2,1)}), bf16[8,192,576]{2,1,0:T(8,128)(2,1)S(1)}, u32[]{:S(2)}, u32[]{:S(2)}) async-start(bf16[8,192,576]{2,1,0:T(8,128)(2,1)} %pad_maximum_fusion), calls=%async_computation | async-start | bytes 3932160 | tf_op jit(solution)/shard_map/all_to_all | solution.py:67
  19.0 166.6 %all-gather.4.cloned.1.call-start = ((), (), s32[]{:S(2)}) async-start(), calls=%async_computation.2 | async-start | bytes 5013504 | tf_op jit(solution)/shard_map/all_gather | solution.py:50
  19.0 5.6 %collective-permute-start.1 = (bf16[48,1536]{1,0:T(8,128)(2,1)S(1)}, bf16[48,1536]{1,0:T(8,128)(2,1)S(1)}, u32[]{:S(2)}, u32[]{:S(2)}) collective-permute-start(bf16[48,1536]{1,0:T(8,128)(2,1)S(1)} %copy-done.5), channel_id=1, source_target_pairs={{0,1},{1,0},{2,3},{3,2},{4,5},{5,4},{6,7},{7,6},{8,9},{9,8},{10,11... | collective-permute-start | bytes 442376 | tf_op jit(solution)/shard_map/ppermute | solution.py:45
  65.5 62.6 %collective-permute-start = (bf16[1536,384]{1,0:T(8,128)(2,1)}, bf16[1536,384]{1,0:T(8,128)(2,1)}, u32[]{:S(2)}, u32[]{:S(2)}) collective-permute-start(bf16[1536,384]{1,0:T(8,128)(2,1)} %slice.17), channel_id=1, source_target_pairs={{0,16},{16,0},{1,17},{17,1},{2,18},{18,2},{3,19},{19,3},{4,20},{20... | collective-permute-start | bytes 3538952 | tf_op jit(solution)/shard_map/ppermute | solution.py:82
  81.1 67.4 %collective-permute-start.2 = (bf16[768,1536]{1,0:T(8,128)(2,1)}, bf16[768,1536]{1,0:T(8,128)(2,1)}, u32[]{:S(2)}, u32[]{:S(2)}) collective-permute-start(bf16[768,1536]{1,0:T(8,128)(2,1)} %bitcast.69), channel_id=1, source_target_pairs={{0,2},{2,0},{1,3},{3,1},{4,6},{6,4},{5,7},{7,5},{8,10},{10,8},{9,1... | collective-permute-start | bytes 7077896 | tf_op jit(solution)/shard_map/ppermute | solution.py:57
  133.0 1.4 copy-start.1
  137.1 1.4 copy-start.1
  141.1 1.4 copy-start.1
  144.0 4.5 %copy-start = (bf16[1,768,1536]{2,1,0:T(8,128)(2,1)S(1)}, bf16[1,768,1536]{2,1,0:T(8,128)(2,1)}, u32[]{:S(2)}) copy-start(bf16[1,768,1536]{2,1,0:T(8,128)(2,1)} %all-gather.6.cloned.1.call-done) | copy-start | bytes 7077892
  148.5 2.0 %copy-start.4 = (bf16[1536,192]{0,1:T(8,128)(2,1)S(1)}, bf16[1536,192]{0,1:T(8,128)(2,1)}, u32[]{:S(2)}) copy-start(bf16[1536,192]{0,1:T(8,128)(2,1)} %reshape.31) | copy-start | bytes 1769476
  152.0 15.0 %collective-permute-start.3 = (f32[2,48,1536]{2,1,0:T(8,128)S(1)}, f32[2,48,1536]{2,1,0:T(8,128)S(1)}, u32[]{:S(2)}, u32[]{:S(2)}) collective-permute-start(f32[2,48,1536]{2,1,0:T(8,128)S(1)} %dynamic-slice_bitcast_fusion), channel_id=1, source_target_pairs={{0,1},{1,0},{2,3},{3,2},{4,5},{5,4},{6,7},{7,6},{8,9},{9,8},{10,11... | collective-permute-start | bytes 1769480 | tf_op jit(solution)/shard_map/ppermute | solution.py:112
  154.9 28.7 %all-to-all-start.1 = ((bf16[8,192,192]{2,1,0:T(8,128)(2,1)}), bf16[8,192,192]{2,1,0:T(8,128)(2,1)S(1)}, u32[]{:S(2)}, u32[]{:S(2)}) async-start(bf16[8,192,192]{2,1,0:T(8,128)(2,1)} %bitcast.7), calls=%async_computation.1 | async-start | bytes 1572864 | tf_op jit(solution)/shard_map/all_to_all | solution.py:67
  167.1 17.7 %collective-permute-start.4 = (f32[48,1536]{1,0:T(8,128)S(1)}, f32[48,1536]{1,0:T(8,128)S(1)}, u32[]{:S(2)}, u32[]{:S(2)}) collective-permute-start(f32[48,1536]{1,0:T(8,128)S(1)} %get-tuple-element.47), channel_id=1, source_target_pairs={{0,0},{1,1},{2,4},{3,5},{4,8},{5,9},{6,12},{7,13},{8,16},{9,17},{1... | collective-permute-start | bytes 884744 | tf_op jit(solution)/shard_map/ppermute | solution.py:126
  170.8 14.0 %collective-permute-start.5 = (f32[48,1536]{1,0:T(8,128)S(1)}, f32[48,1536]{1,0:T(8,128)S(1)}, u32[]{:S(2)}, u32[]{:S(2)}) collective-permute-start(f32[48,1536]{1,0:T(8,128)S(1)} %get-tuple-element.46), channel_id=1, source_target_pairs={{0,2},{1,3},{2,6},{3,7},{4,10},{5,11},{6,14},{7,15},{8,18},{9,19},... | collective-permute-start | bytes 884744 | tf_op jit(solution)/shard_map/ppermute | solution.py:126
Sparse Core Ops, SparseCore 0:
  9.6 71.5 all-gather.5
  83.4 77.2 all-gather.3

commit v7 on v5

--- a/solution.py
+++ b/solution.py
@@ -58,20 +58,20 @@
         return tensor[0].reshape(row_count, head_count, head_width).transpose(1, 0, 2)
 
     side_index = lax.axis_index("side")
-    stacked = jnp.concatenate(
-        [by_head(queries), by_head(key_vectors), by_head(value_vectors)], axis=2
-    )
+    kv_raw = jnp.concatenate([by_head(key_vectors), by_head(value_vectors)], axis=2)
+    kv_crossed = [
+        lax.ppermute(kv_raw, "side", [(g, (g + step) % side_count) for g in range(side_count)])
+        for step in range(1, side_count)
+    ]
+    stacked = jnp.concatenate([by_head(queries), kv_raw], axis=2)
     got = a2a(stacked).reshape(head_count * row_count, 3 * head_width)
     query_here = got[:, :head_width]
-    kv_side = got[:, head_width:]
-    kv_parts = [kv_side]
-    for step in range(1, side_count):
-        perm = [(g, (g + step) % side_count) for g in range(side_count)]
-        kv_parts.append(lax.ppermute(kv_side, "side", perm))
+    kv_parts = [got[:, head_width:]]
+    for crossed in kv_crossed:
+        kv_parts.append(a2a(crossed).reshape(head_count * row_count, 2 * head_width))
     kv_all = jnp.concatenate(kv_parts, axis=0)
     key_all = kv_all[:, :head_width]
     value_all = kv_all[:, head_width:]
-    del side_index
 
     attended_here = attend(query_here, key_all, value_all)
 

time: 194 us -> 186 us (0.959)
  waiting for transfers between devices: 121 us -> 101 us
  starting transfers between devices: 19.5 us -> 27.7 us
  other arithmetic: 12.1 us -> 14.4 us
    all_to_all x2 -> x3, waiting for transfers between devices: 47.2 us -> 34 us  [a2a(): lax.all_to_all(tensor, 'inner', split_axis=0, concat_axis=0, tiled=True)]
    all_to_all x2 -> x3, starting transfers between devices: 9.65 us -> 17.5 us  [a2a(): lax.all_to_all(tensor, 'inner', split_axis=0, concat_axis=0, tiled=True)]
    ppermute x1, waiting for transfers between devices: 61.2 us -> 54.3 us  [local(): lax.ppermute(kv_raw, 'side', [(g, (g + step) % side_count) for g in range...]
  transfers between devices with their start and end apart: 9 -> 10, of which waited for: 7 -> 8; matrix products, arithmetic and copies ran while one was open for 18% -> 21% of each run, Pallas kernels for 0% -> 0%
where the time goes in v7:
time: 186 us; the launch traced here: 183 us
  waiting for transfers between devices  101 us (54%)
  starting transfers between devices  27.7 us (15%)
  matrix products  15.4 us (8%)
  other arithmetic  14.4 us (8%)
  between operations  14.2 us (8%)
  local copies, waits for them, and re-layouts  10.3 us (6%)
    ppermute x1, waiting for transfers between devices, local(): lax.ppermute(kv_raw, 'side', [(g, (g + step) % side_count) for g in range...  54.3 us
    all_to_all x3, waiting for transfers between devices, a2a(): lax.all_to_all(tensor, 'inner', split_axis=0, concat_axis=0, tiled=True)  34 us
    all_to_all x3, starting transfers between devices, a2a(): lax.all_to_all(tensor, 'inner', split_axis=0, concat_axis=0, tiled=True)  17.5 us
    ppermute x2, waiting for transfers between devices, local(): arrived = lax.ppermute(outgoing, ALL, perm)  7.51 us
    ppermute x2, starting transfers between devices, local(): arrived = lax.ppermute(outgoing, ALL, perm)  5.32 us
    dot_general x3, matrix products, one_block(): mixed = jnp.dot(weights, value_all, preferred_element_type=jnp.float32)  4.42 us
    dot_general x1, matrix products, local(): jnp.dot(attended, w_full, preferred_element_type=jnp.float32)  4.23 us
    ppermute x1, waiting for transfers between devices, local(): lax.ppermute(w_out, 'dp', [(p, (p + 1) % dp_count) for p in range(dp_coun...  4.22 us
  transfers between devices with their start and end apart: 10, of which 8 were waited for; matrix products, arithmetic and copies ran while one was open for 21% of the time, Pallas kernels for 0%

profile of v7, /device:TPU:1, one launch (start us, length us, event | category | flops | bytes accessed | tf_op | source)
XLA Modules:
  0.0 183.4 jit_solution(7569056541322604658)
XLA Ops:
  7.2 0.0 copy-start.1
  7.2 0.0 copy-start.2
  7.2 0.0 all-gather.6.cloned.1.call-start
  7.2 0.7 all-gather.6.cloned.1.call-update
  7.9 1.7 reshape_squeeze.11
  9.7 0.0 copy-done.1
  9.7 1.5 reshape_squeeze.10
  11.2 0.0 copy-done.2
  11.2 0.6 reshape_squeeze.9
  11.8 0.2 copy.27
  11.9 1.5 copy_bitcast_fusion
  13.4 2.1 %pad_maximum_fusion = bf16[8,192,576]{2,1,0:T(8,128)(2,1)} fusion(bf16[8,192,192]{2,1,0:T(8,128)(2,1)S(1)} %get-tuple-element.48, bf16[8,192,192]{2,1,0:T(8,128)(2,1)S(1)} %get-tuple-element.49, bf16[8,192,192]{2,1,0:T(8,128)(2,1)S(1)} %bitcast.66), kind=kLoop, calls=%fused_computation.22 | loop fusion | flops 5308416 | bytes 3538944 | tf_op jit(solution)/shard_map/concatenate | solution.py:66
  15.5 5.3 %all-to-all-start = ((bf16[8,192,576]{2,1,0:T(8,128)(2,1)}), bf16[8,192,576]{2,1,0:T(8,128)(2,1)S(1)}, u32[]{:S(2)}, u32[]{:S(2)}) async-start(bf16[8,192,576]{2,1,0:T(8,128)(2,1)} %pad_maximum_fusion), calls=%async_computation | async-start | bytes 3932160 | tf_op jit(solution)/shard_map/all_to_all | solution.py:55
  20.8 0.0 all-gather.4.cloned.1.call-start
  20.8 1.5 pad_maximum_fusion.2
  22.4 2.3 %collective-permute-start = (bf16[8,192,384]{2,1,0:T(8,128)(2,1)}, bf16[8,192,384]{2,1,0:T(8,128)(2,1)}, u32[]{:S(2)}, u32[]{:S(2)}) collective-permute-start(bf16[8,192,384]{2,1,0:T(8,128)(2,1)} %pad_maximum_fusion.2), channel_id=1, source_target_pairs={{0,16},{16,0},{1,17},{17,1},{2,18},{18,2},{3,19},{19,3},{4,20},{20... | collective-permute-start | bytes 3538952 | tf_op jit(solution)/shard_map/ppermute | solution.py:63
  24.7 1.2 collective-permute-start.1
  25.9 4.2 %collective-permute-done.1 = bf16[48,1536]{1,0:T(8,128)(2,1)S(1)} collective-permute-done((bf16[48,1536]{1,0:T(8,128)(2,1)}, bf16[48,1536]{1,0:T(8,128)(2,1)S(1)}, u32[]{:S(2)}, u32[]{:S(2)}) %collective-permute-start.1) | collective-permute-done | bytes 147488 | tf_op jit(solution)/shard_map/ppermute | solution.py:44
  30.1 0.9 select_bitcast_fusion.1
  31.0 0.7 pad_maximum_fusion.3
  31.8 0.0 all-gather.4.cloned.1.call-update
  31.8 54.3 %collective-permute-done = bf16[8,192,384]{2,1,0:T(8,128)(2,1)} collective-permute-done((bf16[8,192,384]{2,1,0:T(8,128)(2,1)}, bf16[8,192,384]{2,1,0:T(8,128)(2,1)}, u32[]{:S(2)}, u32[]{:S(2)}) %collective-permute-start) | collective-permute-done | bytes 1179680 | tf_op jit(solution)/shard_map/ppermute | solution.py:63
  86.1 1.5 all-to-all-done
  87.6 5.7 %all-to-all-start.1 = ((bf16[8,192,384]{2,1,0:T(8,128)(2,1)}), bf16[8,192,384]{2,1,0:T(8,128)(2,1)}, u32[]{:S(2)}, u32[]{:S(2)}) async-start(bf16[8,192,384]{2,1,0:T(8,128)(2,1)} %collective-permute-done), calls=%async_computation.1 | async-start | bytes 2359296 | tf_op jit(solution)/shard_map/all_to_all | solution.py:55
  93.3 0.1 slice.16
  93.3 1.6 slice.17
  94.9 20.5 %all-to-all-done.1 = bf16[8,192,384]{2,1,0:T(8,128)(2,1)} async-done(((bf16[8,192,384]{2,1,0:T(8,128)(2,1)}), bf16[8,192,384]{2,1,0:T(8,128)(2,1)}, u32[]{:S(2)}, u32[]{:S(2)}) %all-to-all-start.1) | async-done | bytes 1179680 | tf_op jit(solution)/shard_map/all_to_all | solution.py:55
  115.4 3.8 %pad_maximum_fusion.1 = (bf16[3072,192]{1,0:T(8,128)(2,1)}, bf16[3072,192]{1,0:T(8,128)(2,1)S(1)}) fusion(bf16[1536,384]{1,0:T(8,128)(2,1)} %bitcast.7, bf16[1536,384]{1,0:T(8,128)(2,1)} %slice.17), kind=kLoop, calls=%fused_computation.24 | loop fusion | flops 4718592 | bytes 4718592 | tf_op jit(solution)/shard_map/concatenate | solution.py:72
  119.2 12.0 %while.10 = (s32[]{:T(128)}, bf16[3,512,192]{1,2,0:T(8,128)(2,1)S(1)}, bf16[3,512,192]{2,1,0:T(8,128)(2,1)S(1)}, bf16[3072,192]{1,0:T(8,128)(2,1)S(1)}, bf16[3072,192]{1,0:T(8,128)(2,1)}, /*index=5*/s32[]{:T(128)}) while((s32[]{:T(128)}, bf16[3,512,192]{1,2,0:T(8,128)(2,1)S(1)}, bf16[3,512,192]{2,1,0:T(8,128)(2,1)S(1)}, ...), condition=%wide.region_3.4_spmd, body=%wide.region_0.3_spmd.sunk | while | flops 1220738048 | bytes 27207792 | solution.py:26
  119.2 1.1 multiply_reduce_fusion.2
  120.4 0.0 copy-start
  120.4 1.2 fusion.40
  121.5 0.2 copy-done
  121.8 1.5 fusion.41
  123.3 1.1 multiply_reduce_fusion.2
  124.4 0.0 copy-start
  124.4 1.2 fusion.40
  125.5 0.2 copy-done
  125.8 1.5 fusion.41
  127.3 1.1 multiply_reduce_fusion.2
  128.4 0.0 copy-start
  128.4 1.2 fusion.40
  129.6 0.2 copy-done
  129.8 1.5 fusion.41
  131.3 1.1 copy.19
  132.4 6.5 %all-to-all-start.2 = ((bf16[8,192,192]{2,1,0:T(8,128)(2,1)}), bf16[8,192,192]{2,1,0:T(8,128)(2,1)S(1)}, u32[]{:S(2)}, u32[]{:S(2)}) async-start(bf16[8,192,192]{2,1,0:T(8,128)(2,1)} %bitcast.8), calls=%async_computation.2 | async-start | bytes 1572864 | tf_op jit(solution)/shard_map/all_to_all | solution.py:55
  139.0 0.0 all-gather.6.cloned.1.call-done
  139.0 3.5 %fusion.23 = f32[2,2,48,1536]{3,2,1,0:T(8,128)S(1)} fusion(bf16[2,2,48,1536]{3,2,1,0:T(8,128)(2,1)S(1)} %bitcast.67, bf16[1,1536,1536]{2,1,0:T(8,128)(2,1)} %all-gather.6.cloned.1.call-done), kind=kOutput, calls=%fused_computation.16 | convolution fusion | flops 905969664 | bytes 6488064 | tf_op jit(solution)/shard_map/dot_general | solution.py:78
  142.6 1.3 collective-permute-start.2
  143.8 12.0 %all-to-all-done.2 = bf16[8,192,192]{2,1,0:T(8,128)(2,1)S(1)} async-done(((bf16[8,192,192]{2,1,0:T(8,128)(2,1)}), bf16[8,192,192]{2,1,0:T(8,128)(2,1)S(1)}, u32[]{:S(2)}, u32[]{:S(2)}) %all-to-all-start.2) | async-done | bytes 589856 | tf_op jit(solution)/shard_map/all_to_all | solution.py:55
  155.9 0.4 copy.20
  156.3 0.7 reshape.32
  157.0 0.5 collective-permute-done.2
  157.5 1.1 bitcast_add_fusion
  158.7 4.1 %collective-permute-start.3 = (f32[48,1536]{1,0:T(8,128)S(1)}, f32[48,1536]{1,0:T(8,128)S(1)}, u32[]{:S(2)}, u32[]{:S(2)}) collective-permute-start(f32[48,1536]{1,0:T(8,128)S(1)} %get-tuple-element.45), channel_id=1, source_target_pairs={{0,0},{1,1},{2,4},{3,5},{4,8},{5,9},{6,12},{7,13},{8,16},{9,17},{1... | collective-permute-start | bytes 884744 | tf_op jit(solution)/shard_map/ppermute | solution.py:109
  162.8 1.2 collective-permute-start.4
  164.1 0.0 all-gather.4.cloned.1.call-done
  164.1 4.2 %fusion.25 = bf16[1,192,1536]{2,1,0:T(8,128)(2,1)} fusion(bf16[192,1536]{1,0:T(8,128)(2,1)S(1)} %reshape.32, bf16[1536,1536]{1,0:T(8,128)(2,1)} %bitcast.69), kind=kOutput, calls=%fused_computation.19 | convolution fusion | flops 906264576 | bytes 5898240 | tf_op jit(solution)/shard_map/dot_general | solution.py:84
  168.3 2.5 %collective-permute-done.3 = f32[48,1536]{1,0:T(8,128)S(1)} collective-permute-done((f32[48,1536]{1,0:T(8,128)S(1)}, f32[48,1536]{1,0:T(8,128)S(1)}, u32[]{:S(2)}, u32[]{:S(2)}) %collective-permute-start.3) | collective-permute-done | bytes 294944 | tf_op jit(solution)/shard_map/ppermute | solution.py:109
  170.8 5.0 %collective-permute-done.4 = f32[48,1536]{1,0:T(8,128)S(1)} collective-permute-done((f32[48,1536]{1,0:T(8,128)S(1)}, f32[48,1536]{1,0:T(8,128)S(1)}, u32[]{:S(2)}, u32[]{:S(2)}) %collective-permute-start.4) | collective-permute-done | bytes 294944 | tf_op jit(solution)/shard_map/ppermute | solution.py:109
  175.8 0.7 add.42
  (4 shorter events, 0.1 us)
Async XLA Ops:
  7.2 2.5 %copy-start.1 = (bf16[1,192,1536]{2,1,0:T(8,128)(2,1)S(1)}, bf16[1,192,1536]{2,1,0:T(8,128)(2,1)}, u32[]{:S(2)}) copy-start(bf16[1,192,1536]{2,1,0:T(8,128)(2,1)} %param.8) | copy-start | bytes 1769476
  7.2 4.0 %copy-start.2 = (bf16[1,192,1536]{2,1,0:T(8,128)(2,1)S(1)}, bf16[1,192,1536]{2,1,0:T(8,128)(2,1)}, u32[]{:S(2)}) copy-start(bf16[1,192,1536]{2,1,0:T(8,128)(2,1)} %param.7) | copy-start | bytes 1769476
  7.2 131.9 %all-gather.6.cloned.1.call-start = ((), (), s32[]{:S(2)}) async-start(), calls=%async_computation.4 | async-start | bytes 5308416 | tf_op jit(solution)/shard_map/all_gather | solution.py:52
  15.5 72.1 %all-to-all-start = ((bf16[8,192,576]{2,1,0:T(8,128)(2,1)}), bf16[8,192,576]{2,1,0:T(8,128)(2,1)S(1)}, u32[]{:S(2)}, u32[]{:S(2)}) async-start(bf16[8,192,576]{2,1,0:T(8,128)(2,1)} %pad_maximum_fusion), calls=%async_computation | async-start | bytes 3932160 | tf_op jit(solution)/shard_map/all_to_all | solution.py:55
  20.8 143.2 %all-gather.4.cloned.1.call-start = ((), (), s32[]{:S(2)}) async-start(), calls=%async_computation.3 | async-start | bytes 5013504 | tf_op jit(solution)/shard_map/all_gather | solution.py:49
  22.4 63.8 %collective-permute-start = (bf16[8,192,384]{2,1,0:T(8,128)(2,1)}, bf16[8,192,384]{2,1,0:T(8,128)(2,1)}, u32[]{:S(2)}, u32[]{:S(2)}) collective-permute-start(bf16[8,192,384]{2,1,0:T(8,128)(2,1)} %pad_maximum_fusion.2), channel_id=1, source_target_pairs={{0,16},{16,0},{1,17},{17,1},{2,18},{18,2},{3,19},{19,3},{4,20},{20... | collective-permute-start | bytes 3538952 | tf_op jit(solution)/shard_map/ppermute | solution.py:63
  24.7 5.4 %collective-permute-start.1 = (bf16[48,1536]{1,0:T(8,128)(2,1)}, bf16[48,1536]{1,0:T(8,128)(2,1)S(1)}, u32[]{:S(2)}, u32[]{:S(2)}) collective-permute-start(bf16[48,1536]{1,0:T(8,128)(2,1)} %param.10), channel_id=1, source_target_pairs={{0,1},{1,0},{2,3},{3,2},{4,5},{5,4},{6,7},{7,6},{8,9},{9,8},{10,11... | collective-permute-start | bytes 442376 | tf_op jit(solution)/shard_map/ppermute | solution.py:44
  87.6 27.8 %all-to-all-start.1 = ((bf16[8,192,384]{2,1,0:T(8,128)(2,1)}), bf16[8,192,384]{2,1,0:T(8,128)(2,1)}, u32[]{:S(2)}, u32[]{:S(2)}) async-start(bf16[8,192,384]{2,1,0:T(8,128)(2,1)} %collective-permute-done), calls=%async_computation.1 | async-start | bytes 2359296 | tf_op jit(solution)/shard_map/all_to_all | solution.py:55
  120.4 1.4 copy-start
  124.4 1.4 copy-start
  128.4 1.4 copy-start
  132.4 23.4 %all-to-all-start.2 = ((bf16[8,192,192]{2,1,0:T(8,128)(2,1)}), bf16[8,192,192]{2,1,0:T(8,128)(2,1)S(1)}, u32[]{:S(2)}, u32[]{:S(2)}) async-start(bf16[8,192,192]{2,1,0:T(8,128)(2,1)} %bitcast.8), calls=%async_computation.2 | async-start | bytes 1572864 | tf_op jit(solution)/shard_map/all_to_all | solution.py:55
  142.6 15.0 %collective-permute-start.2 = (f32[2,48,1536]{2,1,0:T(8,128)S(1)}, f32[2,48,1536]{2,1,0:T(8,128)}, u32[]{:S(2)}, u32[]{:S(2)}) collective-permute-start(f32[2,48,1536]{2,1,0:T(8,128)S(1)} %dynamic-slice_bitcast_fusion), channel_id=1, source_target_pairs={{0,1},{1,0},{2,3},{3,2},{4,5},{5,4},{6,7},{7,6},{8,9},{9,8},{10,11... | collective-permute-start | bytes 1769480 | tf_op jit(solution)/shard_map/ppermute | solution.py:95
  158.7 12.1 %collective-permute-start.3 = (f32[48,1536]{1,0:T(8,128)S(1)}, f32[48,1536]{1,0:T(8,128)S(1)}, u32[]{:S(2)}, u32[]{:S(2)}) collective-permute-start(f32[48,1536]{1,0:T(8,128)S(1)} %get-tuple-element.45), channel_id=1, source_target_pairs={{0,0},{1,1},{2,4},{3,5},{4,8},{5,9},{6,12},{7,13},{8,16},{9,17},{1... | collective-permute-start | bytes 884744 | tf_op jit(solution)/shard_map/ppermute | solution.py:109
  162.8 13.0 %collective-permute-start.4 = (f32[48,1536]{1,0:T(8,128)S(1)}, f32[48,1536]{1,0:T(8,128)S(1)}, u32[]{:S(2)}, u32[]{:S(2)}) collective-permute-start(f32[48,1536]{1,0:T(8,128)S(1)} %get-tuple-element.44), channel_id=1, source_target_pairs={{0,2},{1,3},{2,6},{3,7},{4,10},{5,11},{6,14},{7,15},{8,18},{9,19},... | collective-permute-start | bytes 884744 | tf_op jit(solution)/shard_map/ppermute | solution.py:109
Sparse Core Ops, SparseCore 0:
  9.7 77.0 all-gather.5
  89.6 62.8 all-gather.3

commit v8 on v7

--- a/solution.py
+++ b/solution.py
@@ -59,17 +59,23 @@
 
     side_index = lax.axis_index("side")
     kv_raw = jnp.concatenate([by_head(key_vectors), by_head(value_vectors)], axis=2)
-    kv_crossed = [
-        lax.ppermute(kv_raw, "side", [(g, (g + step) % side_count) for g in range(side_count)])
-        for step in range(1, side_count)
-    ]
+    inner_index = lax.axis_index("inner")
+    kv_crossed = []
+    for step in range(1, side_count):
+        for shift in range(head_count):
+            perm = [
+                (g * head_count + i, ((g + step) % side_count) * head_count + (i + shift) % head_count)
+                for g in range(side_count)
+                for i in range(head_count)
+            ]
+            outgoing = lax.dynamic_index_in_dim(
+                kv_raw, (inner_index + shift) % head_count, axis=0, keepdims=False
+            )
+            kv_crossed.append(lax.ppermute(outgoing, ("side", "inner"), perm))
     stacked = jnp.concatenate([by_head(queries), kv_raw], axis=2)
     got = a2a(stacked).reshape(head_count * row_count, 3 * head_width)
     query_here = got[:, :head_width]
-    kv_parts = [got[:, head_width:]]
-    for crossed in kv_crossed:
-        kv_parts.append(a2a(crossed).reshape(head_count * row_count, 2 * head_width))
-    kv_all = jnp.concatenate(kv_parts, axis=0)
+    kv_all = jnp.concatenate([got[:, head_width:]] + kv_crossed, axis=0)
     key_all = kv_all[:, :head_width]
     value_all = kv_all[:, head_width:]
 

time: 186 us -> 175 us (0.941)
  waiting for transfers between devices: 101 us -> 87.1 us
  local copies, waits for them, and re-layouts: 10.3 us -> 15.9 us
  other arithmetic: 14.4 us -> 11.3 us
    ppermute x1 -> x8, waiting for transfers between devices: 54.3 us -> 27.7 us  [local(): kv_crossed.append(lax.ppermute(outgoing, ('side', 'inner'), perm))]
    ppermute x1 -> x8, starting transfers between devices: 2.31 us -> 12.1 us  [local(): kv_crossed.append(lax.ppermute(outgoing, ('side', 'inner'), perm))]
    all_to_all x3 -> x2, waiting for transfers between devices: 34 us -> 43.7 us  [a2a(): lax.all_to_all(tensor, 'inner', split_axis=0, concat_axis=0, tiled=True)]
    all_to_all x3 -> x2, starting transfers between devices: 17.5 us -> 9.01 us  [a2a(): lax.all_to_all(tensor, 'inner', split_axis=0, concat_axis=0, tiled=True)]
    concatenate x2 -> x0, other arithmetic: 5.34 us -> none  [the longest x1 3.81 us: local(): kv_all = jnp.concatenate(kv_parts, axis=0)]
    unnamed x4 -> x20, local copies, waits for them, and re-layouts: 0.01 us -> 5.23 us
    ppermute x1, waiting for transfers between devices: 0.53 us -> 3.19 us  [local(): kept = kept + lax.ppermute(sent, 'dp', [(0, 1), (1, 0)])]
    squeeze x0 -> x2, other arithmetic: none -> 2.1 us  [local(): lax.dynamic_index_in_dim(kv_raw, (inner_index + shift) % head_count, axis...]
  transfers between devices with their start and end apart: 10 -> 16, of which waited for: 8 -> 9; matrix products, arithmetic and copies ran while one was open for 21% -> 24% of each run, Pallas kernels for 0% -> 0%
where the time goes in v8:
time: 175 us; the launch traced here: 172 us
  waiting for transfers between devices  87.1 us (50%)
  starting transfers between devices  27.9 us (16%)
  local copies, waits for them, and re-layouts  15.9 us (9%)
  matrix products  15.4 us (9%)
  between operations  14.4 us (8%)
  other arithmetic  11.3 us (6%)
    all_to_all x2, waiting for transfers between devices, a2a(): lax.all_to_all(tensor, 'inner', split_axis=0, concat_axis=0, tiled=True)  43.7 us
    ppermute x8, waiting for transfers between devices, local(): kv_crossed.append(lax.ppermute(outgoing, ('side', 'inner'), perm))  27.7 us
    ppermute x8, starting transfers between devices, local(): kv_crossed.append(lax.ppermute(outgoing, ('side', 'inner'), perm))  12.1 us
    all_to_all x2, starting transfers between devices, a2a(): lax.all_to_all(tensor, 'inner', split_axis=0, concat_axis=0, tiled=True)  9.01 us
    ppermute x2, waiting for transfers between devices, local(): arrived = lax.ppermute(outgoing, ALL, perm)  7.38 us
    unnamed x20, local copies, waits for them, and re-layouts  5.23 us
    ppermute x1, waiting for transfers between devices, local(): lax.ppermute(w_out, 'dp', [(p, (p + 1) % dp_count) for p in range(dp_coun...  4.5 us
    dot_general x3, matrix products, one_block(): mixed = jnp.dot(weights, value_all, preferred_element_type=jnp.float32)  4.41 us
  transfers between devices with their start and end apart: 16, of which 9 were waited for; matrix products, arithmetic and copies ran while one was open for 24% of the time, Pallas kernels for 0%

profile of v8, /device:TPU:1, one launch (start us, length us, event | category | flops | bytes accessed | tf_op | source)
XLA Modules:
  0.0 172.1 jit_solution(5317191508961217877)
XLA Ops:
  7.2 0.0 all-gather.6.cloned.1.call-start
  7.2 0.7 all-gather.6.cloned.1.call-update
  7.9 1.7 %reshape_squeeze.10 = bf16[192,8,192]{2,1,0:T(8,128)(2,1)S(1)} reshape(bf16[1,192,1536]{2,1,0:T(8,128)(2,1)} %param.8) | data formatting | bytes 1179648 | tf_op jit(solution)/shard_map/reshape;squeeze | solution.py:58
  9.7 1.5 reshape_squeeze.11
  11.2 0.6 reshape_squeeze.9
  11.8 0.2 copy.27
  12.0 1.5 copy_bitcast_fusion
  13.4 2.1 %pad_maximum_fusion = bf16[8,192,576]{2,1,0:T(8,128)(2,1)} fusion(bf16[8,192,192]{2,1,0:T(8,128)(2,1)S(1)} %get-tuple-element.56, bf16[8,192,192]{2,1,0:T(8,128)(2,1)S(1)} %get-tuple-element.57, bf16[8,192,192]{2,1,0:T(8,128)(2,1)S(1)} %bitcast.81), kind=kLoop, calls=%fused_computation.20 | loop fusion | flops 5308416 | bytes 3538944 | tf_op jit(solution)/shard_map/concatenate | solution.py:75
  15.5 5.3 %all-to-all-start = ((bf16[8,192,576]{2,1,0:T(8,128)(2,1)}), bf16[8,192,576]{2,1,0:T(8,128)(2,1)S(1)}, u32[]{:S(2)}, u32[]{:S(2)}) async-start(bf16[8,192,576]{2,1,0:T(8,128)(2,1)} %pad_maximum_fusion), calls=%async_computation | async-start | bytes 3932160 | tf_op jit(solution)/shard_map/all_to_all | solution.py:55
  20.8 1.2 collective-permute-start.8
  22.1 4.5 %collective-permute-done.8 = bf16[48,1536]{1,0:T(8,128)(2,1)} collective-permute-done((bf16[48,1536]{1,0:T(8,128)(2,1)}, bf16[48,1536]{1,0:T(8,128)(2,1)}, u32[]{:S(2)}, u32[]{:S(2)}) %collective-permute-start.8) | collective-permute-done | bytes 147488 | tf_op jit(solution)/shard_map/ppermute | solution.py:44
  26.6 1.0 select_bitcast_fusion.1
  27.6 0.7 pad_maximum_fusion.1
  28.4 1.3 fusion.41
  29.7 2.3 %collective-permute-start = (bf16[192,384]{1,0:T(8,128)(2,1)}, bf16[192,384]{1,0:T(8,128)(2,1)}, u32[]{:S(2)}, u32[]{:S(2)}) collective-permute-start(bf16[192,384]{1,0:T(8,128)(2,1)} %get-tuple-element.45), channel_id=1, source_target_pairs={{0,16},{2,18},{4,20},{6,22},{8,24},{10,26},{12,28},{14,30},{16,0},... | collective-permute-start | bytes 442376 | tf_op jit(solution)/shard_map/ppermute | solution.py:74
  32.0 2.2 %collective-permute-start.1 = (bf16[192,384]{1,0:T(8,128)(2,1)}, bf16[192,384]{1,0:T(8,128)(2,1)}, u32[]{:S(2)}, u32[]{:S(2)}) collective-permute-start(bf16[192,384]{1,0:T(8,128)(2,1)} %get-tuple-element.46), channel_id=1, source_target_pairs={{0,18},{2,20},{4,22},{6,24},{8,26},{10,28},{12,30},{14,16},{16,2},... | collective-permute-start | bytes 442376 | tf_op jit(solution)/shard_map/ppermute | solution.py:74
  34.1 2.3 %collective-permute-start.2 = (bf16[192,384]{1,0:T(8,128)(2,1)}, bf16[192,384]{1,0:T(8,128)(2,1)}, u32[]{:S(2)}, u32[]{:S(2)}) collective-permute-start(bf16[192,384]{1,0:T(8,128)(2,1)} %get-tuple-element.47), channel_id=1, source_target_pairs={{0,20},{2,22},{4,24},{6,26},{8,28},{10,30},{12,16},{14,18},{16,4},... | collective-permute-start | bytes 442376 | tf_op jit(solution)/shard_map/ppermute | solution.py:74
  36.5 1.2 collective-permute-start.3
  37.7 1.3 collective-permute-start.4
  38.9 0.8 fusion.34
  39.8 33.8 %all-to-all-done = bf16[8,192,576]{2,1,0:T(8,128)(2,1)S(1)} async-done(((bf16[8,192,576]{2,1,0:T(8,128)(2,1)}), bf16[8,192,576]{2,1,0:T(8,128)(2,1)S(1)}, u32[]{:S(2)}, u32[]{:S(2)}) %all-to-all-start) | async-done | bytes 1769504 | tf_op jit(solution)/shard_map/all_to_all | solution.py:55
  73.6 0.5 slice_dynamic-update-slice_fusion
  74.1 0.1 collective-permute-start.5
  74.1 0.9 constant_dynamic-update-slice_fusion.7
  75.1 2.8 %collective-permute-start.6 = (bf16[192,384]{1,0:T(8,128)(2,1)S(1)}, bf16[192,384]{1,0:T(8,128)(2,1)S(1)}, u32[]{:S(2)}, u32[]{:S(2)}) collective-permute-start(bf16[192,384]{1,0:T(8,128)(2,1)S(1)} %copy-done.4), channel_id=1, source_target_pairs={{0,28},{2,30},{4,16},{6,18},{8,20},{10,22},{12,24},{14,26},{16,12}... | collective-permute-start | bytes 442376 | tf_op jit(solution)/shard_map/ppermute | solution.py:74
  77.9 0.9 constant_dynamic-update-slice_fusion.6
  78.8 0.1 collective-permute-start.7
  78.9 0.9 constant_dynamic-update-slice_fusion.5
  79.8 0.9 constant_dynamic-update-slice_fusion.4
  80.8 0.9 constant_dynamic-update-slice_fusion.3
  81.7 6.4 %collective-permute-done.5 = bf16[192,384]{1,0:T(8,128)(2,1)S(1)} collective-permute-done((bf16[192,384]{1,0:T(8,128)(2,1)S(1)}, bf16[192,384]{1,0:T(8,128)(2,1)S(1)}, u32[]{:S(2)}, u32[]{:S(2)}) %collective-permute-start.5) | collective-permute-done | bytes 147488 | tf_op jit(solution)/shard_map/ppermute | solution.py:74
  88.1 0.1 slice.16
  88.2 18.5 %collective-permute-done.6 = bf16[192,384]{1,0:T(8,128)(2,1)S(1)} collective-permute-done((bf16[192,384]{1,0:T(8,128)(2,1)S(1)}, bf16[192,384]{1,0:T(8,128)(2,1)S(1)}, u32[]{:S(2)}, u32[]{:S(2)}) %collective-permute-start.6) | collective-permute-done | bytes 147488 | tf_op jit(solution)/shard_map/ppermute | solution.py:74
  106.7 2.8 %collective-permute-done.7 = bf16[192,384]{1,0:T(8,128)(2,1)S(1)} collective-permute-done((bf16[192,384]{1,0:T(8,128)(2,1)S(1)}, bf16[192,384]{1,0:T(8,128)(2,1)S(1)}, u32[]{:S(2)}, u32[]{:S(2)}) %collective-permute-start.7) | collective-permute-done | bytes 147488 | tf_op jit(solution)/shard_map/ppermute | solution.py:74
  109.6 1.9 %fusion.42 = (bf16[3072,192]{1,0:T(8,128)(2,1)}, bf16[3072,192]{1,0:T(8,128)(2,1)S(1)}) fusion(bf16[3072,384]{1,0:T(8,128)(2,1)S(1)} %constant_dynamic-update-slice_fusion), kind=kLoop, calls=%fused_computation.72 | loop fusion | bytes 4718592 | tf_op jit(solution)/shard_map/slice | solution.py:80
  111.5 12.1 %while.10 = (s32[]{:T(128)}, bf16[3,512,192]{1,2,0:T(8,128)(2,1)S(1)}, bf16[3,512,192]{2,1,0:T(8,128)(2,1)S(1)}, bf16[3072,192]{1,0:T(8,128)(2,1)S(1)}, bf16[3072,192]{1,0:T(8,128)(2,1)}, /*index=5*/s32[]{:T(128)}) while((s32[]{:T(128)}, bf16[3,512,192]{1,2,0:T(8,128)(2,1)S(1)}, bf16[3,512,192]{2,1,0:T(8,128)(2,1)S(1)}, ...), condition=%wide.region_3.4_spmd, body=%wide.region_0.3_spmd.sunk | while | flops 1220738048 | bytes 27207784 | solution.py:26
  111.5 1.1 multiply_reduce_fusion.2
  112.6 1.2 fusion.56
  113.7 0.2 copy-done.1
  114.0 1.5 fusion.57
  115.5 1.1 multiply_reduce_fusion.2
  116.6 1.2 fusion.56
  117.8 0.3 copy-done.1
  118.0 1.5 fusion.57
  119.5 1.1 multiply_reduce_fusion.2
  120.6 1.2 fusion.56
  121.8 0.2 copy-done.1
  122.0 1.5 fusion.57
  123.5 1.2 copy.19
  124.7 3.7 %all-to-all-start.1 = ((bf16[8,192,192]{2,1,0:T(8,128)(2,1)}), bf16[8,192,192]{2,1,0:T(8,128)(2,1)S(1)}, u32[]{:S(2)}, u32[]{:S(2)}) async-start(bf16[8,192,192]{2,1,0:T(8,128)(2,1)} %bitcast.15), calls=%async_computation.1 | async-start | bytes 1572864 | tf_op jit(solution)/shard_map/all_to_all | solution.py:55
  128.4 0.0 all-gather.6.cloned.1.call-done
  128.5 3.4 %fusion.23 = f32[2,2,48,1536]{3,2,1,0:T(8,128)S(1)} fusion(bf16[2,2,48,1536]{3,2,1,0:T(8,128)(2,1)S(1)} %bitcast.82, bf16[1,1536,1536]{2,1,0:T(8,128)(2,1)} %all-gather.6.cloned.1.call-done), kind=kOutput, calls=%fused_computation.16 | convolution fusion | flops 905969664 | bytes 6488064 | tf_op jit(solution)/shard_map/dot_general | solution.py:84
  132.0 1.3 collective-permute-start.9
  133.2 9.9 %all-to-all-done.1 = bf16[8,192,192]{2,1,0:T(8,128)(2,1)S(1)} async-done(((bf16[8,192,192]{2,1,0:T(8,128)(2,1)}), bf16[8,192,192]{2,1,0:T(8,128)(2,1)S(1)}, u32[]{:S(2)}, u32[]{:S(2)}) %all-to-all-start.1) | async-done | bytes 589856 | tf_op jit(solution)/shard_map/all_to_all | solution.py:55
  143.1 0.4 copy.20
  143.5 0.7 reshape.28
  144.2 3.2 %collective-permute-done.9 = f32[2,48,1536]{2,1,0:T(8,128)} collective-permute-done((f32[2,48,1536]{2,1,0:T(8,128)S(1)}, f32[2,48,1536]{2,1,0:T(8,128)}, u32[]{:S(2)}, u32[]{:S(2)}) %collective-permute-start.9) | collective-permute-done | bytes 589856 | tf_op jit(solution)/shard_map/ppermute | solution.py:101
  147.4 1.1 bitcast_add_fusion
  148.6 3.0 %collective-permute-start.10 = (f32[48,1536]{1,0:T(8,128)S(1)}, f32[48,1536]{1,0:T(8,128)S(1)}, u32[]{:S(2)}, u32[]{:S(2)}) collective-permute-start(f32[48,1536]{1,0:T(8,128)S(1)} %get-tuple-element.53), channel_id=1, source_target_pairs={{0,0},{1,1},{2,4},{3,5},{4,8},{5,9},{6,12},{7,13},{8,16},{9,17},{1... | collective-permute-start | bytes 884744 | tf_op jit(solution)/shard_map/ppermute | solution.py:115
  151.7 1.2 collective-permute-start.11
  152.9 4.2 %fusion.25 = bf16[1,192,1536]{2,1,0:T(8,128)(2,1)} fusion(bf16[192,1536]{1,0:T(8,128)(2,1)S(1)} %reshape.28, bf16[1536,1536]{1,0:T(8,128)(2,1)} %bitcast.84), kind=kOutput, calls=%fused_computation.19 | convolution fusion | flops 906264576 | bytes 5898240 | tf_op jit(solution)/shard_map/dot_general | solution.py:90
  157.1 3.6 %collective-permute-done.10 = f32[48,1536]{1,0:T(8,128)S(1)} collective-permute-done((f32[48,1536]{1,0:T(8,128)S(1)}, f32[48,1536]{1,0:T(8,128)S(1)}, u32[]{:S(2)}, u32[]{:S(2)}) %collective-permute-start.10) | collective-permute-done | bytes 294944 | tf_op jit(solution)/shard_map/ppermute | solution.py:115
  160.7 3.8 %collective-permute-done.11 = f32[48,1536]{1,0:T(8,128)S(1)} collective-permute-done((f32[48,1536]{1,0:T(8,128)S(1)}, f32[48,1536]{1,0:T(8,128)S(1)}, u32[]{:S(2)}, u32[]{:S(2)}) %collective-permute-start.11) | collective-permute-done | bytes 294944 | tf_op jit(solution)/shard_map/ppermute | solution.py:115
  164.5 0.7 add.135
  (30 shorter events, 0.3 us)
Async XLA Ops:
  7.2 2.5 %copy-start.2 = (bf16[1,192,1536]{2,1,0:T(8,128)(2,1)S(1)}, bf16[1,192,1536]{2,1,0:T(8,128)(2,1)}, u32[]{:S(2)}) copy-start(bf16[1,192,1536]{2,1,0:T(8,128)(2,1)} %param.9) | copy-start | bytes 1769476
  7.2 4.0 %copy-start.3 = (bf16[1,192,1536]{2,1,0:T(8,128)(2,1)S(1)}, bf16[1,192,1536]{2,1,0:T(8,128)(2,1)}, u32[]{:S(2)}) copy-start(bf16[1,192,1536]{2,1,0:T(8,128)(2,1)} %param.7) | copy-start | bytes 1769476
  7.2 121.3 %all-gather.6.cloned.1.call-start = ((), (), s32[]{:S(2)}) async-start(), calls=%async_computation.3 | async-start | bytes 5308416 | tf_op jit(solution)/shard_map/all_gather | solution.py:52
  15.5 58.1 %all-to-all-start = ((bf16[8,192,576]{2,1,0:T(8,128)(2,1)}), bf16[8,192,576]{2,1,0:T(8,128)(2,1)S(1)}, u32[]{:S(2)}, u32[]{:S(2)}) async-start(bf16[8,192,576]{2,1,0:T(8,128)(2,1)} %pad_maximum_fusion), calls=%async_computation | async-start | bytes 3932160 | tf_op jit(solution)/shard_map/all_to_all | solution.py:55
  20.8 132.0 %all-gather.4.cloned.1.call-start = ((), (), s32[]{:S(2)}) async-start(), calls=%async_computation.2 | async-start | bytes 5013504 | tf_op jit(solution)/shard_map/all_gather | solution.py:49
  20.8 5.7 %collective-permute-start.8 = (bf16[48,1536]{1,0:T(8,128)(2,1)}, bf16[48,1536]{1,0:T(8,128)(2,1)}, u32[]{:S(2)}, u32[]{:S(2)}) collective-permute-start(bf16[48,1536]{1,0:T(8,128)(2,1)} %param.10), channel_id=1, source_target_pairs={{0,1},{1,0},{2,3},{3,2},{4,5},{5,4},{6,7},{7,6},{8,9},{9,8},{10,11... | collective-permute-start | bytes 442376 | tf_op jit(solution)/shard_map/ppermute | solution.py:44
  29.7 44.4 %collective-permute-start = (bf16[192,384]{1,0:T(8,128)(2,1)}, bf16[192,384]{1,0:T(8,128)(2,1)}, u32[]{:S(2)}, u32[]{:S(2)}) collective-permute-start(bf16[192,384]{1,0:T(8,128)(2,1)} %get-tuple-element.45), channel_id=1, source_target_pairs={{0,16},{2,18},{4,20},{6,22},{8,24},{10,26},{12,28},{14,30},{16,0},... | collective-permute-start | bytes 442376 | tf_op jit(solution)/shard_map/ppermute | solution.py:74
  32.0 43.1 %collective-permute-start.1 = (bf16[192,384]{1,0:T(8,128)(2,1)}, bf16[192,384]{1,0:T(8,128)(2,1)}, u32[]{:S(2)}, u32[]{:S(2)}) collective-permute-start(bf16[192,384]{1,0:T(8,128)(2,1)} %get-tuple-element.46), channel_id=1, source_target_pairs={{0,18},{2,20},{4,22},{6,24},{8,26},{10,28},{12,30},{14,16},{16,2},... | collective-permute-start | bytes 442376 | tf_op jit(solution)/shard_map/ppermute | solution.py:74
  34.1 44.6 %collective-permute-start.2 = (bf16[192,384]{1,0:T(8,128)(2,1)}, bf16[192,384]{1,0:T(8,128)(2,1)}, u32[]{:S(2)}, u32[]{:S(2)}) collective-permute-start(bf16[192,384]{1,0:T(8,128)(2,1)} %get-tuple-element.47), channel_id=1, source_target_pairs={{0,20},{2,22},{4,24},{6,26},{8,28},{10,30},{12,16},{14,18},{16,4},... | collective-permute-start | bytes 442376 | tf_op jit(solution)/shard_map/ppermute | solution.py:74
  36.5 43.4 %collective-permute-start.3 = (bf16[192,384]{1,0:T(8,128)(2,1)}, bf16[192,384]{1,0:T(8,128)(2,1)}, u32[]{:S(2)}, u32[]{:S(2)}) collective-permute-start(bf16[192,384]{1,0:T(8,128)(2,1)} %get-tuple-element.48), channel_id=1, source_target_pairs={{0,22},{2,24},{4,26},{6,28},{8,30},{10,16},{12,18},{14,20},{16,6},... | collective-permute-start | bytes 442376 | tf_op jit(solution)/shard_map/ppermute | solution.py:74
  37.7 43.1 %collective-permute-start.4 = (bf16[192,384]{1,0:T(8,128)(2,1)}, bf16[192,384]{1,0:T(8,128)(2,1)}, u32[]{:S(2)}, u32[]{:S(2)}) collective-permute-start(bf16[192,384]{1,0:T(8,128)(2,1)} %get-tuple-element.49), channel_id=1, source_target_pairs={{0,24},{2,26},{4,28},{6,30},{8,16},{10,18},{12,20},{14,22},{16,8},... | collective-permute-start | bytes 442376 | tf_op jit(solution)/shard_map/ppermute | solution.py:74
  39.8 34.3 %copy-start.5 = (bf16[192,384]{1,0:T(8,128)(2,1)S(1)}, bf16[192,384]{1,0:T(8,128)(2,1)}, u32[]{:S(2)}) copy-start(bf16[192,384]{1,0:T(8,128)(2,1)} %get-tuple-element.51) | copy-start | bytes 442372
  39.8 35.3 %copy-start.4 = (bf16[192,384]{1,0:T(8,128)(2,1)S(1)}, bf16[192,384]{1,0:T(8,128)(2,1)}, u32[]{:S(2)}) copy-start(bf16[192,384]{1,0:T(8,128)(2,1)} %get-tuple-element.50) | copy-start | bytes 442372
  39.8 39.0 %copy-start.6 = (bf16[192,384]{1,0:T(8,128)(2,1)S(1)}, bf16[192,384]{1,0:T(8,128)(2,1)}, u32[]{:S(2)}) copy-start(bf16[192,384]{1,0:T(8,128)(2,1)} %get-tuple-element.44) | copy-start | bytes 442372
  74.1 14.0 %collective-permute-start.5 = (bf16[192,384]{1,0:T(8,128)(2,1)S(1)}, bf16[192,384]{1,0:T(8,128)(2,1)S(1)}, u32[]{:S(2)}, u32[]{:S(2)}) collective-permute-start(bf16[192,384]{1,0:T(8,128)(2,1)S(1)} %copy-done.5), channel_id=1, source_target_pairs={{0,26},{2,28},{4,30},{6,16},{8,18},{10,20},{12,22},{14,24},{16,10}... | collective-permute-start | bytes 442376 | tf_op jit(solution)/shard_map/ppermute | solution.py:74
  75.1 31.6 %collective-permute-start.6 = (bf16[192,384]{1,0:T(8,128)(2,1)S(1)}, bf16[192,384]{1,0:T(8,128)(2,1)S(1)}, u32[]{:S(2)}, u32[]{:S(2)}) collective-permute-start(bf16[192,384]{1,0:T(8,128)(2,1)S(1)} %copy-done.4), channel_id=1, source_target_pairs={{0,28},{2,30},{4,16},{6,18},{8,20},{10,22},{12,24},{14,26},{16,12}... | collective-permute-start | bytes 442376 | tf_op jit(solution)/shard_map/ppermute | solution.py:74
  78.8 30.7 %collective-permute-start.7 = (bf16[192,384]{1,0:T(8,128)(2,1)S(1)}, bf16[192,384]{1,0:T(8,128)(2,1)S(1)}, u32[]{:S(2)}, u32[]{:S(2)}) collective-permute-start(bf16[192,384]{1,0:T(8,128)(2,1)S(1)} %copy-done.6), channel_id=1, source_target_pairs={{0,30},{2,16},{4,18},{6,20},{8,22},{10,24},{12,26},{14,28},{16,14}... | collective-permute-start | bytes 442376 | tf_op jit(solution)/shard_map/ppermute | solution.py:74
  109.5 1.9 %copy-start = (bf16[3,512,192]{1,2,0:T(8,128)(2,1)S(1)}, bf16[3,512,192]{1,2,0:T(8,128)(2,1)}, u32[]{:S(2)}) copy-start(bf16[3,512,192]{1,2,0:T(8,128)(2,1)} %custom-call.1) | copy-start | bytes 1769476
  112.6 1.4 copy-start.1
  116.6 1.4 copy-start.1
  120.6 1.4 copy-start.1
  124.7 18.4 %all-to-all-start.1 = ((bf16[8,192,192]{2,1,0:T(8,128)(2,1)}), bf16[8,192,192]{2,1,0:T(8,128)(2,1)S(1)}, u32[]{:S(2)}, u32[]{:S(2)}) async-start(bf16[8,192,192]{2,1,0:T(8,128)(2,1)} %bitcast.15), calls=%async_computation.1 | async-start | bytes 1572864 | tf_op jit(solution)/shard_map/all_to_all | solution.py:55
  132.0 15.5 %collective-permute-start.9 = (f32[2,48,1536]{2,1,0:T(8,128)S(1)}, f32[2,48,1536]{2,1,0:T(8,128)}, u32[]{:S(2)}, u32[]{:S(2)}) collective-permute-start(f32[2,48,1536]{2,1,0:T(8,128)S(1)} %dynamic-slice_bitcast_fusion), channel_id=1, source_target_pairs={{0,1},{1,0},{2,3},{3,2},{4,5},{5,4},{6,7},{7,6},{8,9},{9,8},{10,11... | collective-permute-start | bytes 1769480 | tf_op jit(solution)/shard_map/ppermute | solution.py:101
  148.6 12.1 %collective-permute-start.10 = (f32[48,1536]{1,0:T(8,128)S(1)}, f32[48,1536]{1,0:T(8,128)S(1)}, u32[]{:S(2)}, u32[]{:S(2)}) collective-permute-start(f32[48,1536]{1,0:T(8,128)S(1)} %get-tuple-element.53), channel_id=1, source_target_pairs={{0,0},{1,1},{2,4},{3,5},{4,8},{5,9},{6,12},{7,13},{8,16},{9,17},{1... | collective-permute-start | bytes 884744 | tf_op jit(solution)/shard_map/ppermute | solution.py:115
  151.7 12.8 %collective-permute-start.11 = (f32[48,1536]{1,0:T(8,128)S(1)}, f32[48,1536]{1,0:T(8,128)S(1)}, u32[]{:S(2)}, u32[]{:S(2)}) collective-permute-start(f32[48,1536]{1,0:T(8,128)S(1)} %get-tuple-element.52), channel_id=1, source_target_pairs={{0,2},{1,3},{2,6},{3,7},{4,10},{5,11},{6,14},{7,15},{8,18},{9,19},... | collective-permute-start | bytes 884744 | tf_op jit(solution)/shard_map/ppermute | solution.py:115
Sparse Core Ops, SparseCore 0:
  9.7 62.8 all-gather.5
  75.4 63.8 all-gather.3

commit v9 on v8

--- a/solution.py
+++ b/solution.py
@@ -29,7 +29,9 @@
     return blocks.reshape(query_count, head_width)
 
 
-ALL = ("side", "inner", "dp")
+ALL = ("side", "chip", "core", "dp")
+INNER = ("chip", "core")
+SEQ = ("side", "chip", "core")
 
 
 def local(queries, key_vectors, value_vectors, w_out, cotangent):
@@ -41,25 +43,29 @@
     width = queries.shape[2]
 
     dp_index = lax.axis_index("dp")
-    w_other = lax.ppermute(w_out, "dp", [(p, (p + 1) % dp_count) for p in range(dp_count)])
+    chip_count = lax.axis_size("chip")
+    core_count = lax.axis_size("core")
+    core_index = lax.axis_index("core")
     if dp_count == 2:
+        w_other = lax.ppermute(w_out, "dp", [(0, 1), (1, 0)])
         w_pair = jnp.stack(
             [jnp.where(dp_index == 0, w_out, w_other), jnp.where(dp_index == 0, w_other, w_out)]
         )
-        w_full = lax.all_gather(w_pair, ("side", "inner"), axis=0, tiled=True).reshape(-1, width)
+        w_core = lax.all_gather(w_pair, ("side", "chip"), axis=0, tiled=True).reshape(-1, width)
     else:
-        w_full = lax.all_gather(w_out, ALL, axis=0, tiled=True)
-    cot_side = lax.all_gather(cotangent[0], "inner", axis=0, tiled=True)
+        w_core = lax.all_gather(w_out, ("side", "chip", "dp"), axis=0, tiled=True)
+    w_partner = lax.ppermute(w_core, "core", [(0, 1), (1, 0)])
+    cot_side = lax.all_gather(cotangent[0], INNER, axis=0, tiled=True)
 
     def a2a(tensor):
-        return lax.all_to_all(tensor, "inner", split_axis=0, concat_axis=0, tiled=True)
+        return lax.all_to_all(tensor, INNER, split_axis=0, concat_axis=0, tiled=True)
 
     def by_head(tensor):
         return tensor[0].reshape(row_count, head_count, head_width).transpose(1, 0, 2)
 
     side_index = lax.axis_index("side")
     kv_raw = jnp.concatenate([by_head(key_vectors), by_head(value_vectors)], axis=2)
-    inner_index = lax.axis_index("inner")
+    inner_index = lax.axis_index("chip") * core_count + core_index
     kv_crossed = []
     for step in range(1, side_count):
         for shift in range(head_count):
@@ -71,7 +77,7 @@
             outgoing = lax.dynamic_index_in_dim(
                 kv_raw, (inner_index + shift) % head_count, axis=0, keepdims=False
             )
-            kv_crossed.append(lax.ppermute(outgoing, ("side", "inner"), perm))
+            kv_crossed.append(lax.ppermute(outgoing, SEQ, perm))
     stacked = jnp.concatenate([by_head(queries), kv_raw], axis=2)
     got = a2a(stacked).reshape(head_count * row_count, 3 * head_width)
     query_here = got[:, :head_width]
@@ -80,6 +86,7 @@
     value_all = kv_all[:, head_width:]
 
     attended_here = attend(query_here, key_all, value_all)
+    w_partner, attended_here = lax.optimization_barrier((w_partner, attended_here))
 
     partial = lax.dot_general(
         attended_here, cot_side, (((0,), (0,)), ((), ())), preferred_element_type=jnp.float32
@@ -87,9 +94,13 @@
 
     returned = a2a(attended_here.reshape(head_count, row_count, head_width))
     attended = returned.transpose(1, 0, 2).reshape(row_count, width)
-    projected = jnp.dot(attended, w_full, preferred_element_type=jnp.float32).astype(
-        jnp.bfloat16
-    )
+    by_core = attended.reshape(row_count, side_count * chip_count, core_count, -1)
+    mine = lax.dynamic_index_in_dim(by_core, core_index, axis=2, keepdims=False)
+    theirs = lax.dynamic_index_in_dim(by_core, 1 - core_index, axis=2, keepdims=False)
+    projected = (
+        jnp.dot(mine.reshape(row_count, -1), w_core, preferred_element_type=jnp.float32)
+        + jnp.dot(theirs.reshape(row_count, -1), w_partner, preferred_element_type=jnp.float32)
+    ).astype(jnp.bfloat16)
 
     chunk_count = side_count * dp_count
     chunk = head_width // chunk_count
@@ -138,10 +149,8 @@
 def solution(mesh):
     seq_count = mesh.shape["seq"]
     dp_count = mesh.shape["dp"]
-    fine = Mesh(
-        mesh.devices.reshape(seq_count // HEADS, HEADS, dp_count), ("side", "inner", "dp")
-    )
-    seq = ("side", "inner")
+    fine = Mesh(mesh.devices.reshape(seq_count // HEADS, HEADS // 2, 2, dp_count), ALL)
+    seq = SEQ
     placed = (
         P("dp", seq, None),
         P("dp", seq, None),

time: 175 us -> 192 us (1.097)
  the two profiles are of different devices: /device:TPU:1 before, /device:TPU:0 now
where the time goes in v9:
time: 192 us; the launch traced here: 191 us
  waiting for transfers between devices  103 us (54%)
  starting transfers between devices  31.4 us (16%)
  matrix products  16.6 us (9%)
  local copies, waits for them, and re-layouts  15.4 us (8%)
  between operations  14.4 us (8%)
  other arithmetic  10.2 us (5%)
    all_to_all x2, waiting for transfers between devices, a2a(): lax.all_to_all(tensor, INNER, split_axis=0, concat_axis=0, tiled=True)  50.5 us
    ppermute x2, waiting for transfers between devices, local(): arrived = lax.ppermute(outgoing, ALL, perm)  16.9 us
    ppermute x8, starting transfers between devices, local(): kv_crossed.append(lax.ppermute(outgoing, SEQ, perm))  14.9 us
    ppermute x8, waiting for transfers between devices, local(): kv_crossed.append(lax.ppermute(outgoing, SEQ, perm))  13.7 us
    ppermute x1, waiting for transfers between devices, local(): kept = kept + lax.ppermute(sent, 'dp', [(0, 1), (1, 0)])  10.8 us
    all_to_all x2, starting transfers between devices, a2a(): lax.all_to_all(tensor, INNER, split_axis=0, concat_axis=0, tiled=True)  7.62 us
    all_gather x1, waiting for transfers between devices, local(): cot_side = lax.all_gather(cotangent[0], INNER, axis=0, tiled=True)  6.59 us
    unnamed x20, local copies, waits for them, and re-layouts  5.23 us
  transfers between devices with their start and end apart: 17, of which 9 were waited for; matrix products, arithmetic and copies ran while one was open for 20% of the time, Pallas kernels for 0%

profile of v9, /device:TPU:0, one launch (start us, length us, event | category | flops | bytes accessed | tf_op | source)
XLA Modules:
  0.0 191.3 jit_solution(15537184116614068260)
XLA Ops:
  7.2 3.0 %collective-permute-start = (bf16[48,1536]{1,0:T(8,128)(2,1)}, bf16[48,1536]{1,0:T(8,128)(2,1)S(1)}, u32[]{:S(2)}, u32[]{:S(2)}) collective-permute-start(bf16[48,1536]{1,0:T(8,128)(2,1)} %param.10), channel_id=1, source_target_pairs={{0,1},{1,0},{2,3},{3,2},{4,5},{5,4},{6,7},{7,6},{8,9},{9,8},{10,11... | collective-permute-start | bytes 442376 | tf_op jit(solution)/shard_map/ppermute | solution.py:50
  10.2 4.1 %collective-permute-done = bf16[48,1536]{1,0:T(8,128)(2,1)S(1)} collective-permute-done((bf16[48,1536]{1,0:T(8,128)(2,1)}, bf16[48,1536]{1,0:T(8,128)(2,1)S(1)}, u32[]{:S(2)}, u32[]{:S(2)}) %collective-permute-start) | collective-permute-done | bytes 147488 | tf_op jit(solution)/shard_map/ppermute | solution.py:50
  14.3 0.9 select_bitcast_fusion.1
  15.2 0.7 pad_maximum_fusion.1
  16.0 1.7 reshape_squeeze.10
  17.7 1.5 reshape_squeeze.11
  19.3 0.6 reshape_squeeze.9
  19.9 0.2 copy.34
  20.0 1.5 copy_bitcast_fusion
  21.5 2.1 %pad_maximum_fusion = bf16[8,192,576]{2,1,0:T(8,128)(2,1)} fusion(bf16[8,192,192]{2,1,0:T(8,128)(2,1)S(1)} %get-tuple-element.62, bf16[8,192,192]{2,1,0:T(8,128)(2,1)S(1)} %get-tuple-element.63, bf16[8,192,192]{2,1,0:T(8,128)(2,1)S(1)} %bitcast.85), kind=kLoop, calls=%fused_computation.21 | loop fusion | flops 5308416 | bytes 3538944 | tf_op jit(solution)/shard_map/concatenate | solution.py:81
  23.7 4.1 %all-to-all-start = ((bf16[8,192,576]{2,1,0:T(8,128)(2,1)}), bf16[8,192,576]{2,1,0:T(8,128)(2,1)S(1)}, u32[]{:S(2)}, u32[]{:S(2)}) async-start(bf16[8,192,576]{2,1,0:T(8,128)(2,1)} %pad_maximum_fusion), calls=%async_computation | async-start | bytes 3932160 | tf_op jit(solution)/shard_map/all_to_all | solution.py:61
  27.8 0.7 all-gather.6.cloned.1.call-update
  28.5 1.2 fusion.42
  29.8 2.6 %collective-permute-start.2 = (bf16[192,384]{1,0:T(8,128)(2,1)}, bf16[192,384]{1,0:T(8,128)(2,1)}, u32[]{:S(2)}, u32[]{:S(2)}) collective-permute-start(bf16[192,384]{1,0:T(8,128)(2,1)} %get-tuple-element.49), channel_id=1, source_target_pairs={{0,16},{2,18},{4,20},{6,22},{8,24},{10,26},{12,28},{14,30},{16,0},... | collective-permute-start | bytes 442376 | tf_op jit(solution)/shard_map/ppermute | solution.py:80
  32.4 0.2 collective-permute-start.3
  32.5 3.7 %collective-permute-start.4 = (bf16[192,384]{1,0:T(8,128)(2,1)}, bf16[192,384]{1,0:T(8,128)(2,1)}, u32[]{:S(2)}, u32[]{:S(2)}) collective-permute-start(bf16[192,384]{1,0:T(8,128)(2,1)} %get-tuple-element.51), channel_id=1, source_target_pairs={{0,20},{2,22},{4,24},{6,26},{8,28},{10,30},{12,16},{14,18},{16,4},... | collective-permute-start | bytes 442376 | tf_op jit(solution)/shard_map/ppermute | solution.py:80
  36.2 1.2 collective-permute-start.5
  37.4 2.6 %collective-permute-start.6 = (bf16[192,384]{1,0:T(8,128)(2,1)}, bf16[192,384]{1,0:T(8,128)(2,1)}, u32[]{:S(2)}, u32[]{:S(2)}) collective-permute-start(bf16[192,384]{1,0:T(8,128)(2,1)} %get-tuple-element.53), channel_id=1, source_target_pairs={{0,24},{2,26},{4,28},{6,30},{8,16},{10,18},{12,20},{14,22},{16,8},... | collective-permute-start | bytes 442376 | tf_op jit(solution)/shard_map/ppermute | solution.py:80
  40.0 0.8 fusion.35
  40.9 49.6 %all-to-all-done = bf16[8,192,576]{2,1,0:T(8,128)(2,1)S(1)} async-done(((bf16[8,192,576]{2,1,0:T(8,128)(2,1)}), bf16[8,192,576]{2,1,0:T(8,128)(2,1)S(1)}, u32[]{:S(2)}, u32[]{:S(2)}) %all-to-all-start) | async-done | bytes 1769504 | tf_op jit(solution)/shard_map/all_to_all | solution.py:61
  90.5 0.5 slice_dynamic-update-slice_fusion
  91.0 4.6 %collective-permute-start.7 = (bf16[192,384]{1,0:T(8,128)(2,1)S(1)}, bf16[192,384]{1,0:T(8,128)(2,1)S(1)}, u32[]{:S(2)}, u32[]{:S(2)}) collective-permute-start(bf16[192,384]{1,0:T(8,128)(2,1)S(1)} %copy-done.5), channel_id=1, source_target_pairs={{0,26},{2,28},{4,30},{6,16},{8,18},{10,20},{12,22},{14,24},{16,10}... | collective-permute-start | bytes 442376 | tf_op jit(solution)/shard_map/ppermute | solution.py:80
  95.5 0.9 constant_dynamic-update-slice_fusion.7
  96.5 0.1 collective-permute-start.8
  96.6 0.9 constant_dynamic-update-slice_fusion.6
  97.5 0.1 collective-permute-start.9
  97.6 0.9 constant_dynamic-update-slice_fusion.5
  98.5 0.9 constant_dynamic-update-slice_fusion.4
  99.5 0.9 constant_dynamic-update-slice_fusion.3
  100.4 10.2 %collective-permute-done.7 = bf16[192,384]{1,0:T(8,128)(2,1)S(1)} collective-permute-done((bf16[192,384]{1,0:T(8,128)(2,1)S(1)}, bf16[192,384]{1,0:T(8,128)(2,1)S(1)}, u32[]{:S(2)}, u32[]{:S(2)}) %collective-permute-start.7) | collective-permute-done | bytes 147488 | tf_op jit(solution)/shard_map/ppermute | solution.py:80
  110.7 0.1 slice.16
  110.8 1.3 collective-permute-done.8
  112.1 2.1 %collective-permute-done.9 = bf16[192,384]{1,0:T(8,128)(2,1)S(1)} collective-permute-done((bf16[192,384]{1,0:T(8,128)(2,1)S(1)}, bf16[192,384]{1,0:T(8,128)(2,1)S(1)}, u32[]{:S(2)}, u32[]{:S(2)}) %collective-permute-start.9) | collective-permute-done | bytes 147488 | tf_op jit(solution)/shard_map/ppermute | solution.py:80
  114.3 1.9 %fusion.43 = (bf16[3072,192]{1,0:T(8,128)(2,1)}, bf16[3072,192]{1,0:T(8,128)(2,1)S(1)}) fusion(bf16[3072,384]{1,0:T(8,128)(2,1)S(1)} %constant_dynamic-update-slice_fusion), kind=kLoop, calls=%fused_computation.75 | loop fusion | bytes 4718592 | tf_op jit(solution)/shard_map/slice | solution.py:86
  116.2 0.8 collective-permute-start.1
  117.0 12.1 %while.10 = (s32[]{:T(128)}, bf16[3,512,192]{1,2,0:T(8,128)(2,1)S(1)}, bf16[3,512,192]{2,1,0:T(8,128)(2,1)S(1)}, bf16[3072,192]{1,0:T(8,128)(2,1)S(1)}, bf16[3072,192]{1,0:T(8,128)(2,1)}, /*index=5*/s32[]{:T(128)}) while((s32[]{:T(128)}, bf16[3,512,192]{1,2,0:T(8,128)(2,1)S(1)}, bf16[3,512,192]{2,1,0:T(8,128)(2,1)S(1)}, ...), condition=%wide.region_3.4_spmd, body=%wide.region_0.3_spmd.sunk | while | flops 1220738048 | bytes 27207784 | solution.py:26
  117.0 1.1 multiply_reduce_fusion.2
  118.1 1.2 fusion.60
  119.3 0.2 copy-done
  119.5 1.5 fusion.61
  121.0 1.1 multiply_reduce_fusion.2
  122.1 1.2 fusion.60
  123.3 0.3 copy-done
  123.6 1.5 fusion.61
  125.1 1.1 multiply_reduce_fusion.2
  126.2 1.2 fusion.60
  127.3 0.3 copy-done
  127.6 1.5 fusion.61
  129.2 0.6 reshape.39
  129.8 1.1 copy.25
  130.8 3.6 %all-to-all-start.1 = ((bf16[8,192,192]{1,2,0:T(8,128)(2,1)}), bf16[8,192,192]{1,2,0:T(8,128)(2,1)S(1)}, u32[]{:S(2)}, u32[]{:S(2)}) async-start(bf16[8,192,192]{1,2,0:T(8,128)(2,1)} %copy.25), calls=%async_computation.1 | async-start | bytes 1572864 | tf_op jit(solution)/shard_map/all_to_all | solution.py:61
  134.4 6.6 %all-gather.6.cloned.1.call-done = bf16[1,1536,1536]{2,1,0:T(8,128)(2,1)} async-done(((bf16[1,192,1536]{2,1,0:T(8,128)(2,1)}), bf16[1,1536,1536]{2,1,0:T(8,128)(2,1)}) %all-gather.6.cloned.1.call-update) | async-done | bytes 4718608 | tf_op jit(solution)/shard_map/all_gather | solution.py:58
  141.0 3.4 %fusion.23 = f32[192,1536]{1,0:T(8,128)S(1)} fusion(bf16[1536,192]{0,1:T(8,128)(2,1)S(1)} %bitcast.81, bf16[1,1536,1536]{2,1,0:T(8,128)(2,1)} %all-gather.6.cloned.1.call-done), kind=kOutput, calls=%fused_computation.16 | convolution fusion | flops 905969664 | bytes 6488064 | tf_op jit(solution)/shard_map/dot_general | solution.py:91
  144.5 1.5 collective-permute-start.10
  145.9 0.9 all-to-all-done.1
  146.8 0.1 constant_dynamic-slice_fusion
  146.9 2.3 %fusion.44 = f32[192,1536]{1,0:T(8,128)S(1)} fusion(bf16[192,768]{0,1:T(8,128)(2,1)S(1)} %bitcast.89, bf16[768,1536]{1,0:T(8,128)(2,1)} %bitcast.87), kind=kOutput, calls=%fused_computation.76 | convolution fusion | flops 452984832 | bytes 3833856 | tf_op jit(solution)/shard_map/dot_general | solution.py:101
  149.2 10.8 %collective-permute-done.10 = f32[2,48,1536]{2,1,0:T(8,128)S(1)} collective-permute-done((f32[2,48,1536]{2,1,0:T(8,128)S(1)}, f32[2,48,1536]{2,1,0:T(8,128)S(1)}, u32[]{:S(2)}, u32[]{:S(2)}) %collective-permute-start.10) | collective-permute-done | bytes 589856 | tf_op jit(solution)/shard_map/ppermute | solution.py:112
  160.0 0.1 bitcast_add_fusion
  160.1 0.7 collective-permute-start.11
  160.8 2.8 %collective-permute-start.12 = (f32[48,1536]{1,0:T(8,128)S(1)}, f32[48,1536]{1,0:T(8,128)S(1)}, u32[]{:S(2)}, u32[]{:S(2)}) collective-permute-start(f32[48,1536]{1,0:T(8,128)S(1)} %get-tuple-element.58), channel_id=1, source_target_pairs={{0,2},{1,3},{2,6},{3,7},{4,10},{5,11},{6,14},{7,15},{8,18},{9,19},... | collective-permute-start | bytes 884744 | tf_op jit(solution)/shard_map/ppermute | solution.py:126
  163.6 3.1 %fusion.26 = bf16[1,192,1536]{2,1,0:T(8,128)(2,1)} fusion(f32[192,1536]{1,0:T(8,128)S(1)} %fusion.44, bf16[192,768]{0,1:T(8,128)(2,1)S(1)} %bitcast.88, bf16[768,1536]{1,0:T(8,128)(2,1)} %collective-permute-done.1), kind=kOutput, calls=%fused_computation.20 | convolution fusion | flops 453574656 | bytes 4423680 | tf_op jit(solution)/shard_map/dot_general | solution.py:102
  166.7 16.9 %collective-permute-done.12 = f32[48,1536]{1,0:T(8,128)S(1)} collective-permute-done((f32[48,1536]{1,0:T(8,128)S(1)}, f32[48,1536]{1,0:T(8,128)S(1)}, u32[]{:S(2)}, u32[]{:S(2)}) %collective-permute-start.12) | collective-permute-done | bytes 294944 | tf_op jit(solution)/shard_map/ppermute | solution.py:126
  183.7 0.7 add.153
  (33 shorter events, 0.4 us)
Async XLA Ops:
  7.2 10.6 %copy-start.2 = (bf16[1,192,1536]{2,1,0:T(8,128)(2,1)S(1)}, bf16[1,192,1536]{2,1,0:T(8,128)(2,1)}, u32[]{:S(2)}) copy-start(bf16[1,192,1536]{2,1,0:T(8,128)(2,1)} %param.9) | copy-start | bytes 1769476
  7.2 12.1 %copy-start.3 = (bf16[1,192,1536]{2,1,0:T(8,128)(2,1)S(1)}, bf16[1,192,1536]{2,1,0:T(8,128)(2,1)}, u32[]{:S(2)}) copy-start(bf16[1,192,1536]{2,1,0:T(8,128)(2,1)} %param.7) | copy-start | bytes 1769476
  7.2 109.0 %all-gather.4.cloned.1.call-start = ((), (), s32[]{:S(2)}) async-start(), calls=%async_computation.2 | async-start | bytes 2654208 | tf_op jit(solution)/shard_map/all_gather | solution.py:54
  7.2 7.1 %collective-permute-start = (bf16[48,1536]{1,0:T(8,128)(2,1)}, bf16[48,1536]{1,0:T(8,128)(2,1)S(1)}, u32[]{:S(2)}, u32[]{:S(2)}) collective-permute-start(bf16[48,1536]{1,0:T(8,128)(2,1)} %param.10), channel_id=1, source_target_pairs={{0,1},{1,0},{2,3},{3,2},{4,5},{5,4},{6,7},{7,6},{8,9},{9,8},{10,11... | collective-permute-start | bytes 442376 | tf_op jit(solution)/shard_map/ppermute | solution.py:50
  23.7 66.8 %all-to-all-start = ((bf16[8,192,576]{2,1,0:T(8,128)(2,1)}), bf16[8,192,576]{2,1,0:T(8,128)(2,1)S(1)}, u32[]{:S(2)}, u32[]{:S(2)}) async-start(bf16[8,192,576]{2,1,0:T(8,128)(2,1)} %pad_maximum_fusion), calls=%async_computation | async-start | bytes 3932160 | tf_op jit(solution)/shard_map/all_to_all | solution.py:61
  27.7 113.3 %all-gather.6.cloned.1.call-start = ((), (), s32[]{:S(2)}) async-start(), calls=%async_computation.3 | async-start | bytes 5308416 | tf_op jit(solution)/shard_map/all_gather | solution.py:58
  29.8 61.2 %collective-permute-start.2 = (bf16[192,384]{1,0:T(8,128)(2,1)}, bf16[192,384]{1,0:T(8,128)(2,1)}, u32[]{:S(2)}, u32[]{:S(2)}) collective-permute-start(bf16[192,384]{1,0:T(8,128)(2,1)} %get-tuple-element.49), channel_id=1, source_target_pairs={{0,16},{2,18},{4,20},{6,22},{8,24},{10,26},{12,28},{14,30},{16,0},... | collective-permute-start | bytes 442376 | tf_op jit(solution)/shard_map/ppermute | solution.py:80
  32.4 64.1 %collective-permute-start.3 = (bf16[192,384]{1,0:T(8,128)(2,1)}, bf16[192,384]{1,0:T(8,128)(2,1)}, u32[]{:S(2)}, u32[]{:S(2)}) collective-permute-start(bf16[192,384]{1,0:T(8,128)(2,1)} %get-tuple-element.50), channel_id=1, source_target_pairs={{0,18},{2,20},{4,22},{6,24},{8,26},{10,28},{12,30},{14,16},{16,2},... | collective-permute-start | bytes 442376 | tf_op jit(solution)/shard_map/ppermute | solution.py:80
  32.5 65.0 %collective-permute-start.4 = (bf16[192,384]{1,0:T(8,128)(2,1)}, bf16[192,384]{1,0:T(8,128)(2,1)}, u32[]{:S(2)}, u32[]{:S(2)}) collective-permute-start(bf16[192,384]{1,0:T(8,128)(2,1)} %get-tuple-element.51), channel_id=1, source_target_pairs={{0,20},{2,22},{4,24},{6,26},{8,28},{10,30},{12,16},{14,18},{16,4},... | collective-permute-start | bytes 442376 | tf_op jit(solution)/shard_map/ppermute | solution.py:80
  36.2 62.3 %collective-permute-start.5 = (bf16[192,384]{1,0:T(8,128)(2,1)}, bf16[192,384]{1,0:T(8,128)(2,1)}, u32[]{:S(2)}, u32[]{:S(2)}) collective-permute-start(bf16[192,384]{1,0:T(8,128)(2,1)} %get-tuple-element.52), channel_id=1, source_target_pairs={{0,22},{2,24},{4,26},{6,28},{8,30},{10,16},{12,18},{14,20},{16,6},... | collective-permute-start | bytes 442376 | tf_op jit(solution)/shard_map/ppermute | solution.py:80
  37.4 62.1 %collective-permute-start.6 = (bf16[192,384]{1,0:T(8,128)(2,1)}, bf16[192,384]{1,0:T(8,128)(2,1)}, u32[]{:S(2)}, u32[]{:S(2)}) collective-permute-start(bf16[192,384]{1,0:T(8,128)(2,1)} %get-tuple-element.53), channel_id=1, source_target_pairs={{0,24},{2,26},{4,28},{6,30},{8,16},{10,18},{12,20},{14,22},{16,8},... | collective-permute-start | bytes 442376 | tf_op jit(solution)/shard_map/ppermute | solution.py:80
  40.9 50.1 %copy-start.5 = (bf16[192,384]{1,0:T(8,128)(2,1)S(1)}, bf16[192,384]{1,0:T(8,128)(2,1)}, u32[]{:S(2)}) copy-start(bf16[192,384]{1,0:T(8,128)(2,1)} %get-tuple-element.55) | copy-start | bytes 442372
  40.9 55.6 %copy-start.4 = (bf16[192,384]{1,0:T(8,128)(2,1)S(1)}, bf16[192,384]{1,0:T(8,128)(2,1)}, u32[]{:S(2)}) copy-start(bf16[192,384]{1,0:T(8,128)(2,1)} %get-tuple-element.54) | copy-start | bytes 442372
  40.9 56.7 %copy-start.6 = (bf16[192,384]{1,0:T(8,128)(2,1)S(1)}, bf16[192,384]{1,0:T(8,128)(2,1)}, u32[]{:S(2)}) copy-start(bf16[192,384]{1,0:T(8,128)(2,1)} %get-tuple-element.48) | copy-start | bytes 442372
  91.0 19.7 %collective-permute-start.7 = (bf16[192,384]{1,0:T(8,128)(2,1)S(1)}, bf16[192,384]{1,0:T(8,128)(2,1)S(1)}, u32[]{:S(2)}, u32[]{:S(2)}) collective-permute-start(bf16[192,384]{1,0:T(8,128)(2,1)S(1)} %copy-done.5), channel_id=1, source_target_pairs={{0,26},{2,28},{4,30},{6,16},{8,18},{10,20},{12,22},{14,24},{16,10}... | collective-permute-start | bytes 442376 | tf_op jit(solution)/shard_map/ppermute | solution.py:80
  96.5 15.6 %collective-permute-start.8 = (bf16[192,384]{1,0:T(8,128)(2,1)S(1)}, bf16[192,384]{1,0:T(8,128)(2,1)S(1)}, u32[]{:S(2)}, u32[]{:S(2)}) collective-permute-start(bf16[192,384]{1,0:T(8,128)(2,1)S(1)} %copy-done.4), channel_id=1, source_target_pairs={{0,28},{2,30},{4,16},{6,18},{8,20},{10,22},{12,24},{14,26},{16,12}... | collective-permute-start | bytes 442376 | tf_op jit(solution)/shard_map/ppermute | solution.py:80
  97.5 16.7 %collective-permute-start.9 = (bf16[192,384]{1,0:T(8,128)(2,1)S(1)}, bf16[192,384]{1,0:T(8,128)(2,1)S(1)}, u32[]{:S(2)}, u32[]{:S(2)}) collective-permute-start(bf16[192,384]{1,0:T(8,128)(2,1)S(1)} %copy-done.6), channel_id=1, source_target_pairs={{0,30},{2,16},{4,18},{6,20},{8,22},{10,24},{12,26},{14,28},{16,14}... | collective-permute-start | bytes 442376 | tf_op jit(solution)/shard_map/ppermute | solution.py:80
  114.2 2.8 %copy-start.1 = (bf16[3,512,192]{1,2,0:T(8,128)(2,1)S(1)}, bf16[3,512,192]{1,2,0:T(8,128)(2,1)}, u32[]{:S(2)}) copy-start(bf16[3,512,192]{1,2,0:T(8,128)(2,1)} %custom-call.1) | copy-start | bytes 1769476
  116.2 13.0 %collective-permute-start.1 = (bf16[768,1536]{1,0:T(8,128)(2,1)}, bf16[768,1536]{1,0:T(8,128)(2,1)}, u32[]{:S(2)}, u32[]{:S(2)}) collective-permute-start(bf16[768,1536]{1,0:T(8,128)(2,1)} %bitcast.86), channel_id=1, source_target_pairs={{0,2},{2,0},{1,3},{3,1},{4,6},{6,4},{5,7},{7,5},{8,10},{10,8},{9,1... | collective-permute-start | bytes 7077896 | tf_op jit(solution)/shard_map/ppermute | solution.py:57
  118.1 1.4 copy-start
  122.1 1.4 copy-start
  126.2 1.5 copy-start
  130.8 16.0 %all-to-all-start.1 = ((bf16[8,192,192]{1,2,0:T(8,128)(2,1)}), bf16[8,192,192]{1,2,0:T(8,128)(2,1)S(1)}, u32[]{:S(2)}, u32[]{:S(2)}) async-start(bf16[8,192,192]{1,2,0:T(8,128)(2,1)} %copy.25), calls=%async_computation.1 | async-start | bytes 1572864 | tf_op jit(solution)/shard_map/all_to_all | solution.py:61
  144.5 15.5 %collective-permute-start.10 = (f32[2,48,1536]{2,1,0:T(8,128)S(1)}, f32[2,48,1536]{2,1,0:T(8,128)S(1)}, u32[]{:S(2)}, u32[]{:S(2)}) collective-permute-start(f32[2,48,1536]{2,1,0:T(8,128)S(1)} %dynamic-slice_bitcast_fusion), channel_id=1, source_target_pairs={{0,1},{1,0},{2,3},{3,2},{4,5},{5,4},{6,7},{7,6},{8,9},{9,8},{10,11... | collective-permute-start | bytes 1769480 | tf_op jit(solution)/shard_map/ppermute | solution.py:112
  160.1 6.6 %collective-permute-start.11 = (f32[48,1536]{1,0:T(8,128)S(1)}, f32[48,1536]{1,0:T(8,128)S(1)}, u32[]{:S(2)}, u32[]{:S(2)}) collective-permute-start(f32[48,1536]{1,0:T(8,128)S(1)} %get-tuple-element.59), channel_id=1, source_target_pairs={{0,0},{1,1},{2,4},{3,5},{4,8},{5,9},{6,12},{7,13},{8,16},{9,17},{1... | collective-permute-start | bytes 884744 | tf_op jit(solution)/shard_map/ppermute | solution.py:126
  160.8 22.9 %collective-permute-start.12 = (f32[48,1536]{1,0:T(8,128)S(1)}, f32[48,1536]{1,0:T(8,128)S(1)}, u32[]{:S(2)}, u32[]{:S(2)}) collective-permute-start(f32[48,1536]{1,0:T(8,128)S(1)} %get-tuple-element.58), channel_id=1, source_target_pairs={{0,2},{1,3},{2,6},{3,7},{4,10},{5,11},{6,14},{7,15},{8,18},{9,19},... | collective-permute-start | bytes 884744 | tf_op jit(solution)/shard_map/ppermute | solution.py:126
Sparse Core Ops, SparseCore 0:
  16.1 80.0 all-gather.3
  97.8 43.1 all-gather.5

commit v10 on v8

--- a/solution.py
+++ b/solution.py
@@ -8,25 +8,42 @@
 HEAD_DIM = 192
 
 
-def attend(query_here, key_all, value_all):
+def attend_part(query_here, key_part, value_part):
     query_count = query_here.shape[0]
     head_width = query_here.shape[1]
     block_size = min(512, query_count)
     score_scale = HEAD_DIM ** (-0.5)
 
     def one_block(query_block):
-        scores = jnp.dot(query_block, key_all.T, preferred_element_type=jnp.float32) * score_scale
+        scores = jnp.dot(query_block, key_part.T, preferred_element_type=jnp.float32) * score_scale
         largest = jnp.max(scores, axis=1, keepdims=True)
         raised = jnp.exp(scores - largest)
         denominator = jnp.sum(raised, axis=1, keepdims=True)
         weights = raised.astype(jnp.bfloat16)
-        mixed = jnp.dot(weights, value_all, preferred_element_type=jnp.float32)
-        return (mixed / denominator).astype(jnp.bfloat16)
+        mixed = jnp.dot(weights, value_part, preferred_element_type=jnp.float32)
+        return mixed, largest, denominator
 
-    blocks = lax.map(
+    mixed, largest, denominator = lax.map(
         one_block, query_here.reshape(query_count // block_size, block_size, head_width)
     )
-    return blocks.reshape(query_count, head_width)
+    return (
+        mixed.reshape(query_count, -1),
+        largest.reshape(query_count, 1),
+        denominator.reshape(query_count, 1),
+    )
+
+
+def combine(results):
+    largest = results[0][1]
+    for _, part_largest, _ in results[1:]:
+        largest = jnp.maximum(largest, part_largest)
+    mixed = 0.0
+    denominator = 0.0
+    for part_mixed, part_largest, part_denominator in results:
+        scale = jnp.exp(part_largest - largest)
+        mixed = mixed + part_mixed * scale
+        denominator = denominator + part_denominator * scale
+    return (mixed / denominator).astype(jnp.bfloat16)
 
 
 ALL = ("side", "inner", "dp")
@@ -75,11 +92,13 @@
     stacked = jnp.concatenate([by_head(queries), kv_raw], axis=2)
     got = a2a(stacked).reshape(head_count * row_count, 3 * head_width)
     query_here = got[:, :head_width]
-    kv_all = jnp.concatenate([got[:, head_width:]] + kv_crossed, axis=0)
-    key_all = kv_all[:, :head_width]
-    value_all = kv_all[:, head_width:]
+    kv_here = got[:, head_width:]
+    near = attend_part(query_here, kv_here[:, :head_width], kv_here[:, head_width:])
+    kv_crossed, near = lax.optimization_barrier((kv_crossed, near))
+    kv_there = jnp.concatenate(kv_crossed, axis=0)
+    far = attend_part(query_here, kv_there[:, :head_width], kv_there[:, head_width:])
 
-    attended_here = attend(query_here, key_all, value_all)
+    attended_here = combine([near, far])
 
     partial = lax.dot_general(
         attended_here, cot_side, (((0,), (0,)), ((), ())), preferred_element_type=jnp.float32

time: 175 us -> 218 us (1.25)
  local copies, waits for them, and re-layouts: 15.9 us -> 77.7 us
  waiting for transfers between devices: 87.1 us -> 59.7 us
  starting transfers between devices: 27.9 us -> 34.2 us
    dynamic_update_slice x0 -> x18, local copies, waits for them, and re-layouts: none -> 53.9 us  [attend_part(): lax.map(one_block, query_here.reshape(query_count // block_size, block_si...]
    ppermute x8, waiting for transfers between devices: 27.7 us -> 0.02 us  [local(): kv_crossed.append(lax.ppermute(outgoing, ('side', 'inner'), perm))]
    unnamed x20 -> x25, local copies, waits for them, and re-layouts: 5.23 us -> 11.9 us
    ppermute x1, waiting for transfers between devices: 4.5 us -> 0.01 us  [local(): lax.ppermute(w_out, 'dp', [(p, (p + 1) % dp_count) for p in range(dp_coun...]
    ppermute x8, starting transfers between devices: 12.1 us -> 15.6 us  [local(): kv_crossed.append(lax.ppermute(outgoing, ('side', 'inner'), perm))]
    ppermute x1, waiting for transfers between devices: 3.19 us -> 6.56 us  [local(): kept = kept + lax.ppermute(sent, 'dp', [(0, 1), (1, 0)])]
    all_to_all x2, starting transfers between devices: 9.01 us -> 12 us  [a2a(): lax.all_to_all(tensor, 'inner', split_axis=0, concat_axis=0, tiled=True)]
    another operation x0 -> x6, local copies, waits for them, and re-layouts: none -> 2.69 us
  transfers between devices with their start and end apart: 16 -> 16, of which waited for: 9 -> 5; matrix products, arithmetic and copies ran while one was open for 24% -> 48% of each run, Pallas kernels for 0% -> 0%
where the time goes in v10:
time: 218 us; the launch traced here: 214 us
  local copies, waits for them, and re-layouts  77.7 us (36%)
  waiting for transfers between devices  59.7 us (27%)
  starting transfers between devices  34.2 us (16%)
  matrix products  16.7 us (8%)
  between operations  14.3 us (7%)
  other arithmetic  11.4 us (5%)
    dynamic_update_slice x18, local copies, waits for them, and re-layouts, attend_part(): lax.map(one_block, query_here.reshape(query_count // block_size, block_si...  53.9 us
    all_to_all x2, waiting for transfers between devices, a2a(): lax.all_to_all(tensor, 'inner', split_axis=0, concat_axis=0, tiled=True)  45.6 us
    ppermute x8, starting transfers between devices, local(): kv_crossed.append(lax.ppermute(outgoing, ('side', 'inner'), perm))  15.6 us
    all_to_all x2, starting transfers between devices, a2a(): lax.all_to_all(tensor, 'inner', split_axis=0, concat_axis=0, tiled=True)  12 us
    unnamed x25, local copies, waits for them, and re-layouts  11.9 us
    ppermute x2, waiting for transfers between devices, local(): arrived = lax.ppermute(outgoing, ALL, perm)  6.8 us
    ppermute x1, waiting for transfers between devices, local(): kept = kept + lax.ppermute(sent, 'dp', [(0, 1), (1, 0)])  6.56 us
    ppermute x2, starting transfers between devices, local(): arrived = lax.ppermute(outgoing, ALL, perm)  5.24 us
  transfers between devices with their start and end apart: 16, of which 5 were waited for; matrix products, arithmetic and copies ran while one was open for 48% of the time, Pallas kernels for 0%

profile of v10, /device:TPU:1, one launch (start us, length us, event | category | flops | bytes accessed | tf_op | source)
XLA Modules:
  0.0 214.2 jit_solution(10541002402509865163)
XLA Ops:
  7.2 0.7 all-gather.6.cloned.1.call-update
  7.9 1.7 reshape_squeeze.10
  9.7 1.5 reshape_squeeze.11
  11.2 0.6 reshape_squeeze.9
  12.0 1.0 copy-done.2
  13.3 2.1 pad_maximum_fusion
  15.3 5.3 %all-to-all-start = ((bf16[8,192,576]{2,1,0:T(8,128)(2,1)}), bf16[8,192,576]{2,1,0:T(8,128)(2,1)S(1)}, u32[]{:S(2)}, u32[]{:S(2)}) async-start(bf16[8,192,576]{2,1,0:T(8,128)(2,1)} %pad_maximum_fusion), calls=%async_computation | async-start | bytes 3932160 | tf_op jit(solution)/shard_map/all_to_all | solution.py:72
  20.6 1.2 collective-permute-start.8
  21.9 1.2 fusion.40
  23.1 2.3 %collective-permute-start = (bf16[192,384]{1,0:T(8,128)(2,1)}, bf16[192,384]{1,0:T(8,128)(2,1)}, u32[]{:S(2)}, u32[]{:S(2)}) collective-permute-start(bf16[192,384]{1,0:T(8,128)(2,1)} %get-tuple-element.151), channel_id=1, source_target_pairs={{0,16},{2,18},{4,20},{6,22},{8,24},{10,26},{12,28},{14,30},{16,0},... | collective-permute-start | bytes 442376 | tf_op jit(solution)/shard_map/ppermute | solution.py:91
  25.4 1.9 collective-permute-start.1
  27.3 2.3 %collective-permute-start.2 = (bf16[192,384]{1,0:T(8,128)(2,1)}, bf16[192,384]{1,0:T(8,128)(2,1)}, u32[]{:S(2)}, u32[]{:S(2)}) collective-permute-start(bf16[192,384]{1,0:T(8,128)(2,1)} %get-tuple-element.153), channel_id=1, source_target_pairs={{0,20},{2,22},{4,24},{6,26},{8,28},{10,30},{12,16},{14,18},{16,4},... | collective-permute-start | bytes 442376 | tf_op jit(solution)/shard_map/ppermute | solution.py:91
  29.6 1.2 collective-permute-start.3
  30.9 0.9 fusion.33
  31.7 1.8 collective-permute-start.4
  33.5 0.9 select_bitcast_fusion.1
  34.5 0.7 pad_maximum_fusion.1
  35.2 38.3 %all-to-all-done = bf16[8,192,576]{2,1,0:T(8,128)(2,1)S(1)} async-done(((bf16[8,192,576]{2,1,0:T(8,128)(2,1)}), bf16[8,192,576]{2,1,0:T(8,128)(2,1)S(1)}, u32[]{:S(2)}, u32[]{:S(2)}) %all-to-all-start) | async-done | bytes 1769504 | tf_op jit(solution)/shard_map/all_to_all | solution.py:72
  73.6 1.3 copy-done
  74.9 2.2 %fusion.47 = (bf16[1536,192]{1,0:T(8,128)(2,1)S(1)}, bf16[1536,192]{1,0:T(8,128)(2,1)S(1)}, bf16[1536,192]{1,0:T(8,128)(2,1)S(1)}) fusion(bf16[1536,576]{1,0:T(8,128)(2,1)} %bitcast.111), kind=kLoop, calls=%fused_computation.89 | loop fusion | bytes 3538944 | tf_op jit(solution)/shard_map/slice | solution.py:96
  77.0 5.8 %collective-permute-start.7 = (bf16[192,384]{1,0:T(8,128)(2,1)}, bf16[192,384]{1,0:T(8,128)(2,1)S(1)}, u32[]{:S(2)}, u32[]{:S(2)}) collective-permute-start(bf16[192,384]{1,0:T(8,128)(2,1)} %get-tuple-element.150), channel_id=1, source_target_pairs={{0,30},{2,16},{4,18},{6,20},{8,22},{10,24},{12,26},{14,28},{16,14}... | collective-permute-start | bytes 442376 | tf_op jit(solution)/shard_map/ppermute | solution.py:91
  83.2 1.3 broadcast.24.clone2
  84.5 33.3 %while.28 = (s32[]{:T(128)}, f32[3,512,192]{1,0,2:T(4,128)}, f32[3,512,1]{1,2,0:T(1,128)S(1)}, f32[3,512,1]{1,2,0:T(1,128)S(1)}, bf16[3,512,192]{2,1,0:T(8,128)(...) while((s32[]{:T(128)}, f32[3,512,192]{1,0,2:T(4,128)}, ...), condition=%wide.region_3.4_spmd, body=%wide.region_0.3_spmd.sunk | while | flops 608697344 | bytes 13058153 | solution.py:26
  84.5 0.7 fusion.71
  85.8 0.8 fusion.72
  87.0 8.6 %dynamic_update_slice.29 = f32[3,512,192]{1,0,2:T(4,128)} dynamic-update-slice(f32[3,512,192]{1,0,2:T(4,128)} %get-tuple-element.278, f32[1,512,192]{1,0,2:T(1,128)S(1)} %copy.36, s32[]{:T(128)} %get-tuple-element.277, s32[]{:T(128)} %constant.134.clone.1..sunk, s32[]{:T(128)} %constant.134.clone.1..sunk) | dynamic-update-slice | bytes 786436 | tf_op jit(solution)/shard_map/while/body/jit(dynamic_update_index_in_dim)/dynamic_update_slice | solution.py:26
  95.6 0.7 fusion.71
  96.9 0.8 fusion.72
  98.1 8.6 %dynamic_update_slice.29 = f32[3,512,192]{1,0,2:T(4,128)} dynamic-update-slice(f32[3,512,192]{1,0,2:T(4,128)} %get-tuple-element.278, f32[1,512,192]{1,0,2:T(1,128)S(1)} %copy.36, s32[]{:T(128)} %get-tuple-element.277, s32[]{:T(128)} %constant.134.clone.1..sunk, s32[]{:T(128)} %constant.134.clone.1..sunk) | dynamic-update-slice | bytes 786436 | tf_op jit(solution)/shard_map/while/body/jit(dynamic_update_index_in_dim)/dynamic_update_slice | solution.py:26
  106.7 0.7 fusion.71
  107.4 0.6 fusion.73
  107.9 0.8 fusion.72
  109.2 8.6 %dynamic_update_slice.29 = f32[3,512,192]{1,0,2:T(4,128)} dynamic-update-slice(f32[3,512,192]{1,0,2:T(4,128)} %get-tuple-element.278, f32[1,512,192]{1,0,2:T(1,128)S(1)} %copy.36, s32[]{:T(128)} %get-tuple-element.277, s32[]{:T(128)} %constant.134.clone.1..sunk, s32[]{:T(128)} %constant.134.clone.1..sunk) | dynamic-update-slice | bytes 786436 | tf_op jit(solution)/shard_map/while/body/jit(dynamic_update_index_in_dim)/dynamic_update_slice | solution.py:26
  117.8 2.9 %copy.28 = f32[24,8,3,512]{3,1,2,0:T(8,128)} copy(f32[24,8,3,512]{3,2,1,0:T(4,128)} %bitcast.113) | data formatting | bytes 2359296
  120.7 0.9 constant_dynamic-update-slice_fusion.11
  121.6 0.9 constant_dynamic-update-slice_fusion.10
  122.6 0.9 constant_dynamic-update-slice_fusion.9
  123.5 0.9 constant_dynamic-update-slice_fusion.8
  124.5 0.9 constant_dynamic-update-slice_fusion.5
  125.9 1.3 broadcast.24.clone
  127.2 33.2 %while.29 = (s32[]{:T(128)}, f32[3,512,192]{1,0,2:T(4,128)}, f32[3,512,1]{1,2,0:T(1,128)S(1)}, f32[3,512,1]{1,2,0:T(1,128)S(1)}, bf16[3,512,192]{2,1,0:T(8,128)(...) while((s32[]{:T(128)}, f32[3,512,192]{1,0,2:T(4,128)}, ...), condition=%wide.region_7.8_spmd, body=%wide.region_4.7_spmd.sunk | while | flops 608697344 | bytes 13058153 | solution.py:26
  127.2 0.7 fusion.77
  128.5 0.8 fusion.78
  129.7 8.6 %dynamic_update_slice.31 = f32[3,512,192]{1,0,2:T(4,128)} dynamic-update-slice(f32[3,512,192]{1,0,2:T(4,128)} %get-tuple-element.305, f32[1,512,192]{1,0,2:T(1,128)S(1)} %copy.37, s32[]{:T(128)} %get-tuple-element.304, s32[]{:T(128)} %constant.134.clone.1..sunk.1, s32[]{:T(128)} %constant.134.clone.1..sunk.1) | dynamic-update-slice | bytes 786436 | tf_op jit(solution)/shard_map/while/body/jit(dynamic_update_index_in_dim)/dynamic_update_slice | solution.py:26
  138.3 0.7 fusion.77
  139.6 0.8 fusion.78
  140.8 8.6 %dynamic_update_slice.31 = f32[3,512,192]{1,0,2:T(4,128)} dynamic-update-slice(f32[3,512,192]{1,0,2:T(4,128)} %get-tuple-element.305, f32[1,512,192]{1,0,2:T(1,128)S(1)} %copy.37, s32[]{:T(128)} %get-tuple-element.304, s32[]{:T(128)} %constant.134.clone.1..sunk.1, s32[]{:T(128)} %constant.134.clone.1..sunk.1) | dynamic-update-slice | bytes 786436 | tf_op jit(solution)/shard_map/while/body/jit(dynamic_update_index_in_dim)/dynamic_update_slice | solution.py:26
  149.4 0.7 fusion.77
  150.7 0.8 fusion.78
  151.9 8.6 %dynamic_update_slice.31 = f32[3,512,192]{1,0,2:T(4,128)} dynamic-update-slice(f32[3,512,192]{1,0,2:T(4,128)} %get-tuple-element.305, f32[1,512,192]{1,0,2:T(1,128)S(1)} %copy.37, s32[]{:T(128)} %get-tuple-element.304, s32[]{:T(128)} %constant.134.clone.1..sunk.1, s32[]{:T(128)} %constant.134.clone.1..sunk.1) | dynamic-update-slice | bytes 786436 | tf_op jit(solution)/shard_map/while/body/jit(dynamic_update_index_in_dim)/dynamic_update_slice | solution.py:26
  160.5 2.0 copy.29
  162.7 1.1 copy.23
  163.9 6.7 %all-to-all-start.1 = ((bf16[8,192,192]{2,1,0:T(8,128)(2,1)}), bf16[8,192,192]{2,1,0:T(8,128)(2,1)S(1)}, u32[]{:S(2)}, u32[]{:S(2)}) async-start(bf16[8,192,192]{2,1,0:T(8,128)(2,1)} %bitcast.25), calls=%async_computation.1 | async-start | bytes 1572864 | tf_op jit(solution)/shard_map/all_to_all | solution.py:72
  170.6 3.4 %fusion.22 = f32[192,1536]{1,0:T(8,128)S(1)} fusion(bf16[1536,192]{0,1:T(8,128)(2,1)S(1)} %divide_convert_fusion, bf16[1,1536,1536]{2,1,0:T(8,128)(2,1)} %all-gather.6.cloned.1.call-done), kind=kOutput, calls=%fused_computation.24 | convolution fusion | flops 905969664 | bytes 6488064 | tf_op jit(solution)/shard_map/dot_general | solution.py:103
  174.1 7.3 %all-to-all-done.1 = bf16[8,192,192]{2,1,0:T(8,128)(2,1)S(1)} async-done(((bf16[8,192,192]{2,1,0:T(8,128)(2,1)}), bf16[8,192,192]{2,1,0:T(8,128)(2,1)S(1)}, u32[]{:S(2)}, u32[]{:S(2)}) %all-to-all-start.1) | async-done | bytes 589856 | tf_op jit(solution)/shard_map/all_to_all | solution.py:72
  181.9 0.7 reshape.59
  182.6 6.6 %collective-permute-done.9 = f32[2,48,1536]{2,1,0:T(8,128)} collective-permute-done((f32[2,48,1536]{2,1,0:T(8,128)S(1)}, f32[2,48,1536]{2,1,0:T(8,128)}, u32[]{:S(2)}, u32[]{:S(2)}) %collective-permute-start.9) | collective-permute-done | bytes 589856 | tf_op jit(solution)/shard_map/ppermute | solution.py:120
  189.1 1.1 bitcast_add_fusion
  190.3 4.5 %collective-permute-start.10 = (f32[48,1536]{1,0:T(8,128)S(1)}, f32[48,1536]{1,0:T(8,128)S(1)}, u32[]{:S(2)}, u32[]{:S(2)}) collective-permute-start(f32[48,1536]{1,0:T(8,128)S(1)} %get-tuple-element.161), channel_id=1, source_target_pairs={{0,0},{1,1},{2,4},{3,5},{4,8},{5,9},{6,12},{7,13},{8,16},{9,17},{1... | collective-permute-start | bytes 884744 | tf_op jit(solution)/shard_map/ppermute | solution.py:134
  194.8 0.8 collective-permute-start.11
  195.6 4.2 %fusion.24 = bf16[1,192,1536]{2,1,0:T(8,128)(2,1)} fusion(bf16[192,1536]{1,0:T(8,128)(2,1)S(1)} %reshape.59, bf16[1536,1536]{1,0:T(8,128)(2,1)} %bitcast.127), kind=kOutput, calls=%fused_computation.27 | convolution fusion | flops 906264576 | bytes 5898240 | tf_op jit(solution)/shard_map/dot_general | solution.py:109
  199.8 1.5 collective-permute-done.10
  201.3 5.3 %collective-permute-done.11 = f32[48,1536]{1,0:T(8,128)S(1)} collective-permute-done((f32[48,1536]{1,0:T(8,128)S(1)}, f32[48,1536]{1,0:T(8,128)S(1)}, u32[]{:S(2)}, u32[]{:S(2)}) %collective-permute-start.11) | collective-permute-done | bytes 294944 | tf_op jit(solution)/shard_map/ppermute | solution.py:134
  206.6 0.7 add.146
  (63 shorter events, 7.6 us)
Async XLA Ops:
  7.2 2.5 %copy-start.3 = (bf16[1,192,1536]{2,1,0:T(8,128)(2,1)S(1)}, bf16[1,192,1536]{2,1,0:T(8,128)(2,1)}, u32[]{:S(2)}) copy-start(bf16[1,192,1536]{2,1,0:T(8,128)(2,1)} %param.9) | copy-start | bytes 1769476
  7.2 4.0 %copy-start.4 = (bf16[1,192,1536]{2,1,0:T(8,128)(2,1)S(1)}, bf16[1,192,1536]{2,1,0:T(8,128)(2,1)}, u32[]{:S(2)}) copy-start(bf16[1,192,1536]{2,1,0:T(8,128)(2,1)} %param.10) | copy-start | bytes 1769476
  7.2 163.4 %all-gather.6.cloned.1.call-start = ((), (), s32[]{:S(2)}) async-start(), calls=%async_computation.3 | async-start | bytes 5308416 | tf_op jit(solution)/shard_map/all_gather | solution.py:69
  11.8 1.1 copy-start.2
  15.3 58.2 %all-to-all-start = ((bf16[8,192,576]{2,1,0:T(8,128)(2,1)}), bf16[8,192,576]{2,1,0:T(8,128)(2,1)S(1)}, u32[]{:S(2)}, u32[]{:S(2)}) async-start(bf16[8,192,576]{2,1,0:T(8,128)(2,1)} %pad_maximum_fusion), calls=%async_computation | async-start | bytes 3932160 | tf_op jit(solution)/shard_map/all_to_all | solution.py:72
  20.6 174.9 %all-gather.4.cloned.1.call-start = ((), (), s32[]{:S(2)}) async-start(), calls=%async_computation.2 | async-start | bytes 5013504 | tf_op jit(solution)/shard_map/all_gather | solution.py:66
  20.6 11.1 %collective-permute-start.8 = (bf16[48,1536]{1,0:T(8,128)(2,1)}, bf16[48,1536]{1,0:T(8,128)(2,1)}, u32[]{:S(2)}, u32[]{:S(2)}) collective-permute-start(bf16[48,1536]{1,0:T(8,128)(2,1)} %param.12), channel_id=1, source_target_pairs={{0,1},{1,0},{2,3},{3,2},{4,5},{5,4},{6,7},{7,6},{8,9},{9,8},{10,11... | collective-permute-start | bytes 442376 | tf_op jit(solution)/shard_map/ppermute | solution.py:61
  23.1 53.9 %collective-permute-start = (bf16[192,384]{1,0:T(8,128)(2,1)}, bf16[192,384]{1,0:T(8,128)(2,1)}, u32[]{:S(2)}, u32[]{:S(2)}) collective-permute-start(bf16[192,384]{1,0:T(8,128)(2,1)} %get-tuple-element.151), channel_id=1, source_target_pairs={{0,16},{2,18},{4,20},{6,22},{8,24},{10,26},{12,28},{14,30},{16,0},... | collective-permute-start | bytes 442376 | tf_op jit(solution)/shard_map/ppermute | solution.py:91
  25.4 57.5 %collective-permute-start.1 = (bf16[192,384]{1,0:T(8,128)(2,1)}, bf16[192,384]{1,0:T(8,128)(2,1)}, u32[]{:S(2)}, u32[]{:S(2)}) collective-permute-start(bf16[192,384]{1,0:T(8,128)(2,1)} %get-tuple-element.152), channel_id=1, source_target_pairs={{0,18},{2,20},{4,22},{6,24},{8,26},{10,28},{12,30},{14,16},{16,2},... | collective-permute-start | bytes 442376 | tf_op jit(solution)/shard_map/ppermute | solution.py:91
  27.3 55.5 %collective-permute-start.2 = (bf16[192,384]{1,0:T(8,128)(2,1)}, bf16[192,384]{1,0:T(8,128)(2,1)}, u32[]{:S(2)}, u32[]{:S(2)}) collective-permute-start(bf16[192,384]{1,0:T(8,128)(2,1)} %get-tuple-element.153), channel_id=1, source_target_pairs={{0,20},{2,22},{4,24},{6,26},{8,28},{10,30},{12,16},{14,18},{16,4},... | collective-permute-start | bytes 442376 | tf_op jit(solution)/shard_map/ppermute | solution.py:91
  29.6 91.0 %collective-permute-start.3 = (bf16[192,384]{1,0:T(8,128)(2,1)}, bf16[192,384]{1,0:T(8,128)(2,1)}, u32[]{:S(2)}, u32[]{:S(2)}) collective-permute-start(bf16[192,384]{1,0:T(8,128)(2,1)} %get-tuple-element.154), channel_id=1, source_target_pairs={{0,22},{2,24},{4,26},{6,28},{8,30},{10,16},{12,18},{14,20},{16,6},... | collective-permute-start | bytes 442376 | tf_op jit(solution)/shard_map/ppermute | solution.py:91
  30.9 2.7 %copy-start.7 = (bf16[48,1536]{1,0:T(8,128)(2,1)S(1)}, bf16[48,1536]{1,0:T(8,128)(2,1)}, u32[]{:S(2)}) copy-start(bf16[48,1536]{1,0:T(8,128)(2,1)} %param.12) | copy-start | bytes 442372
  31.7 89.0 %collective-permute-start.4 = (bf16[192,384]{1,0:T(8,128)(2,1)}, bf16[192,384]{1,0:T(8,128)(2,1)S(1)}, u32[]{:S(2)}, u32[]{:S(2)}) collective-permute-start(bf16[192,384]{1,0:T(8,128)(2,1)} %get-tuple-element.155), channel_id=1, source_target_pairs={{0,24},{2,26},{4,28},{6,30},{8,16},{10,18},{12,20},{14,22},{16,8},... | collective-permute-start | bytes 442376 | tf_op jit(solution)/shard_map/ppermute | solution.py:91
  73.6 1.3 copy-start
  74.8 8.0 %copy-start.6 = (bf16[192,384]{1,0:T(8,128)(2,1)S(1)}, bf16[192,384]{1,0:T(8,128)(2,1)}, u32[]{:S(2)}) copy-start(bf16[192,384]{1,0:T(8,128)(2,1)} %get-tuple-element.157) | copy-start | bytes 442372
  74.8 8.1 %copy-start.5 = (bf16[192,384]{1,0:T(8,128)(2,1)S(1)}, bf16[192,384]{1,0:T(8,128)(2,1)}, u32[]{:S(2)}) copy-start(bf16[192,384]{1,0:T(8,128)(2,1)} %get-tuple-element.156) | copy-start | bytes 442372
  77.0 43.6 %collective-permute-start.7 = (bf16[192,384]{1,0:T(8,128)(2,1)}, bf16[192,384]{1,0:T(8,128)(2,1)S(1)}, u32[]{:S(2)}, u32[]{:S(2)}) collective-permute-start(bf16[192,384]{1,0:T(8,128)(2,1)} %get-tuple-element.150), channel_id=1, source_target_pairs={{0,30},{2,16},{4,18},{6,20},{8,22},{10,24},{12,26},{14,28},{16,14}... | collective-permute-start | bytes 442376 | tf_op jit(solution)/shard_map/ppermute | solution.py:91
  82.9 37.8 %collective-permute-start.5 = (bf16[192,384]{1,0:T(8,128)(2,1)S(1)}, bf16[192,384]{1,0:T(8,128)(2,1)S(1)}, u32[]{:S(2)}, u32[]{:S(2)}) collective-permute-start(bf16[192,384]{1,0:T(8,128)(2,1)S(1)} %copy-done.6), channel_id=1, source_target_pairs={{0,26},{2,28},{4,30},{6,16},{8,18},{10,20},{12,22},{14,24},{16,10}... | collective-permute-start | bytes 442376 | tf_op jit(solution)/shard_map/ppermute | solution.py:91
  82.9 37.8 %collective-permute-start.6 = (bf16[192,384]{1,0:T(8,128)(2,1)S(1)}, bf16[192,384]{1,0:T(8,128)(2,1)}, u32[]{:S(2)}, u32[]{:S(2)}) collective-permute-start(bf16[192,384]{1,0:T(8,128)(2,1)S(1)} %copy-done.5), channel_id=1, source_target_pairs={{0,28},{2,30},{4,16},{6,18},{8,20},{10,22},{12,24},{14,26},{16,12}... | collective-permute-start | bytes 442376 | tf_op jit(solution)/shard_map/ppermute | solution.py:91
  160.4 2.0 copy-start.1
  163.9 17.6 %all-to-all-start.1 = ((bf16[8,192,192]{2,1,0:T(8,128)(2,1)}), bf16[8,192,192]{2,1,0:T(8,128)(2,1)S(1)}, u32[]{:S(2)}, u32[]{:S(2)}) async-start(bf16[8,192,192]{2,1,0:T(8,128)(2,1)} %bitcast.25), calls=%async_computation.1 | async-start | bytes 1572864 | tf_op jit(solution)/shard_map/all_to_all | solution.py:72
  174.0 15.1 %collective-permute-start.9 = (f32[2,48,1536]{2,1,0:T(8,128)S(1)}, f32[2,48,1536]{2,1,0:T(8,128)}, u32[]{:S(2)}, u32[]{:S(2)}) collective-permute-start(f32[2,48,1536]{2,1,0:T(8,128)S(1)} %dynamic-slice_bitcast_fusion), channel_id=1, source_target_pairs={{0,1},{1,0},{2,3},{3,2},{4,5},{5,4},{6,7},{7,6},{8,9},{9,8},{10,11... | collective-permute-start | bytes 1769480 | tf_op jit(solution)/shard_map/ppermute | solution.py:120
  190.3 11.0 %collective-permute-start.10 = (f32[48,1536]{1,0:T(8,128)S(1)}, f32[48,1536]{1,0:T(8,128)S(1)}, u32[]{:S(2)}, u32[]{:S(2)}) collective-permute-start(f32[48,1536]{1,0:T(8,128)S(1)} %get-tuple-element.161), channel_id=1, source_target_pairs={{0,0},{1,1},{2,4},{3,5},{4,8},{5,9},{6,12},{7,13},{8,16},{9,17},{1... | collective-permute-start | bytes 884744 | tf_op jit(solution)/shard_map/ppermute | solution.py:134
  194.8 11.8 %collective-permute-start.11 = (f32[48,1536]{1,0:T(8,128)S(1)}, f32[48,1536]{1,0:T(8,128)S(1)}, u32[]{:S(2)}, u32[]{:S(2)}) collective-permute-start(f32[48,1536]{1,0:T(8,128)S(1)} %get-tuple-element.160), channel_id=1, source_target_pairs={{0,2},{1,3},{2,6},{3,7},{4,10},{5,11},{6,14},{7,15},{8,18},{9,19},... | collective-permute-start | bytes 884744 | tf_op jit(solution)/shard_map/ppermute | solution.py:134
Sparse Core Ops, SparseCore 0:
  9.7 63.0 all-gather.5
  75.7 62.6 all-gather.3

commit v11 on v8

--- a/solution.py
+++ b/solution.py
@@ -41,14 +41,7 @@
     width = queries.shape[2]
 
     dp_index = lax.axis_index("dp")
-    w_other = lax.ppermute(w_out, "dp", [(p, (p + 1) % dp_count) for p in range(dp_count)])
-    if dp_count == 2:
-        w_pair = jnp.stack(
-            [jnp.where(dp_index == 0, w_out, w_other), jnp.where(dp_index == 0, w_other, w_out)]
-        )
-        w_full = lax.all_gather(w_pair, ("side", "inner"), axis=0, tiled=True).reshape(-1, width)
-    else:
-        w_full = lax.all_gather(w_out, ALL, axis=0, tiled=True)
+    w_full = lax.all_gather(w_out, ALL, axis=0, tiled=True)
     cot_side = lax.all_gather(cotangent[0], "inner", axis=0, tiled=True)
 
     def a2a(tensor):

time: 175 us -> 175 us (level); the launches traced: 172 us -> 174 us
  waiting for transfers between devices: 87.1 us -> 90.5 us
  other arithmetic: 11.3 us -> 9.47 us
    all_to_all x2, waiting for transfers between devices: 43.7 us -> 52.9 us  [a2a(): lax.all_to_all(tensor, 'inner', split_axis=0, concat_axis=0, tiled=True)]
    ppermute x8, waiting for transfers between devices: 27.7 us -> 21.4 us  [local(): kv_crossed.append(lax.ppermute(outgoing, ('side', 'inner'), perm))]
    ppermute x1 -> x0, waiting for transfers between devices: 4.5 us -> none  [local(): lax.ppermute(w_out, 'dp', [(p, (p + 1) % dp_count) for p in range(dp_coun...]
    ppermute x1, waiting for transfers between devices: 3.19 us -> 6.91 us  [local(): kept = kept + lax.ppermute(sent, 'dp', [(0, 1), (1, 0)])]
  transfers between devices with their start and end apart: 16 -> 15, of which waited for: 9 -> 7; matrix products, arithmetic and copies ran while one was open for 24% -> 23% of each run, Pallas kernels for 0% -> 0%
where the time goes in v11:
time: 175 us; the launch traced here: 174 us
  waiting for transfers between devices  90.5 us (52%)
  starting transfers between devices  27.5 us (16%)
  local copies, waits for them, and re-layouts  16.8 us (10%)
  matrix products  15.4 us (9%)
  between operations  14.4 us (8%)
  other arithmetic  9.47 us (5%)
    all_to_all x2, waiting for transfers between devices, a2a(): lax.all_to_all(tensor, 'inner', split_axis=0, concat_axis=0, tiled=True)  52.9 us
    ppermute x8, waiting for transfers between devices, local(): kv_crossed.append(lax.ppermute(outgoing, ('side', 'inner'), perm))  21.4 us
    ppermute x8, starting transfers between devices, local(): kv_crossed.append(lax.ppermute(outgoing, ('side', 'inner'), perm))  12.5 us
    all_to_all x2, starting transfers between devices, a2a(): lax.all_to_all(tensor, 'inner', split_axis=0, concat_axis=0, tiled=True)  9.15 us
    ppermute x2, waiting for transfers between devices, local(): arrived = lax.ppermute(outgoing, ALL, perm)  7.95 us
    ppermute x1, waiting for transfers between devices, local(): kept = kept + lax.ppermute(sent, 'dp', [(0, 1), (1, 0)])  6.91 us
    unnamed x20, local copies, waits for them, and re-layouts  5.23 us
    ppermute x2, starting transfers between devices, local(): arrived = lax.ppermute(outgoing, ALL, perm)  4.61 us
  transfers between devices with their start and end apart: 15, of which 7 were waited for; matrix products, arithmetic and copies ran while one was open for 23% of the time, Pallas kernels for 0%

profile of v11, /device:TPU:1, one launch (start us, length us, event | category | flops | bytes accessed | tf_op | source)
XLA Modules:
  0.0 174.1 jit_solution(10870818603327907409)
XLA Ops:
  7.2 0.0 all-gather.6.cloned.1.call-start
  7.2 0.7 all-gather.6.cloned.1.call-update
  7.9 1.7 reshape_squeeze.10
  9.7 1.5 reshape_squeeze.11
  11.2 0.6 reshape_squeeze.9
  11.8 0.2 copy.21
  11.9 1.5 copy_bitcast_fusion
  13.4 2.0 %pad_maximum_fusion = bf16[8,192,576]{2,1,0:T(8,128)(2,1)} fusion(bf16[8,192,192]{2,1,0:T(8,128)(2,1)S(1)} %get-tuple-element.54, bf16[8,192,192]{2,1,0:T(8,128)(2,1)S(1)} %get-tuple-element.55, bf16[8,192,192]{2,1,0:T(8,128)(2,1)S(1)} %bitcast.76), kind=kLoop, calls=%fused_computation.20 | loop fusion | flops 5308416 | bytes 3538944 | tf_op jit(solution)/shard_map/concatenate | solution.py:68
  15.5 5.3 %all-to-all-start = ((bf16[8,192,576]{2,1,0:T(8,128)(2,1)}), bf16[8,192,576]{2,1,0:T(8,128)(2,1)S(1)}, u32[]{:S(2)}, u32[]{:S(2)}) async-start(bf16[8,192,576]{2,1,0:T(8,128)(2,1)} %pad_maximum_fusion), calls=%async_computation | async-start | bytes 3932160 | tf_op jit(solution)/shard_map/all_to_all | solution.py:48
  20.8 0.7 all-gather.4.cloned.1.call-update
  21.6 1.2 fusion.41
  22.8 2.3 %collective-permute-start = (bf16[192,384]{1,0:T(8,128)(2,1)}, bf16[192,384]{1,0:T(8,128)(2,1)}, u32[]{:S(2)}, u32[]{:S(2)}) collective-permute-start(bf16[192,384]{1,0:T(8,128)(2,1)} %get-tuple-element.45), channel_id=1, source_target_pairs={{0,16},{2,18},{4,20},{6,22},{8,24},{10,26},{12,28},{14,30},{16,0},... | collective-permute-start | bytes 442376 | tf_op jit(solution)/shard_map/ppermute | solution.py:67
  25.1 1.7 collective-permute-start.1
  26.8 2.3 %collective-permute-start.2 = (bf16[192,384]{1,0:T(8,128)(2,1)}, bf16[192,384]{1,0:T(8,128)(2,1)}, u32[]{:S(2)}, u32[]{:S(2)}) collective-permute-start(bf16[192,384]{1,0:T(8,128)(2,1)} %get-tuple-element.47), channel_id=1, source_target_pairs={{0,20},{2,22},{4,24},{6,26},{8,28},{10,30},{12,16},{14,18},{16,4},... | collective-permute-start | bytes 442376 | tf_op jit(solution)/shard_map/ppermute | solution.py:67
  29.1 1.2 collective-permute-start.3
  30.3 2.1 %collective-permute-start.4 = (bf16[192,384]{1,0:T(8,128)(2,1)}, bf16[192,384]{1,0:T(8,128)(2,1)}, u32[]{:S(2)}, u32[]{:S(2)}) collective-permute-start(bf16[192,384]{1,0:T(8,128)(2,1)} %get-tuple-element.49), channel_id=1, source_target_pairs={{0,24},{2,26},{4,28},{6,30},{8,16},{10,18},{12,20},{14,22},{16,8},... | collective-permute-start | bytes 442376 | tf_op jit(solution)/shard_map/ppermute | solution.py:67
  32.4 0.8 fusion.34
  33.3 40.3 %all-to-all-done = bf16[8,192,576]{2,1,0:T(8,128)(2,1)S(1)} async-done(((bf16[8,192,576]{2,1,0:T(8,128)(2,1)}), bf16[8,192,576]{2,1,0:T(8,128)(2,1)S(1)}, u32[]{:S(2)}, u32[]{:S(2)}) %all-to-all-start) | async-done | bytes 1769504 | tf_op jit(solution)/shard_map/all_to_all | solution.py:48
  73.5 0.5 slice_dynamic-update-slice_fusion
  74.0 0.0 collective-permute-done
  74.1 0.1 collective-permute-start.5
  74.1 0.9 constant_dynamic-update-slice_fusion.7
  75.1 2.8 %collective-permute-start.6 = (bf16[192,384]{1,0:T(8,128)(2,1)S(1)}, bf16[192,384]{1,0:T(8,128)(2,1)S(1)}, u32[]{:S(2)}, u32[]{:S(2)}) collective-permute-start(bf16[192,384]{1,0:T(8,128)(2,1)S(1)} %copy-done.5), channel_id=1, source_target_pairs={{0,28},{2,30},{4,16},{6,18},{8,20},{10,22},{12,24},{14,26},{16,12}... | collective-permute-start | bytes 442376 | tf_op jit(solution)/shard_map/ppermute | solution.py:67
  77.8 0.9 constant_dynamic-update-slice_fusion.6
  78.8 0.0 collective-permute-done.2
  78.8 0.1 collective-permute-start.7
  78.9 0.9 constant_dynamic-update-slice_fusion.5
  79.8 0.9 constant_dynamic-update-slice_fusion.4
  80.7 0.0 collective-permute-done.4
  80.8 0.9 constant_dynamic-update-slice_fusion.3
  81.7 8.8 %collective-permute-done.5 = bf16[192,384]{1,0:T(8,128)(2,1)S(1)} collective-permute-done((bf16[192,384]{1,0:T(8,128)(2,1)S(1)}, bf16[192,384]{1,0:T(8,128)(2,1)S(1)}, u32[]{:S(2)}, u32[]{:S(2)}) %collective-permute-start.5) | collective-permute-done | bytes 147488 | tf_op jit(solution)/shard_map/ppermute | solution.py:67
  90.5 0.1 slice.16
  90.5 9.8 %collective-permute-done.6 = bf16[192,384]{1,0:T(8,128)(2,1)S(1)} collective-permute-done((bf16[192,384]{1,0:T(8,128)(2,1)S(1)}, bf16[192,384]{1,0:T(8,128)(2,1)S(1)}, u32[]{:S(2)}, u32[]{:S(2)}) %collective-permute-start.6) | collective-permute-done | bytes 147488 | tf_op jit(solution)/shard_map/ppermute | solution.py:67
  100.4 2.8 %collective-permute-done.7 = bf16[192,384]{1,0:T(8,128)(2,1)S(1)} collective-permute-done((bf16[192,384]{1,0:T(8,128)(2,1)}, bf16[192,384]{1,0:T(8,128)(2,1)S(1)}, u32[]{:S(2)}, u32[]{:S(2)}) %collective-permute-start.7) | collective-permute-done | bytes 147488 | tf_op jit(solution)/shard_map/ppermute | solution.py:67
  103.2 0.0 copy-start
  103.2 1.9 %fusion.42 = (bf16[3072,192]{1,0:T(8,128)(2,1)}, bf16[3072,192]{1,0:T(8,128)(2,1)S(1)}) fusion(bf16[3072,384]{1,0:T(8,128)(2,1)S(1)} %constant_dynamic-update-slice_fusion), kind=kLoop, calls=%fused_computation.69 | loop fusion | bytes 4718592 | tf_op jit(solution)/shard_map/slice | solution.py:73
  105.1 12.2 %while.10 = (s32[]{:T(128)}, bf16[3,512,192]{1,2,0:T(8,128)(2,1)S(1)}, bf16[3,512,192]{2,1,0:T(8,128)(2,1)S(1)}, bf16[3072,192]{1,0:T(8,128)(2,1)S(1)}, bf16[3072,192]{1,0:T(8,128)(2,1)}, /*index=5*/s32[]{:T(128)}) while((s32[]{:T(128)}, bf16[3,512,192]{1,2,0:T(8,128)(2,1)S(1)}, bf16[3,512,192]{2,1,0:T(8,128)(2,1)S(1)}, ...), condition=%wide.region_3.4_spmd, body=%wide.region_0.3_spmd.sunk | while | flops 1220738048 | bytes 27207784 | solution.py:26
  105.1 1.1 multiply_reduce_fusion.2
  106.3 1.2 fusion.56
  107.4 0.4 copy-done.1
  107.8 1.5 fusion.57
  109.3 1.1 multiply_reduce_fusion.2
  110.4 1.2 fusion.56
  111.6 0.3 copy-done.1
  111.8 1.5 fusion.57
  113.3 1.1 multiply_reduce_fusion.2
  114.4 1.2 fusion.56
  115.6 0.3 copy-done.1
  115.8 1.5 fusion.57
  117.3 1.2 copy.13
  118.5 3.8 %all-to-all-start.1 = ((bf16[8,192,192]{2,1,0:T(8,128)(2,1)}), bf16[8,192,192]{2,1,0:T(8,128)(2,1)S(1)}, u32[]{:S(2)}, u32[]{:S(2)}) async-start(bf16[8,192,192]{2,1,0:T(8,128)(2,1)} %bitcast.15), calls=%async_computation.1 | async-start | bytes 1572864 | tf_op jit(solution)/shard_map/all_to_all | solution.py:48
  122.4 3.4 %fusion.23 = f32[2,2,48,1536]{3,2,1,0:T(8,128)S(1)} fusion(bf16[2,2,48,1536]{3,2,1,0:T(8,128)(2,1)S(1)} %bitcast.77, bf16[1,1536,1536]{2,1,0:T(8,128)(2,1)} %all-gather.6.cloned.1.call-done), kind=kOutput, calls=%fused_computation.16 | convolution fusion | flops 905969664 | bytes 6488064 | tf_op jit(solution)/shard_map/dot_general | solution.py:77
  125.8 1.2 collective-permute-start.8
  127.0 12.6 %all-to-all-done.1 = bf16[8,192,192]{2,1,0:T(8,128)(2,1)S(1)} async-done(((bf16[8,192,192]{2,1,0:T(8,128)(2,1)}), bf16[8,192,192]{2,1,0:T(8,128)(2,1)S(1)}, u32[]{:S(2)}, u32[]{:S(2)}) %all-to-all-start.1) | async-done | bytes 589856 | tf_op jit(solution)/shard_map/all_to_all | solution.py:48
  139.6 0.4 copy.14
  140.0 1.5 reshape.25
  141.5 6.9 %collective-permute-done.8 = f32[2,48,1536]{2,1,0:T(8,128)} collective-permute-done((f32[2,48,1536]{2,1,0:T(8,128)S(1)}, f32[2,48,1536]{2,1,0:T(8,128)}, u32[]{:S(2)}, u32[]{:S(2)}) %collective-permute-start.8) | collective-permute-done | bytes 589856 | tf_op jit(solution)/shard_map/ppermute | solution.py:94
  148.4 1.1 bitcast_add_fusion
  149.6 1.2 collective-permute-start.10
  150.9 3.4 %collective-permute-start.9 = (f32[48,1536]{1,0:T(8,128)S(1)}, f32[48,1536]{1,0:T(8,128)S(1)}, u32[]{:S(2)}, u32[]{:S(2)}) collective-permute-start(f32[48,1536]{1,0:T(8,128)S(1)} %get-tuple-element.53), channel_id=1, source_target_pairs={{0,0},{1,1},{2,4},{3,5},{4,8},{5,9},{6,12},{7,13},{8,16},{9,17},{1... | collective-permute-start | bytes 884744 | tf_op jit(solution)/shard_map/ppermute | solution.py:108
  154.3 0.0 all-gather.4.cloned.1.call-done
  154.3 4.2 %fusion.25 = bf16[1,192,1536]{2,1,0:T(8,128)(2,1)} fusion(bf16[192,1536]{1,0:T(8,128)(2,1)S(1)} %copy-done.4, bf16[1536,1536]{1,0:T(8,128)(2,1)} %all-gather.4.cloned.1.call-done), kind=kOutput, calls=%fused_computation.19 | convolution fusion | flops 906264576 | bytes 5898240 | tf_op jit(solution)/shard_map/dot_general | solution.py:83
  158.5 7.9 %collective-permute-done.9 = f32[48,1536]{1,0:T(8,128)S(1)} collective-permute-done((f32[48,1536]{1,0:T(8,128)S(1)}, f32[48,1536]{1,0:T(8,128)S(1)}, u32[]{:S(2)}, u32[]{:S(2)}) %collective-permute-start.9) | collective-permute-done | bytes 294944 | tf_op jit(solution)/shard_map/ppermute | solution.py:108
  166.5 0.7 add.135
  (26 shorter events, 0.2 us)
Async XLA Ops:
  7.2 2.5 %copy-start.2 = (bf16[1,192,1536]{2,1,0:T(8,128)(2,1)S(1)}, bf16[1,192,1536]{2,1,0:T(8,128)(2,1)}, u32[]{:S(2)}) copy-start(bf16[1,192,1536]{2,1,0:T(8,128)(2,1)} %param.9) | copy-start | bytes 1769476
  7.2 4.0 %copy-start.3 = (bf16[1,192,1536]{2,1,0:T(8,128)(2,1)S(1)}, bf16[1,192,1536]{2,1,0:T(8,128)(2,1)}, u32[]{:S(2)}) copy-start(bf16[1,192,1536]{2,1,0:T(8,128)(2,1)} %param.7) | copy-start | bytes 1769476
  7.2 115.2 %all-gather.6.cloned.1.call-start = ((), (), s32[]{:S(2)}) async-start(), calls=%async_computation.3 | async-start | bytes 5308416 | tf_op jit(solution)/shard_map/all_gather | solution.py:45
  15.5 58.1 %all-to-all-start = ((bf16[8,192,576]{2,1,0:T(8,128)(2,1)}), bf16[8,192,576]{2,1,0:T(8,128)(2,1)S(1)}, u32[]{:S(2)}, u32[]{:S(2)}) async-start(bf16[8,192,576]{2,1,0:T(8,128)(2,1)} %pad_maximum_fusion), calls=%async_computation | async-start | bytes 3932160 | tf_op jit(solution)/shard_map/all_to_all | solution.py:48
  20.8 133.5 %all-gather.4.cloned.1.call-start = ((), (), s32[]{:S(2)}) async-start(), calls=%async_computation.2 | async-start | bytes 4866048 | tf_op jit(solution)/shard_map/all_gather | solution.py:44
  22.8 51.2 %collective-permute-start = (bf16[192,384]{1,0:T(8,128)(2,1)}, bf16[192,384]{1,0:T(8,128)(2,1)}, u32[]{:S(2)}, u32[]{:S(2)}) collective-permute-start(bf16[192,384]{1,0:T(8,128)(2,1)} %get-tuple-element.45), channel_id=1, source_target_pairs={{0,16},{2,18},{4,20},{6,22},{8,24},{10,26},{12,28},{14,30},{16,0},... | collective-permute-start | bytes 442376 | tf_op jit(solution)/shard_map/ppermute | solution.py:67
  25.1 49.9 %collective-permute-start.1 = (bf16[192,384]{1,0:T(8,128)(2,1)}, bf16[192,384]{1,0:T(8,128)(2,1)}, u32[]{:S(2)}, u32[]{:S(2)}) collective-permute-start(bf16[192,384]{1,0:T(8,128)(2,1)} %get-tuple-element.46), channel_id=1, source_target_pairs={{0,18},{2,20},{4,22},{6,24},{8,26},{10,28},{12,30},{14,16},{16,2},... | collective-permute-start | bytes 442376 | tf_op jit(solution)/shard_map/ppermute | solution.py:67
  26.8 52.0 %collective-permute-start.2 = (bf16[192,384]{1,0:T(8,128)(2,1)}, bf16[192,384]{1,0:T(8,128)(2,1)}, u32[]{:S(2)}, u32[]{:S(2)}) collective-permute-start(bf16[192,384]{1,0:T(8,128)(2,1)} %get-tuple-element.47), channel_id=1, source_target_pairs={{0,20},{2,22},{4,24},{6,26},{8,28},{10,30},{12,16},{14,18},{16,4},... | collective-permute-start | bytes 442376 | tf_op jit(solution)/shard_map/ppermute | solution.py:67
  29.1 50.7 %collective-permute-start.3 = (bf16[192,384]{1,0:T(8,128)(2,1)}, bf16[192,384]{1,0:T(8,128)(2,1)}, u32[]{:S(2)}, u32[]{:S(2)}) collective-permute-start(bf16[192,384]{1,0:T(8,128)(2,1)} %get-tuple-element.48), channel_id=1, source_target_pairs={{0,22},{2,24},{4,26},{6,28},{8,30},{10,16},{12,18},{14,20},{16,6},... | collective-permute-start | bytes 442376 | tf_op jit(solution)/shard_map/ppermute | solution.py:67
  30.3 50.4 %collective-permute-start.4 = (bf16[192,384]{1,0:T(8,128)(2,1)}, bf16[192,384]{1,0:T(8,128)(2,1)}, u32[]{:S(2)}, u32[]{:S(2)}) collective-permute-start(bf16[192,384]{1,0:T(8,128)(2,1)} %get-tuple-element.49), channel_id=1, source_target_pairs={{0,24},{2,26},{4,28},{6,30},{8,16},{10,18},{12,20},{14,22},{16,8},... | collective-permute-start | bytes 442376 | tf_op jit(solution)/shard_map/ppermute | solution.py:67
  33.3 40.8 %copy-start.6 = (bf16[192,384]{1,0:T(8,128)(2,1)S(1)}, bf16[192,384]{1,0:T(8,128)(2,1)}, u32[]{:S(2)}) copy-start(bf16[192,384]{1,0:T(8,128)(2,1)} %get-tuple-element.51) | copy-start | bytes 442372
  33.3 41.8 %copy-start.5 = (bf16[192,384]{1,0:T(8,128)(2,1)S(1)}, bf16[192,384]{1,0:T(8,128)(2,1)}, u32[]{:S(2)}) copy-start(bf16[192,384]{1,0:T(8,128)(2,1)} %get-tuple-element.50) | copy-start | bytes 442372
  74.1 16.4 %collective-permute-start.5 = (bf16[192,384]{1,0:T(8,128)(2,1)S(1)}, bf16[192,384]{1,0:T(8,128)(2,1)S(1)}, u32[]{:S(2)}, u32[]{:S(2)}) collective-permute-start(bf16[192,384]{1,0:T(8,128)(2,1)S(1)} %copy-done.6), channel_id=1, source_target_pairs={{0,26},{2,28},{4,30},{6,16},{8,18},{10,20},{12,22},{14,24},{16,10}... | collective-permute-start | bytes 442376 | tf_op jit(solution)/shard_map/ppermute | solution.py:67
  75.1 25.2 %collective-permute-start.6 = (bf16[192,384]{1,0:T(8,128)(2,1)S(1)}, bf16[192,384]{1,0:T(8,128)(2,1)S(1)}, u32[]{:S(2)}, u32[]{:S(2)}) collective-permute-start(bf16[192,384]{1,0:T(8,128)(2,1)S(1)} %copy-done.5), channel_id=1, source_target_pairs={{0,28},{2,30},{4,16},{6,18},{8,20},{10,22},{12,24},{14,26},{16,12}... | collective-permute-start | bytes 442376 | tf_op jit(solution)/shard_map/ppermute | solution.py:67
  78.8 24.4 %collective-permute-start.7 = (bf16[192,384]{1,0:T(8,128)(2,1)}, bf16[192,384]{1,0:T(8,128)(2,1)S(1)}, u32[]{:S(2)}, u32[]{:S(2)}) collective-permute-start(bf16[192,384]{1,0:T(8,128)(2,1)} %get-tuple-element.44), channel_id=1, source_target_pairs={{0,30},{2,16},{4,18},{6,20},{8,22},{10,24},{12,26},{14,28},{16,14}... | collective-permute-start | bytes 442376 | tf_op jit(solution)/shard_map/ppermute | solution.py:67
  103.2 1.9 %copy-start = (bf16[3,512,192]{1,2,0:T(8,128)(2,1)S(1)}, bf16[3,512,192]{1,2,0:T(8,128)(2,1)}, u32[]{:S(2)}) copy-start(bf16[3,512,192]{1,2,0:T(8,128)(2,1)} %custom-call.1) | copy-start | bytes 1769476
  106.3 1.5 copy-start.1
  110.4 1.4 copy-start.1
  114.4 1.4 copy-start.1
  118.5 21.1 %all-to-all-start.1 = ((bf16[8,192,192]{2,1,0:T(8,128)(2,1)}), bf16[8,192,192]{2,1,0:T(8,128)(2,1)S(1)}, u32[]{:S(2)}, u32[]{:S(2)}) async-start(bf16[8,192,192]{2,1,0:T(8,128)(2,1)} %bitcast.15), calls=%async_computation.1 | async-start | bytes 1572864 | tf_op jit(solution)/shard_map/all_to_all | solution.py:48
  125.8 22.6 %collective-permute-start.8 = (f32[2,48,1536]{2,1,0:T(8,128)S(1)}, f32[2,48,1536]{2,1,0:T(8,128)}, u32[]{:S(2)}, u32[]{:S(2)}) collective-permute-start(f32[2,48,1536]{2,1,0:T(8,128)S(1)} %dynamic-slice_bitcast_fusion), channel_id=1, source_target_pairs={{0,1},{1,0},{2,3},{3,2},{4,5},{5,4},{6,7},{7,6},{8,9},{9,8},{10,11... | collective-permute-start | bytes 1769480 | tf_op jit(solution)/shard_map/ppermute | solution.py:94
  141.5 12.8 %copy-start.4 = (bf16[192,1536]{1,0:T(8,128)(2,1)S(1)}, bf16[192,1536]{1,0:T(8,128)(2,1)}, u32[]{:S(2)}) copy-start(bf16[192,1536]{1,0:T(8,128)(2,1)} %reshape.25) | copy-start | bytes 1769476
  149.6 8.9 %collective-permute-start.10 = (f32[48,1536]{1,0:T(8,128)S(1)}, f32[48,1536]{1,0:T(8,128)S(1)}, u32[]{:S(2)}, u32[]{:S(2)}) collective-permute-start(f32[48,1536]{1,0:T(8,128)S(1)} %get-tuple-element.52), channel_id=1, source_target_pairs={{0,2},{1,3},{2,6},{3,7},{4,10},{5,11},{6,14},{7,15},{8,18},{9,19},... | collective-permute-start | bytes 884744 | tf_op jit(solution)/shard_map/ppermute | solution.py:108
  150.9 15.6 %collective-permute-start.9 = (f32[48,1536]{1,0:T(8,128)S(1)}, f32[48,1536]{1,0:T(8,128)S(1)}, u32[]{:S(2)}, u32[]{:S(2)}) collective-permute-start(f32[48,1536]{1,0:T(8,128)S(1)} %get-tuple-element.53), channel_id=1, source_target_pairs={{0,0},{1,1},{2,4},{3,5},{4,8},{5,9},{6,12},{7,13},{8,16},{9,17},{1... | collective-permute-start | bytes 884744 | tf_op jit(solution)/shard_map/ppermute | solution.py:108
Sparse Core Ops, SparseCore 0:
  9.7 62.8 all-gather.5
  75.5 78.4 all-gather.3

commit v12 on v11

--- a/solution.py
+++ b/solution.py
@@ -53,18 +53,38 @@
     side_index = lax.axis_index("side")
     kv_raw = jnp.concatenate([by_head(key_vectors), by_head(value_vectors)], axis=2)
     inner_index = lax.axis_index("inner")
+    chip_count = head_count // 2
+    chip_index = inner_index // 2
+    parity = inner_index % 2
+    by_chip = kv_raw.reshape(chip_count, 2, row_count, 2 * head_width)
+    seq_count = side_count * head_count
     kv_crossed = []
     for step in range(1, side_count):
-        for shift in range(head_count):
+        own_pieces = []
+        partner_pieces = []
+        for shift in range(chip_count):
             perm = [
-                (g * head_count + i, ((g + step) % side_count) * head_count + (i + shift) % head_count)
+                (
+                    g * head_count + 2 * c + k,
+                    ((g + step) % side_count) * head_count + 2 * ((c + shift) % chip_count) + k,
+                )
                 for g in range(side_count)
-                for i in range(head_count)
+                for c in range(chip_count)
+                for k in range(2)
             ]
             outgoing = lax.dynamic_index_in_dim(
-                kv_raw, (inner_index + shift) % head_count, axis=0, keepdims=False
+                by_chip, (chip_index + shift) % chip_count, axis=0, keepdims=False
             )
-            kv_crossed.append(lax.ppermute(outgoing, ("side", "inner"), perm))
+            arrived = lax.ppermute(outgoing, ("side", "inner"), perm)
+            own_pieces.append(lax.dynamic_index_in_dim(arrived, parity, axis=0, keepdims=False))
+            partner_pieces.append(
+                lax.dynamic_index_in_dim(arrived, 1 - parity, axis=0, keepdims=False)
+            )
+        swapped = lax.ppermute(
+            jnp.stack(partner_pieces), ("side", "inner"), [(s, s ^ 1) for s in range(seq_count)]
+        )
+        kv_crossed.append(jnp.stack(own_pieces).reshape(-1, 2 * head_width))
+        kv_crossed.append(swapped.reshape(-1, 2 * head_width))
     stacked = jnp.concatenate([by_head(queries), kv_raw], axis=2)
     got = a2a(stacked).reshape(head_count * row_count, 3 * head_width)
     query_here = got[:, :head_width]

time: 175 us -> 179 us (1.023)
  waiting for transfers between devices: 90.5 us -> 97.4 us
  local copies, waits for them, and re-layouts: 16.8 us -> 13.9 us
    all_to_all x2, waiting for transfers between devices: 52.9 us -> 11.6 us  [a2a(): lax.all_to_all(tensor, 'inner', split_axis=0, concat_axis=0, tiled=True)]
    ppermute x8 -> x5, waiting for transfers between devices: 21.4 us -> 55.7 us  [the longest x4 54.4 us: local(): arrived = lax.ppermute(outgoing, ('side', 'inner'), perm)]
    all_gather x1, waiting for transfers between devices: 0.02 us -> 27.6 us  [local(): w_full = lax.all_gather(w_out, ALL, axis=0, tiled=True)]
    ppermute x2, waiting for transfers between devices: 7.95 us -> 0.01 us  [local(): arrived = lax.ppermute(outgoing, ALL, perm)]
    ppermute x1, waiting for transfers between devices: 6.91 us -> 1.08 us  [local(): kept = kept + lax.ppermute(sent, 'dp', [(0, 1), (1, 0)])]
    unnamed x20 -> x4, local copies, waits for them, and re-layouts: 5.23 us -> 0.01 us
    ppermute x8 -> x5, starting transfers between devices: 12.5 us -> 8.1 us  [the longest x4 7.63 us: local(): arrived = lax.ppermute(outgoing, ('side', 'inner'), perm)]
    all_to_all x2, starting transfers between devices: 9.15 us -> 12.5 us  [a2a(): lax.all_to_all(tensor, 'inner', split_axis=0, concat_axis=0, tiled=True)]
  transfers between devices with their start and end apart: 15 -> 12, of which waited for: 7 -> 8; matrix products, arithmetic and copies ran while one was open for 23% -> 21% of each run, Pallas kernels for 0% -> 0%
where the time goes in v12:
time: 179 us; the launch traced here: 178 us
  waiting for transfers between devices  97.4 us (54%)
  starting transfers between devices  26.7 us (15%)
  matrix products  15.7 us (9%)
  between operations  14.3 us (8%)
  local copies, waits for them, and re-layouts  13.9 us (8%)
  other arithmetic  10.2 us (6%)
    ppermute x4, waiting for transfers between devices, local(): arrived = lax.ppermute(outgoing, ('side', 'inner'), perm)  54.4 us
    all_gather x1, waiting for transfers between devices, local(): w_full = lax.all_gather(w_out, ALL, axis=0, tiled=True)  27.6 us
    all_to_all x2, starting transfers between devices, a2a(): lax.all_to_all(tensor, 'inner', split_axis=0, concat_axis=0, tiled=True)  12.5 us
    all_to_all x2, waiting for transfers between devices, a2a(): lax.all_to_all(tensor, 'inner', split_axis=0, concat_axis=0, tiled=True)  11.6 us
    ppermute x4, starting transfers between devices, local(): arrived = lax.ppermute(outgoing, ('side', 'inner'), perm)  7.63 us
    another operation x4, local copies, waits for them, and re-layouts, by_head(): tensor[0].reshape(row_count, head_count, head_width).transpose(1, 0, 2)  4.9 us
    ppermute x2, starting transfers between devices, local(): arrived = lax.ppermute(outgoing, ALL, perm)  4.81 us
    dot_general x1, matrix products, local(): jnp.dot(attended, w_full, preferred_element_type=jnp.float32)  4.43 us
  transfers between devices with their start and end apart: 12, of which 8 were waited for; matrix products, arithmetic and copies ran while one was open for 21% of the time, Pallas kernels for 0%

profile of v12, /device:TPU:1, one launch (start us, length us, event | category | flops | bytes accessed | tf_op | source)
XLA Modules:
  0.0 178.2 jit_solution(14661271777557691633)
XLA Ops:
  7.2 0.0 copy-start.2
  7.2 0.0 all-gather.6.cloned.1.call-start
  7.2 0.7 all-gather.6.cloned.1.call-update
  7.9 1.7 reshape_squeeze.10
  9.6 2.4 %reshape_squeeze.11 = bf16[192,8,192]{2,1,0:T(8,128)(2,1)} reshape(bf16[1,192,1536]{2,1,0:T(8,128)(2,1)} %param.9) | data formatting | bytes 1179648 | tf_op jit(solution)/shard_map/reshape;squeeze | solution.py:51
  12.1 0.0 copy-done.2
  12.1 0.6 reshape_squeeze.9
  12.7 0.2 copy.21
  12.8 1.5 copy_bitcast_fusion
  14.3 2.1 %pad_maximum_fusion.1 = bf16[8,192,576]{2,1,0:T(8,128)(2,1)} fusion(bf16[8,192,192]{2,1,0:T(8,128)(2,1)S(1)} %get-tuple-element.58, bf16[8,192,192]{2,1,0:T(8,128)(2,1)S(1)} %get-tuple-element.59, bf16[8,192,192]{2,1,0:T(8,128)(2,1)S(1)} %bitcast.72), kind=kLoop, calls=%fused_computation.21 | loop fusion | flops 5308416 | bytes 3538944 | tf_op jit(solution)/shard_map/concatenate | solution.py:88
  16.4 5.3 %all-to-all-start = ((bf16[8,192,576]{2,1,0:T(8,128)(2,1)}), bf16[8,192,576]{2,1,0:T(8,128)(2,1)S(1)}, u32[]{:S(2)}, u32[]{:S(2)}) async-start(bf16[8,192,576]{2,1,0:T(8,128)(2,1)} %pad_maximum_fusion.1), calls=%async_computation | async-start | bytes 3932160 | tf_op jit(solution)/shard_map/all_to_all | solution.py:48
  21.7 0.0 all-gather.4.cloned.1.call-start
  21.7 0.7 all-gather.4.cloned.1.call-update
  22.5 0.4 pad_maximum_fusion.2
  23.0 1.0 dynamic-slice_bitcast_fusion.6
  23.9 2.3 %collective-permute-start = (bf16[2,192,384]{2,1,0:T(8,128)(2,1)S(1)}, bf16[2,192,384]{2,1,0:T(8,128)(2,1)S(1)}, u32[]{:S(2)}, u32[]{:S(2)}) collective-permute-start(bf16[2,192,384]{2,1,0:T(8,128)(2,1)S(1)} %get-tuple-element.44), channel_id=1, source_target_pairs={{0,16},{2,18},{4,20},{6,22},{8,24},{10,26},{12,28},{14,30},{16,0},... | collective-permute-start | bytes 884744 | tf_op jit(solution)/shard_map/ppermute | solution.py:78
  26.2 1.2 collective-permute-start.1
  27.4 3.2 %collective-permute-start.2 = (bf16[2,192,384]{2,1,0:T(8,128)(2,1)}, bf16[2,192,384]{2,1,0:T(8,128)(2,1)S(1)}, u32[]{:S(2)}, u32[]{:S(2)}) collective-permute-start(bf16[2,192,384]{2,1,0:T(8,128)(2,1)} %get-tuple-element.46), channel_id=1, source_target_pairs={{0,24},{2,26},{4,28},{6,30},{8,16},{10,18},{12,20},{14,22},{16,8},... | collective-permute-start | bytes 884744 | tf_op jit(solution)/shard_map/ppermute | solution.py:78
  30.6 1.0 collective-permute-start.3
  31.6 35.4 %collective-permute-done = bf16[2,192,384]{2,1,0:T(8,128)(2,1)S(1)} collective-permute-done((bf16[2,192,384]{2,1,0:T(8,128)(2,1)S(1)}, bf16[2,192,384]{2,1,0:T(8,128)(2,1)S(1)}, u32[]{:S(2)}, u32[]{:S(2)}) %collective-permute-start) | collective-permute-done | bytes 294944 | tf_op jit(solution)/shard_map/ppermute | solution.py:78
  67.0 11.1 %collective-permute-done.1 = bf16[2,192,384]{2,1,0:T(8,128)(2,1)S(1)} collective-permute-done((bf16[2,192,384]{2,1,0:T(8,128)(2,1)}, bf16[2,192,384]{2,1,0:T(8,128)(2,1)S(1)}, u32[]{:S(2)}, u32[]{:S(2)}) %collective-permute-start.1) | collective-permute-done | bytes 294944 | tf_op jit(solution)/shard_map/ppermute | solution.py:78
  78.2 5.0 %collective-permute-done.2 = bf16[2,192,384]{2,1,0:T(8,128)(2,1)S(1)} collective-permute-done((bf16[2,192,384]{2,1,0:T(8,128)(2,1)}, bf16[2,192,384]{2,1,0:T(8,128)(2,1)S(1)}, u32[]{:S(2)}, u32[]{:S(2)}) %collective-permute-start.2) | collective-permute-done | bytes 294944 | tf_op jit(solution)/shard_map/ppermute | solution.py:78
  83.2 2.8 %collective-permute-done.3 = bf16[2,192,384]{2,1,0:T(8,128)(2,1)S(1)} collective-permute-done((bf16[2,192,384]{2,1,0:T(8,128)(2,1)}, bf16[2,192,384]{2,1,0:T(8,128)(2,1)S(1)}, u32[]{:S(2)}, u32[]{:S(2)}) %collective-permute-start.3) | collective-permute-done | bytes 294944 | tf_op jit(solution)/shard_map/ppermute | solution.py:78
  86.1 0.9 pad_maximum_fusion.4
  87.0 0.5 collective-permute-start.4
  87.4 0.1 pad_maximum_fusion.3
  87.5 0.0 all-to-all-done
  87.6 0.5 slice.17
  88.1 0.1 slice.16
  88.1 1.3 collective-permute-done.4
  89.4 1.3 pad_maximum_fusion
  90.7 0.0 copy-start
  90.7 1.9 %fusion.26 = (bf16[3072,192]{1,0:T(8,128)(2,1)}, bf16[3072,192]{1,0:T(8,128)(2,1)S(1)}) fusion(bf16[3072,384]{1,0:T(8,128)(2,1)S(1)} %pad_maximum_fusion), kind=kLoop, calls=%fused_computation.44 | loop fusion | bytes 4718592 | tf_op jit(solution)/shard_map/slice | solution.py:93
  92.6 0.0 copy-done
  92.6 12.0 %while.10 = (s32[]{:T(128)}, bf16[3,512,192]{1,2,0:T(8,128)(2,1)S(1)}, bf16[3,512,192]{2,1,0:T(8,128)(2,1)S(1)}, bf16[3072,192]{1,0:T(8,128)(2,1)S(1)}, bf16[3072,192]{1,0:T(8,128)(2,1)}, /*index=5*/s32[]{:T(128)}) while((s32[]{:T(128)}, bf16[3,512,192]{1,2,0:T(8,128)(2,1)S(1)}, bf16[3,512,192]{2,1,0:T(8,128)(2,1)S(1)}, ...), condition=%wide.region_3.4_spmd, body=%wide.region_0.3_spmd.sunk | while | flops 1220738048 | bytes 27207784 | solution.py:26
  92.6 1.1 multiply_reduce_fusion.2
  93.7 0.0 copy-start.1
  93.7 1.2 fusion.40
  94.9 0.2 copy-done.1
  95.2 1.5 fusion.41
  96.6 1.1 multiply_reduce_fusion.2
  97.8 1.2 fusion.40
  98.9 0.2 copy-done.1
  99.2 1.5 fusion.41
  100.7 1.1 multiply_reduce_fusion.2
  101.8 1.2 fusion.40
  103.0 0.2 copy-done.1
  103.2 1.5 fusion.41
  104.7 1.2 copy.13
  105.9 7.2 %all-to-all-start.1 = ((bf16[8,192,192]{2,1,0:T(8,128)(2,1)}), bf16[8,192,192]{2,1,0:T(8,128)(2,1)S(1)}, u32[]{:S(2)}, u32[]{:S(2)}) async-start(bf16[8,192,192]{2,1,0:T(8,128)(2,1)} %bitcast.14), calls=%async_computation.1 | async-start | bytes 1572864 | tf_op jit(solution)/shard_map/all_to_all | solution.py:48
  113.0 3.5 %fusion.23 = f32[2,2,48,1536]{3,2,1,0:T(8,128)S(1)} fusion(bf16[2,2,48,1536]{3,2,1,0:T(8,128)(2,1)S(1)} %bitcast.74, bf16[1,1536,1536]{2,1,0:T(8,128)(2,1)} %all-gather.6.cloned.1.call-done), kind=kOutput, calls=%fused_computation.16 | convolution fusion | flops 905969664 | bytes 6488064 | tf_op jit(solution)/shard_map/dot_general | solution.py:97
  116.6 1.3 collective-permute-start.5
  117.9 11.6 %all-to-all-done.1 = bf16[8,192,192]{2,1,0:T(8,128)(2,1)S(1)} async-done(((bf16[8,192,192]{2,1,0:T(8,128)(2,1)}), bf16[8,192,192]{2,1,0:T(8,128)(2,1)S(1)}, u32[]{:S(2)}, u32[]{:S(2)}) %all-to-all-start.1) | async-done | bytes 589856 | tf_op jit(solution)/shard_map/all_to_all | solution.py:48
  129.5 0.4 copy.14
  130.0 1.5 reshape.37
  131.5 1.1 collective-permute-done.5
  132.6 1.1 bitcast_add_fusion
  133.8 3.5 %collective-permute-start.6 = (f32[48,1536]{1,0:T(8,128)S(1)}, f32[48,1536]{1,0:T(8,128)S(1)}, u32[]{:S(2)}, u32[]{:S(2)}) collective-permute-start(f32[48,1536]{1,0:T(8,128)S(1)} %get-tuple-element.49), channel_id=1, source_target_pairs={{0,0},{1,1},{2,4},{3,5},{4,8},{5,9},{6,12},{7,13},{8,16},{9,17},{1... | collective-permute-start | bytes 884744 | tf_op jit(solution)/shard_map/ppermute | solution.py:128
  137.3 1.3 collective-permute-start.7
  138.6 27.6 %all-gather.4.cloned.1.call-done = bf16[1536,1536]{1,0:T(8,128)(2,1)} async-done(((bf16[48,1536]{1,0:T(8,128)(2,1)}), bf16[1536,1536]{1,0:T(8,128)(2,1)}) %all-gather.4.cloned.1.call-update) | async-done | bytes 4718608 | tf_op jit(solution)/shard_map/all_gather | solution.py:44
  166.2 4.4 %fusion.25 = bf16[1,192,1536]{2,1,0:T(8,128)(2,1)} fusion(bf16[192,1536]{1,0:T(8,128)(2,1)} %reshape.37, bf16[1536,1536]{1,0:T(8,128)(2,1)} %all-gather.4.cloned.1.call-done), kind=kOutput, calls=%fused_computation.19 | convolution fusion | flops 906264576 | bytes 5898240 | tf_op jit(solution)/shard_map/dot_general | solution.py:103
  170.6 0.0 collective-permute-done.6
  170.6 0.0 collective-permute-done.7
  170.6 0.7 add.108
  (11 shorter events, 0.3 us)
Async XLA Ops:
  7.2 4.9 %copy-start.2 = (bf16[1,192,1536]{2,1,0:T(8,128)(2,1)S(1)}, bf16[1,192,1536]{2,1,0:T(8,128)(2,1)}, u32[]{:S(2)}) copy-start(bf16[1,192,1536]{2,1,0:T(8,128)(2,1)} %param.7) | copy-start | bytes 1769476
  7.2 105.9 %all-gather.6.cloned.1.call-start = ((), (), s32[]{:S(2)}) async-start(), calls=%async_computation.3 | async-start | bytes 5308416 | tf_op jit(solution)/shard_map/all_gather | solution.py:45
  16.4 71.2 %all-to-all-start = ((bf16[8,192,576]{2,1,0:T(8,128)(2,1)}), bf16[8,192,576]{2,1,0:T(8,128)(2,1)S(1)}, u32[]{:S(2)}, u32[]{:S(2)}) async-start(bf16[8,192,576]{2,1,0:T(8,128)(2,1)} %pad_maximum_fusion.1), calls=%async_computation | async-start | bytes 3932160 | tf_op jit(solution)/shard_map/all_to_all | solution.py:48
  21.7 144.5 %all-gather.4.cloned.1.call-start = ((), (), s32[]{:S(2)}) async-start(), calls=%async_computation.2 | async-start | bytes 4866048 | tf_op jit(solution)/shard_map/all_gather | solution.py:44
  23.9 43.0 %collective-permute-start = (bf16[2,192,384]{2,1,0:T(8,128)(2,1)S(1)}, bf16[2,192,384]{2,1,0:T(8,128)(2,1)S(1)}, u32[]{:S(2)}, u32[]{:S(2)}) collective-permute-start(bf16[2,192,384]{2,1,0:T(8,128)(2,1)S(1)} %get-tuple-element.44), channel_id=1, source_target_pairs={{0,16},{2,18},{4,20},{6,22},{8,24},{10,26},{12,28},{14,30},{16,0},... | collective-permute-start | bytes 884744 | tf_op jit(solution)/shard_map/ppermute | solution.py:78
  26.2 51.9 %collective-permute-start.1 = (bf16[2,192,384]{2,1,0:T(8,128)(2,1)}, bf16[2,192,384]{2,1,0:T(8,128)(2,1)S(1)}, u32[]{:S(2)}, u32[]{:S(2)}) collective-permute-start(bf16[2,192,384]{2,1,0:T(8,128)(2,1)} %get-tuple-element.47), channel_id=1, source_target_pairs={{0,20},{2,22},{4,24},{6,26},{8,28},{10,30},{12,16},{14,18},{16,4},... | collective-permute-start | bytes 884744 | tf_op jit(solution)/shard_map/ppermute | solution.py:78
  27.4 55.8 %collective-permute-start.2 = (bf16[2,192,384]{2,1,0:T(8,128)(2,1)}, bf16[2,192,384]{2,1,0:T(8,128)(2,1)S(1)}, u32[]{:S(2)}, u32[]{:S(2)}) collective-permute-start(bf16[2,192,384]{2,1,0:T(8,128)(2,1)} %get-tuple-element.46), channel_id=1, source_target_pairs={{0,24},{2,26},{4,28},{6,30},{8,16},{10,18},{12,20},{14,22},{16,8},... | collective-permute-start | bytes 884744 | tf_op jit(solution)/shard_map/ppermute | solution.py:78
  30.6 55.4 %collective-permute-start.3 = (bf16[2,192,384]{2,1,0:T(8,128)(2,1)}, bf16[2,192,384]{2,1,0:T(8,128)(2,1)S(1)}, u32[]{:S(2)}, u32[]{:S(2)}) collective-permute-start(bf16[2,192,384]{2,1,0:T(8,128)(2,1)} %get-tuple-element.45), channel_id=1, source_target_pairs={{0,28},{2,30},{4,16},{6,18},{8,20},{10,22},{12,24},{14,26},{16,12}... | collective-permute-start | bytes 884744 | tf_op jit(solution)/shard_map/ppermute | solution.py:78
  87.0 2.4 %collective-permute-start.4 = (bf16[4,192,384]{2,1,0:T(8,128)(2,1)}, bf16[4,192,384]{2,1,0:T(8,128)(2,1)}, u32[]{:S(2)}, u32[]{:S(2)}) collective-permute-start(bf16[4,192,384]{2,1,0:T(8,128)(2,1)} %pad_maximum_fusion.4), channel_id=1, source_target_pairs={{0,2},{2,0},{4,6},{6,4},{8,10},{10,8},{12,14},{14,12},{16,18},{18,... | collective-permute-start | bytes 1769480 | tf_op jit(solution)/shard_map/ppermute | solution.py:83
  90.7 1.9 %copy-start = (bf16[3,512,192]{1,2,0:T(8,128)(2,1)S(1)}, bf16[3,512,192]{1,2,0:T(8,128)(2,1)}, u32[]{:S(2)}) copy-start(bf16[3,512,192]{1,2,0:T(8,128)(2,1)} %custom-call) | copy-start | bytes 1769476
  93.7 1.4 copy-start.1
  97.8 1.4 copy-start.1
  101.8 1.4 copy-start.1
  105.9 23.7 %all-to-all-start.1 = ((bf16[8,192,192]{2,1,0:T(8,128)(2,1)}), bf16[8,192,192]{2,1,0:T(8,128)(2,1)S(1)}, u32[]{:S(2)}, u32[]{:S(2)}) async-start(bf16[8,192,192]{2,1,0:T(8,128)(2,1)} %bitcast.14), calls=%async_computation.1 | async-start | bytes 1572864 | tf_op jit(solution)/shard_map/all_to_all | solution.py:48
  116.6 15.9 %collective-permute-start.5 = (f32[2,48,1536]{2,1,0:T(8,128)S(1)}, f32[2,48,1536]{2,1,0:T(8,128)}, u32[]{:S(2)}, u32[]{:S(2)}) collective-permute-start(f32[2,48,1536]{2,1,0:T(8,128)S(1)} %dynamic-slice_bitcast_fusion), channel_id=1, source_target_pairs={{0,1},{1,0},{2,3},{3,2},{4,5},{5,4},{6,7},{7,6},{8,9},{9,8},{10,11... | collective-permute-start | bytes 1769480 | tf_op jit(solution)/shard_map/ppermute | solution.py:114
  133.8 36.9 %collective-permute-start.6 = (f32[48,1536]{1,0:T(8,128)S(1)}, f32[48,1536]{1,0:T(8,128)S(1)}, u32[]{:S(2)}, u32[]{:S(2)}) collective-permute-start(f32[48,1536]{1,0:T(8,128)S(1)} %get-tuple-element.49), channel_id=1, source_target_pairs={{0,0},{1,1},{2,4},{3,5},{4,8},{5,9},{6,12},{7,13},{8,16},{9,17},{1... | collective-permute-start | bytes 884744 | tf_op jit(solution)/shard_map/ppermute | solution.py:128
  137.3 33.3 %collective-permute-start.7 = (f32[48,1536]{1,0:T(8,128)S(1)}, f32[48,1536]{1,0:T(8,128)S(1)}, u32[]{:S(2)}, u32[]{:S(2)}) collective-permute-start(f32[48,1536]{1,0:T(8,128)S(1)} %get-tuple-element.48), channel_id=1, source_target_pairs={{0,2},{1,3},{2,6},{3,7},{4,10},{5,11},{6,14},{7,15},{8,18},{9,19},... | collective-permute-start | bytes 884744 | tf_op jit(solution)/shard_map/ppermute | solution.py:128
Sparse Core Ops, SparseCore 0:
  9.6 63.3 all-gather.5
  76.0 90.1 all-gather.3

commit v13 on v11

--- a/solution.py
+++ b/solution.py
@@ -11,7 +11,7 @@
 def attend(query_here, key_all, value_all):
     query_count = query_here.shape[0]
     head_width = query_here.shape[1]
-    block_size = min(512, query_count)
+    block_size = min(768, query_count)
     score_scale = HEAD_DIM ** (-0.5)
 
     def one_block(query_block):

time: 175 us -> 177 us (1.011)
  waiting for transfers between devices: 90.5 us -> 96.1 us
  starting transfers between devices: 27.5 us -> 24.8 us
    ppermute x1, waiting for transfers between devices: 6.91 us -> 16.1 us  [local(): kept = kept + lax.ppermute(sent, 'dp', [(0, 1), (1, 0)])]
    ppermute x2, waiting for transfers between devices: 7.95 us -> 0.01 us  [local(): arrived = lax.ppermute(outgoing, ALL, perm)]
    all_gather x1, waiting for transfers between devices: 0.02 us -> 7.34 us  [local(): w_full = lax.all_gather(w_out, ALL, axis=0, tiled=True)]
    all_to_all x2, waiting for transfers between devices: 52.9 us -> 50.1 us  [a2a(): lax.all_to_all(tensor, 'inner', split_axis=0, concat_axis=0, tiled=True)]
    ppermute x2, starting transfers between devices: 4.61 us -> 1.99 us  [local(): arrived = lax.ppermute(outgoing, ALL, perm)]
    dot_general x3 -> x2, matrix products: 4.41 us -> 4.54 us  [one_block(): mixed = jnp.dot(weights, value_all, preferred_element_type=jnp.float32)]
    unnamed x20 -> x18, local copies, waits for them, and re-layouts: 5.23 us -> 5.23 us
where the time goes in v13:
time: 177 us; the launch traced here: 176 us
  waiting for transfers between devices  96.1 us (54%)
  starting transfers between devices  24.8 us (14%)
  local copies, waits for them, and re-layouts  16 us (9%)
  matrix products  15.3 us (9%)
  between operations  14.4 us (8%)
  other arithmetic  9.31 us (5%)
    all_to_all x2, waiting for transfers between devices, a2a(): lax.all_to_all(tensor, 'inner', split_axis=0, concat_axis=0, tiled=True)  50.1 us
    ppermute x8, waiting for transfers between devices, local(): kv_crossed.append(lax.ppermute(outgoing, ('side', 'inner'), perm))  21.2 us
    ppermute x1, waiting for transfers between devices, local(): kept = kept + lax.ppermute(sent, 'dp', [(0, 1), (1, 0)])  16.1 us
    ppermute x8, starting transfers between devices, local(): kv_crossed.append(lax.ppermute(outgoing, ('side', 'inner'), perm))  12.7 us
    all_to_all x2, starting transfers between devices, a2a(): lax.all_to_all(tensor, 'inner', split_axis=0, concat_axis=0, tiled=True)  8.85 us
    all_gather x1, waiting for transfers between devices, local(): w_full = lax.all_gather(w_out, ALL, axis=0, tiled=True)  7.34 us
    unnamed x18, local copies, waits for them, and re-layouts  5.23 us
    dot_general x2, matrix products, one_block(): mixed = jnp.dot(weights, value_all, preferred_element_type=jnp.float32)  4.54 us
  transfers between devices with their start and end apart: 15, of which 7 were waited for; matrix products, arithmetic and copies ran while one was open for 23% of the time, Pallas kernels for 0%

profile of v13, /device:TPU:1, one launch (start us, length us, event | category | flops | bytes accessed | tf_op | source)
XLA Modules:
  0.0 175.9 jit_solution(9784605138872211775)
XLA Ops:
  7.2 0.0 copy-start.2
  7.2 0.0 all-gather.6.cloned.1.call-start
  7.2 0.7 all-gather.6.cloned.1.call-update
  7.9 1.7 reshape_squeeze.10
  9.7 1.5 reshape_squeeze.11
  11.2 0.6 reshape_squeeze.9
  11.8 0.2 copy.29
  11.9 1.5 copy_bitcast_fusion
  13.4 2.1 %pad_maximum_fusion = bf16[8,192,576]{2,1,0:T(8,128)(2,1)} fusion(bf16[8,192,192]{2,1,0:T(8,128)(2,1)S(1)} %get-tuple-element.54, bf16[8,192,192]{2,1,0:T(8,128)(2,1)S(1)} %get-tuple-element.55, bf16[8,192,192]{2,1,0:T(8,128)(2,1)S(1)} %bitcast.78), kind=kLoop, calls=%fused_computation.20 | loop fusion | flops 5308416 | bytes 3538944 | tf_op jit(solution)/shard_map/concatenate | solution.py:68
  15.5 5.3 %all-to-all-start = ((bf16[8,192,576]{2,1,0:T(8,128)(2,1)}), bf16[8,192,576]{2,1,0:T(8,128)(2,1)S(1)}, u32[]{:S(2)}, u32[]{:S(2)}) async-start(bf16[8,192,576]{2,1,0:T(8,128)(2,1)} %pad_maximum_fusion), calls=%async_computation | async-start | bytes 3932160 | tf_op jit(solution)/shard_map/all_to_all | solution.py:48
  20.8 0.7 all-gather.4.cloned.1.call-update
  21.6 1.2 fusion.41
  22.8 2.3 %collective-permute-start = (bf16[192,384]{1,0:T(8,128)(2,1)}, bf16[192,384]{1,0:T(8,128)(2,1)}, u32[]{:S(2)}, u32[]{:S(2)}) collective-permute-start(bf16[192,384]{1,0:T(8,128)(2,1)} %get-tuple-element.45), channel_id=1, source_target_pairs={{0,16},{2,18},{4,20},{6,22},{8,24},{10,26},{12,28},{14,30},{16,0},... | collective-permute-start | bytes 442376 | tf_op jit(solution)/shard_map/ppermute | solution.py:67
  25.1 1.7 collective-permute-start.1
  26.8 2.3 %collective-permute-start.2 = (bf16[192,384]{1,0:T(8,128)(2,1)}, bf16[192,384]{1,0:T(8,128)(2,1)}, u32[]{:S(2)}, u32[]{:S(2)}) collective-permute-start(bf16[192,384]{1,0:T(8,128)(2,1)} %get-tuple-element.47), channel_id=1, source_target_pairs={{0,20},{2,22},{4,24},{6,26},{8,28},{10,30},{12,16},{14,18},{16,4},... | collective-permute-start | bytes 442376 | tf_op jit(solution)/shard_map/ppermute | solution.py:67
  29.1 1.2 collective-permute-start.3
  30.3 2.1 %collective-permute-start.4 = (bf16[192,384]{1,0:T(8,128)(2,1)}, bf16[192,384]{1,0:T(8,128)(2,1)}, u32[]{:S(2)}, u32[]{:S(2)}) collective-permute-start(bf16[192,384]{1,0:T(8,128)(2,1)} %get-tuple-element.49), channel_id=1, source_target_pairs={{0,24},{2,26},{4,28},{6,30},{8,16},{10,18},{12,20},{14,22},{16,8},... | collective-permute-start | bytes 442376 | tf_op jit(solution)/shard_map/ppermute | solution.py:67
  32.4 0.8 fusion.34
  33.3 40.3 %all-to-all-done = bf16[8,192,576]{2,1,0:T(8,128)(2,1)S(1)} async-done(((bf16[8,192,576]{2,1,0:T(8,128)(2,1)}), bf16[8,192,576]{2,1,0:T(8,128)(2,1)S(1)}, u32[]{:S(2)}, u32[]{:S(2)}) %all-to-all-start) | async-done | bytes 1769504 | tf_op jit(solution)/shard_map/all_to_all | solution.py:48
  73.6 0.5 slice_dynamic-update-slice_fusion
  74.0 0.0 collective-permute-done
  74.1 0.1 collective-permute-start.5
  74.1 0.9 constant_dynamic-update-slice_fusion.7
  75.1 0.0 collective-permute-done.1
  75.1 2.8 %collective-permute-start.6 = (bf16[192,384]{1,0:T(8,128)(2,1)S(1)}, bf16[192,384]{1,0:T(8,128)(2,1)S(1)}, u32[]{:S(2)}, u32[]{:S(2)}) collective-permute-start(bf16[192,384]{1,0:T(8,128)(2,1)S(1)} %copy-done.4), channel_id=1, source_target_pairs={{0,28},{2,30},{4,16},{6,18},{8,20},{10,22},{12,24},{14,26},{16,12}... | collective-permute-start | bytes 442376 | tf_op jit(solution)/shard_map/ppermute | solution.py:67
  77.9 0.9 constant_dynamic-update-slice_fusion.6
  78.8 0.0 collective-permute-done.2
  78.8 0.2 collective-permute-start.7
  79.1 0.9 constant_dynamic-update-slice_fusion.5
  80.0 0.0 collective-permute-done.3
  80.0 0.9 constant_dynamic-update-slice_fusion.4
  80.9 0.0 collective-permute-done.4
  81.0 0.9 constant_dynamic-update-slice_fusion.3
  81.9 8.7 %collective-permute-done.5 = bf16[192,384]{1,0:T(8,128)(2,1)S(1)} collective-permute-done((bf16[192,384]{1,0:T(8,128)(2,1)S(1)}, bf16[192,384]{1,0:T(8,128)(2,1)S(1)}, u32[]{:S(2)}, u32[]{:S(2)}) %collective-permute-start.5) | collective-permute-done | bytes 147488 | tf_op jit(solution)/shard_map/ppermute | solution.py:67
  90.7 0.1 slice.16
  90.7 9.5 %collective-permute-done.6 = bf16[192,384]{1,0:T(8,128)(2,1)S(1)} collective-permute-done((bf16[192,384]{1,0:T(8,128)(2,1)S(1)}, bf16[192,384]{1,0:T(8,128)(2,1)S(1)}, u32[]{:S(2)}, u32[]{:S(2)}) %collective-permute-start.6) | collective-permute-done | bytes 147488 | tf_op jit(solution)/shard_map/ppermute | solution.py:67
  100.3 2.9 %collective-permute-done.7 = bf16[192,384]{1,0:T(8,128)(2,1)S(1)} collective-permute-done((bf16[192,384]{1,0:T(8,128)(2,1)}, bf16[192,384]{1,0:T(8,128)(2,1)S(1)}, u32[]{:S(2)}, u32[]{:S(2)}) %collective-permute-start.7) | collective-permute-done | bytes 147488 | tf_op jit(solution)/shard_map/ppermute | solution.py:67
  103.2 0.0 copy-start
  103.2 1.9 %fusion.42 = (bf16[3072,192]{1,0:T(8,128)(2,1)}, bf16[3072,192]{1,0:T(8,128)(2,1)S(1)}) fusion(bf16[3072,384]{1,0:T(8,128)(2,1)S(1)} %constant_dynamic-update-slice_fusion), kind=kLoop, calls=%fused_computation.69 | loop fusion | bytes 4718592 | tf_op jit(solution)/shard_map/slice | solution.py:73
  105.1 10.9 %while.10 = (s32[]{:T(128)}, bf16[2,768,192]{1,2,0:T(8,128)(2,1)S(1)}, bf16[2,768,192]{2,1,0:T(8,128)(2,1)S(1)}, bf16[3072,192]{1,0:T(8,128)(2,1)S(1)}, bf16[3072,192]{1,0:T(8,128)(2,1)}, /*index=5*/s32[]{:T(128)}) while((s32[]{:T(128)}, bf16[2,768,192]{1,2,0:T(8,128)(2,1)S(1)}, bf16[2,768,192]{2,1,0:T(8,128)(2,1)S(1)}, ...), condition=%wide.region_3.4_spmd, body=%wide.region_0.3_spmd.sunk | while | flops 1831107072 | bytes 36881512 | solution.py:26
  105.1 1.5 multiply_reduce_fusion.2
  106.7 1.7 fusion.56
  108.3 2.3 %fusion.57 = bf16[2,768,192]{1,2,0:T(8,128)(2,1)S(1)} fusion(bf16[2,768,192]{1,2,0:T(8,128)(2,1)S(1)} %get-tuple-element.98, s32[]{:T(128)} %get-tuple-element.97, bf16[3072,192]{1,0:T(8,128)(2,1)S(1)} %copy-done.1, f32[768,3072]{1,0:T(8,128)S(1)} %get-tuple-element.89, f32[768]{0:T(1024)S(1)} %get-tuple-element.90, f32[768]{0:T(1024)S(1)} %fusion.56), kind=kOutput, calls=%fused_computation.10.clone.1 | convolution fusion | flops 913342464 | bytes 11313156 | tf_op jit(solution)/shard_map/while/body/eval_jaxpr/dot_general | solution.py:23
  110.6 1.5 multiply_reduce_fusion.2
  112.1 1.7 fusion.56
  113.8 2.3 %fusion.57 = bf16[2,768,192]{1,2,0:T(8,128)(2,1)S(1)} fusion(bf16[2,768,192]{1,2,0:T(8,128)(2,1)S(1)} %get-tuple-element.98, s32[]{:T(128)} %get-tuple-element.97, bf16[3072,192]{1,0:T(8,128)(2,1)S(1)} %copy-done.1, f32[768,3072]{1,0:T(8,128)S(1)} %get-tuple-element.89, f32[768]{0:T(1024)S(1)} %get-tuple-element.90, f32[768]{0:T(1024)S(1)} %fusion.56), kind=kOutput, calls=%fused_computation.10.clone.1 | convolution fusion | flops 913342464 | bytes 11313156 | tf_op jit(solution)/shard_map/while/body/eval_jaxpr/dot_general | solution.py:23
  116.1 0.0 all-gather.6.cloned.1.call-done
  116.2 3.4 %fusion.23 = f32[2,2,48,1536]{3,2,1,0:T(8,128)S(1)} fusion(bf16[2,2,48,1536]{3,2,1,0:T(8,128)(2,1)S(1)} %bitcast.79, bf16[1,1536,1536]{2,1,0:T(8,128)(2,1)} %all-gather.6.cloned.1.call-done), kind=kOutput, calls=%fused_computation.16 | convolution fusion | flops 905969664 | bytes 6488064 | tf_op jit(solution)/shard_map/dot_general | solution.py:77
  119.6 0.9 dynamic-slice_bitcast_fusion
  120.5 1.2 collective-permute-start.8
  121.7 0.6 copy.19
  122.3 0.7 reshape_reshape.3
  123.0 1.1 copy.20
  124.1 3.5 %all-to-all-start.1 = ((bf16[8,192,192]{1,2,0:T(8,128)(2,1)}), bf16[8,192,192]{1,2,0:T(8,128)(2,1)S(1)}, u32[]{:S(2)}, u32[]{:S(2)}) async-start(bf16[8,192,192]{1,2,0:T(8,128)(2,1)} %copy.20), calls=%async_computation.1 | async-start | bytes 1572864 | tf_op jit(solution)/shard_map/all_to_all | solution.py:48
  127.7 16.1 %collective-permute-done.8 = f32[2,48,1536]{2,1,0:T(8,128)} collective-permute-done((f32[2,48,1536]{2,1,0:T(8,128)}, f32[2,48,1536]{2,1,0:T(8,128)}, u32[]{:S(2)}, u32[]{:S(2)}) %collective-permute-start.8) | collective-permute-done | bytes 589856 | tf_op jit(solution)/shard_map/ppermute | solution.py:94
  143.7 1.1 bitcast_add_fusion
  144.9 0.1 collective-permute-start.10
  145.0 1.9 %collective-permute-start.9 = (f32[48,1536]{1,0:T(8,128)S(1)}, f32[48,1536]{1,0:T(8,128)S(1)}, u32[]{:S(2)}, u32[]{:S(2)}) collective-permute-start(f32[48,1536]{1,0:T(8,128)S(1)} %get-tuple-element.53), channel_id=1, source_target_pairs={{0,0},{1,1},{2,4},{3,5},{4,8},{5,9},{6,12},{7,13},{8,16},{9,17},{1... | collective-permute-start | bytes 884744 | tf_op jit(solution)/shard_map/ppermute | solution.py:108
  146.9 9.8 %all-to-all-done.1 = bf16[8,192,192]{1,2,0:T(8,128)(2,1)S(1)} async-done(((bf16[8,192,192]{1,2,0:T(8,128)(2,1)}), bf16[8,192,192]{1,2,0:T(8,128)(2,1)S(1)}, u32[]{:S(2)}, u32[]{:S(2)}) %all-to-all-start.1) | async-done | bytes 589856 | tf_op jit(solution)/shard_map/all_to_all | solution.py:48
  156.7 7.3 %all-gather.4.cloned.1.call-done = bf16[1536,1536]{1,0:T(8,128)(2,1)} async-done(((bf16[48,1536]{1,0:T(8,128)(2,1)}), bf16[1536,1536]{1,0:T(8,128)(2,1)}) %all-gather.4.cloned.1.call-update) | async-done | bytes 4718608 | tf_op jit(solution)/shard_map/all_gather | solution.py:44
  164.0 4.3 %fusion.25 = bf16[1,192,1536]{2,1,0:T(8,128)(2,1)} fusion(bf16[192,1536]{0,1:T(8,128)(2,1)S(1)} %bitcast.81, bf16[1536,1536]{1,0:T(8,128)(2,1)} %all-gather.4.cloned.1.call-done), kind=kOutput, calls=%fused_computation.19 | convolution fusion | flops 906264576 | bytes 5898240 | tf_op jit(solution)/shard_map/dot_general | solution.py:83
  168.3 0.0 collective-permute-done.10
  168.3 0.0 collective-permute-done.9
  168.3 0.7 add.135
  (19 shorter events, 0.2 us)
Async XLA Ops:
  7.2 2.5 %copy-start.2 = (bf16[1,192,1536]{2,1,0:T(8,128)(2,1)S(1)}, bf16[1,192,1536]{2,1,0:T(8,128)(2,1)}, u32[]{:S(2)}) copy-start(bf16[1,192,1536]{2,1,0:T(8,128)(2,1)} %param.9) | copy-start | bytes 1769476
  7.2 4.0 %copy-start.3 = (bf16[1,192,1536]{2,1,0:T(8,128)(2,1)S(1)}, bf16[1,192,1536]{2,1,0:T(8,128)(2,1)}, u32[]{:S(2)}) copy-start(bf16[1,192,1536]{2,1,0:T(8,128)(2,1)} %param.7) | copy-start | bytes 1769476
  7.2 109.0 %all-gather.6.cloned.1.call-start = ((), (), s32[]{:S(2)}) async-start(), calls=%async_computation.3 | async-start | bytes 5308416 | tf_op jit(solution)/shard_map/all_gather | solution.py:45
  15.5 58.1 %all-to-all-start = ((bf16[8,192,576]{2,1,0:T(8,128)(2,1)}), bf16[8,192,576]{2,1,0:T(8,128)(2,1)S(1)}, u32[]{:S(2)}, u32[]{:S(2)}) async-start(bf16[8,192,576]{2,1,0:T(8,128)(2,1)} %pad_maximum_fusion), calls=%async_computation | async-start | bytes 3932160 | tf_op jit(solution)/shard_map/all_to_all | solution.py:48
  20.8 143.2 %all-gather.4.cloned.1.call-start = ((), (), s32[]{:S(2)}) async-start(), calls=%async_computation.2 | async-start | bytes 4866048 | tf_op jit(solution)/shard_map/all_gather | solution.py:44
  22.8 51.2 %collective-permute-start = (bf16[192,384]{1,0:T(8,128)(2,1)}, bf16[192,384]{1,0:T(8,128)(2,1)}, u32[]{:S(2)}, u32[]{:S(2)}) collective-permute-start(bf16[192,384]{1,0:T(8,128)(2,1)} %get-tuple-element.45), channel_id=1, source_target_pairs={{0,16},{2,18},{4,20},{6,22},{8,24},{10,26},{12,28},{14,30},{16,0},... | collective-permute-start | bytes 442376 | tf_op jit(solution)/shard_map/ppermute | solution.py:67
  25.1 49.9 %collective-permute-start.1 = (bf16[192,384]{1,0:T(8,128)(2,1)}, bf16[192,384]{1,0:T(8,128)(2,1)}, u32[]{:S(2)}, u32[]{:S(2)}) collective-permute-start(bf16[192,384]{1,0:T(8,128)(2,1)} %get-tuple-element.46), channel_id=1, source_target_pairs={{0,18},{2,20},{4,22},{6,24},{8,26},{10,28},{12,30},{14,16},{16,2},... | collective-permute-start | bytes 442376 | tf_op jit(solution)/shard_map/ppermute | solution.py:67
  26.8 52.0 %collective-permute-start.2 = (bf16[192,384]{1,0:T(8,128)(2,1)}, bf16[192,384]{1,0:T(8,128)(2,1)}, u32[]{:S(2)}, u32[]{:S(2)}) collective-permute-start(bf16[192,384]{1,0:T(8,128)(2,1)} %get-tuple-element.47), channel_id=1, source_target_pairs={{0,20},{2,22},{4,24},{6,26},{8,28},{10,30},{12,16},{14,18},{16,4},... | collective-permute-start | bytes 442376 | tf_op jit(solution)/shard_map/ppermute | solution.py:67
  29.1 50.9 %collective-permute-start.3 = (bf16[192,384]{1,0:T(8,128)(2,1)}, bf16[192,384]{1,0:T(8,128)(2,1)}, u32[]{:S(2)}, u32[]{:S(2)}) collective-permute-start(bf16[192,384]{1,0:T(8,128)(2,1)} %get-tuple-element.48), channel_id=1, source_target_pairs={{0,22},{2,24},{4,26},{6,28},{8,30},{10,16},{12,18},{14,20},{16,6},... | collective-permute-start | bytes 442376 | tf_op jit(solution)/shard_map/ppermute | solution.py:67
  30.3 50.6 %collective-permute-start.4 = (bf16[192,384]{1,0:T(8,128)(2,1)}, bf16[192,384]{1,0:T(8,128)(2,1)}, u32[]{:S(2)}, u32[]{:S(2)}) collective-permute-start(bf16[192,384]{1,0:T(8,128)(2,1)} %get-tuple-element.49), channel_id=1, source_target_pairs={{0,24},{2,26},{4,28},{6,30},{8,16},{10,18},{12,20},{14,22},{16,8},... | collective-permute-start | bytes 442376 | tf_op jit(solution)/shard_map/ppermute | solution.py:67
  33.3 40.8 %copy-start.5 = (bf16[192,384]{1,0:T(8,128)(2,1)S(1)}, bf16[192,384]{1,0:T(8,128)(2,1)}, u32[]{:S(2)}) copy-start(bf16[192,384]{1,0:T(8,128)(2,1)} %get-tuple-element.51) | copy-start | bytes 442372
  33.3 41.8 %copy-start.4 = (bf16[192,384]{1,0:T(8,128)(2,1)S(1)}, bf16[192,384]{1,0:T(8,128)(2,1)}, u32[]{:S(2)}) copy-start(bf16[192,384]{1,0:T(8,128)(2,1)} %get-tuple-element.50) | copy-start | bytes 442372
  74.1 16.6 %collective-permute-start.5 = (bf16[192,384]{1,0:T(8,128)(2,1)S(1)}, bf16[192,384]{1,0:T(8,128)(2,1)S(1)}, u32[]{:S(2)}, u32[]{:S(2)}) collective-permute-start(bf16[192,384]{1,0:T(8,128)(2,1)S(1)} %copy-done.5), channel_id=1, source_target_pairs={{0,26},{2,28},{4,30},{6,16},{8,18},{10,20},{12,22},{14,24},{16,10}... | collective-permute-start | bytes 442376 | tf_op jit(solution)/shard_map/ppermute | solution.py:67
  75.1 25.2 %collective-permute-start.6 = (bf16[192,384]{1,0:T(8,128)(2,1)S(1)}, bf16[192,384]{1,0:T(8,128)(2,1)S(1)}, u32[]{:S(2)}, u32[]{:S(2)}) collective-permute-start(bf16[192,384]{1,0:T(8,128)(2,1)S(1)} %copy-done.4), channel_id=1, source_target_pairs={{0,28},{2,30},{4,16},{6,18},{8,20},{10,22},{12,24},{14,26},{16,12}... | collective-permute-start | bytes 442376 | tf_op jit(solution)/shard_map/ppermute | solution.py:67
  78.8 24.4 %collective-permute-start.7 = (bf16[192,384]{1,0:T(8,128)(2,1)}, bf16[192,384]{1,0:T(8,128)(2,1)S(1)}, u32[]{:S(2)}, u32[]{:S(2)}) collective-permute-start(bf16[192,384]{1,0:T(8,128)(2,1)} %get-tuple-element.44), channel_id=1, source_target_pairs={{0,30},{2,16},{4,18},{6,20},{8,22},{10,24},{12,26},{14,28},{16,14}... | collective-permute-start | bytes 442376 | tf_op jit(solution)/shard_map/ppermute | solution.py:67
  103.2 1.9 %copy-start = (bf16[2,768,192]{1,2,0:T(8,128)(2,1)S(1)}, bf16[2,768,192]{1,2,0:T(8,128)(2,1)}, u32[]{:S(2)}) copy-start(bf16[2,768,192]{1,2,0:T(8,128)(2,1)} %custom-call.1) | copy-start | bytes 1769476
  106.6 1.7 copy-start.1
  112.1 1.7 copy-start.1
  120.5 23.3 %collective-permute-start.8 = (f32[2,48,1536]{2,1,0:T(8,128)}, f32[2,48,1536]{2,1,0:T(8,128)}, u32[]{:S(2)}, u32[]{:S(2)}) collective-permute-start(f32[2,48,1536]{2,1,0:T(8,128)} %dynamic-slice_bitcast_fusion), channel_id=1, source_target_pairs={{0,1},{1,0},{2,3},{3,2},{4,5},{5,4},{6,7},{7,6},{8,9},{9,8},{10,11... | collective-permute-start | bytes 1769480 | tf_op jit(solution)/shard_map/ppermute | solution.py:94
  124.1 32.6 %all-to-all-start.1 = ((bf16[8,192,192]{1,2,0:T(8,128)(2,1)}), bf16[8,192,192]{1,2,0:T(8,128)(2,1)S(1)}, u32[]{:S(2)}, u32[]{:S(2)}) async-start(bf16[8,192,192]{1,2,0:T(8,128)(2,1)} %copy.20), calls=%async_computation.1 | async-start | bytes 1572864 | tf_op jit(solution)/shard_map/all_to_all | solution.py:48
  144.9 23.4 %collective-permute-start.10 = (f32[48,1536]{1,0:T(8,128)S(1)}, f32[48,1536]{1,0:T(8,128)S(1)}, u32[]{:S(2)}, u32[]{:S(2)}) collective-permute-start(f32[48,1536]{1,0:T(8,128)S(1)} %get-tuple-element.52), channel_id=1, source_target_pairs={{0,2},{1,3},{2,6},{3,7},{4,10},{5,11},{6,14},{7,15},{8,18},{9,19},... | collective-permute-start | bytes 884744 | tf_op jit(solution)/shard_map/ppermute | solution.py:108
  145.0 23.3 %collective-permute-start.9 = (f32[48,1536]{1,0:T(8,128)S(1)}, f32[48,1536]{1,0:T(8,128)S(1)}, u32[]{:S(2)}, u32[]{:S(2)}) collective-permute-start(f32[48,1536]{1,0:T(8,128)S(1)} %get-tuple-element.53), channel_id=1, source_target_pairs={{0,0},{1,1},{2,4},{3,5},{4,8},{5,9},{6,12},{7,13},{8,16},{9,17},{1... | collective-permute-start | bytes 884744 | tf_op jit(solution)/shard_map/ppermute | solution.py:108
Sparse Core Ops, SparseCore 0:
  9.7 62.8 all-gather.5
  75.5 88.4 all-gather.3

commit v14 on v11

--- a/solution.py
+++ b/solution.py
@@ -29,7 +29,9 @@
     return blocks.reshape(query_count, head_width)
 
 
-ALL = ("side", "inner", "dp")
+ALL = ("side", "chip", "core", "dp")
+INNER = ("chip", "core")
+SEQ = ("side", "chip", "core")
 
 
 def local(queries, key_vectors, value_vectors, w_out, cotangent):
@@ -41,18 +43,29 @@
     width = queries.shape[2]
 
     dp_index = lax.axis_index("dp")
+    chip_count = lax.axis_size("chip")
+    core_count = lax.axis_size("core")
+    core_index = lax.axis_index("core")
     w_full = lax.all_gather(w_out, ALL, axis=0, tiled=True)
-    cot_side = lax.all_gather(cotangent[0], "inner", axis=0, tiled=True)
+    cot_core = lax.all_gather(cotangent[0], "chip", axis=0, tiled=True)
+    cot_other = lax.ppermute(cot_core, "core", [(0, 1), (1, 0)])
+    cot_side = jnp.concatenate(
+        [
+            jnp.where(core_index == 0, cot_core, cot_other),
+            jnp.where(core_index == 0, cot_other, cot_core),
+        ],
+        axis=0,
+    )
 
     def a2a(tensor):
-        return lax.all_to_all(tensor, "inner", split_axis=0, concat_axis=0, tiled=True)
+        return lax.all_to_all(tensor, INNER, split_axis=0, concat_axis=0, tiled=True)
 
     def by_head(tensor):
         return tensor[0].reshape(row_count, head_count, head_width).transpose(1, 0, 2)
 
     side_index = lax.axis_index("side")
     kv_raw = jnp.concatenate([by_head(key_vectors), by_head(value_vectors)], axis=2)
-    inner_index = lax.axis_index("inner")
+    inner_index = lax.axis_index("chip") * core_count + core_index
     kv_crossed = []
     for step in range(1, side_count):
         for shift in range(head_count):
@@ -64,7 +77,7 @@
             outgoing = lax.dynamic_index_in_dim(
                 kv_raw, (inner_index + shift) % head_count, axis=0, keepdims=False
             )
-            kv_crossed.append(lax.ppermute(outgoing, ("side", "inner"), perm))
+            kv_crossed.append(lax.ppermute(outgoing, SEQ, perm))
     stacked = jnp.concatenate([by_head(queries), kv_raw], axis=2)
     got = a2a(stacked).reshape(head_count * row_count, 3 * head_width)
     query_here = got[:, :head_width]
@@ -74,8 +87,13 @@
 
     attended_here = attend(query_here, key_all, value_all)
 
+    attended_rows = (
+        attended_here.reshape(chip_count, core_count, row_count, head_width)
+        .transpose(1, 0, 2, 3)
+        .reshape(core_count * chip_count * row_count, head_width)
+    )
     partial = lax.dot_general(
-        attended_here, cot_side, (((0,), (0,)), ((), ())), preferred_element_type=jnp.float32
+        attended_rows, cot_side, (((0,), (0,)), ((), ())), preferred_element_type=jnp.float32
     )
 
     returned = a2a(attended_here.reshape(head_count, row_count, head_width))
@@ -131,10 +149,8 @@
 def solution(mesh):
     seq_count = mesh.shape["seq"]
     dp_count = mesh.shape["dp"]
-    fine = Mesh(
-        mesh.devices.reshape(seq_count // HEADS, HEADS, dp_count), ("side", "inner", "dp")
-    )
-    seq = ("side", "inner")
+    fine = Mesh(mesh.devices.reshape(seq_count // HEADS, HEADS // 2, 2, dp_count), ALL)
+    seq = SEQ
     placed = (
         P("dp", seq, None),
         P("dp", seq, None),

time: 175 us -> 186 us (1.063)
  starting transfers between devices: 27.5 us -> 33.8 us
  waiting for transfers between devices: 90.5 us -> 93.9 us
  local copies, waits for them, and re-layouts: 16.8 us -> 19.2 us
  matrix products: 15.4 us -> 13.3 us
    all_to_all x2, waiting for transfers between devices: 52.9 us -> 40.4 us  [a2a(): lax.all_to_all(tensor, INNER, split_axis=0, concat_axis=0, tiled=True)]
    all_gather x1, waiting for transfers between devices: 0.02 us -> 10 us  [local(): w_full = lax.all_gather(w_out, ALL, axis=0, tiled=True)]
    ppermute x2, waiting for transfers between devices: 7.95 us -> 16.8 us  [local(): arrived = lax.ppermute(outgoing, ALL, perm)]
    ppermute x8 -> x9, waiting for transfers between devices: 21.4 us -> 13.2 us  [the longest x8 13.2 us: local(): kv_crossed.append(lax.ppermute(outgoing, SEQ, perm))]
    ppermute x8 -> x9, starting transfers between devices: 12.5 us -> 18.6 us  [the longest x8 18.6 us: local(): kv_crossed.append(lax.ppermute(outgoing, SEQ, perm))]
    ppermute x1, waiting for transfers between devices: 6.91 us -> 12.8 us  [local(): kept = kept + lax.ppermute(sent, 'dp', [(0, 1), (1, 0)])]
    dot_general x1, matrix products: 3.41 us -> 1.32 us  [local(): lax.dot_general(attended_rows, cot_side, (((0,), (0,)), ((), ())), prefer...]
    select_n x0 -> x1, other arithmetic: none -> 2.03 us  [local(): jnp.where(core_index == 0, cot_core, cot_other)]
  transfers between devices with their start and end apart: 15 -> 16, of which waited for: 7 -> 7; matrix products, arithmetic and copies ran while one was open for 23% -> 21% of each run, Pallas kernels for 0% -> 0%
where the time goes in v14:
time: 186 us; the launch traced here: 185 us
  waiting for transfers between devices  93.9 us (50%)
  starting transfers between devices  33.8 us (18%)
  local copies, waits for them, and re-layouts  19.2 us (10%)
  between operations  14.4 us (8%)
  matrix products  13.3 us (7%)
  other arithmetic  10.6 us (6%)
    all_to_all x2, waiting for transfers between devices, a2a(): lax.all_to_all(tensor, INNER, split_axis=0, concat_axis=0, tiled=True)  40.4 us
    ppermute x8, starting transfers between devices, local(): kv_crossed.append(lax.ppermute(outgoing, SEQ, perm))  18.6 us
    ppermute x2, waiting for transfers between devices, local(): arrived = lax.ppermute(outgoing, ALL, perm)  16.8 us
    ppermute x8, waiting for transfers between devices, local(): kv_crossed.append(lax.ppermute(outgoing, SEQ, perm))  13.2 us
    ppermute x1, waiting for transfers between devices, local(): kept = kept + lax.ppermute(sent, 'dp', [(0, 1), (1, 0)])  12.8 us
    all_gather x1, waiting for transfers between devices, local(): w_full = lax.all_gather(w_out, ALL, axis=0, tiled=True)  10 us
    all_to_all x2, starting transfers between devices, a2a(): lax.all_to_all(tensor, INNER, split_axis=0, concat_axis=0, tiled=True)  9.54 us
    unnamed x22, local copies, waits for them, and re-layouts  5.23 us
  transfers between devices with their start and end apart: 16, of which 7 were waited for; matrix products, arithmetic and copies ran while one was open for 21% of the time, Pallas kernels for 0%

profile of v14, /device:TPU:1, one launch (start us, length us, event | category | flops | bytes accessed | tf_op | source)
XLA Modules:
  0.0 185.3 jit_solution(7176831501874379387)
XLA Ops:
  7.2 0.0 all-gather.6.cloned.1.call-start
  7.2 0.7 all-gather.6.cloned.1.call-update
  7.9 1.7 reshape_squeeze.10
  9.7 1.5 reshape_squeeze.11
  11.2 0.6 reshape_squeeze.9
  11.8 0.2 copy.27
  11.9 1.5 copy_bitcast_fusion
  13.4 2.1 %pad_maximum_fusion = bf16[8,192,576]{2,1,0:T(8,128)(2,1)} fusion(bf16[8,192,192]{2,1,0:T(8,128)(2,1)S(1)} %get-tuple-element.56, bf16[8,192,192]{2,1,0:T(8,128)(2,1)S(1)} %get-tuple-element.57, bf16[8,192,192]{2,1,0:T(8,128)(2,1)S(1)} %bitcast.79), kind=kLoop, calls=%fused_computation.24 | loop fusion | flops 5308416 | bytes 3538944 | tf_op jit(solution)/shard_map/concatenate | solution.py:81
  15.6 5.3 %all-to-all-start = ((bf16[8,192,576]{2,1,0:T(8,128)(2,1)}), bf16[8,192,576]{2,1,0:T(8,128)(2,1)S(1)}, u32[]{:S(2)}, u32[]{:S(2)}) async-start(bf16[8,192,576]{2,1,0:T(8,128)(2,1)} %pad_maximum_fusion), calls=%async_computation | async-start | bytes 3932160 | tf_op jit(solution)/shard_map/all_to_all | solution.py:61
  20.9 1.2 fusion.42
  22.1 2.3 %collective-permute-start = (bf16[192,384]{1,0:T(8,128)(2,1)}, bf16[192,384]{1,0:T(8,128)(2,1)}, u32[]{:S(2)}, u32[]{:S(2)}) collective-permute-start(bf16[192,384]{1,0:T(8,128)(2,1)} %get-tuple-element.47), channel_id=1, source_target_pairs={{0,16},{2,18},{4,20},{6,22},{8,24},{10,26},{12,28},{14,30},{16,0},... | collective-permute-start | bytes 442376 | tf_op jit(solution)/shard_map/ppermute | solution.py:80
  24.4 1.7 collective-permute-start.1
  26.1 2.3 %collective-permute-start.2 = (bf16[192,384]{1,0:T(8,128)(2,1)}, bf16[192,384]{1,0:T(8,128)(2,1)}, u32[]{:S(2)}, u32[]{:S(2)}) collective-permute-start(bf16[192,384]{1,0:T(8,128)(2,1)} %get-tuple-element.49), channel_id=1, source_target_pairs={{0,20},{2,22},{4,24},{6,26},{8,28},{10,30},{12,16},{14,18},{16,4},... | collective-permute-start | bytes 442376 | tf_op jit(solution)/shard_map/ppermute | solution.py:80
  28.4 1.2 collective-permute-start.3
  29.6 2.1 %collective-permute-start.4 = (bf16[192,384]{1,0:T(8,128)(2,1)}, bf16[192,384]{1,0:T(8,128)(2,1)}, u32[]{:S(2)}, u32[]{:S(2)}) collective-permute-start(bf16[192,384]{1,0:T(8,128)(2,1)} %get-tuple-element.51), channel_id=1, source_target_pairs={{0,24},{2,26},{4,28},{6,30},{8,16},{10,18},{12,20},{14,22},{16,8},... | collective-permute-start | bytes 442376 | tf_op jit(solution)/shard_map/ppermute | solution.py:80
  31.7 0.0 all-gather.4.cloned.1.call-update
  31.8 0.9 fusion.35
  32.7 40.4 %all-to-all-done = bf16[8,192,576]{2,1,0:T(8,128)(2,1)S(1)} async-done(((bf16[8,192,576]{2,1,0:T(8,128)(2,1)}), bf16[8,192,576]{2,1,0:T(8,128)(2,1)S(1)}, u32[]{:S(2)}, u32[]{:S(2)}) %all-to-all-start) | async-done | bytes 1769504 | tf_op jit(solution)/shard_map/all_to_all | solution.py:61
  73.0 0.5 slice_dynamic-update-slice_fusion
  73.5 0.0 collective-permute-done
  73.5 5.1 %collective-permute-start.5 = (bf16[192,384]{1,0:T(8,128)(2,1)S(1)}, bf16[192,384]{1,0:T(8,128)(2,1)S(1)}, u32[]{:S(2)}, u32[]{:S(2)}) collective-permute-start(bf16[192,384]{1,0:T(8,128)(2,1)S(1)} %copy-done.7), channel_id=1, source_target_pairs={{0,26},{2,28},{4,30},{6,16},{8,18},{10,20},{12,22},{14,24},{16,10}... | collective-permute-start | bytes 442376 | tf_op jit(solution)/shard_map/ppermute | solution.py:80
  78.7 0.9 constant_dynamic-update-slice_fusion.7
  79.6 3.7 %collective-permute-start.6 = (bf16[192,384]{1,0:T(8,128)(2,1)S(1)}, bf16[192,384]{1,0:T(8,128)(2,1)S(1)}, u32[]{:S(2)}, u32[]{:S(2)}) collective-permute-start(bf16[192,384]{1,0:T(8,128)(2,1)S(1)} %copy-done.6), channel_id=1, source_target_pairs={{0,28},{2,30},{4,16},{6,18},{8,20},{10,22},{12,24},{14,26},{16,12}... | collective-permute-start | bytes 442376 | tf_op jit(solution)/shard_map/ppermute | solution.py:80
  83.3 0.9 constant_dynamic-update-slice_fusion.6
  84.2 0.2 collective-permute-start.7
  84.5 0.9 constant_dynamic-update-slice_fusion.5
  85.4 0.9 constant_dynamic-update-slice_fusion.4
  86.4 0.9 constant_dynamic-update-slice_fusion.3
  87.4 0.1 slice.16
  87.4 9.8 %collective-permute-done.6 = bf16[192,384]{1,0:T(8,128)(2,1)S(1)} collective-permute-done((bf16[192,384]{1,0:T(8,128)(2,1)S(1)}, bf16[192,384]{1,0:T(8,128)(2,1)S(1)}, u32[]{:S(2)}, u32[]{:S(2)}) %collective-permute-start.6) | collective-permute-done | bytes 147488 | tf_op jit(solution)/shard_map/ppermute | solution.py:80
  97.3 3.4 %collective-permute-done.7 = bf16[192,384]{1,0:T(8,128)(2,1)S(1)} collective-permute-done((bf16[192,384]{1,0:T(8,128)(2,1)}, bf16[192,384]{1,0:T(8,128)(2,1)S(1)}, u32[]{:S(2)}, u32[]{:S(2)}) %collective-permute-start.7) | collective-permute-done | bytes 147488 | tf_op jit(solution)/shard_map/ppermute | solution.py:80
  100.7 0.0 copy-start.4
  100.7 1.9 %fusion.44 = (bf16[3072,192]{1,0:T(8,128)(2,1)}, bf16[3072,192]{1,0:T(8,128)(2,1)S(1)}) fusion(bf16[3072,384]{1,0:T(8,128)(2,1)S(1)} %constant_dynamic-update-slice_fusion), kind=kLoop, calls=%fused_computation.74 | loop fusion | bytes 4718592 | tf_op jit(solution)/shard_map/slice | solution.py:86
  102.6 12.1 %while.10 = (s32[]{:T(128)}, bf16[3,512,192]{1,2,0:T(8,128)(2,1)S(1)}, bf16[3,512,192]{2,1,0:T(8,128)(2,1)S(1)}, bf16[3072,192]{1,0:T(8,128)(2,1)S(1)}, bf16[3072,192]{1,0:T(8,128)(2,1)}, /*index=5*/s32[]{:T(128)}) while((s32[]{:T(128)}, bf16[3,512,192]{1,2,0:T(8,128)(2,1)S(1)}, bf16[3,512,192]{2,1,0:T(8,128)(2,1)S(1)}, ...), condition=%wide.region_3.4_spmd, body=%wide.region_0.3_spmd.sunk | while | flops 1220738048 | bytes 27207784 | solution.py:26
  102.6 1.1 multiply_reduce_fusion.2
  103.7 1.2 fusion.58
  104.9 0.3 copy-done.1
  105.2 1.5 fusion.59
  106.7 1.1 multiply_reduce_fusion.2
  107.8 1.2 fusion.58
  109.0 0.2 copy-done.1
  109.2 1.5 fusion.59
  110.7 1.1 multiply_reduce_fusion.2
  111.8 1.2 fusion.58
  113.0 0.3 copy-done.1
  113.2 1.5 fusion.59
  114.7 1.2 copy.19
  115.9 1.6 copy.22
  117.6 1.7 reshape.27
  119.2 2.0 %broadcast_select_fusion.1 = (bf16[768,1536]{1,0:T(8,128)(2,1)S(1)}, bf16[768,1536]{1,0:T(8,128)(2,1)S(1)}) fusion(bf16[768,1536]{1,0:T(8,128)(2,1)} %collective-permute-done.8, pred[]{:T(512)S(6)} %eq.15, bf16[1,768,1536]{2,1,0:T(8,128)(2,1)S(1)} %copy-done), kind=kLoop, calls=%fused_computation.23 | loop fusion | flops 2359296 | bytes 9437185 | tf_op jit(solution)/shard_map/jit(_where)/select_n | solution.py:54
  121.3 1.3 fusion.23
  122.7 1.1 collective-permute-start.9
  123.8 4.2 %all-to-all-start.1 = ((bf16[8,192,192]{2,1,0:T(8,128)(2,1)}), bf16[8,192,192]{2,1,0:T(8,128)(2,1)S(1)}, u32[]{:S(2)}, u32[]{:S(2)}) async-start(bf16[8,192,192]{2,1,0:T(8,128)(2,1)} %bitcast.15), calls=%async_computation.1 | async-start | bytes 1572864 | tf_op jit(solution)/shard_map/all_to_all | solution.py:61
  128.1 12.8 %collective-permute-done.9 = f32[2,48,1536]{2,1,0:T(8,128)S(1)} collective-permute-done((f32[2,48,1536]{2,1,0:T(8,128)S(1)}, f32[2,48,1536]{2,1,0:T(8,128)S(1)}, u32[]{:S(2)}, u32[]{:S(2)}) %collective-permute-start.9) | collective-permute-done | bytes 589856 | tf_op jit(solution)/shard_map/ppermute | solution.py:112
  140.8 0.1 bitcast_add_fusion
  141.0 3.8 %collective-permute-start.10 = (f32[48,1536]{1,0:T(8,128)S(1)}, f32[48,1536]{1,0:T(8,128)S(1)}, u32[]{:S(2)}, u32[]{:S(2)}) collective-permute-start(f32[48,1536]{1,0:T(8,128)S(1)} %get-tuple-element.55), channel_id=1, source_target_pairs={{0,0},{1,1},{2,4},{3,5},{4,8},{5,9},{6,12},{7,13},{8,16},{9,17},{1... | collective-permute-start | bytes 884744 | tf_op jit(solution)/shard_map/ppermute | solution.py:126
  144.8 0.7 collective-permute-start.11
  145.5 0.4 copy.20
  145.9 0.7 reshape.25
  146.6 12.3 %collective-permute-done.10 = f32[48,1536]{1,0:T(8,128)S(1)} collective-permute-done((f32[48,1536]{1,0:T(8,128)S(1)}, f32[48,1536]{1,0:T(8,128)S(1)}, u32[]{:S(2)}, u32[]{:S(2)}) %collective-permute-start.10) | collective-permute-done | bytes 294944 | tf_op jit(solution)/shard_map/ppermute | solution.py:126
  158.9 4.5 %collective-permute-done.11 = f32[48,1536]{1,0:T(8,128)S(1)} collective-permute-done((f32[48,1536]{1,0:T(8,128)S(1)}, f32[48,1536]{1,0:T(8,128)S(1)}, u32[]{:S(2)}, u32[]{:S(2)}) %collective-permute-start.11) | collective-permute-done | bytes 294944 | tf_op jit(solution)/shard_map/ppermute | solution.py:126
  163.4 0.7 add.139
  164.2 10.0 %all-gather.4.cloned.1.call-done = bf16[1536,1536]{1,0:T(8,128)(2,1)} async-done(((bf16[48,1536]{1,0:T(8,128)(2,1)}), bf16[1536,1536]{1,0:T(8,128)(2,1)}) %all-gather.4.cloned.1.call-update) | async-done | bytes 4718608 | tf_op jit(solution)/shard_map/all_gather | solution.py:49
  174.2 4.2 %fusion.26 = bf16[1,192,1536]{2,1,0:T(8,128)(2,1)} fusion(bf16[192,1536]{1,0:T(8,128)(2,1)S(1)} %reshape.25, bf16[1536,1536]{1,0:T(8,128)(2,1)} %all-gather.4.cloned.1.call-done), kind=kOutput, calls=%fused_computation.21 | convolution fusion | flops 906264576 | bytes 5898240 | tf_op jit(solution)/shard_map/dot_general | solution.py:101
  (32 shorter events, 0.2 us)
Async XLA Ops:
  7.2 2.5 %copy-start.2 = (bf16[1,192,1536]{2,1,0:T(8,128)(2,1)S(1)}, bf16[1,192,1536]{2,1,0:T(8,128)(2,1)}, u32[]{:S(2)}) copy-start(bf16[1,192,1536]{2,1,0:T(8,128)(2,1)} %param.9) | copy-start | bytes 1769476
  7.2 4.0 %copy-start.3 = (bf16[1,192,1536]{2,1,0:T(8,128)(2,1)S(1)}, bf16[1,192,1536]{2,1,0:T(8,128)(2,1)}, u32[]{:S(2)}) copy-start(bf16[1,192,1536]{2,1,0:T(8,128)(2,1)} %param.7) | copy-start | bytes 1769476
  7.2 95.4 %all-gather.6.cloned.1.call-start = ((), (), s32[]{:S(2)}) async-start(), calls=%async_computation.3 | async-start | bytes 2949120 | tf_op jit(solution)/shard_map/all_gather | solution.py:50
  15.6 57.5 %all-to-all-start = ((bf16[8,192,576]{2,1,0:T(8,128)(2,1)}), bf16[8,192,576]{2,1,0:T(8,128)(2,1)S(1)}, u32[]{:S(2)}, u32[]{:S(2)}) async-start(bf16[8,192,576]{2,1,0:T(8,128)(2,1)} %pad_maximum_fusion), calls=%async_computation | async-start | bytes 3932160 | tf_op jit(solution)/shard_map/all_to_all | solution.py:61
  20.9 153.3 %all-gather.4.cloned.1.call-start = ((), (), s32[]{:S(2)}) async-start(), calls=%async_computation.2 | async-start | bytes 4866048 | tf_op jit(solution)/shard_map/all_gather | solution.py:49
  22.1 51.4 %collective-permute-start = (bf16[192,384]{1,0:T(8,128)(2,1)}, bf16[192,384]{1,0:T(8,128)(2,1)}, u32[]{:S(2)}, u32[]{:S(2)}) collective-permute-start(bf16[192,384]{1,0:T(8,128)(2,1)} %get-tuple-element.47), channel_id=1, source_target_pairs={{0,16},{2,18},{4,20},{6,22},{8,24},{10,26},{12,28},{14,30},{16,0},... | collective-permute-start | bytes 442376 | tf_op jit(solution)/shard_map/ppermute | solution.py:80
  24.4 55.2 %collective-permute-start.1 = (bf16[192,384]{1,0:T(8,128)(2,1)}, bf16[192,384]{1,0:T(8,128)(2,1)}, u32[]{:S(2)}, u32[]{:S(2)}) collective-permute-start(bf16[192,384]{1,0:T(8,128)(2,1)} %get-tuple-element.48), channel_id=1, source_target_pairs={{0,18},{2,20},{4,22},{6,24},{8,26},{10,28},{12,30},{14,16},{16,2},... | collective-permute-start | bytes 442376 | tf_op jit(solution)/shard_map/ppermute | solution.py:80
  26.1 58.1 %collective-permute-start.2 = (bf16[192,384]{1,0:T(8,128)(2,1)}, bf16[192,384]{1,0:T(8,128)(2,1)}, u32[]{:S(2)}, u32[]{:S(2)}) collective-permute-start(bf16[192,384]{1,0:T(8,128)(2,1)} %get-tuple-element.49), channel_id=1, source_target_pairs={{0,20},{2,22},{4,24},{6,26},{8,28},{10,30},{12,16},{14,18},{16,4},... | collective-permute-start | bytes 442376 | tf_op jit(solution)/shard_map/ppermute | solution.py:80
  28.4 57.0 %collective-permute-start.3 = (bf16[192,384]{1,0:T(8,128)(2,1)}, bf16[192,384]{1,0:T(8,128)(2,1)}, u32[]{:S(2)}, u32[]{:S(2)}) collective-permute-start(bf16[192,384]{1,0:T(8,128)(2,1)} %get-tuple-element.50), channel_id=1, source_target_pairs={{0,22},{2,24},{4,26},{6,28},{8,30},{10,16},{12,18},{14,20},{16,6},... | collective-permute-start | bytes 442376 | tf_op jit(solution)/shard_map/ppermute | solution.py:80
  29.6 56.7 %collective-permute-start.4 = (bf16[192,384]{1,0:T(8,128)(2,1)}, bf16[192,384]{1,0:T(8,128)(2,1)}, u32[]{:S(2)}, u32[]{:S(2)}) collective-permute-start(bf16[192,384]{1,0:T(8,128)(2,1)} %get-tuple-element.51), channel_id=1, source_target_pairs={{0,24},{2,26},{4,28},{6,30},{8,16},{10,18},{12,20},{14,22},{16,8},... | collective-permute-start | bytes 442376 | tf_op jit(solution)/shard_map/ppermute | solution.py:80
  32.7 40.9 %copy-start.7 = (bf16[192,384]{1,0:T(8,128)(2,1)S(1)}, bf16[192,384]{1,0:T(8,128)(2,1)}, u32[]{:S(2)}) copy-start(bf16[192,384]{1,0:T(8,128)(2,1)} %get-tuple-element.53) | copy-start | bytes 442372
  32.7 47.0 %copy-start.6 = (bf16[192,384]{1,0:T(8,128)(2,1)S(1)}, bf16[192,384]{1,0:T(8,128)(2,1)}, u32[]{:S(2)}) copy-start(bf16[192,384]{1,0:T(8,128)(2,1)} %get-tuple-element.52) | copy-start | bytes 442372
  73.5 13.8 %collective-permute-start.5 = (bf16[192,384]{1,0:T(8,128)(2,1)S(1)}, bf16[192,384]{1,0:T(8,128)(2,1)S(1)}, u32[]{:S(2)}, u32[]{:S(2)}) collective-permute-start(bf16[192,384]{1,0:T(8,128)(2,1)S(1)} %copy-done.7), channel_id=1, source_target_pairs={{0,26},{2,28},{4,30},{6,16},{8,18},{10,20},{12,22},{14,24},{16,10}... | collective-permute-start | bytes 442376 | tf_op jit(solution)/shard_map/ppermute | solution.py:80
  79.6 17.6 %collective-permute-start.6 = (bf16[192,384]{1,0:T(8,128)(2,1)S(1)}, bf16[192,384]{1,0:T(8,128)(2,1)S(1)}, u32[]{:S(2)}, u32[]{:S(2)}) collective-permute-start(bf16[192,384]{1,0:T(8,128)(2,1)S(1)} %copy-done.6), channel_id=1, source_target_pairs={{0,28},{2,30},{4,16},{6,18},{8,20},{10,22},{12,24},{14,26},{16,12}... | collective-permute-start | bytes 442376 | tf_op jit(solution)/shard_map/ppermute | solution.py:80
  84.2 16.4 %collective-permute-start.7 = (bf16[192,384]{1,0:T(8,128)(2,1)}, bf16[192,384]{1,0:T(8,128)(2,1)S(1)}, u32[]{:S(2)}, u32[]{:S(2)}) collective-permute-start(bf16[192,384]{1,0:T(8,128)(2,1)} %get-tuple-element.46), channel_id=1, source_target_pairs={{0,30},{2,16},{4,18},{6,20},{8,22},{10,24},{12,26},{14,28},{16,14}... | collective-permute-start | bytes 442376 | tf_op jit(solution)/shard_map/ppermute | solution.py:80
  100.7 1.9 %copy-start.4 = (bf16[3,512,192]{1,2,0:T(8,128)(2,1)S(1)}, bf16[3,512,192]{1,2,0:T(8,128)(2,1)}, u32[]{:S(2)}) copy-start(bf16[3,512,192]{1,2,0:T(8,128)(2,1)} %custom-call.1) | copy-start | bytes 1769476
  102.6 16.6 %collective-permute-start.8 = (bf16[768,1536]{1,0:T(8,128)(2,1)}, bf16[768,1536]{1,0:T(8,128)(2,1)}, u32[]{:S(2)}, u32[]{:S(2)}) collective-permute-start(bf16[768,1536]{1,0:T(8,128)(2,1)} %bitcast.80), channel_id=1, source_target_pairs={{0,2},{2,0},{1,3},{3,1},{4,6},{6,4},{5,7},{7,5},{8,10},{10,8},{9,1... | collective-permute-start | bytes 7077896 | tf_op jit(solution)/shard_map/ppermute | solution.py:51
  103.7 1.4 copy-start.1
  107.8 1.4 copy-start.1
  111.8 1.4 copy-start.1
  114.7 4.5 %copy-start = (bf16[1,768,1536]{2,1,0:T(8,128)(2,1)S(1)}, bf16[1,768,1536]{2,1,0:T(8,128)(2,1)}, u32[]{:S(2)}) copy-start(bf16[1,768,1536]{2,1,0:T(8,128)(2,1)} %all-gather.6.cloned.1.call-done) | copy-start | bytes 7077892
  119.2 2.0 %copy-start.5 = (bf16[1536,192]{0,1:T(8,128)(2,1)S(1)}, bf16[1536,192]{0,1:T(8,128)(2,1)}, u32[]{:S(2)}) copy-start(bf16[1536,192]{0,1:T(8,128)(2,1)} %reshape.27) | copy-start | bytes 1769476
  122.7 18.2 %collective-permute-start.9 = (f32[2,48,1536]{2,1,0:T(8,128)S(1)}, f32[2,48,1536]{2,1,0:T(8,128)S(1)}, u32[]{:S(2)}, u32[]{:S(2)}) collective-permute-start(f32[2,48,1536]{2,1,0:T(8,128)S(1)} %dynamic-slice_bitcast_fusion), channel_id=1, source_target_pairs={{0,1},{1,0},{2,3},{3,2},{4,5},{5,4},{6,7},{7,6},{8,9},{9,8},{10,11... | collective-permute-start | bytes 1769480 | tf_op jit(solution)/shard_map/ppermute | solution.py:112
  123.8 21.6 %all-to-all-start.1 = ((bf16[8,192,192]{2,1,0:T(8,128)(2,1)}), bf16[8,192,192]{2,1,0:T(8,128)(2,1)S(1)}, u32[]{:S(2)}, u32[]{:S(2)}) async-start(bf16[8,192,192]{2,1,0:T(8,128)(2,1)} %bitcast.15), calls=%async_computation.1 | async-start | bytes 1572864 | tf_op jit(solution)/shard_map/all_to_all | solution.py:61
  141.0 17.9 %collective-permute-start.10 = (f32[48,1536]{1,0:T(8,128)S(1)}, f32[48,1536]{1,0:T(8,128)S(1)}, u32[]{:S(2)}, u32[]{:S(2)}) collective-permute-start(f32[48,1536]{1,0:T(8,128)S(1)} %get-tuple-element.55), channel_id=1, source_target_pairs={{0,0},{1,1},{2,4},{3,5},{4,8},{5,9},{6,12},{7,13},{8,16},{9,17},{1... | collective-permute-start | bytes 884744 | tf_op jit(solution)/shard_map/ppermute | solution.py:126
  144.8 18.6 %collective-permute-start.11 = (f32[48,1536]{1,0:T(8,128)S(1)}, f32[48,1536]{1,0:T(8,128)S(1)}, u32[]{:S(2)}, u32[]{:S(2)}) collective-permute-start(f32[48,1536]{1,0:T(8,128)S(1)} %get-tuple-element.54), channel_id=1, source_target_pairs={{0,2},{1,3},{2,6},{3,7},{4,10},{5,11},{6,14},{7,15},{8,18},{9,19},... | collective-permute-start | bytes 884744 | tf_op jit(solution)/shard_map/ppermute | solution.py:126
Sparse Core Ops, SparseCore 0:
  9.6 81.7 all-gather.5
  94.3 79.8 all-gather.3

commit v15 on v11

--- a/solution.py
+++ b/solution.py
@@ -51,7 +51,7 @@
         return tensor[0].reshape(row_count, head_count, head_width).transpose(1, 0, 2)
 
     side_index = lax.axis_index("side")
-    kv_raw = jnp.concatenate([by_head(key_vectors), by_head(value_vectors)], axis=2)
+    kv_raw = jnp.concatenate([by_head(key_vectors), by_head(value_vectors)], axis=1)
     inner_index = lax.axis_index("inner")
     kv_crossed = []
     for step in range(1, side_count):
@@ -65,12 +65,16 @@
                 kv_raw, (inner_index + shift) % head_count, axis=0, keepdims=False
             )
             kv_crossed.append(lax.ppermute(outgoing, ("side", "inner"), perm))
-    stacked = jnp.concatenate([by_head(queries), kv_raw], axis=2)
-    got = a2a(stacked).reshape(head_count * row_count, 3 * head_width)
-    query_here = got[:, :head_width]
-    kv_all = jnp.concatenate([got[:, head_width:]] + kv_crossed, axis=0)
-    key_all = kv_all[:, :head_width]
-    value_all = kv_all[:, head_width:]
+    stacked = jnp.concatenate([by_head(queries), kv_raw], axis=1)
+    got = a2a(stacked)
+    query_here = got[:, :row_count].reshape(head_count * row_count, head_width)
+    key_parts = [got[:, row_count : 2 * row_count].reshape(-1, head_width)]
+    value_parts = [got[:, 2 * row_count :].reshape(-1, head_width)]
+    for crossed in kv_crossed:
+        key_parts.append(crossed[:row_count])
+        value_parts.append(crossed[row_count:])
+    key_all = jnp.concatenate(key_parts, axis=0)
+    value_all = jnp.concatenate(value_parts, axis=0)
 
     attended_here = attend(query_here, key_all, value_all)
 

time: 175 us -> 177 us (1.011)
  waiting for transfers between devices: 90.5 us -> 79.7 us
  local copies, waits for them, and re-layouts: 16.8 us -> 25.9 us
  matrix products: 15.4 us -> 17.6 us
  starting transfers between devices: 27.5 us -> 29.4 us
    all_to_all x2, waiting for transfers between devices: 52.9 us -> 11.8 us  [a2a(): lax.all_to_all(tensor, 'inner', split_axis=0, concat_axis=0, tiled=True)]
    ppermute x8, waiting for transfers between devices: 21.4 us -> 54.4 us  [local(): kv_crossed.append(lax.ppermute(outgoing, ('side', 'inner'), perm))]
    slice x2 -> x12, local copies, waits for them, and re-layouts: 1.96 us -> 11.8 us  [the longest x8 8.17 us: local(): value_parts.append(crossed[row_count:])]
    another operation x4 -> x0, local copies, waits for them, and re-layouts: 3.98 us -> none  [by_head(): tensor[0].reshape(row_count, head_count, head_width).transpose(1, 0, 2)]
    while x1 -> x3, local copies, waits for them, and re-layouts: 1.16 us -> 4.48 us  [attend(): lax.map(one_block, query_here.reshape(query_count // block_size, block_si...]
    unnamed x20 -> x21, local copies, waits for them, and re-layouts: 5.23 us -> 1.91 us
    ppermute x1, waiting for transfers between devices: 6.91 us -> 4.27 us  [local(): kept = kept + lax.ppermute(sent, 'dp', [(0, 1), (1, 0)])]
    concatenate x1 -> x2, local copies, waits for them, and re-layouts: 0.02 us -> 2.45 us  [the longest x1 1.89 us: local(): value_all = jnp.concatenate(value_parts, axis=0)]
  transfers between devices with their start and end apart: 15 -> 15, of which waited for: 7 -> 9; matrix products, arithmetic and copies ran while one was open for 23% -> 29% of each run, Pallas kernels for 0% -> 0%
where the time goes in v15:
time: 177 us; the launch traced here: 176 us
  waiting for transfers between devices  79.7 us (45%)
  starting transfers between devices  29.4 us (17%)
  local copies, waits for them, and re-layouts  25.9 us (15%)
  matrix products  17.6 us (10%)
  between operations  14.4 us (8%)
  other arithmetic  8.76 us (5%)
    ppermute x8, waiting for transfers between devices, local(): kv_crossed.append(lax.ppermute(outgoing, ('side', 'inner'), perm))  54.4 us
    ppermute x8, starting transfers between devices, local(): kv_crossed.append(lax.ppermute(outgoing, ('side', 'inner'), perm))  11.9 us
    all_to_all x2, waiting for transfers between devices, a2a(): lax.all_to_all(tensor, 'inner', split_axis=0, concat_axis=0, tiled=True)  11.8 us
    all_to_all x2, starting transfers between devices, a2a(): lax.all_to_all(tensor, 'inner', split_axis=0, concat_axis=0, tiled=True)  11.4 us
    slice x8, local copies, waits for them, and re-layouts, local(): value_parts.append(crossed[row_count:])  8.17 us
    ppermute x2, waiting for transfers between devices, local(): arrived = lax.ppermute(outgoing, ALL, perm)  7.88 us
    dot_general x3, matrix products, one_block(): mixed = jnp.dot(weights, value_all, preferred_element_type=jnp.float32)  6.45 us
    ppermute x2, starting transfers between devices, local(): arrived = lax.ppermute(outgoing, ALL, perm)  4.59 us
  transfers between devices with their start and end apart: 15, of which 9 were waited for; matrix products, arithmetic and copies ran while one was open for 29% of the time, Pallas kernels for 0%

profile of v15, /device:TPU:1, one launch (start us, length us, event | category | flops | bytes accessed | tf_op | source)
XLA Modules:
  0.0 175.8 jit_solution(1153695565178500865)
XLA Ops:
  7.2 0.7 all-gather.6.cloned.1.call-update
  7.9 1.3 copy.23
  9.3 0.3 copy.24
  9.6 0.3 copy.22
  9.8 2.1 %pad_maximum_fusion = bf16[8,576,192]{1,2,0:T(8,128)(2,1)} fusion(bf16[8,192,192]{1,2,0:T(8,128)(2,1)S(1)} %bitcast.80, bf16[8,192,192]{1,2,0:T(8,128)(2,1)S(1)} %bitcast.77, bf16[8,192,192]{1,2,0:T(8,128)(2,1)S(1)} %bitcast.85), kind=kLoop, calls=%fused_computation.20 | loop fusion | flops 5308416 | bytes 3538944 | tf_op jit(solution)/shard_map/concatenate | solution.py:68
  11.9 5.3 %all-to-all-start = ((bf16[8,576,192]{1,2,0:T(8,128)(2,1)}), bf16[8,576,192]{1,2,0:T(8,128)(2,1)S(1)}, u32[]{:S(2)}, u32[]{:S(2)}) async-start(bf16[8,576,192]{1,2,0:T(8,128)(2,1)} %pad_maximum_fusion), calls=%async_computation | async-start | bytes 3932160 | tf_op jit(solution)/shard_map/all_to_all | solution.py:48
  17.2 0.7 all-gather.4.cloned.1.call-update
  18.0 1.2 fusion.41
  19.2 2.2 %collective-permute-start.7 = (bf16[384,192]{0,1:T(8,128)(2,1)}, bf16[384,192]{0,1:T(8,128)(2,1)}, u32[]{:S(2)}, u32[]{:S(2)}) collective-permute-start(bf16[384,192]{0,1:T(8,128)(2,1)} %get-tuple-element.50), channel_id=1, source_target_pairs={{0,30},{2,16},{4,18},{6,20},{8,22},{10,24},{12,26},{14,28},{16,14}... | collective-permute-start | bytes 442376 | tf_op jit(solution)/shard_map/ppermute | solution.py:67
  21.4 1.5 collective-permute-start.4
  22.9 4.4 %collective-permute-start.3 = (bf16[384,192]{0,1:T(8,128)(2,1)}, bf16[384,192]{0,1:T(8,128)(2,1)}, u32[]{:S(2)}, u32[]{:S(2)}) collective-permute-start(bf16[384,192]{0,1:T(8,128)(2,1)} %get-tuple-element.54), channel_id=1, source_target_pairs={{0,22},{2,24},{4,26},{6,28},{8,30},{10,16},{12,18},{14,20},{16,6},... | collective-permute-start | bytes 442376 | tf_op jit(solution)/shard_map/ppermute | solution.py:67
  27.4 1.7 collective-permute-start.1
  29.2 30.0 %collective-permute-done.7 = bf16[384,192]{0,1:T(8,128)(2,1)} collective-permute-done((bf16[384,192]{0,1:T(8,128)(2,1)}, bf16[384,192]{0,1:T(8,128)(2,1)}, u32[]{:S(2)}, u32[]{:S(2)}) %collective-permute-start.7) | collective-permute-done | bytes 147488 | tf_op jit(solution)/shard_map/ppermute | solution.py:67
  59.2 2.0 %collective-permute-start = (bf16[384,192]{0,1:T(8,128)(2,1)}, bf16[384,192]{0,1:T(8,128)(2,1)S(1)}, u32[]{:S(2)}, u32[]{:S(2)}) collective-permute-start(bf16[384,192]{0,1:T(8,128)(2,1)} %get-tuple-element.51), channel_id=1, source_target_pairs={{0,16},{2,18},{4,20},{6,22},{8,24},{10,26},{12,28},{14,30},{16,0},... | collective-permute-start | bytes 442376 | tf_op jit(solution)/shard_map/ppermute | solution.py:67
  61.3 1.1 fusion.43
  62.3 5.7 %collective-permute-done.4 = bf16[384,192]{0,1:T(8,128)(2,1)} collective-permute-done((bf16[384,192]{0,1:T(8,128)(2,1)}, bf16[384,192]{0,1:T(8,128)(2,1)}, u32[]{:S(2)}, u32[]{:S(2)}) %collective-permute-start.4) | collective-permute-done | bytes 147488 | tf_op jit(solution)/shard_map/ppermute | solution.py:67
  68.0 1.1 fusion.46
  69.1 3.7 %collective-permute-done.3 = bf16[384,192]{0,1:T(8,128)(2,1)} collective-permute-done((bf16[384,192]{0,1:T(8,128)(2,1)}, bf16[384,192]{0,1:T(8,128)(2,1)}, u32[]{:S(2)}, u32[]{:S(2)}) %collective-permute-start.3) | collective-permute-done | bytes 147488 | tf_op jit(solution)/shard_map/ppermute | solution.py:67
  72.8 1.1 fusion.47
  73.9 1.4 collective-permute-done.2
  75.2 1.1 fusion.48
  76.3 1.7 fusion.49
  78.0 10.0 %collective-permute-done = bf16[384,192]{0,1:T(8,128)(2,1)S(1)} collective-permute-done((bf16[384,192]{0,1:T(8,128)(2,1)}, bf16[384,192]{0,1:T(8,128)(2,1)S(1)}, u32[]{:S(2)}, u32[]{:S(2)}) %collective-permute-start) | collective-permute-done | bytes 147488 | tf_op jit(solution)/shard_map/ppermute | solution.py:67
  88.1 0.7 fusion.50
  88.8 3.6 %collective-permute-done.6 = bf16[384,192]{0,1:T(8,128)(2,1)S(1)} collective-permute-done((bf16[384,192]{0,1:T(8,128)(2,1)S(1)}, bf16[384,192]{0,1:T(8,128)(2,1)S(1)}, u32[]{:S(2)}, u32[]{:S(2)}) %collective-permute-start.6) | collective-permute-done | bytes 147488 | tf_op jit(solution)/shard_map/ppermute | solution.py:67
  92.4 0.7 fusion.44
  93.1 0.7 fusion.45
  93.9 1.3 fusion.42
  95.1 0.4 copy.27
  95.6 0.7 reshape.24
  96.3 1.9 %concatenate.16 = bf16[3072,192]{0,1:T(8,128)(2,1)S(1)} concatenate(bf16[1536,192]{0,1:T(8,128)(2,1)S(1)} %reshape.24, bf16[192,192]{0,1:T(8,128)(2,1)S(1)} %copy-done.9, bf16[192,192]{0,1:T(8,128)(2,1)S(1)} %copy-done.8, bf16[192,192]{0,1:T(8,128)(2,1)S(1)} %get-tuple-element.70, bf16[192,192]{0,1:T(8,128)(2,1)S(1)} %get-tuple-element.68, ...), dimensions={0} | concatenate | bytes 2359296 | tf_op jit(solution)/shard_map/concatenate | solution.py:77
  98.2 1.6 copy.29
  99.8 0.4 copy.26
  100.2 0.7 reshape.23
  100.9 0.6 concatenate.15
  101.5 0.7 copy.28
  102.2 1.5 copy.25
  103.7 14.0 %while.10 = (s32[]{:T(128)}, bf16[3,512,192]{1,2,0:T(8,128)(2,1)}, bf16[3,512,192]{2,1,0:T(8,128)(2,1)S(1)}, bf16[3072,192]{1,0:T(8,128)(2,1)S(1)}, bf16[3072,192]{1,0:T(8,128)(2,1)}, /*index=5*/s32[]{:T(128)}) while((s32[]{:T(128)}, bf16[3,512,192]{1,2,0:T(8,128)(2,1)}, bf16[3,512,192]{2,1,0:T(8,128)(2,1)S(1)}, ...), condition=%wide.region_3.4_spmd, body=%wide.region_0.3_spmd.sunk | while | flops 1220738048 | bytes 26815076 | solution.py:26
  103.7 1.1 multiply_reduce_fusion.2
  104.8 1.2 fusion.64
  106.0 0.2 copy-done
  106.2 2.2 %fusion.65 = bf16[3,512,192]{1,2,0:T(8,128)(2,1)} fusion(bf16[3,512,192]{1,2,0:T(8,128)(2,1)} %get-tuple-element.118, s32[]{:T(128)} %get-tuple-element.117, bf16[3072,192]{1,0:T(8,128)(2,1)S(1)} %copy-done, f32[512,3072]{1,0:T(8,128)S(1)} %get-tuple-element.109, f32[512]{0:T(512)S(1)} %get-tuple-element.110, f32[512]{0:T(512)S(1)} %fusion.64), kind=kOutput, calls=%fused_computation.10.clone.1 | convolution fusion | flops 608894976 | bytes 7672320 | tf_op jit(solution)/shard_map/while/body/eval_jaxpr/dot_general | solution.py:23
  108.4 1.1 multiply_reduce_fusion.2
  109.5 1.2 fusion.64
  110.9 2.2 %fusion.65 = bf16[3,512,192]{1,2,0:T(8,128)(2,1)} fusion(bf16[3,512,192]{1,2,0:T(8,128)(2,1)} %get-tuple-element.118, s32[]{:T(128)} %get-tuple-element.117, bf16[3072,192]{1,0:T(8,128)(2,1)S(1)} %copy-done, f32[512,3072]{1,0:T(8,128)S(1)} %get-tuple-element.109, f32[512]{0:T(512)S(1)} %get-tuple-element.110, f32[512]{0:T(512)S(1)} %fusion.64), kind=kOutput, calls=%fused_computation.10.clone.1 | convolution fusion | flops 608894976 | bytes 7672320 | tf_op jit(solution)/shard_map/while/body/eval_jaxpr/dot_general | solution.py:23
  113.0 1.1 multiply_reduce_fusion.2
  114.1 1.2 fusion.64
  115.3 0.3 copy-done
  115.5 2.2 %fusion.65 = bf16[3,512,192]{1,2,0:T(8,128)(2,1)} fusion(bf16[3,512,192]{1,2,0:T(8,128)(2,1)} %get-tuple-element.118, s32[]{:T(128)} %get-tuple-element.117, bf16[3072,192]{1,0:T(8,128)(2,1)S(1)} %copy-done, f32[512,3072]{1,0:T(8,128)S(1)} %get-tuple-element.109, f32[512]{0:T(512)S(1)} %get-tuple-element.110, f32[512]{0:T(512)S(1)} %fusion.64), kind=kOutput, calls=%fused_computation.10.clone.1 | convolution fusion | flops 608894976 | bytes 7672320 | tf_op jit(solution)/shard_map/while/body/eval_jaxpr/dot_general | solution.py:23
  117.7 2.2 %copy.30 = bf16[3,512,192]{2,1,0:T(8,128)(2,1)} copy(bf16[3,512,192]{1,2,0:T(8,128)(2,1)} %get-tuple-element.29) | data formatting | bytes 1179648 | tf_op jit(solution)/shard_map/while | solution.py:26
  119.9 1.1 copy.34
  121.0 6.1 %all-to-all-start.1 = ((bf16[8,192,192]{2,1,0:T(8,128)(2,1)}), bf16[8,192,192]{2,1,0:T(8,128)(2,1)S(1)}, u32[]{:S(2)}, u32[]{:S(2)}) async-start(bf16[8,192,192]{2,1,0:T(8,128)(2,1)} %bitcast.19), calls=%async_computation.1 | async-start | bytes 1572864 | tf_op jit(solution)/shard_map/all_to_all | solution.py:48
  127.1 3.6 %fusion.23 = f32[2,2,48,1536]{3,2,1,0:T(8,128)S(1)} fusion(bf16[2,2,48,1536]{3,2,1,0:T(8,128)(2,1)S(1)} %bitcast.86, bf16[1,1536,1536]{2,1,0:T(8,128)(2,1)} %all-gather.6.cloned.1.call-done), kind=kOutput, calls=%fused_computation.16 | convolution fusion | flops 905969664 | bytes 6488064 | tf_op jit(solution)/shard_map/dot_general | solution.py:81
  130.8 1.5 collective-permute-start.8
  132.3 11.8 %all-to-all-done.1 = bf16[8,192,192]{2,1,0:T(8,128)(2,1)S(1)} async-done(((bf16[8,192,192]{2,1,0:T(8,128)(2,1)}), bf16[8,192,192]{2,1,0:T(8,128)(2,1)S(1)}, u32[]{:S(2)}, u32[]{:S(2)}) %all-to-all-start.1) | async-done | bytes 589856 | tf_op jit(solution)/shard_map/all_to_all | solution.py:48
  144.1 0.4 copy.31
  144.5 1.5 reshape.25
  146.0 4.3 %collective-permute-done.8 = f32[2,48,1536]{2,1,0:T(8,128)} collective-permute-done((f32[2,48,1536]{2,1,0:T(8,128)S(1)}, f32[2,48,1536]{2,1,0:T(8,128)}, u32[]{:S(2)}, u32[]{:S(2)}) %collective-permute-start.8) | collective-permute-done | bytes 589856 | tf_op jit(solution)/shard_map/ppermute | solution.py:98
  150.3 1.1 bitcast_add_fusion
  151.5 1.2 collective-permute-start.10
  152.7 3.4 %collective-permute-start.9 = (f32[48,1536]{1,0:T(8,128)S(1)}, f32[48,1536]{1,0:T(8,128)S(1)}, u32[]{:S(2)}, u32[]{:S(2)}) collective-permute-start(f32[48,1536]{1,0:T(8,128)S(1)} %get-tuple-element.59), channel_id=1, source_target_pairs={{0,0},{1,1},{2,4},{3,5},{4,8},{5,9},{6,12},{7,13},{8,16},{9,17},{1... | collective-permute-start | bytes 884744 | tf_op jit(solution)/shard_map/ppermute | solution.py:112
  156.1 4.2 %fusion.25 = bf16[1,192,1536]{2,1,0:T(8,128)(2,1)} fusion(bf16[192,1536]{1,0:T(8,128)(2,1)S(1)} %copy-done.3, bf16[1536,1536]{1,0:T(8,128)(2,1)} %all-gather.4.cloned.1.call-done), kind=kOutput, calls=%fused_computation.19 | convolution fusion | flops 906264576 | bytes 5898240 | tf_op jit(solution)/shard_map/dot_general | solution.py:87
  160.3 7.9 %collective-permute-done.9 = f32[48,1536]{1,0:T(8,128)S(1)} collective-permute-done((f32[48,1536]{1,0:T(8,128)S(1)}, f32[48,1536]{1,0:T(8,128)S(1)}, u32[]{:S(2)}, u32[]{:S(2)}) %collective-permute-start.9) | collective-permute-done | bytes 294944 | tf_op jit(solution)/shard_map/ppermute | solution.py:112
  168.2 0.7 add.135
  (37 shorter events, 0.6 us)
Async XLA Ops:
  7.2 2.1 %copy-start.1 = (bf16[1,192,1536]{2,1,0:T(8,128)(2,1)S(1)}, bf16[1,192,1536]{2,1,0:T(8,128)(2,1)}, u32[]{:S(2)}) copy-start(bf16[1,192,1536]{2,1,0:T(8,128)(2,1)} %param.9) | copy-start | bytes 1769476
  7.2 2.4 %copy-start.2 = (bf16[1,192,1536]{2,1,0:T(8,128)(2,1)S(1)}, bf16[1,192,1536]{2,1,0:T(8,128)(2,1)}, u32[]{:S(2)}) copy-start(bf16[1,192,1536]{2,1,0:T(8,128)(2,1)} %param.7) | copy-start | bytes 1769476
  7.2 119.9 %all-gather.6.cloned.1.call-start = ((), (), s32[]{:S(2)}) async-start(), calls=%async_computation.3 | async-start | bytes 5308416 | tf_op jit(solution)/shard_map/all_gather | solution.py:45
  11.9 82.0 %all-to-all-start = ((bf16[8,576,192]{1,2,0:T(8,128)(2,1)}), bf16[8,576,192]{1,2,0:T(8,128)(2,1)S(1)}, u32[]{:S(2)}, u32[]{:S(2)}) async-start(bf16[8,576,192]{1,2,0:T(8,128)(2,1)} %pad_maximum_fusion), calls=%async_computation | async-start | bytes 3932160 | tf_op jit(solution)/shard_map/all_to_all | solution.py:48
  17.2 138.9 %all-gather.4.cloned.1.call-start = ((), (), s32[]{:S(2)}) async-start(), calls=%async_computation.2 | async-start | bytes 4866048 | tf_op jit(solution)/shard_map/all_gather | solution.py:44
  19.2 40.0 %collective-permute-start.7 = (bf16[384,192]{0,1:T(8,128)(2,1)}, bf16[384,192]{0,1:T(8,128)(2,1)}, u32[]{:S(2)}, u32[]{:S(2)}) collective-permute-start(bf16[384,192]{0,1:T(8,128)(2,1)} %get-tuple-element.50), channel_id=1, source_target_pairs={{0,30},{2,16},{4,18},{6,20},{8,22},{10,24},{12,26},{14,28},{16,14}... | collective-permute-start | bytes 442376 | tf_op jit(solution)/shard_map/ppermute | solution.py:67
  21.4 46.6 %collective-permute-start.4 = (bf16[384,192]{0,1:T(8,128)(2,1)}, bf16[384,192]{0,1:T(8,128)(2,1)}, u32[]{:S(2)}, u32[]{:S(2)}) collective-permute-start(bf16[384,192]{0,1:T(8,128)(2,1)} %get-tuple-element.55), channel_id=1, source_target_pairs={{0,24},{2,26},{4,28},{6,30},{8,16},{10,18},{12,20},{14,22},{16,8},... | collective-permute-start | bytes 442376 | tf_op jit(solution)/shard_map/ppermute | solution.py:67
  22.9 49.8 %collective-permute-start.3 = (bf16[384,192]{0,1:T(8,128)(2,1)}, bf16[384,192]{0,1:T(8,128)(2,1)}, u32[]{:S(2)}, u32[]{:S(2)}) collective-permute-start(bf16[384,192]{0,1:T(8,128)(2,1)} %get-tuple-element.54), channel_id=1, source_target_pairs={{0,22},{2,24},{4,26},{6,28},{8,30},{10,16},{12,18},{14,20},{16,6},... | collective-permute-start | bytes 442376 | tf_op jit(solution)/shard_map/ppermute | solution.py:67
  27.4 47.9 %collective-permute-start.2 = (bf16[384,192]{0,1:T(8,128)(2,1)}, bf16[384,192]{0,1:T(8,128)(2,1)}, u32[]{:S(2)}, u32[]{:S(2)}) collective-permute-start(bf16[384,192]{0,1:T(8,128)(2,1)} %get-tuple-element.53), channel_id=1, source_target_pairs={{0,20},{2,22},{4,24},{6,26},{8,28},{10,30},{12,16},{14,18},{16,4},... | collective-permute-start | bytes 442376 | tf_op jit(solution)/shard_map/ppermute | solution.py:67
  27.4 48.9 %collective-permute-start.1 = (bf16[384,192]{0,1:T(8,128)(2,1)}, bf16[384,192]{0,1:T(8,128)(2,1)}, u32[]{:S(2)}, u32[]{:S(2)}) collective-permute-start(bf16[384,192]{0,1:T(8,128)(2,1)} %get-tuple-element.52), channel_id=1, source_target_pairs={{0,18},{2,20},{4,22},{6,24},{8,26},{10,28},{12,30},{14,16},{16,2},... | collective-permute-start | bytes 442376 | tf_op jit(solution)/shard_map/ppermute | solution.py:67
  59.2 28.8 %collective-permute-start = (bf16[384,192]{0,1:T(8,128)(2,1)}, bf16[384,192]{0,1:T(8,128)(2,1)S(1)}, u32[]{:S(2)}, u32[]{:S(2)}) collective-permute-start(bf16[384,192]{0,1:T(8,128)(2,1)} %get-tuple-element.51), channel_id=1, source_target_pairs={{0,16},{2,18},{4,20},{6,22},{8,24},{10,26},{12,28},{14,30},{16,0},... | collective-permute-start | bytes 442376 | tf_op jit(solution)/shard_map/ppermute | solution.py:67
  68.0 24.3 %collective-permute-start.6 = (bf16[384,192]{0,1:T(8,128)(2,1)S(1)}, bf16[384,192]{0,1:T(8,128)(2,1)S(1)}, u32[]{:S(2)}, u32[]{:S(2)}) collective-permute-start(bf16[384,192]{0,1:T(8,128)(2,1)S(1)} %get-tuple-element.56), channel_id=1, source_target_pairs={{0,28},{2,30},{4,16},{6,18},{8,20},{10,22},{12,24},{14,26},{16,12}... | collective-permute-start | bytes 442376 | tf_op jit(solution)/shard_map/ppermute | solution.py:67
  72.8 20.3 %collective-permute-start.5 = (bf16[384,192]{0,1:T(8,128)(2,1)S(1)}, bf16[384,192]{0,1:T(8,128)(2,1)S(1)}, u32[]{:S(2)}, u32[]{:S(2)}) collective-permute-start(bf16[384,192]{0,1:T(8,128)(2,1)S(1)} %get-tuple-element.57), channel_id=1, source_target_pairs={{0,26},{2,28},{4,30},{6,16},{8,18},{10,20},{12,22},{14,24},{16,10}... | collective-permute-start | bytes 442376 | tf_op jit(solution)/shard_map/ppermute | solution.py:67
  95.1 1.1 copy-start.8
  95.1 1.1 copy-start.9
  99.8 1.1 copy-start.4
  99.8 1.2 copy-start.5
  99.8 1.2 copy-start.6
  99.8 1.2 copy-start.7
  104.8 1.4 copy-start
  109.5 1.4 copy-start
  114.1 1.4 copy-start
  121.0 23.0 %all-to-all-start.1 = ((bf16[8,192,192]{2,1,0:T(8,128)(2,1)}), bf16[8,192,192]{2,1,0:T(8,128)(2,1)S(1)}, u32[]{:S(2)}, u32[]{:S(2)}) async-start(bf16[8,192,192]{2,1,0:T(8,128)(2,1)} %bitcast.19), calls=%async_computation.1 | async-start | bytes 1572864 | tf_op jit(solution)/shard_map/all_to_all | solution.py:48
  130.8 19.5 %collective-permute-start.8 = (f32[2,48,1536]{2,1,0:T(8,128)S(1)}, f32[2,48,1536]{2,1,0:T(8,128)}, u32[]{:S(2)}, u32[]{:S(2)}) collective-permute-start(f32[2,48,1536]{2,1,0:T(8,128)S(1)} %dynamic-slice_bitcast_fusion), channel_id=1, source_target_pairs={{0,1},{1,0},{2,3},{3,2},{4,5},{5,4},{6,7},{7,6},{8,9},{9,8},{10,11... | collective-permute-start | bytes 1769480 | tf_op jit(solution)/shard_map/ppermute | solution.py:98
  146.0 10.1 %copy-start.3 = (bf16[192,1536]{1,0:T(8,128)(2,1)S(1)}, bf16[192,1536]{1,0:T(8,128)(2,1)}, u32[]{:S(2)}) copy-start(bf16[192,1536]{1,0:T(8,128)(2,1)} %reshape.25) | copy-start | bytes 1769476
  151.5 8.9 %collective-permute-start.10 = (f32[48,1536]{1,0:T(8,128)S(1)}, f32[48,1536]{1,0:T(8,128)S(1)}, u32[]{:S(2)}, u32[]{:S(2)}) collective-permute-start(f32[48,1536]{1,0:T(8,128)S(1)} %get-tuple-element.58), channel_id=1, source_target_pairs={{0,2},{1,3},{2,6},{3,7},{4,10},{5,11},{6,14},{7,15},{8,18},{9,19},... | collective-permute-start | bytes 884744 | tf_op jit(solution)/shard_map/ppermute | solution.py:112
  152.7 15.5 %collective-permute-start.9 = (f32[48,1536]{1,0:T(8,128)S(1)}, f32[48,1536]{1,0:T(8,128)S(1)}, u32[]{:S(2)}, u32[]{:S(2)}) collective-permute-start(f32[48,1536]{1,0:T(8,128)S(1)} %get-tuple-element.59), channel_id=1, source_target_pairs={{0,0},{1,1},{2,4},{3,5},{4,8},{5,9},{6,12},{7,13},{8,16},{9,17},{1... | collective-permute-start | bytes 884744 | tf_op jit(solution)/shard_map/ppermute | solution.py:112
Sparse Core Ops, SparseCore 0:
  9.7 69.5 all-gather.5
  82.2 72.1 all-gather.3

commit v16 on v11

--- a/solution.py
+++ b/solution.py
@@ -47,8 +47,14 @@
     def a2a(tensor):
         return lax.all_to_all(tensor, "inner", split_axis=0, concat_axis=0, tiled=True)
 
+    half_heads = head_count // 2
+
+    def head_of(j):
+        return j // 2 + half_heads * (j % 2)
+
     def by_head(tensor):
-        return tensor[0].reshape(row_count, head_count, head_width).transpose(1, 0, 2)
+        tensor = tensor[0].reshape(row_count, 2, half_heads, head_width).transpose(2, 1, 0, 3)
+        return tensor.reshape(head_count, row_count, head_width)
 
     side_index = lax.axis_index("side")
     kv_raw = jnp.concatenate([by_head(key_vectors), by_head(value_vectors)], axis=2)
@@ -79,7 +85,11 @@
     )
 
     returned = a2a(attended_here.reshape(head_count, row_count, head_width))
-    attended = returned.transpose(1, 0, 2).reshape(row_count, width)
+    attended = (
+        returned.reshape(half_heads, 2, row_count, head_width)
+        .transpose(2, 1, 0, 3)
+        .reshape(row_count, width)
+    )
     projected = jnp.dot(attended, w_full, preferred_element_type=jnp.float32).astype(
         jnp.bfloat16
     )
@@ -100,7 +110,7 @@
                     for p in range(dp_count):
                         owner_side = (g + step) % side_count
                         source = (g * head_count + h) * dp_count + p
-                        target = (side_count * h + owner_side) * dp_count + p
+                        target = (side_count * head_of(h) + owner_side) * dp_count + p
                         perm.append((source, target))
             outgoing = lax.dynamic_index_in_dim(
                 kept, (side_index + step) % side_count, axis=0, keepdims=False
@@ -118,7 +128,7 @@
                     for p in range(dp_count):
                         c = (g * dp_count + p + step) % chunk_count
                         source = (g * head_count + h) * dp_count + p
-                        target = (side_count * h + c // dp_count) * dp_count + c % dp_count
+                        target = (side_count * head_of(h) + c // dp_count) * dp_count + c % dp_count
                         perm.append((source, target))
             outgoing = lax.dynamic_index_in_dim(
                 pieces, (holder + step) % chunk_count, axis=0, keepdims=False

time: 175 us -> 175 us (level)
    another operation x4 -> x3, local copies, waits for them, and re-layouts: 3.98 us -> 5.53 us  [by_head(): tensor[0].reshape(row_count, 2, half_heads, head_width)]
    unnamed x20 -> x18, local copies, waits for them, and re-layouts: 5.23 us -> 5.23 us
where the time goes in v16:
time: 175 us; the launch traced here: 174 us
  waiting for transfers between devices  89.8 us (51%)
  starting transfers between devices  27.7 us (16%)
  local copies, waits for them, and re-layouts  17.7 us (10%)
  matrix products  15.4 us (9%)
  between operations  14.4 us (8%)
  other arithmetic  9.49 us (5%)
    all_to_all x2, waiting for transfers between devices, a2a(): lax.all_to_all(tensor, 'inner', split_axis=0, concat_axis=0, tiled=True)  51.5 us
    ppermute x8, waiting for transfers between devices, local(): kv_crossed.append(lax.ppermute(outgoing, ('side', 'inner'), perm))  21.2 us
    ppermute x8, starting transfers between devices, local(): kv_crossed.append(lax.ppermute(outgoing, ('side', 'inner'), perm))  12.7 us
    all_to_all x2, starting transfers between devices, a2a(): lax.all_to_all(tensor, 'inner', split_axis=0, concat_axis=0, tiled=True)  8.82 us
    ppermute x1, waiting for transfers between devices, local(): kept = kept + lax.ppermute(sent, 'dp', [(0, 1), (1, 0)])  7.97 us
    ppermute x2, waiting for transfers between devices, local(): arrived = lax.ppermute(outgoing, ALL, perm)  7.7 us
    another operation x3, local copies, waits for them, and re-layouts, by_head(): tensor[0].reshape(row_count, 2, half_heads, head_width)  5.53 us
    unnamed x18, local copies, waits for them, and re-layouts  5.23 us
  transfers between devices with their start and end apart: 15, of which 7 were waited for; matrix products, arithmetic and copies ran while one was open for 23% of the time, Pallas kernels for 0%

profile of v16, /device:TPU:1, one launch (start us, length us, event | category | flops | bytes accessed | tf_op | source)
XLA Modules:
  0.0 174.5 jit_solution(10574653862799533542)
XLA Ops:
  7.2 0.0 all-gather.6.cloned.1.call-start
  7.2 0.7 all-gather.6.cloned.1.call-update
  7.9 2.4 %reshape_squeeze.10 = bf16[192,2,4,192]{3,2,1,0:T(4,128)(2,1)S(1)} reshape(bf16[1,192,1536]{2,1,0:T(8,128)(2,1)} %param.8) | data formatting | bytes 1179648 | tf_op jit(solution)/shard_map/reshape;squeeze | solution.py:56
  10.3 0.2 copy.11
  10.5 0.7 reshape_squeeze.11
  11.2 0.2 copy.12
  11.4 2.4 %reshape_squeeze.9 = bf16[192,2,4,192]{3,2,1,0:T(4,128)(2,1)S(1)} reshape(bf16[1,192,1536]{2,1,0:T(8,128)(2,1)} %param.7) | data formatting | bytes 1179648 | tf_op jit(solution)/shard_map/reshape;squeeze | solution.py:56
  13.8 0.2 copy.10
  14.0 2.1 %pad_maximum_fusion = bf16[8,192,576]{2,1,0:T(8,128)(2,1)} fusion(bf16[8,192,192]{2,1,0:T(8,128)(2,1)S(1)} %bitcast.77, bf16[8,192,192]{2,1,0:T(8,128)(2,1)S(1)} %bitcast.74, bf16[8,192,192]{2,1,0:T(8,128)(2,1)S(1)} %bitcast.88), kind=kLoop, calls=%fused_computation.20 | loop fusion | flops 5308416 | bytes 3538944 | tf_op jit(solution)/shard_map/concatenate | solution.py:74
  16.0 5.3 %all-to-all-start = ((bf16[8,192,576]{2,1,0:T(8,128)(2,1)}), bf16[8,192,576]{2,1,0:T(8,128)(2,1)S(1)}, u32[]{:S(2)}, u32[]{:S(2)}) async-start(bf16[8,192,576]{2,1,0:T(8,128)(2,1)} %pad_maximum_fusion), calls=%async_computation | async-start | bytes 3932160 | tf_op jit(solution)/shard_map/all_to_all | solution.py:48
  21.3 0.7 all-gather.4.cloned.1.call-update
  22.1 1.2 fusion.41
  23.4 2.3 %collective-permute-start = (bf16[192,384]{1,0:T(8,128)(2,1)}, bf16[192,384]{1,0:T(8,128)(2,1)}, u32[]{:S(2)}, u32[]{:S(2)}) collective-permute-start(bf16[192,384]{1,0:T(8,128)(2,1)} %get-tuple-element.45), channel_id=1, source_target_pairs={{0,16},{2,18},{4,20},{6,22},{8,24},{10,26},{12,28},{14,30},{16,0},... | collective-permute-start | bytes 442376 | tf_op jit(solution)/shard_map/ppermute | solution.py:73
  25.7 1.7 collective-permute-start.1
  27.4 2.3 %collective-permute-start.2 = (bf16[192,384]{1,0:T(8,128)(2,1)}, bf16[192,384]{1,0:T(8,128)(2,1)}, u32[]{:S(2)}, u32[]{:S(2)}) collective-permute-start(bf16[192,384]{1,0:T(8,128)(2,1)} %get-tuple-element.47), channel_id=1, source_target_pairs={{0,20},{2,22},{4,24},{6,26},{8,28},{10,30},{12,16},{14,18},{16,4},... | collective-permute-start | bytes 442376 | tf_op jit(solution)/shard_map/ppermute | solution.py:73
  29.7 1.2 collective-permute-start.3
  30.9 2.1 %collective-permute-start.4 = (bf16[192,384]{1,0:T(8,128)(2,1)}, bf16[192,384]{1,0:T(8,128)(2,1)}, u32[]{:S(2)}, u32[]{:S(2)}) collective-permute-start(bf16[192,384]{1,0:T(8,128)(2,1)} %get-tuple-element.49), channel_id=1, source_target_pairs={{0,24},{2,26},{4,28},{6,30},{8,16},{10,18},{12,20},{14,22},{16,8},... | collective-permute-start | bytes 442376 | tf_op jit(solution)/shard_map/ppermute | solution.py:73
  33.0 0.8 fusion.34
  33.8 39.7 %all-to-all-done = bf16[8,192,576]{2,1,0:T(8,128)(2,1)S(1)} async-done(((bf16[8,192,576]{2,1,0:T(8,128)(2,1)}), bf16[8,192,576]{2,1,0:T(8,128)(2,1)S(1)}, u32[]{:S(2)}, u32[]{:S(2)}) %all-to-all-start) | async-done | bytes 1769504 | tf_op jit(solution)/shard_map/all_to_all | solution.py:48
  73.5 0.5 slice_dynamic-update-slice_fusion
  74.0 0.0 collective-permute-done
  74.0 0.1 collective-permute-start.5
  74.1 0.9 constant_dynamic-update-slice_fusion.7
  75.1 2.8 %collective-permute-start.6 = (bf16[192,384]{1,0:T(8,128)(2,1)S(1)}, bf16[192,384]{1,0:T(8,128)(2,1)S(1)}, u32[]{:S(2)}, u32[]{:S(2)}) collective-permute-start(bf16[192,384]{1,0:T(8,128)(2,1)S(1)} %copy-done.4), channel_id=1, source_target_pairs={{0,28},{2,30},{4,16},{6,18},{8,20},{10,22},{12,24},{14,26},{16,12}... | collective-permute-start | bytes 442376 | tf_op jit(solution)/shard_map/ppermute | solution.py:73
  77.9 0.9 constant_dynamic-update-slice_fusion.6
  78.8 0.2 collective-permute-start.7
  79.0 0.9 constant_dynamic-update-slice_fusion.5
  80.0 0.9 constant_dynamic-update-slice_fusion.4
  80.9 0.9 constant_dynamic-update-slice_fusion.3
  81.9 8.8 %collective-permute-done.5 = bf16[192,384]{1,0:T(8,128)(2,1)S(1)} collective-permute-done((bf16[192,384]{1,0:T(8,128)(2,1)S(1)}, bf16[192,384]{1,0:T(8,128)(2,1)S(1)}, u32[]{:S(2)}, u32[]{:S(2)}) %collective-permute-start.5) | collective-permute-done | bytes 147488 | tf_op jit(solution)/shard_map/ppermute | solution.py:73
  90.7 0.1 slice.16
  90.8 9.5 %collective-permute-done.6 = bf16[192,384]{1,0:T(8,128)(2,1)S(1)} collective-permute-done((bf16[192,384]{1,0:T(8,128)(2,1)S(1)}, bf16[192,384]{1,0:T(8,128)(2,1)S(1)}, u32[]{:S(2)}, u32[]{:S(2)}) %collective-permute-start.6) | collective-permute-done | bytes 147488 | tf_op jit(solution)/shard_map/ppermute | solution.py:73
  100.3 2.9 %collective-permute-done.7 = bf16[192,384]{1,0:T(8,128)(2,1)S(1)} collective-permute-done((bf16[192,384]{1,0:T(8,128)(2,1)}, bf16[192,384]{1,0:T(8,128)(2,1)S(1)}, u32[]{:S(2)}, u32[]{:S(2)}) %collective-permute-start.7) | collective-permute-done | bytes 147488 | tf_op jit(solution)/shard_map/ppermute | solution.py:73
  103.2 0.0 copy-start
  103.2 1.9 %fusion.42 = (bf16[3072,192]{1,0:T(8,128)(2,1)}, bf16[3072,192]{1,0:T(8,128)(2,1)S(1)}) fusion(bf16[3072,384]{1,0:T(8,128)(2,1)S(1)} %constant_dynamic-update-slice_fusion), kind=kLoop, calls=%fused_computation.67 | loop fusion | bytes 4718592 | tf_op jit(solution)/shard_map/slice | solution.py:79
  105.1 12.2 %while.10 = (s32[]{:T(128)}, bf16[3,512,192]{1,2,0:T(8,128)(2,1)S(1)}, bf16[3,512,192]{2,1,0:T(8,128)(2,1)S(1)}, bf16[3072,192]{1,0:T(8,128)(2,1)S(1)}, bf16[3072,192]{1,0:T(8,128)(2,1)}, /*index=5*/s32[]{:T(128)}) while((s32[]{:T(128)}, bf16[3,512,192]{1,2,0:T(8,128)(2,1)S(1)}, bf16[3,512,192]{2,1,0:T(8,128)(2,1)S(1)}, ...), condition=%wide.region_3.4_spmd, body=%wide.region_0.3_spmd.sunk | while | flops 1220738048 | bytes 27207784 | solution.py:26
  105.1 1.1 multiply_reduce_fusion.2
  106.3 1.2 fusion.56
  107.4 0.4 copy-done.1
  107.8 1.5 fusion.57
  109.3 1.1 multiply_reduce_fusion.2
  110.4 1.2 fusion.56
  111.6 0.3 copy-done.1
  111.8 1.5 fusion.57
  113.3 1.1 multiply_reduce_fusion.2
  114.4 1.2 fusion.56
  115.6 0.3 copy-done.1
  115.8 1.5 fusion.57
  117.3 1.1 copy.13
  118.5 3.5 %all-to-all-start.1 = ((bf16[8,192,192]{2,1,0:T(8,128)(2,1)}), bf16[8,192,192]{2,1,0:T(8,128)(2,1)S(1)}, u32[]{:S(2)}, u32[]{:S(2)}) async-start(bf16[8,192,192]{2,1,0:T(8,128)(2,1)} %bitcast.18), calls=%async_computation.1 | async-start | bytes 1572864 | tf_op jit(solution)/shard_map/all_to_all | solution.py:48
  122.0 0.0 all-gather.6.cloned.1.call-done
  122.1 3.4 %fusion.23 = f32[2,2,48,1536]{3,2,1,0:T(8,128)S(1)} fusion(bf16[2,2,48,1536]{3,2,1,0:T(8,128)(2,1)S(1)} %bitcast.89, bf16[1,1536,1536]{2,1,0:T(8,128)(2,1)} %all-gather.6.cloned.1.call-done), kind=kOutput, calls=%fused_computation.16 | convolution fusion | flops 905969664 | bytes 6488064 | tf_op jit(solution)/shard_map/dot_general | solution.py:83
  125.5 1.3 collective-permute-start.8
  126.8 11.8 %all-to-all-done.1 = bf16[8,192,192]{2,1,0:T(8,128)(2,1)S(1)} async-done(((bf16[8,192,192]{2,1,0:T(8,128)(2,1)}), bf16[8,192,192]{2,1,0:T(8,128)(2,1)S(1)}, u32[]{:S(2)}, u32[]{:S(2)}) %all-to-all-start.1) | async-done | bytes 589856 | tf_op jit(solution)/shard_map/all_to_all | solution.py:48
  138.6 0.6 copy.19
  139.2 1.7 reshape.41
  140.9 8.0 %collective-permute-done.8 = f32[2,48,1536]{2,1,0:T(8,128)} collective-permute-done((f32[2,48,1536]{2,1,0:T(8,128)S(1)}, f32[2,48,1536]{2,1,0:T(8,128)}, u32[]{:S(2)}, u32[]{:S(2)}) %collective-permute-start.8) | collective-permute-done | bytes 589856 | tf_op jit(solution)/shard_map/ppermute | solution.py:104
  148.9 1.1 bitcast_add_fusion
  150.1 0.1 collective-permute-start.10
  150.1 4.8 %collective-permute-start.9 = (f32[48,1536]{1,0:T(8,128)S(1)}, f32[48,1536]{1,0:T(8,128)S(1)}, u32[]{:S(2)}, u32[]{:S(2)}) collective-permute-start(f32[48,1536]{1,0:T(8,128)S(1)} %get-tuple-element.53), channel_id=1, source_target_pairs={{0,0},{1,1},{2,16},{3,17},{4,4},{5,5},{6,20},{7,21},{8,8},{9,9},{1... | collective-permute-start | bytes 884744 | tf_op jit(solution)/shard_map/ppermute | solution.py:118
  154.9 0.0 all-gather.4.cloned.1.call-done
  155.0 4.2 %fusion.25 = bf16[1,192,1536]{2,1,0:T(8,128)(2,1)} fusion(bf16[192,1536]{1,0:T(8,128)(2,1)S(1)} %copy-done.3, bf16[1536,1536]{1,0:T(8,128)(2,1)} %all-gather.4.cloned.1.call-done), kind=kOutput, calls=%fused_computation.19 | convolution fusion | flops 906264576 | bytes 5898240 | tf_op jit(solution)/shard_map/dot_general | solution.py:93
  159.2 7.7 %collective-permute-done.9 = f32[48,1536]{1,0:T(8,128)S(1)} collective-permute-done((f32[48,1536]{1,0:T(8,128)S(1)}, f32[48,1536]{1,0:T(8,128)S(1)}, u32[]{:S(2)}, u32[]{:S(2)}) %collective-permute-start.9) | collective-permute-done | bytes 294944 | tf_op jit(solution)/shard_map/ppermute | solution.py:118
  166.9 0.7 add.135
  (25 shorter events, 0.2 us)
Async XLA Ops:
  7.2 3.3 %copy-start.2 = (bf16[1,192,1536]{2,1,0:T(8,128)(2,1)S(1)}, bf16[1,192,1536]{2,1,0:T(8,128)(2,1)}, u32[]{:S(2)}) copy-start(bf16[1,192,1536]{2,1,0:T(8,128)(2,1)} %param.9) | copy-start | bytes 1769476
  7.2 114.9 %all-gather.6.cloned.1.call-start = ((), (), s32[]{:S(2)}) async-start(), calls=%async_computation.3 | async-start | bytes 5308416 | tf_op jit(solution)/shard_map/all_gather | solution.py:45
  16.0 57.5 %all-to-all-start = ((bf16[8,192,576]{2,1,0:T(8,128)(2,1)}), bf16[8,192,576]{2,1,0:T(8,128)(2,1)S(1)}, u32[]{:S(2)}, u32[]{:S(2)}) async-start(bf16[8,192,576]{2,1,0:T(8,128)(2,1)} %pad_maximum_fusion), calls=%async_computation | async-start | bytes 3932160 | tf_op jit(solution)/shard_map/all_to_all | solution.py:48
  21.3 133.6 %all-gather.4.cloned.1.call-start = ((), (), s32[]{:S(2)}) async-start(), calls=%async_computation.2 | async-start | bytes 4866048 | tf_op jit(solution)/shard_map/all_gather | solution.py:44
  23.4 50.7 %collective-permute-start = (bf16[192,384]{1,0:T(8,128)(2,1)}, bf16[192,384]{1,0:T(8,128)(2,1)}, u32[]{:S(2)}, u32[]{:S(2)}) collective-permute-start(bf16[192,384]{1,0:T(8,128)(2,1)} %get-tuple-element.45), channel_id=1, source_target_pairs={{0,16},{2,18},{4,20},{6,22},{8,24},{10,26},{12,28},{14,30},{16,0},... | collective-permute-start | bytes 442376 | tf_op jit(solution)/shard_map/ppermute | solution.py:73
  25.7 49.4 %collective-permute-start.1 = (bf16[192,384]{1,0:T(8,128)(2,1)}, bf16[192,384]{1,0:T(8,128)(2,1)}, u32[]{:S(2)}, u32[]{:S(2)}) collective-permute-start(bf16[192,384]{1,0:T(8,128)(2,1)} %get-tuple-element.46), channel_id=1, source_target_pairs={{0,18},{2,20},{4,22},{6,24},{8,26},{10,28},{12,30},{14,16},{16,2},... | collective-permute-start | bytes 442376 | tf_op jit(solution)/shard_map/ppermute | solution.py:73
  27.4 51.4 %collective-permute-start.2 = (bf16[192,384]{1,0:T(8,128)(2,1)}, bf16[192,384]{1,0:T(8,128)(2,1)}, u32[]{:S(2)}, u32[]{:S(2)}) collective-permute-start(bf16[192,384]{1,0:T(8,128)(2,1)} %get-tuple-element.47), channel_id=1, source_target_pairs={{0,20},{2,22},{4,24},{6,26},{8,28},{10,30},{12,16},{14,18},{16,4},... | collective-permute-start | bytes 442376 | tf_op jit(solution)/shard_map/ppermute | solution.py:73
  29.7 50.3 %collective-permute-start.3 = (bf16[192,384]{1,0:T(8,128)(2,1)}, bf16[192,384]{1,0:T(8,128)(2,1)}, u32[]{:S(2)}, u32[]{:S(2)}) collective-permute-start(bf16[192,384]{1,0:T(8,128)(2,1)} %get-tuple-element.48), channel_id=1, source_target_pairs={{0,22},{2,24},{4,26},{6,28},{8,30},{10,16},{12,18},{14,20},{16,6},... | collective-permute-start | bytes 442376 | tf_op jit(solution)/shard_map/ppermute | solution.py:73
  30.9 50.1 %collective-permute-start.4 = (bf16[192,384]{1,0:T(8,128)(2,1)}, bf16[192,384]{1,0:T(8,128)(2,1)}, u32[]{:S(2)}, u32[]{:S(2)}) collective-permute-start(bf16[192,384]{1,0:T(8,128)(2,1)} %get-tuple-element.49), channel_id=1, source_target_pairs={{0,24},{2,26},{4,28},{6,30},{8,16},{10,18},{12,20},{14,22},{16,8},... | collective-permute-start | bytes 442376 | tf_op jit(solution)/shard_map/ppermute | solution.py:73
  33.8 40.2 %copy-start.5 = (bf16[192,384]{1,0:T(8,128)(2,1)S(1)}, bf16[192,384]{1,0:T(8,128)(2,1)}, u32[]{:S(2)}) copy-start(bf16[192,384]{1,0:T(8,128)(2,1)} %get-tuple-element.51) | copy-start | bytes 442372
  33.8 41.2 %copy-start.4 = (bf16[192,384]{1,0:T(8,128)(2,1)S(1)}, bf16[192,384]{1,0:T(8,128)(2,1)}, u32[]{:S(2)}) copy-start(bf16[192,384]{1,0:T(8,128)(2,1)} %get-tuple-element.50) | copy-start | bytes 442372
  74.0 16.6 %collective-permute-start.5 = (bf16[192,384]{1,0:T(8,128)(2,1)S(1)}, bf16[192,384]{1,0:T(8,128)(2,1)S(1)}, u32[]{:S(2)}, u32[]{:S(2)}) collective-permute-start(bf16[192,384]{1,0:T(8,128)(2,1)S(1)} %copy-done.5), channel_id=1, source_target_pairs={{0,26},{2,28},{4,30},{6,16},{8,18},{10,20},{12,22},{14,24},{16,10}... | collective-permute-start | bytes 442376 | tf_op jit(solution)/shard_map/ppermute | solution.py:73
  75.1 25.2 %collective-permute-start.6 = (bf16[192,384]{1,0:T(8,128)(2,1)S(1)}, bf16[192,384]{1,0:T(8,128)(2,1)S(1)}, u32[]{:S(2)}, u32[]{:S(2)}) collective-permute-start(bf16[192,384]{1,0:T(8,128)(2,1)S(1)} %copy-done.4), channel_id=1, source_target_pairs={{0,28},{2,30},{4,16},{6,18},{8,20},{10,22},{12,24},{14,26},{16,12}... | collective-permute-start | bytes 442376 | tf_op jit(solution)/shard_map/ppermute | solution.py:73
  78.8 24.4 %collective-permute-start.7 = (bf16[192,384]{1,0:T(8,128)(2,1)}, bf16[192,384]{1,0:T(8,128)(2,1)S(1)}, u32[]{:S(2)}, u32[]{:S(2)}) collective-permute-start(bf16[192,384]{1,0:T(8,128)(2,1)} %get-tuple-element.44), channel_id=1, source_target_pairs={{0,30},{2,16},{4,18},{6,20},{8,22},{10,24},{12,26},{14,28},{16,14}... | collective-permute-start | bytes 442376 | tf_op jit(solution)/shard_map/ppermute | solution.py:73
  103.2 1.9 %copy-start = (bf16[3,512,192]{1,2,0:T(8,128)(2,1)S(1)}, bf16[3,512,192]{1,2,0:T(8,128)(2,1)}, u32[]{:S(2)}) copy-start(bf16[3,512,192]{1,2,0:T(8,128)(2,1)} %custom-call.1) | copy-start | bytes 1769476
  106.3 1.5 copy-start.1
  110.4 1.4 copy-start.1
  114.4 1.4 copy-start.1
  118.5 20.1 %all-to-all-start.1 = ((bf16[8,192,192]{2,1,0:T(8,128)(2,1)}), bf16[8,192,192]{2,1,0:T(8,128)(2,1)S(1)}, u32[]{:S(2)}, u32[]{:S(2)}) async-start(bf16[8,192,192]{2,1,0:T(8,128)(2,1)} %bitcast.18), calls=%async_computation.1 | async-start | bytes 1572864 | tf_op jit(solution)/shard_map/all_to_all | solution.py:48
  125.5 23.3 %collective-permute-start.8 = (f32[2,48,1536]{2,1,0:T(8,128)S(1)}, f32[2,48,1536]{2,1,0:T(8,128)}, u32[]{:S(2)}, u32[]{:S(2)}) collective-permute-start(f32[2,48,1536]{2,1,0:T(8,128)S(1)} %dynamic-slice_bitcast_fusion), channel_id=1, source_target_pairs={{0,1},{1,0},{2,3},{3,2},{4,5},{5,4},{6,7},{7,6},{8,9},{9,8},{10,11... | collective-permute-start | bytes 1769480 | tf_op jit(solution)/shard_map/ppermute | solution.py:104
  140.9 14.1 %copy-start.3 = (bf16[192,1536]{1,0:T(8,128)(2,1)S(1)}, bf16[192,1536]{1,0:T(8,128)(2,1)}, u32[]{:S(2)}) copy-start(bf16[192,1536]{1,0:T(8,128)(2,1)} %reshape.41) | copy-start | bytes 1769476
  150.1 9.2 %collective-permute-start.10 = (f32[48,1536]{1,0:T(8,128)S(1)}, f32[48,1536]{1,0:T(8,128)S(1)}, u32[]{:S(2)}, u32[]{:S(2)}) collective-permute-start(f32[48,1536]{1,0:T(8,128)S(1)} %get-tuple-element.52), channel_id=1, source_target_pairs={{0,2},{1,3},{2,18},{3,19},{4,6},{5,7},{6,22},{7,23},{8,10},{9,11},... | collective-permute-start | bytes 884744 | tf_op jit(solution)/shard_map/ppermute | solution.py:118
  150.1 16.8 %collective-permute-start.9 = (f32[48,1536]{1,0:T(8,128)S(1)}, f32[48,1536]{1,0:T(8,128)S(1)}, u32[]{:S(2)}, u32[]{:S(2)}) collective-permute-start(f32[48,1536]{1,0:T(8,128)S(1)} %get-tuple-element.53), channel_id=1, source_target_pairs={{0,0},{1,1},{2,16},{3,17},{4,4},{5,5},{6,20},{7,21},{8,8},{9,9},{1... | collective-permute-start | bytes 884744 | tf_op jit(solution)/shard_map/ppermute | solution.py:118
Sparse Core Ops, SparseCore 0:
  9.6 62.1 all-gather.5
  74.8 79.2 all-gather.3

commit v17 on v16

--- a/solution.py
+++ b/solution.py
@@ -84,7 +84,8 @@
         attended_here, cot_side, (((0,), (0,)), ((), ())), preferred_element_type=jnp.float32
     )
 
-    returned = a2a(attended_here.reshape(head_count, row_count, head_width))
+    partial, attended_back = lax.optimization_barrier((partial, attended_here))
+    returned = a2a(attended_back.reshape(head_count, row_count, head_width))
     attended = (
         returned.reshape(half_heads, 2, row_count, head_width)
         .transpose(2, 1, 0, 3)

time: 175 us -> 176 us (level)
  waiting for transfers between devices: 89.8 us -> 93 us
    all_to_all x2, waiting for transfers between devices: 51.5 us -> 39.7 us  [a2a(): lax.all_to_all(tensor, 'inner', split_axis=0, concat_axis=0, tiled=True)]
    ppermute x1, waiting for transfers between devices: 7.97 us -> 17 us  [local(): kept = kept + lax.ppermute(sent, 'dp', [(0, 1), (1, 0)])]
    ppermute x2, waiting for transfers between devices: 7.7 us -> 13.7 us  [local(): arrived = lax.ppermute(outgoing, ALL, perm)]
    unnamed x18 -> x16, local copies, waits for them, and re-layouts: 5.23 us -> 5.22 us
  transfers between devices with their start and end apart: 15 -> 15, of which waited for: 7 -> 7; matrix products, arithmetic and copies ran while one was open for 23% -> 20% of each run, Pallas kernels for 0% -> 0%
where the time goes in v17:
time: 176 us; the launch traced here: 175 us
  waiting for transfers between devices  93 us (53%)
  starting transfers between devices  27.2 us (15%)
  local copies, waits for them, and re-layouts  16.9 us (10%)
  matrix products  15.4 us (9%)
  between operations  14.4 us (8%)
  other arithmetic  8.45 us (5%)
    all_to_all x2, waiting for transfers between devices, a2a(): lax.all_to_all(tensor, 'inner', split_axis=0, concat_axis=0, tiled=True)  39.7 us
    ppermute x8, waiting for transfers between devices, local(): kv_crossed.append(lax.ppermute(outgoing, ('side', 'inner'), perm))  21.2 us
    ppermute x1, waiting for transfers between devices, local(): kept = kept + lax.ppermute(sent, 'dp', [(0, 1), (1, 0)])  17 us
    ppermute x2, waiting for transfers between devices, local(): arrived = lax.ppermute(outgoing, ALL, perm)  13.7 us
    ppermute x8, starting transfers between devices, local(): kv_crossed.append(lax.ppermute(outgoing, ('side', 'inner'), perm))  12.7 us
    all_to_all x2, starting transfers between devices, a2a(): lax.all_to_all(tensor, 'inner', split_axis=0, concat_axis=0, tiled=True)  8.8 us
    another operation x3, local copies, waits for them, and re-layouts, by_head(): tensor[0].reshape(row_count, 2, half_heads, head_width)  5.53 us
    unnamed x16, local copies, waits for them, and re-layouts  5.22 us
  transfers between devices with their start and end apart: 15, of which 7 were waited for; matrix products, arithmetic and copies ran while one was open for 20% of the time, Pallas kernels for 0%

profile of v17, /device:TPU:1, one launch (start us, length us, event | category | flops | bytes accessed | tf_op | source)
XLA Modules:
  0.0 175.3 jit_solution(11894795409613376026)
XLA Ops:
  7.2 0.0 all-gather.6.cloned.1.call-start
  7.2 0.7 all-gather.6.cloned.1.call-update
  7.9 2.4 %reshape_squeeze.10 = bf16[192,2,4,192]{3,2,1,0:T(4,128)(2,1)S(1)} reshape(bf16[1,192,1536]{2,1,0:T(8,128)(2,1)} %param.8) | data formatting | bytes 1179648 | tf_op jit(solution)/shard_map/reshape;squeeze | solution.py:56
  10.3 0.2 copy.15
  10.5 0.7 reshape_squeeze.11
  11.2 0.2 copy.16
  11.4 2.4 %reshape_squeeze.9 = bf16[192,2,4,192]{3,2,1,0:T(4,128)(2,1)S(1)} reshape(bf16[1,192,1536]{2,1,0:T(8,128)(2,1)} %param.7) | data formatting | bytes 1179648 | tf_op jit(solution)/shard_map/reshape;squeeze | solution.py:56
  13.8 0.2 copy.14
  14.0 2.1 %pad_maximum_fusion = bf16[8,192,576]{2,1,0:T(8,128)(2,1)} fusion(bf16[8,192,192]{2,1,0:T(8,128)(2,1)S(1)} %bitcast.69, bf16[8,192,192]{2,1,0:T(8,128)(2,1)S(1)} %bitcast.66, bf16[8,192,192]{2,1,0:T(8,128)(2,1)S(1)} %bitcast.83), kind=kLoop, calls=%fused_computation.20 | loop fusion | flops 5308416 | bytes 3538944 | tf_op jit(solution)/shard_map/concatenate | solution.py:74
  16.0 5.3 %all-to-all-start = ((bf16[8,192,576]{2,1,0:T(8,128)(2,1)}), bf16[8,192,576]{2,1,0:T(8,128)(2,1)S(1)}, u32[]{:S(2)}, u32[]{:S(2)}) async-start(bf16[8,192,576]{2,1,0:T(8,128)(2,1)} %pad_maximum_fusion), calls=%async_computation | async-start | bytes 3932160 | tf_op jit(solution)/shard_map/all_to_all | solution.py:48
  21.3 0.7 all-gather.4.cloned.1.call-update
  22.1 1.2 fusion.41
  23.4 2.3 %collective-permute-start = (bf16[192,384]{1,0:T(8,128)(2,1)}, bf16[192,384]{1,0:T(8,128)(2,1)}, u32[]{:S(2)}, u32[]{:S(2)}) collective-permute-start(bf16[192,384]{1,0:T(8,128)(2,1)} %get-tuple-element.49), channel_id=1, source_target_pairs={{0,16},{2,18},{4,20},{6,22},{8,24},{10,26},{12,28},{14,30},{16,0},... | collective-permute-start | bytes 442376 | tf_op jit(solution)/shard_map/ppermute | solution.py:73
  25.7 1.7 collective-permute-start.1
  27.4 2.3 %collective-permute-start.2 = (bf16[192,384]{1,0:T(8,128)(2,1)}, bf16[192,384]{1,0:T(8,128)(2,1)}, u32[]{:S(2)}, u32[]{:S(2)}) collective-permute-start(bf16[192,384]{1,0:T(8,128)(2,1)} %get-tuple-element.51), channel_id=1, source_target_pairs={{0,20},{2,22},{4,24},{6,26},{8,28},{10,30},{12,16},{14,18},{16,4},... | collective-permute-start | bytes 442376 | tf_op jit(solution)/shard_map/ppermute | solution.py:73
  29.7 1.2 collective-permute-start.3
  30.9 2.1 %collective-permute-start.4 = (bf16[192,384]{1,0:T(8,128)(2,1)}, bf16[192,384]{1,0:T(8,128)(2,1)}, u32[]{:S(2)}, u32[]{:S(2)}) collective-permute-start(bf16[192,384]{1,0:T(8,128)(2,1)} %get-tuple-element.53), channel_id=1, source_target_pairs={{0,24},{2,26},{4,28},{6,30},{8,16},{10,18},{12,20},{14,22},{16,8},... | collective-permute-start | bytes 442376 | tf_op jit(solution)/shard_map/ppermute | solution.py:73
  33.0 0.9 fusion.34
  33.8 39.7 %all-to-all-done = bf16[8,192,576]{2,1,0:T(8,128)(2,1)S(1)} async-done(((bf16[8,192,576]{2,1,0:T(8,128)(2,1)}), bf16[8,192,576]{2,1,0:T(8,128)(2,1)S(1)}, u32[]{:S(2)}, u32[]{:S(2)}) %all-to-all-start) | async-done | bytes 1769504 | tf_op jit(solution)/shard_map/all_to_all | solution.py:48
  73.5 0.5 slice_dynamic-update-slice_fusion
  74.0 0.1 collective-permute-start.5
  74.1 0.9 constant_dynamic-update-slice_fusion.7
  75.0 0.0 collective-permute-done.1
  75.1 2.8 %collective-permute-start.6 = (bf16[192,384]{1,0:T(8,128)(2,1)S(1)}, bf16[192,384]{1,0:T(8,128)(2,1)S(1)}, u32[]{:S(2)}, u32[]{:S(2)}) collective-permute-start(bf16[192,384]{1,0:T(8,128)(2,1)S(1)} %copy-done.3), channel_id=1, source_target_pairs={{0,28},{2,30},{4,16},{6,18},{8,20},{10,22},{12,24},{14,26},{16,12}... | collective-permute-start | bytes 442376 | tf_op jit(solution)/shard_map/ppermute | solution.py:73
  77.8 0.9 constant_dynamic-update-slice_fusion.6
  78.8 0.2 collective-permute-start.7
  79.0 0.9 constant_dynamic-update-slice_fusion.5
  80.0 0.9 constant_dynamic-update-slice_fusion.4
  80.9 0.9 constant_dynamic-update-slice_fusion.3
  81.9 8.8 %collective-permute-done.5 = bf16[192,384]{1,0:T(8,128)(2,1)S(1)} collective-permute-done((bf16[192,384]{1,0:T(8,128)(2,1)S(1)}, bf16[192,384]{1,0:T(8,128)(2,1)S(1)}, u32[]{:S(2)}, u32[]{:S(2)}) %collective-permute-start.5) | collective-permute-done | bytes 147488 | tf_op jit(solution)/shard_map/ppermute | solution.py:73
  90.7 0.1 slice.16
  90.8 9.5 %collective-permute-done.6 = bf16[192,384]{1,0:T(8,128)(2,1)S(1)} collective-permute-done((bf16[192,384]{1,0:T(8,128)(2,1)S(1)}, bf16[192,384]{1,0:T(8,128)(2,1)S(1)}, u32[]{:S(2)}, u32[]{:S(2)}) %collective-permute-start.6) | collective-permute-done | bytes 147488 | tf_op jit(solution)/shard_map/ppermute | solution.py:73
  100.3 2.9 %collective-permute-done.7 = bf16[192,384]{1,0:T(8,128)(2,1)S(1)} collective-permute-done((bf16[192,384]{1,0:T(8,128)(2,1)}, bf16[192,384]{1,0:T(8,128)(2,1)S(1)}, u32[]{:S(2)}, u32[]{:S(2)}) %collective-permute-start.7) | collective-permute-done | bytes 147488 | tf_op jit(solution)/shard_map/ppermute | solution.py:73
  103.2 0.0 copy-start.1
  103.2 1.9 %fusion.42 = (bf16[3072,192]{1,0:T(8,128)(2,1)}, bf16[3072,192]{1,0:T(8,128)(2,1)S(1)}) fusion(bf16[3072,384]{1,0:T(8,128)(2,1)S(1)} %constant_dynamic-update-slice_fusion), kind=kLoop, calls=%fused_computation.66 | loop fusion | bytes 4718592 | tf_op jit(solution)/shard_map/slice | solution.py:79
  105.1 12.2 %while.10 = (s32[]{:T(128)}, bf16[3,512,192]{1,2,0:T(8,128)(2,1)S(1)}, bf16[3,512,192]{2,1,0:T(8,128)(2,1)S(1)}, bf16[3072,192]{1,0:T(8,128)(2,1)S(1)}, bf16[3072,192]{1,0:T(8,128)(2,1)}, /*index=5*/s32[]{:T(128)}) while((s32[]{:T(128)}, bf16[3,512,192]{1,2,0:T(8,128)(2,1)S(1)}, bf16[3,512,192]{2,1,0:T(8,128)(2,1)S(1)}, ...), condition=%wide.region_3.4_spmd, body=%wide.region_0.3_spmd.sunk | while | flops 1220738048 | bytes 27207784 | solution.py:26
  105.1 1.1 multiply_reduce_fusion.2
  106.3 1.2 fusion.56
  107.4 0.4 copy-done
  107.8 1.5 fusion.57
  109.3 1.1 multiply_reduce_fusion.2
  110.4 1.2 fusion.56
  111.6 0.3 copy-done
  111.8 1.5 fusion.57
  113.3 1.1 multiply_reduce_fusion.2
  114.4 1.2 fusion.56
  115.6 0.3 copy-done
  115.8 1.5 fusion.57
  117.4 0.0 all-gather.6.cloned.1.call-done
  117.4 3.4 %fusion.23 = f32[192,1536]{1,0:T(8,128)S(1)} fusion(bf16[1536,192]{0,1:T(8,128)(2,1)S(1)} %bitcast.75, bf16[1,1536,1536]{2,1,0:T(8,128)(2,1)} %all-gather.6.cloned.1.call-done), kind=kOutput, calls=%fused_computation.16 | convolution fusion | flops 905969664 | bytes 6488064 | tf_op jit(solution)/shard_map/dot_general | solution.py:83
  120.9 1.3 collective-permute-start.8
  122.2 1.2 copy.20
  123.3 3.5 %all-to-all-start.1 = ((bf16[8,192,192]{2,1,0:T(8,128)(2,1)}), bf16[8,192,192]{2,1,0:T(8,128)(2,1)S(1)}, u32[]{:S(2)}, u32[]{:S(2)}) async-start(bf16[8,192,192]{2,1,0:T(8,128)(2,1)} %bitcast.19), calls=%async_computation.1 | async-start | bytes 1572864 | tf_op jit(solution)/shard_map/all_to_all | solution.py:48
  126.9 17.0 %collective-permute-done.8 = f32[2,48,1536]{2,1,0:T(8,128)S(1)} collective-permute-done((f32[2,48,1536]{2,1,0:T(8,128)S(1)}, f32[2,48,1536]{2,1,0:T(8,128)S(1)}, u32[]{:S(2)}, u32[]{:S(2)}) %collective-permute-start.8) | collective-permute-done | bytes 589856 | tf_op jit(solution)/shard_map/ppermute | solution.py:105
  143.8 0.1 bitcast_add_fusion
  144.0 0.1 collective-permute-start.10
  144.0 4.3 %collective-permute-start.9 = (f32[48,1536]{1,0:T(8,128)S(1)}, f32[48,1536]{1,0:T(8,128)S(1)}, u32[]{:S(2)}, u32[]{:S(2)}) collective-permute-start(f32[48,1536]{1,0:T(8,128)S(1)} %get-tuple-element.57), channel_id=1, source_target_pairs={{0,0},{1,1},{2,16},{3,17},{4,4},{5,5},{6,20},{7,21},{8,8},{9,9},{1... | collective-permute-start | bytes 884744 | tf_op jit(solution)/shard_map/ppermute | solution.py:119
  148.3 3.8 %collective-permute-done.10 = f32[48,1536]{1,0:T(8,128)S(1)} collective-permute-done((f32[48,1536]{1,0:T(8,128)S(1)}, f32[48,1536]{1,0:T(8,128)S(1)}, u32[]{:S(2)}, u32[]{:S(2)}) %collective-permute-start.10) | collective-permute-done | bytes 294944 | tf_op jit(solution)/shard_map/ppermute | solution.py:119
  152.2 9.8 %collective-permute-done.9 = f32[48,1536]{1,0:T(8,128)S(1)} collective-permute-done((f32[48,1536]{1,0:T(8,128)S(1)}, f32[48,1536]{1,0:T(8,128)S(1)}, u32[]{:S(2)}, u32[]{:S(2)}) %collective-permute-start.9) | collective-permute-done | bytes 294944 | tf_op jit(solution)/shard_map/ppermute | solution.py:119
  162.0 0.7 add.135
  162.8 0.6 copy.19
  163.4 0.9 reshape.47
  164.2 0.0 all-gather.4.cloned.1.call-done
  164.3 4.2 %fusion.25 = bf16[1,192,1536]{2,1,0:T(8,128)(2,1)} fusion(bf16[192,1536]{1,0:T(8,128)(2,1)S(1)} %reshape.47, bf16[1536,1536]{1,0:T(8,128)(2,1)} %all-gather.4.cloned.1.call-done), kind=kOutput, calls=%fused_computation.19 | convolution fusion | flops 906264576 | bytes 5898240 | tf_op jit(solution)/shard_map/dot_general | solution.py:94
  (23 shorter events, 0.2 us)
Async XLA Ops:
  7.2 3.3 %copy-start.2 = (bf16[1,192,1536]{2,1,0:T(8,128)(2,1)S(1)}, bf16[1,192,1536]{2,1,0:T(8,128)(2,1)}, u32[]{:S(2)}) copy-start(bf16[1,192,1536]{2,1,0:T(8,128)(2,1)} %param.9) | copy-start | bytes 1769476
  7.2 110.2 %all-gather.6.cloned.1.call-start = ((), (), s32[]{:S(2)}) async-start(), calls=%async_computation.3 | async-start | bytes 5308416 | tf_op jit(solution)/shard_map/all_gather | solution.py:45
  16.0 57.5 %all-to-all-start = ((bf16[8,192,576]{2,1,0:T(8,128)(2,1)}), bf16[8,192,576]{2,1,0:T(8,128)(2,1)S(1)}, u32[]{:S(2)}, u32[]{:S(2)}) async-start(bf16[8,192,576]{2,1,0:T(8,128)(2,1)} %pad_maximum_fusion), calls=%async_computation | async-start | bytes 3932160 | tf_op jit(solution)/shard_map/all_to_all | solution.py:48
  21.3 142.9 %all-gather.4.cloned.1.call-start = ((), (), s32[]{:S(2)}) async-start(), calls=%async_computation.2 | async-start | bytes 4866048 | tf_op jit(solution)/shard_map/all_gather | solution.py:44
  23.4 50.6 %collective-permute-start = (bf16[192,384]{1,0:T(8,128)(2,1)}, bf16[192,384]{1,0:T(8,128)(2,1)}, u32[]{:S(2)}, u32[]{:S(2)}) collective-permute-start(bf16[192,384]{1,0:T(8,128)(2,1)} %get-tuple-element.49), channel_id=1, source_target_pairs={{0,16},{2,18},{4,20},{6,22},{8,24},{10,26},{12,28},{14,30},{16,0},... | collective-permute-start | bytes 442376 | tf_op jit(solution)/shard_map/ppermute | solution.py:73
  25.7 49.4 %collective-permute-start.1 = (bf16[192,384]{1,0:T(8,128)(2,1)}, bf16[192,384]{1,0:T(8,128)(2,1)}, u32[]{:S(2)}, u32[]{:S(2)}) collective-permute-start(bf16[192,384]{1,0:T(8,128)(2,1)} %get-tuple-element.50), channel_id=1, source_target_pairs={{0,18},{2,20},{4,22},{6,24},{8,26},{10,28},{12,30},{14,16},{16,2},... | collective-permute-start | bytes 442376 | tf_op jit(solution)/shard_map/ppermute | solution.py:73
  27.4 51.4 %collective-permute-start.2 = (bf16[192,384]{1,0:T(8,128)(2,1)}, bf16[192,384]{1,0:T(8,128)(2,1)}, u32[]{:S(2)}, u32[]{:S(2)}) collective-permute-start(bf16[192,384]{1,0:T(8,128)(2,1)} %get-tuple-element.51), channel_id=1, source_target_pairs={{0,20},{2,22},{4,24},{6,26},{8,28},{10,30},{12,16},{14,18},{16,4},... | collective-permute-start | bytes 442376 | tf_op jit(solution)/shard_map/ppermute | solution.py:73
  29.7 50.3 %collective-permute-start.3 = (bf16[192,384]{1,0:T(8,128)(2,1)}, bf16[192,384]{1,0:T(8,128)(2,1)}, u32[]{:S(2)}, u32[]{:S(2)}) collective-permute-start(bf16[192,384]{1,0:T(8,128)(2,1)} %get-tuple-element.52), channel_id=1, source_target_pairs={{0,22},{2,24},{4,26},{6,28},{8,30},{10,16},{12,18},{14,20},{16,6},... | collective-permute-start | bytes 442376 | tf_op jit(solution)/shard_map/ppermute | solution.py:73
  30.9 50.0 %collective-permute-start.4 = (bf16[192,384]{1,0:T(8,128)(2,1)}, bf16[192,384]{1,0:T(8,128)(2,1)}, u32[]{:S(2)}, u32[]{:S(2)}) collective-permute-start(bf16[192,384]{1,0:T(8,128)(2,1)} %get-tuple-element.53), channel_id=1, source_target_pairs={{0,24},{2,26},{4,28},{6,30},{8,16},{10,18},{12,20},{14,22},{16,8},... | collective-permute-start | bytes 442376 | tf_op jit(solution)/shard_map/ppermute | solution.py:73
  33.8 40.2 %copy-start.4 = (bf16[192,384]{1,0:T(8,128)(2,1)S(1)}, bf16[192,384]{1,0:T(8,128)(2,1)}, u32[]{:S(2)}) copy-start(bf16[192,384]{1,0:T(8,128)(2,1)} %get-tuple-element.55) | copy-start | bytes 442372
  33.8 41.2 %copy-start.3 = (bf16[192,384]{1,0:T(8,128)(2,1)S(1)}, bf16[192,384]{1,0:T(8,128)(2,1)}, u32[]{:S(2)}) copy-start(bf16[192,384]{1,0:T(8,128)(2,1)} %get-tuple-element.54) | copy-start | bytes 442372
  74.0 16.6 %collective-permute-start.5 = (bf16[192,384]{1,0:T(8,128)(2,1)S(1)}, bf16[192,384]{1,0:T(8,128)(2,1)S(1)}, u32[]{:S(2)}, u32[]{:S(2)}) collective-permute-start(bf16[192,384]{1,0:T(8,128)(2,1)S(1)} %copy-done.4), channel_id=1, source_target_pairs={{0,26},{2,28},{4,30},{6,16},{8,18},{10,20},{12,22},{14,24},{16,10}... | collective-permute-start | bytes 442376 | tf_op jit(solution)/shard_map/ppermute | solution.py:73
  75.1 25.2 %collective-permute-start.6 = (bf16[192,384]{1,0:T(8,128)(2,1)S(1)}, bf16[192,384]{1,0:T(8,128)(2,1)S(1)}, u32[]{:S(2)}, u32[]{:S(2)}) collective-permute-start(bf16[192,384]{1,0:T(8,128)(2,1)S(1)} %copy-done.3), channel_id=1, source_target_pairs={{0,28},{2,30},{4,16},{6,18},{8,20},{10,22},{12,24},{14,26},{16,12}... | collective-permute-start | bytes 442376 | tf_op jit(solution)/shard_map/ppermute | solution.py:73
  78.8 24.4 %collective-permute-start.7 = (bf16[192,384]{1,0:T(8,128)(2,1)}, bf16[192,384]{1,0:T(8,128)(2,1)S(1)}, u32[]{:S(2)}, u32[]{:S(2)}) collective-permute-start(bf16[192,384]{1,0:T(8,128)(2,1)} %get-tuple-element.48), channel_id=1, source_target_pairs={{0,30},{2,16},{4,18},{6,20},{8,22},{10,24},{12,26},{14,28},{16,14}... | collective-permute-start | bytes 442376 | tf_op jit(solution)/shard_map/ppermute | solution.py:73
  103.2 1.9 %copy-start.1 = (bf16[3,512,192]{1,2,0:T(8,128)(2,1)S(1)}, bf16[3,512,192]{1,2,0:T(8,128)(2,1)}, u32[]{:S(2)}) copy-start(bf16[3,512,192]{1,2,0:T(8,128)(2,1)} %custom-call.1) | copy-start | bytes 1769476
  106.2 1.5 copy-start
  110.4 1.4 copy-start
  114.4 1.4 copy-start
  120.9 23.0 %collective-permute-start.8 = (f32[2,48,1536]{2,1,0:T(8,128)S(1)}, f32[2,48,1536]{2,1,0:T(8,128)S(1)}, u32[]{:S(2)}, u32[]{:S(2)}) collective-permute-start(f32[2,48,1536]{2,1,0:T(8,128)S(1)} %dynamic-slice_bitcast_fusion), channel_id=1, source_target_pairs={{0,1},{1,0},{2,3},{3,2},{4,5},{5,4},{6,7},{7,6},{8,9},{9,8},{10,11... | collective-permute-start | bytes 1769480 | tf_op jit(solution)/shard_map/ppermute | solution.py:105
  123.3 39.4 %all-to-all-start.1 = ((bf16[8,192,192]{2,1,0:T(8,128)(2,1)}), bf16[8,192,192]{2,1,0:T(8,128)(2,1)S(1)}, u32[]{:S(2)}, u32[]{:S(2)}) async-start(bf16[8,192,192]{2,1,0:T(8,128)(2,1)} %bitcast.19), calls=%async_computation.1 | async-start | bytes 1572864 | tf_op jit(solution)/shard_map/all_to_all | solution.py:48
  144.0 8.2 %collective-permute-start.10 = (f32[48,1536]{1,0:T(8,128)S(1)}, f32[48,1536]{1,0:T(8,128)S(1)}, u32[]{:S(2)}, u32[]{:S(2)}) collective-permute-start(f32[48,1536]{1,0:T(8,128)S(1)} %get-tuple-element.56), channel_id=1, source_target_pairs={{0,2},{1,3},{2,18},{3,19},{4,6},{5,7},{6,22},{7,23},{8,10},{9,11},... | collective-permute-start | bytes 884744 | tf_op jit(solution)/shard_map/ppermute | solution.py:119
  144.0 18.0 %collective-permute-start.9 = (f32[48,1536]{1,0:T(8,128)S(1)}, f32[48,1536]{1,0:T(8,128)S(1)}, u32[]{:S(2)}, u32[]{:S(2)}) collective-permute-start(f32[48,1536]{1,0:T(8,128)S(1)} %get-tuple-element.57), channel_id=1, source_target_pairs={{0,0},{1,1},{2,16},{3,17},{4,4},{5,5},{6,20},{7,21},{8,8},{9,9},{1... | collective-permute-start | bytes 884744 | tf_op jit(solution)/shard_map/ppermute | solution.py:119
Sparse Core Ops, SparseCore 0:
  9.6 62.1 all-gather.5
  74.8 84.2 all-gather.3

commit v18 on v11

--- a/solution.py
+++ b/solution.py
@@ -51,7 +51,10 @@
         return tensor[0].reshape(row_count, head_count, head_width).transpose(1, 0, 2)
 
     side_index = lax.axis_index("side")
-    kv_raw = jnp.concatenate([by_head(key_vectors), by_head(value_vectors)], axis=2)
+    def by_lane(tensor):
+        return tensor[0].reshape(row_count, head_count, head_width)
+
+    kv_raw = jnp.concatenate([by_lane(key_vectors), by_lane(value_vectors)], axis=2)
     inner_index = lax.axis_index("inner")
     kv_crossed = []
     for step in range(1, side_count):
@@ -62,11 +65,13 @@
                 for i in range(head_count)
             ]
             outgoing = lax.dynamic_index_in_dim(
-                kv_raw, (inner_index + shift) % head_count, axis=0, keepdims=False
+                kv_raw, (inner_index + shift) % head_count, axis=1, keepdims=False
             )
             kv_crossed.append(lax.ppermute(outgoing, ("side", "inner"), perm))
-    stacked = jnp.concatenate([by_head(queries), kv_raw], axis=2)
-    got = a2a(stacked).reshape(head_count * row_count, 3 * head_width)
+    stacked = jnp.concatenate([by_lane(queries), kv_raw], axis=2)
+    got = lax.all_to_all(stacked, "inner", split_axis=1, concat_axis=0, tiled=True).reshape(
+        head_count * row_count, 3 * head_width
+    )
     query_here = got[:, :head_width]
     kv_all = jnp.concatenate([got[:, head_width:]] + kv_crossed, axis=0)
     key_all = kv_all[:, :head_width]

time: 175 us -> 174 us (level)
  starting transfers between devices: 27.5 us -> 33.9 us
  waiting for transfers between devices: 90.5 us -> 85.4 us
  local copies, waits for them, and re-layouts: 16.8 us -> 14.7 us
    all_to_all x0 -> x1, waiting for transfers between devices: none -> 41.1 us  [local(): lax.all_to_all(stacked, 'inner', split_axis=1, concat_axis=0, tiled=True)]
    all_to_all x2 -> x1, waiting for transfers between devices: 52.9 us -> 11.9 us  [a2a(): lax.all_to_all(tensor, 'inner', split_axis=0, concat_axis=0, tiled=True)]
    ppermute x8, starting transfers between devices: 12.5 us -> 19 us  [local(): kv_crossed.append(lax.ppermute(outgoing, ('side', 'inner'), perm))]
    ppermute x8, waiting for transfers between devices: 21.4 us -> 14.9 us  [local(): kv_crossed.append(lax.ppermute(outgoing, ('side', 'inner'), perm))]
    all_to_all x2 -> x1, starting transfers between devices: 9.15 us -> 3.69 us  [a2a(): lax.all_to_all(tensor, 'inner', split_axis=0, concat_axis=0, tiled=True)]
    all_to_all x0 -> x1, starting transfers between devices: none -> 5.31 us  [local(): lax.all_to_all(stacked, 'inner', split_axis=1, concat_axis=0, tiled=True)]
    another operation x4 -> x6, local copies, waits for them, and re-layouts: 3.98 us -> 3.39 us  [by_lane(): return tensor[0].reshape(row_count, head_count, head_width)]
  transfers between devices with their start and end apart: 15 -> 15, of which waited for: 7 -> 6; matrix products, arithmetic and copies ran while one was open for 23% -> 22% of each run, Pallas kernels for 0% -> 0%
where the time goes in v18:
time: 174 us; the launch traced here: 173 us
  waiting for transfers between devices  85.4 us (49%)
  starting transfers between devices  33.9 us (19%)
  matrix products  15.4 us (9%)
  local copies, waits for them, and re-layouts  14.7 us (8%)
  between operations  14.4 us (8%)
  other arithmetic  9.48 us (5%)
    all_to_all x1, waiting for transfers between devices, local(): lax.all_to_all(stacked, 'inner', split_axis=1, concat_axis=0, tiled=True)  41.1 us
    ppermute x8, starting transfers between devices, local(): kv_crossed.append(lax.ppermute(outgoing, ('side', 'inner'), perm))  19 us
    ppermute x8, waiting for transfers between devices, local(): kv_crossed.append(lax.ppermute(outgoing, ('side', 'inner'), perm))  14.9 us
    all_to_all x1, waiting for transfers between devices, a2a(): lax.all_to_all(tensor, 'inner', split_axis=0, concat_axis=0, tiled=True)  11.9 us
    ppermute x1, waiting for transfers between devices, local(): kept = kept + lax.ppermute(sent, 'dp', [(0, 1), (1, 0)])  8.34 us
    ppermute x2, waiting for transfers between devices, local(): arrived = lax.ppermute(outgoing, ALL, perm)  7.68 us
    unnamed x20, local copies, waits for them, and re-layouts  5.36 us
    all_to_all x1, starting transfers between devices, local(): lax.all_to_all(stacked, 'inner', split_axis=1, concat_axis=0, tiled=True)  5.31 us
  transfers between devices with their start and end apart: 15, of which 6 were waited for; matrix products, arithmetic and copies ran while one was open for 22% of the time, Pallas kernels for 0%

profile of v18, /device:TPU:1, one launch (start us, length us, event | category | flops | bytes accessed | tf_op | source)
XLA Modules:
  0.0 173.4 jit_solution(8789007625168693955)
XLA Ops:
  7.2 0.0 all-gather.6.cloned.1.call-start
  7.2 0.7 all-gather.6.cloned.1.call-update
  7.9 1.7 reshape_squeeze.10
  9.6 0.0 copy-start.3
  9.7 0.2 copy.13
  9.8 0.6 reshape_squeeze.11
  10.4 0.2 copy.14
  10.6 0.1 copy-done.3
  10.7 0.6 reshape_squeeze.9
  11.3 0.2 copy.12
  11.5 2.1 %pad_maximum_fusion = bf16[192,8,576]{2,0,1:T(8,128)(2,1)} fusion(bf16[192,8,192]{2,0,1:T(8,128)(2,1)S(1)} %copy.14, bf16[192,8,192]{2,0,1:T(8,128)(2,1)S(1)} %copy.13, bf16[192,8,192]{2,0,1:T(8,128)(2,1)S(1)} %copy.12), kind=kLoop, calls=%fused_computation.20 | loop fusion | flops 5308416 | bytes 3538944 | tf_op jit(solution)/shard_map/concatenate | solution.py:71
  13.5 5.3 %all-to-all-start = ((bf16[192,8,576]{2,0,1:T(8,128)(2,1)}), bf16[192,8,576]{2,0,1:T(8,128)(2,1)S(1)}, u32[]{:S(2)}, u32[]{:S(2)}) async-start(bf16[192,8,576]{2,0,1:T(8,128)(2,1)} %pad_maximum_fusion), calls=%async_computation | async-start | bytes 3932160 | tf_op jit(solution)/shard_map/all_to_all | solution.py:72
  18.8 0.7 all-gather.4.cloned.1.call-update
  19.7 1.2 fusion.41
  20.9 2.3 %collective-permute-start = (bf16[192,384]{1,0:T(8,128)(2,1)}, bf16[192,384]{1,0:T(8,128)(2,1)}, u32[]{:S(2)}, u32[]{:S(2)}) collective-permute-start(bf16[192,384]{1,0:T(8,128)(2,1)} %get-tuple-element.45), channel_id=1, source_target_pairs={{0,16},{2,18},{4,20},{6,22},{8,24},{10,26},{12,28},{14,30},{16,0},... | collective-permute-start | bytes 442376 | tf_op jit(solution)/shard_map/ppermute | solution.py:70
  23.2 1.7 collective-permute-start.1
  24.9 2.3 %collective-permute-start.2 = (bf16[192,384]{1,0:T(8,128)(2,1)}, bf16[192,384]{1,0:T(8,128)(2,1)}, u32[]{:S(2)}, u32[]{:S(2)}) collective-permute-start(bf16[192,384]{1,0:T(8,128)(2,1)} %get-tuple-element.47), channel_id=1, source_target_pairs={{0,20},{2,22},{4,24},{6,26},{8,28},{10,30},{12,16},{14,18},{16,4},... | collective-permute-start | bytes 442376 | tf_op jit(solution)/shard_map/ppermute | solution.py:70
  27.2 1.2 collective-permute-start.3
  28.4 2.1 %collective-permute-start.4 = (bf16[192,384]{1,0:T(8,128)(2,1)}, bf16[192,384]{1,0:T(8,128)(2,1)}, u32[]{:S(2)}, u32[]{:S(2)}) collective-permute-start(bf16[192,384]{1,0:T(8,128)(2,1)} %get-tuple-element.49), channel_id=1, source_target_pairs={{0,24},{2,26},{4,28},{6,30},{8,16},{10,18},{12,20},{14,22},{16,8},... | collective-permute-start | bytes 442376 | tf_op jit(solution)/shard_map/ppermute | solution.py:70
  30.5 0.8 fusion.34
  31.3 41.1 %all-to-all-done = bf16[192,8,576]{2,0,1:T(8,128)(2,1)S(1)} async-done(((bf16[192,8,576]{2,0,1:T(8,128)(2,1)}), bf16[192,8,576]{2,0,1:T(8,128)(2,1)S(1)}, u32[]{:S(2)}, u32[]{:S(2)}) %all-to-all-start) | async-done | bytes 1769504 | tf_op jit(solution)/shard_map/all_to_all | solution.py:72
  72.4 0.5 slice_dynamic-update-slice_fusion
  72.9 9.3 %collective-permute-start.5 = (bf16[192,384]{1,0:T(8,128)(2,1)S(1)}, bf16[192,384]{1,0:T(8,128)(2,1)S(1)}, u32[]{:S(2)}, u32[]{:S(2)}) collective-permute-start(bf16[192,384]{1,0:T(8,128)(2,1)S(1)} %copy-done.6), channel_id=1, source_target_pairs={{0,26},{2,28},{4,30},{6,16},{8,18},{10,20},{12,22},{14,24},{16,10}... | collective-permute-start | bytes 442376 | tf_op jit(solution)/shard_map/ppermute | solution.py:70
  82.3 0.9 constant_dynamic-update-slice_fusion.7
  83.2 0.1 collective-permute-start.6
  83.3 0.9 constant_dynamic-update-slice_fusion.6
  84.2 0.1 collective-permute-start.7
  84.3 0.9 constant_dynamic-update-slice_fusion.5
  85.3 0.9 constant_dynamic-update-slice_fusion.4
  86.2 0.9 constant_dynamic-update-slice_fusion.3
  87.2 0.1 slice.16
  87.2 12.0 %collective-permute-done.6 = bf16[192,384]{1,0:T(8,128)(2,1)S(1)} collective-permute-done((bf16[192,384]{1,0:T(8,128)(2,1)S(1)}, bf16[192,384]{1,0:T(8,128)(2,1)S(1)}, u32[]{:S(2)}, u32[]{:S(2)}) %collective-permute-start.6) | collective-permute-done | bytes 147488 | tf_op jit(solution)/shard_map/ppermute | solution.py:70
  99.3 2.9 %collective-permute-done.7 = bf16[192,384]{1,0:T(8,128)(2,1)S(1)} collective-permute-done((bf16[192,384]{1,0:T(8,128)(2,1)}, bf16[192,384]{1,0:T(8,128)(2,1)S(1)}, u32[]{:S(2)}, u32[]{:S(2)}) %collective-permute-start.7) | collective-permute-done | bytes 147488 | tf_op jit(solution)/shard_map/ppermute | solution.py:70
  102.2 0.0 copy-start
  102.2 1.9 %fusion.42 = (bf16[3072,192]{1,0:T(8,128)(2,1)}, bf16[3072,192]{1,0:T(8,128)(2,1)S(1)}) fusion(bf16[3072,384]{1,0:T(8,128)(2,1)S(1)} %constant_dynamic-update-slice_fusion), kind=kLoop, calls=%fused_computation.66 | loop fusion | bytes 4718592 | tf_op jit(solution)/shard_map/slice | solution.py:78
  104.1 12.1 %while.10 = (s32[]{:T(128)}, bf16[3,512,192]{1,2,0:T(8,128)(2,1)S(1)}, bf16[3,512,192]{2,1,0:T(8,128)(2,1)S(1)}, bf16[3072,192]{1,0:T(8,128)(2,1)S(1)}, bf16[3072,192]{1,0:T(8,128)(2,1)}, /*index=5*/s32[]{:T(128)}) while((s32[]{:T(128)}, bf16[3,512,192]{1,2,0:T(8,128)(2,1)S(1)}, bf16[3,512,192]{2,1,0:T(8,128)(2,1)S(1)}, ...), condition=%wide.region_3.4_spmd, body=%wide.region_0.3_spmd.sunk | while | flops 1220738048 | bytes 27207784 | solution.py:26
  104.1 1.1 multiply_reduce_fusion.2
  105.2 1.2 fusion.56
  106.4 0.3 copy-done.1
  106.6 1.5 fusion.57
  108.1 1.1 multiply_reduce_fusion.2
  109.3 1.2 fusion.56
  110.4 0.3 copy-done.1
  110.7 1.5 fusion.57
  112.2 1.1 multiply_reduce_fusion.2
  113.3 1.2 fusion.56
  114.4 0.2 copy-done.1
  114.7 1.5 fusion.57
  116.2 1.2 copy.17
  117.4 3.7 %all-to-all-start.1 = ((bf16[8,192,192]{2,1,0:T(8,128)(2,1)}), bf16[8,192,192]{2,1,0:T(8,128)(2,1)S(1)}, u32[]{:S(2)}, u32[]{:S(2)}) async-start(bf16[8,192,192]{2,1,0:T(8,128)(2,1)} %bitcast.16), calls=%async_computation.1 | async-start | bytes 1572864 | tf_op jit(solution)/shard_map/all_to_all | solution.py:48
  121.1 0.0 all-gather.6.cloned.1.call-done
  121.1 3.4 %fusion.23 = f32[2,2,48,1536]{3,2,1,0:T(8,128)S(1)} fusion(bf16[2,2,48,1536]{3,2,1,0:T(8,128)(2,1)S(1)} %bitcast.73, bf16[1,1536,1536]{2,1,0:T(8,128)(2,1)} %all-gather.6.cloned.1.call-done), kind=kOutput, calls=%fused_computation.16 | convolution fusion | flops 905969664 | bytes 6488064 | tf_op jit(solution)/shard_map/dot_general | solution.py:82
  124.6 1.3 collective-permute-start.8
  125.8 11.9 %all-to-all-done.1 = bf16[8,192,192]{2,1,0:T(8,128)(2,1)S(1)} async-done(((bf16[8,192,192]{2,1,0:T(8,128)(2,1)}), bf16[8,192,192]{2,1,0:T(8,128)(2,1)S(1)}, u32[]{:S(2)}, u32[]{:S(2)}) %all-to-all-start.1) | async-done | bytes 589856 | tf_op jit(solution)/shard_map/all_to_all | solution.py:48
  137.8 0.4 copy.18
  138.2 1.5 reshape.26
  139.7 8.3 %collective-permute-done.8 = f32[2,48,1536]{2,1,0:T(8,128)} collective-permute-done((f32[2,48,1536]{2,1,0:T(8,128)S(1)}, f32[2,48,1536]{2,1,0:T(8,128)}, u32[]{:S(2)}, u32[]{:S(2)}) %collective-permute-start.8) | collective-permute-done | bytes 589856 | tf_op jit(solution)/shard_map/ppermute | solution.py:99
  148.1 1.1 bitcast_add_fusion
  149.2 1.1 collective-permute-start.10
  150.4 3.5 %collective-permute-start.9 = (f32[48,1536]{1,0:T(8,128)S(1)}, f32[48,1536]{1,0:T(8,128)S(1)}, u32[]{:S(2)}, u32[]{:S(2)}) collective-permute-start(f32[48,1536]{1,0:T(8,128)S(1)} %get-tuple-element.53), channel_id=1, source_target_pairs={{0,0},{1,1},{2,4},{3,5},{4,8},{5,9},{6,12},{7,13},{8,16},{9,17},{1... | collective-permute-start | bytes 884744 | tf_op jit(solution)/shard_map/ppermute | solution.py:113
  153.8 0.0 all-gather.4.cloned.1.call-done
  153.9 4.2 %fusion.25 = bf16[1,192,1536]{2,1,0:T(8,128)(2,1)} fusion(bf16[192,1536]{1,0:T(8,128)(2,1)S(1)} %copy-done.4, bf16[1536,1536]{1,0:T(8,128)(2,1)} %all-gather.4.cloned.1.call-done), kind=kOutput, calls=%fused_computation.19 | convolution fusion | flops 906264576 | bytes 5898240 | tf_op jit(solution)/shard_map/dot_general | solution.py:88
  158.1 7.7 %collective-permute-done.9 = f32[48,1536]{1,0:T(8,128)S(1)} collective-permute-done((f32[48,1536]{1,0:T(8,128)S(1)}, f32[48,1536]{1,0:T(8,128)S(1)}, u32[]{:S(2)}, u32[]{:S(2)}) %collective-permute-start.9) | collective-permute-done | bytes 294944 | tf_op jit(solution)/shard_map/ppermute | solution.py:113
  165.8 0.7 add.135
  (27 shorter events, 0.3 us)
Async XLA Ops:
  7.2 2.7 %copy-start.2 = (bf16[1,192,1536]{2,1,0:T(8,128)(2,1)S(1)}, bf16[1,192,1536]{2,1,0:T(8,128)(2,1)}, u32[]{:S(2)}) copy-start(bf16[1,192,1536]{2,1,0:T(8,128)(2,1)} %param.9) | copy-start | bytes 1769476
  7.2 113.9 %all-gather.6.cloned.1.call-start = ((), (), s32[]{:S(2)}) async-start(), calls=%async_computation.3 | async-start | bytes 5308416 | tf_op jit(solution)/shard_map/all_gather | solution.py:45
  9.6 1.1 copy-start.3
  13.5 58.9 %all-to-all-start = ((bf16[192,8,576]{2,0,1:T(8,128)(2,1)}), bf16[192,8,576]{2,0,1:T(8,128)(2,1)S(1)}, u32[]{:S(2)}, u32[]{:S(2)}) async-start(bf16[192,8,576]{2,0,1:T(8,128)(2,1)} %pad_maximum_fusion), calls=%async_computation | async-start | bytes 3932160 | tf_op jit(solution)/shard_map/all_to_all | solution.py:72
  18.8 135.0 %all-gather.4.cloned.1.call-start = ((), (), s32[]{:S(2)}) async-start(), calls=%async_computation.2 | async-start | bytes 4866048 | tf_op jit(solution)/shard_map/all_gather | solution.py:44
  20.9 52.0 %collective-permute-start = (bf16[192,384]{1,0:T(8,128)(2,1)}, bf16[192,384]{1,0:T(8,128)(2,1)}, u32[]{:S(2)}, u32[]{:S(2)}) collective-permute-start(bf16[192,384]{1,0:T(8,128)(2,1)} %get-tuple-element.45), channel_id=1, source_target_pairs={{0,16},{2,18},{4,20},{6,22},{8,24},{10,26},{12,28},{14,30},{16,0},... | collective-permute-start | bytes 442376 | tf_op jit(solution)/shard_map/ppermute | solution.py:70
  23.2 60.0 %collective-permute-start.1 = (bf16[192,384]{1,0:T(8,128)(2,1)}, bf16[192,384]{1,0:T(8,128)(2,1)}, u32[]{:S(2)}, u32[]{:S(2)}) collective-permute-start(bf16[192,384]{1,0:T(8,128)(2,1)} %get-tuple-element.46), channel_id=1, source_target_pairs={{0,18},{2,20},{4,22},{6,24},{8,26},{10,28},{12,30},{14,16},{16,2},... | collective-permute-start | bytes 442376 | tf_op jit(solution)/shard_map/ppermute | solution.py:70
  24.9 59.3 %collective-permute-start.2 = (bf16[192,384]{1,0:T(8,128)(2,1)}, bf16[192,384]{1,0:T(8,128)(2,1)}, u32[]{:S(2)}, u32[]{:S(2)}) collective-permute-start(bf16[192,384]{1,0:T(8,128)(2,1)} %get-tuple-element.47), channel_id=1, source_target_pairs={{0,20},{2,22},{4,24},{6,26},{8,28},{10,30},{12,16},{14,18},{16,4},... | collective-permute-start | bytes 442376 | tf_op jit(solution)/shard_map/ppermute | solution.py:70
  27.2 58.1 %collective-permute-start.3 = (bf16[192,384]{1,0:T(8,128)(2,1)}, bf16[192,384]{1,0:T(8,128)(2,1)}, u32[]{:S(2)}, u32[]{:S(2)}) collective-permute-start(bf16[192,384]{1,0:T(8,128)(2,1)} %get-tuple-element.48), channel_id=1, source_target_pairs={{0,22},{2,24},{4,26},{6,28},{8,30},{10,16},{12,18},{14,20},{16,6},... | collective-permute-start | bytes 442376 | tf_op jit(solution)/shard_map/ppermute | solution.py:70
  28.4 57.8 %collective-permute-start.4 = (bf16[192,384]{1,0:T(8,128)(2,1)}, bf16[192,384]{1,0:T(8,128)(2,1)}, u32[]{:S(2)}, u32[]{:S(2)}) collective-permute-start(bf16[192,384]{1,0:T(8,128)(2,1)} %get-tuple-element.49), channel_id=1, source_target_pairs={{0,24},{2,26},{4,28},{6,30},{8,16},{10,18},{12,20},{14,22},{16,8},... | collective-permute-start | bytes 442376 | tf_op jit(solution)/shard_map/ppermute | solution.py:70
  31.3 41.6 %copy-start.6 = (bf16[192,384]{1,0:T(8,128)(2,1)S(1)}, bf16[192,384]{1,0:T(8,128)(2,1)}, u32[]{:S(2)}) copy-start(bf16[192,384]{1,0:T(8,128)(2,1)} %get-tuple-element.51) | copy-start | bytes 442372
  31.3 51.9 %copy-start.5 = (bf16[192,384]{1,0:T(8,128)(2,1)S(1)}, bf16[192,384]{1,0:T(8,128)(2,1)}, u32[]{:S(2)}) copy-start(bf16[192,384]{1,0:T(8,128)(2,1)} %get-tuple-element.50) | copy-start | bytes 442372
  72.9 14.2 %collective-permute-start.5 = (bf16[192,384]{1,0:T(8,128)(2,1)S(1)}, bf16[192,384]{1,0:T(8,128)(2,1)S(1)}, u32[]{:S(2)}, u32[]{:S(2)}) collective-permute-start(bf16[192,384]{1,0:T(8,128)(2,1)S(1)} %copy-done.6), channel_id=1, source_target_pairs={{0,26},{2,28},{4,30},{6,16},{8,18},{10,20},{12,22},{14,24},{16,10}... | collective-permute-start | bytes 442376 | tf_op jit(solution)/shard_map/ppermute | solution.py:70
  83.2 16.0 %collective-permute-start.6 = (bf16[192,384]{1,0:T(8,128)(2,1)S(1)}, bf16[192,384]{1,0:T(8,128)(2,1)S(1)}, u32[]{:S(2)}, u32[]{:S(2)}) collective-permute-start(bf16[192,384]{1,0:T(8,128)(2,1)S(1)} %copy-done.5), channel_id=1, source_target_pairs={{0,28},{2,30},{4,16},{6,18},{8,20},{10,22},{12,24},{14,26},{16,12}... | collective-permute-start | bytes 442376 | tf_op jit(solution)/shard_map/ppermute | solution.py:70
  84.2 17.9 %collective-permute-start.7 = (bf16[192,384]{1,0:T(8,128)(2,1)}, bf16[192,384]{1,0:T(8,128)(2,1)S(1)}, u32[]{:S(2)}, u32[]{:S(2)}) collective-permute-start(bf16[192,384]{1,0:T(8,128)(2,1)} %get-tuple-element.44), channel_id=1, source_target_pairs={{0,30},{2,16},{4,18},{6,20},{8,22},{10,24},{12,26},{14,28},{16,14}... | collective-permute-start | bytes 442376 | tf_op jit(solution)/shard_map/ppermute | solution.py:70
  102.2 1.9 %copy-start = (bf16[3,512,192]{1,2,0:T(8,128)(2,1)S(1)}, bf16[3,512,192]{1,2,0:T(8,128)(2,1)}, u32[]{:S(2)}) copy-start(bf16[3,512,192]{1,2,0:T(8,128)(2,1)} %custom-call.1) | copy-start | bytes 1769476
  105.2 1.4 copy-start.1
  109.3 1.4 copy-start.1
  113.3 1.4 copy-start.1
  117.4 20.4 %all-to-all-start.1 = ((bf16[8,192,192]{2,1,0:T(8,128)(2,1)}), bf16[8,192,192]{2,1,0:T(8,128)(2,1)S(1)}, u32[]{:S(2)}, u32[]{:S(2)}) async-start(bf16[8,192,192]{2,1,0:T(8,128)(2,1)} %bitcast.16), calls=%async_computation.1 | async-start | bytes 1572864 | tf_op jit(solution)/shard_map/all_to_all | solution.py:48
  124.6 23.5 %collective-permute-start.8 = (f32[2,48,1536]{2,1,0:T(8,128)S(1)}, f32[2,48,1536]{2,1,0:T(8,128)}, u32[]{:S(2)}, u32[]{:S(2)}) collective-permute-start(f32[2,48,1536]{2,1,0:T(8,128)S(1)} %dynamic-slice_bitcast_fusion), channel_id=1, source_target_pairs={{0,1},{1,0},{2,3},{3,2},{4,5},{5,4},{6,7},{7,6},{8,9},{9,8},{10,11... | collective-permute-start | bytes 1769480 | tf_op jit(solution)/shard_map/ppermute | solution.py:99
  139.7 14.1 %copy-start.4 = (bf16[192,1536]{1,0:T(8,128)(2,1)S(1)}, bf16[192,1536]{1,0:T(8,128)(2,1)}, u32[]{:S(2)}) copy-start(bf16[192,1536]{1,0:T(8,128)(2,1)} %reshape.26) | copy-start | bytes 1769476
  149.2 8.9 %collective-permute-start.10 = (f32[48,1536]{1,0:T(8,128)S(1)}, f32[48,1536]{1,0:T(8,128)S(1)}, u32[]{:S(2)}, u32[]{:S(2)}) collective-permute-start(f32[48,1536]{1,0:T(8,128)S(1)} %get-tuple-element.52), channel_id=1, source_target_pairs={{0,2},{1,3},{2,6},{3,7},{4,10},{5,11},{6,14},{7,15},{8,18},{9,19},... | collective-permute-start | bytes 884744 | tf_op jit(solution)/shard_map/ppermute | solution.py:113
  150.4 15.4 %collective-permute-start.9 = (f32[48,1536]{1,0:T(8,128)S(1)}, f32[48,1536]{1,0:T(8,128)S(1)}, u32[]{:S(2)}, u32[]{:S(2)}) collective-permute-start(f32[48,1536]{1,0:T(8,128)S(1)} %get-tuple-element.53), channel_id=1, source_target_pairs={{0,0},{1,1},{2,4},{3,5},{4,8},{5,9},{6,12},{7,13},{8,16},{9,17},{1... | collective-permute-start | bytes 884744 | tf_op jit(solution)/shard_map/ppermute | solution.py:113
Sparse Core Ops, SparseCore 0:
  9.6 63.6 all-gather.5
  76.2 77.0 all-gather.3

commit v19 on v18

--- a/solution.py
+++ b/solution.py
@@ -72,6 +72,9 @@
     got = lax.all_to_all(stacked, "inner", split_axis=1, concat_axis=0, tiled=True).reshape(
         head_count * row_count, 3 * head_width
     )
+    early = min(3, len(kv_crossed))
+    kv_early, got = lax.optimization_barrier((kv_crossed[:early], got))
+    kv_crossed = list(kv_early) + kv_crossed[early:]
     query_here = got[:, :head_width]
     kv_all = jnp.concatenate([got[:, head_width:]] + kv_crossed, axis=0)
     key_all = kv_all[:, :head_width]

time: 174 us -> 171 us (0.983)
  waiting for transfers between devices: 85.4 us -> 81.3 us
    all_to_all x1, waiting for transfers between devices: 41.1 us -> 0.01 us  [local(): lax.all_to_all(stacked, 'inner', split_axis=1, concat_axis=0, tiled=True)]
    ppermute x8, waiting for transfers between devices: 14.9 us -> 55.2 us  [local(): kv_crossed.append(lax.ppermute(outgoing, ('side', 'inner'), perm))]
    ppermute x1, waiting for transfers between devices: 8.34 us -> 4.28 us  [local(): kept = kept + lax.ppermute(sent, 'dp', [(0, 1), (1, 0)])]
    unnamed x20 -> x16, local copies, waits for them, and re-layouts: 5.36 us -> 5.34 us
  transfers between devices with their start and end apart: 15 -> 15, of which waited for: 6 -> 11; matrix products, arithmetic and copies ran while one was open for 22% -> 23% of each run, Pallas kernels for 0% -> 0%
where the time goes in v19:
time: 171 us; the launch traced here: 170 us
  waiting for transfers between devices  81.3 us (48%)
  starting transfers between devices  34.3 us (20%)
  matrix products  16 us (9%)
  local copies, waits for them, and re-layouts  14.7 us (9%)
  between operations  14.3 us (8%)
  other arithmetic  9.53 us (6%)
    ppermute x8, waiting for transfers between devices, local(): kv_crossed.append(lax.ppermute(outgoing, ('side', 'inner'), perm))  55.2 us
    ppermute x8, starting transfers between devices, local(): kv_crossed.append(lax.ppermute(outgoing, ('side', 'inner'), perm))  18 us
    all_to_all x1, waiting for transfers between devices, a2a(): lax.all_to_all(tensor, 'inner', split_axis=0, concat_axis=0, tiled=True)  12.5 us
    ppermute x2, waiting for transfers between devices, local(): arrived = lax.ppermute(outgoing, ALL, perm)  7.89 us
    unnamed x16, local copies, waits for them, and re-layouts  5.34 us
    all_to_all x1, starting transfers between devices, local(): lax.all_to_all(stacked, 'inner', split_axis=1, concat_axis=0, tiled=True)  5.31 us
    all_to_all x1, starting transfers between devices, a2a(): lax.all_to_all(tensor, 'inner', split_axis=0, concat_axis=0, tiled=True)  5.07 us
    ppermute x2, starting transfers between devices, local(): arrived = lax.ppermute(outgoing, ALL, perm)  4.61 us
  transfers between devices with their start and end apart: 15, of which 11 were waited for; matrix products, arithmetic and copies ran while one was open for 23% of the time, Pallas kernels for 0%

profile of v19, /device:TPU:1, one launch (start us, length us, event | category | flops | bytes accessed | tf_op | source)
XLA Modules:
  0.0 170.3 jit_solution(148932651752076561)
XLA Ops:
  7.2 0.0 all-gather.6.cloned.1.call-start
  7.2 0.7 all-gather.6.cloned.1.call-update
  7.9 1.7 %reshape_squeeze.9 = bf16[192,8,192]{2,1,0:T(8,128)(2,1)S(1)} reshape(bf16[1,192,1536]{2,1,0:T(8,128)(2,1)} %param.8) | data formatting | bytes 1179648 | tf_op jit(solution)/shard_map/reshape;squeeze | solution.py:55
  9.7 0.2 copy.12
  9.8 0.6 reshape_squeeze.10
  10.4 0.2 copy.13
  10.6 0.1 copy-done.3
  10.7 0.6 reshape_squeeze.11
  11.3 0.2 copy.14
  11.5 2.1 %pad_maximum_fusion = bf16[192,8,576]{2,0,1:T(8,128)(2,1)} fusion(bf16[192,8,192]{2,0,1:T(8,128)(2,1)S(1)} %copy.13, bf16[192,8,192]{2,0,1:T(8,128)(2,1)S(1)} %copy.12, bf16[192,8,192]{2,0,1:T(8,128)(2,1)S(1)} %copy.14), kind=kLoop, calls=%fused_computation.20 | loop fusion | flops 5308416 | bytes 3538944 | tf_op jit(solution)/shard_map/concatenate | solution.py:71
  13.5 5.3 %all-to-all-start = ((bf16[192,8,576]{2,0,1:T(8,128)(2,1)}), bf16[192,8,576]{2,0,1:T(8,128)(2,1)S(1)}, u32[]{:S(2)}, u32[]{:S(2)}) async-start(bf16[192,8,576]{2,0,1:T(8,128)(2,1)} %pad_maximum_fusion), calls=%async_computation | async-start | bytes 3932160 | tf_op jit(solution)/shard_map/all_to_all | solution.py:72
  18.9 0.7 all-gather.4.cloned.1.call-update
  19.7 1.2 fusion.41
  20.9 2.3 %collective-permute-start = (bf16[192,384]{1,0:T(8,128)(2,1)}, bf16[192,384]{1,0:T(8,128)(2,1)}, u32[]{:S(2)}, u32[]{:S(2)}) collective-permute-start(bf16[192,384]{1,0:T(8,128)(2,1)} %get-tuple-element.53), channel_id=1, source_target_pairs={{0,16},{2,18},{4,20},{6,22},{8,24},{10,26},{12,28},{14,30},{16,0},... | collective-permute-start | bytes 442376 | tf_op jit(solution)/shard_map/ppermute | solution.py:70
  23.2 1.7 collective-permute-start.1
  24.9 2.3 %collective-permute-start.2 = (bf16[192,384]{1,0:T(8,128)(2,1)}, bf16[192,384]{1,0:T(8,128)(2,1)}, u32[]{:S(2)}, u32[]{:S(2)}) collective-permute-start(bf16[192,384]{1,0:T(8,128)(2,1)} %get-tuple-element.55), channel_id=1, source_target_pairs={{0,20},{2,22},{4,24},{6,26},{8,28},{10,30},{12,16},{14,18},{16,4},... | collective-permute-start | bytes 442376 | tf_op jit(solution)/shard_map/ppermute | solution.py:70
  27.2 1.2 collective-permute-start.3
  28.4 2.1 %collective-permute-start.4 = (bf16[192,384]{1,0:T(8,128)(2,1)}, bf16[192,384]{1,0:T(8,128)(2,1)}, u32[]{:S(2)}, u32[]{:S(2)}) collective-permute-start(bf16[192,384]{1,0:T(8,128)(2,1)} %get-tuple-element.57), channel_id=1, source_target_pairs={{0,24},{2,26},{4,28},{6,30},{8,16},{10,18},{12,20},{14,22},{16,8},... | collective-permute-start | bytes 442376 | tf_op jit(solution)/shard_map/ppermute | solution.py:70
  30.5 0.9 fusion.34
  31.4 30.7 %collective-permute-done = bf16[192,384]{1,0:T(8,128)(2,1)} collective-permute-done((bf16[192,384]{1,0:T(8,128)(2,1)}, bf16[192,384]{1,0:T(8,128)(2,1)}, u32[]{:S(2)}, u32[]{:S(2)}) %collective-permute-start) | collective-permute-done | bytes 147488 | tf_op jit(solution)/shard_map/ppermute | solution.py:70
  62.1 3.2 %collective-permute-start.5 = (bf16[192,384]{1,0:T(8,128)(2,1)}, bf16[192,384]{1,0:T(8,128)(2,1)S(1)}, u32[]{:S(2)}, u32[]{:S(2)}) collective-permute-start(bf16[192,384]{1,0:T(8,128)(2,1)} %get-tuple-element.59), channel_id=1, source_target_pairs={{0,26},{2,28},{4,30},{6,16},{8,18},{10,20},{12,22},{14,24},{16,10}... | collective-permute-start | bytes 442376 | tf_op jit(solution)/shard_map/ppermute | solution.py:70
  65.3 0.5 collective-permute-done.1
  65.8 5.2 %collective-permute-start.6 = (bf16[192,384]{1,0:T(8,128)(2,1)}, bf16[192,384]{1,0:T(8,128)(2,1)S(1)}, u32[]{:S(2)}, u32[]{:S(2)}) collective-permute-start(bf16[192,384]{1,0:T(8,128)(2,1)} %get-tuple-element.58), channel_id=1, source_target_pairs={{0,28},{2,30},{4,16},{6,18},{8,20},{10,22},{12,24},{14,26},{16,12}... | collective-permute-start | bytes 442376 | tf_op jit(solution)/shard_map/ppermute | solution.py:70
  71.0 2.7 %collective-permute-done.2 = bf16[192,384]{1,0:T(8,128)(2,1)} collective-permute-done((bf16[192,384]{1,0:T(8,128)(2,1)}, bf16[192,384]{1,0:T(8,128)(2,1)}, u32[]{:S(2)}, u32[]{:S(2)}) %collective-permute-start.2) | collective-permute-done | bytes 147488 | tf_op jit(solution)/shard_map/ppermute | solution.py:70
  73.8 0.5 slice_dynamic-update-slice_fusion
  74.2 0.9 constant_dynamic-update-slice_fusion.7
  75.2 0.9 constant_dynamic-update-slice_fusion.6
  76.1 0.9 constant_dynamic-update-slice_fusion.5
  77.1 0.5 collective-permute-done.3
  77.6 0.9 constant_dynamic-update-slice_fusion.4
  78.5 0.7 collective-permute-done.4
  79.2 0.9 constant_dynamic-update-slice_fusion.3
  80.1 3.1 %collective-permute-done.5 = bf16[192,384]{1,0:T(8,128)(2,1)S(1)} collective-permute-done((bf16[192,384]{1,0:T(8,128)(2,1)}, bf16[192,384]{1,0:T(8,128)(2,1)S(1)}, u32[]{:S(2)}, u32[]{:S(2)}) %collective-permute-start.5) | collective-permute-done | bytes 147488 | tf_op jit(solution)/shard_map/ppermute | solution.py:70
  83.2 0.1 slice.12
  83.3 13.7 %collective-permute-done.6 = bf16[192,384]{1,0:T(8,128)(2,1)S(1)} collective-permute-done((bf16[192,384]{1,0:T(8,128)(2,1)}, bf16[192,384]{1,0:T(8,128)(2,1)S(1)}, u32[]{:S(2)}, u32[]{:S(2)}) %collective-permute-start.6) | collective-permute-done | bytes 147488 | tf_op jit(solution)/shard_map/ppermute | solution.py:70
  97.1 3.3 %collective-permute-done.7 = bf16[192,384]{1,0:T(8,128)(2,1)S(1)} collective-permute-done((bf16[192,384]{1,0:T(8,128)(2,1)}, bf16[192,384]{1,0:T(8,128)(2,1)S(1)}, u32[]{:S(2)}, u32[]{:S(2)}) %collective-permute-start.7) | collective-permute-done | bytes 147488 | tf_op jit(solution)/shard_map/ppermute | solution.py:70
  100.4 1.9 %fusion.42 = (bf16[3072,192]{1,0:T(8,128)(2,1)}, bf16[3072,192]{1,0:T(8,128)(2,1)S(1)}) fusion(bf16[3072,384]{1,0:T(8,128)(2,1)S(1)} %constant_dynamic-update-slice_fusion), kind=kLoop, calls=%fused_computation.66 | loop fusion | bytes 4718592 | tf_op jit(solution)/shard_map/slice | solution.py:81
  102.3 12.1 %while.10 = (s32[]{:T(128)}, bf16[3,512,192]{1,2,0:T(8,128)(2,1)S(1)}, bf16[3,512,192]{2,1,0:T(8,128)(2,1)S(1)}, bf16[3072,192]{1,0:T(8,128)(2,1)S(1)}, bf16[3072,192]{1,0:T(8,128)(2,1)}, /*index=5*/s32[]{:T(128)}) while((s32[]{:T(128)}, bf16[3,512,192]{1,2,0:T(8,128)(2,1)S(1)}, bf16[3,512,192]{2,1,0:T(8,128)(2,1)S(1)}, ...), condition=%wide.region_3.4_spmd, body=%wide.region_0.3_spmd.sunk | while | flops 1220738048 | bytes 27207784 | solution.py:26
  102.3 1.1 multiply_reduce_fusion.2
  103.4 1.2 fusion.56
  104.6 0.2 copy-done.1
  104.8 1.5 fusion.57
  106.3 1.1 multiply_reduce_fusion.2
  107.4 1.2 fusion.56
  108.6 0.3 copy-done.1
  108.9 1.5 fusion.57
  110.3 1.1 multiply_reduce_fusion.2
  111.5 1.2 fusion.56
  112.6 0.3 copy-done.1
  112.9 1.5 fusion.57
  114.4 1.2 copy.17
  115.6 5.1 %all-to-all-start.1 = ((bf16[8,192,192]{2,1,0:T(8,128)(2,1)}), bf16[8,192,192]{2,1,0:T(8,128)(2,1)S(1)}, u32[]{:S(2)}, u32[]{:S(2)}) async-start(bf16[8,192,192]{2,1,0:T(8,128)(2,1)} %bitcast.14), calls=%async_computation.1 | async-start | bytes 1572864 | tf_op jit(solution)/shard_map/all_to_all | solution.py:48
  120.6 4.1 %fusion.23 = f32[2,2,48,1536]{3,2,1,0:T(8,128)S(1)} fusion(bf16[2,2,48,1536]{3,2,1,0:T(8,128)(2,1)S(1)} %bitcast.73, bf16[1,1536,1536]{2,1,0:T(8,128)(2,1)} %all-gather.6.cloned.1.call-done), kind=kOutput, calls=%fused_computation.16 | convolution fusion | flops 905969664 | bytes 6488064 | tf_op jit(solution)/shard_map/dot_general | solution.py:85
  124.8 1.3 collective-permute-start.8
  126.0 12.5 %all-to-all-done.1 = bf16[8,192,192]{2,1,0:T(8,128)(2,1)S(1)} async-done(((bf16[8,192,192]{2,1,0:T(8,128)(2,1)}), bf16[8,192,192]{2,1,0:T(8,128)(2,1)S(1)}, u32[]{:S(2)}, u32[]{:S(2)}) %all-to-all-start.1) | async-done | bytes 589856 | tf_op jit(solution)/shard_map/all_to_all | solution.py:48
  138.5 0.4 copy.18
  139.0 1.5 reshape.26
  140.5 4.3 %collective-permute-done.8 = f32[2,48,1536]{2,1,0:T(8,128)} collective-permute-done((f32[2,48,1536]{2,1,0:T(8,128)S(1)}, f32[2,48,1536]{2,1,0:T(8,128)}, u32[]{:S(2)}, u32[]{:S(2)}) %collective-permute-start.8) | collective-permute-done | bytes 589856 | tf_op jit(solution)/shard_map/ppermute | solution.py:102
  144.7 1.1 bitcast_add_fusion
  145.9 1.3 collective-permute-start.10
  147.2 3.3 %collective-permute-start.9 = (f32[48,1536]{1,0:T(8,128)S(1)}, f32[48,1536]{1,0:T(8,128)S(1)}, u32[]{:S(2)}, u32[]{:S(2)}) collective-permute-start(f32[48,1536]{1,0:T(8,128)S(1)} %get-tuple-element.61), channel_id=1, source_target_pairs={{0,0},{1,1},{2,4},{3,5},{4,8},{5,9},{6,12},{7,13},{8,16},{9,17},{1... | collective-permute-start | bytes 884744 | tf_op jit(solution)/shard_map/ppermute | solution.py:116
  150.6 4.2 %fusion.25 = bf16[1,192,1536]{2,1,0:T(8,128)(2,1)} fusion(bf16[192,1536]{1,0:T(8,128)(2,1)S(1)} %copy-done.4, bf16[1536,1536]{1,0:T(8,128)(2,1)} %all-gather.4.cloned.1.call-done), kind=kOutput, calls=%fused_computation.19 | convolution fusion | flops 906264576 | bytes 5898240 | tf_op jit(solution)/shard_map/dot_general | solution.py:91
  154.8 7.9 %collective-permute-done.9 = f32[48,1536]{1,0:T(8,128)S(1)} collective-permute-done((f32[48,1536]{1,0:T(8,128)S(1)}, f32[48,1536]{1,0:T(8,128)S(1)}, u32[]{:S(2)}, u32[]{:S(2)}) %collective-permute-start.9) | collective-permute-done | bytes 294944 | tf_op jit(solution)/shard_map/ppermute | solution.py:116
  162.7 0.7 add.135
  (23 shorter events, 0.3 us)
Async XLA Ops:
  7.2 2.7 %copy-start.2 = (bf16[1,192,1536]{2,1,0:T(8,128)(2,1)S(1)}, bf16[1,192,1536]{2,1,0:T(8,128)(2,1)}, u32[]{:S(2)}) copy-start(bf16[1,192,1536]{2,1,0:T(8,128)(2,1)} %param.9) | copy-start | bytes 1769476
  7.2 113.5 %all-gather.6.cloned.1.call-start = ((), (), s32[]{:S(2)}) async-start(), calls=%async_computation.3 | async-start | bytes 5308416 | tf_op jit(solution)/shard_map/all_gather | solution.py:45
  9.6 1.1 copy-start.3
  13.5 60.2 %all-to-all-start = ((bf16[192,8,576]{2,0,1:T(8,128)(2,1)}), bf16[192,8,576]{2,0,1:T(8,128)(2,1)S(1)}, u32[]{:S(2)}, u32[]{:S(2)}) async-start(bf16[192,8,576]{2,0,1:T(8,128)(2,1)} %pad_maximum_fusion), calls=%async_computation | async-start | bytes 3932160 | tf_op jit(solution)/shard_map/all_to_all | solution.py:72
  18.9 131.7 %all-gather.4.cloned.1.call-start = ((), (), s32[]{:S(2)}) async-start(), calls=%async_computation.2 | async-start | bytes 4866048 | tf_op jit(solution)/shard_map/all_gather | solution.py:44
  20.9 41.2 %collective-permute-start = (bf16[192,384]{1,0:T(8,128)(2,1)}, bf16[192,384]{1,0:T(8,128)(2,1)}, u32[]{:S(2)}, u32[]{:S(2)}) collective-permute-start(bf16[192,384]{1,0:T(8,128)(2,1)} %get-tuple-element.53), channel_id=1, source_target_pairs={{0,16},{2,18},{4,20},{6,22},{8,24},{10,26},{12,28},{14,30},{16,0},... | collective-permute-start | bytes 442376 | tf_op jit(solution)/shard_map/ppermute | solution.py:70
  23.2 42.6 %collective-permute-start.1 = (bf16[192,384]{1,0:T(8,128)(2,1)}, bf16[192,384]{1,0:T(8,128)(2,1)}, u32[]{:S(2)}, u32[]{:S(2)}) collective-permute-start(bf16[192,384]{1,0:T(8,128)(2,1)} %get-tuple-element.54), channel_id=1, source_target_pairs={{0,18},{2,20},{4,22},{6,24},{8,26},{10,28},{12,30},{14,16},{16,2},... | collective-permute-start | bytes 442376 | tf_op jit(solution)/shard_map/ppermute | solution.py:70
  24.9 48.8 %collective-permute-start.2 = (bf16[192,384]{1,0:T(8,128)(2,1)}, bf16[192,384]{1,0:T(8,128)(2,1)}, u32[]{:S(2)}, u32[]{:S(2)}) collective-permute-start(bf16[192,384]{1,0:T(8,128)(2,1)} %get-tuple-element.55), channel_id=1, source_target_pairs={{0,20},{2,22},{4,24},{6,26},{8,28},{10,30},{12,16},{14,18},{16,4},... | collective-permute-start | bytes 442376 | tf_op jit(solution)/shard_map/ppermute | solution.py:70
  27.2 50.3 %collective-permute-start.3 = (bf16[192,384]{1,0:T(8,128)(2,1)}, bf16[192,384]{1,0:T(8,128)(2,1)}, u32[]{:S(2)}, u32[]{:S(2)}) collective-permute-start(bf16[192,384]{1,0:T(8,128)(2,1)} %get-tuple-element.56), channel_id=1, source_target_pairs={{0,22},{2,24},{4,26},{6,28},{8,30},{10,16},{12,18},{14,20},{16,6},... | collective-permute-start | bytes 442376 | tf_op jit(solution)/shard_map/ppermute | solution.py:70
  28.4 50.8 %collective-permute-start.4 = (bf16[192,384]{1,0:T(8,128)(2,1)}, bf16[192,384]{1,0:T(8,128)(2,1)}, u32[]{:S(2)}, u32[]{:S(2)}) collective-permute-start(bf16[192,384]{1,0:T(8,128)(2,1)} %get-tuple-element.57), channel_id=1, source_target_pairs={{0,24},{2,26},{4,28},{6,30},{8,16},{10,18},{12,20},{14,22},{16,8},... | collective-permute-start | bytes 442376 | tf_op jit(solution)/shard_map/ppermute | solution.py:70
  62.1 21.1 %collective-permute-start.5 = (bf16[192,384]{1,0:T(8,128)(2,1)}, bf16[192,384]{1,0:T(8,128)(2,1)S(1)}, u32[]{:S(2)}, u32[]{:S(2)}) collective-permute-start(bf16[192,384]{1,0:T(8,128)(2,1)} %get-tuple-element.59), channel_id=1, source_target_pairs={{0,26},{2,28},{4,30},{6,16},{8,18},{10,20},{12,22},{14,24},{16,10}... | collective-permute-start | bytes 442376 | tf_op jit(solution)/shard_map/ppermute | solution.py:70
  65.8 31.2 %collective-permute-start.6 = (bf16[192,384]{1,0:T(8,128)(2,1)}, bf16[192,384]{1,0:T(8,128)(2,1)S(1)}, u32[]{:S(2)}, u32[]{:S(2)}) collective-permute-start(bf16[192,384]{1,0:T(8,128)(2,1)} %get-tuple-element.58), channel_id=1, source_target_pairs={{0,28},{2,30},{4,16},{6,18},{8,20},{10,22},{12,24},{14,26},{16,12}... | collective-permute-start | bytes 442376 | tf_op jit(solution)/shard_map/ppermute | solution.py:70
  73.7 26.6 %collective-permute-start.7 = (bf16[192,384]{1,0:T(8,128)(2,1)}, bf16[192,384]{1,0:T(8,128)(2,1)S(1)}, u32[]{:S(2)}, u32[]{:S(2)}) collective-permute-start(bf16[192,384]{1,0:T(8,128)(2,1)} %get-tuple-element.52), channel_id=1, source_target_pairs={{0,30},{2,16},{4,18},{6,20},{8,22},{10,24},{12,26},{14,28},{16,14}... | collective-permute-start | bytes 442376 | tf_op jit(solution)/shard_map/ppermute | solution.py:70
  100.4 1.9 %copy-start = (bf16[3,512,192]{1,2,0:T(8,128)(2,1)S(1)}, bf16[3,512,192]{1,2,0:T(8,128)(2,1)}, u32[]{:S(2)}) copy-start(bf16[3,512,192]{1,2,0:T(8,128)(2,1)} %custom-call.1) | copy-start | bytes 1769476
  103.4 1.4 copy-start.1
  107.4 1.4 copy-start.1
  111.5 1.4 copy-start.1
  115.6 23.0 %all-to-all-start.1 = ((bf16[8,192,192]{2,1,0:T(8,128)(2,1)}), bf16[8,192,192]{2,1,0:T(8,128)(2,1)S(1)}, u32[]{:S(2)}, u32[]{:S(2)}) async-start(bf16[8,192,192]{2,1,0:T(8,128)(2,1)} %bitcast.14), calls=%async_computation.1 | async-start | bytes 1572864 | tf_op jit(solution)/shard_map/all_to_all | solution.py:48
  124.8 20.0 %collective-permute-start.8 = (f32[2,48,1536]{2,1,0:T(8,128)S(1)}, f32[2,48,1536]{2,1,0:T(8,128)}, u32[]{:S(2)}, u32[]{:S(2)}) collective-permute-start(f32[2,48,1536]{2,1,0:T(8,128)S(1)} %dynamic-slice_bitcast_fusion), channel_id=1, source_target_pairs={{0,1},{1,0},{2,3},{3,2},{4,5},{5,4},{6,7},{7,6},{8,9},{9,8},{10,11... | collective-permute-start | bytes 1769480 | tf_op jit(solution)/shard_map/ppermute | solution.py:102
  140.5 10.1 %copy-start.4 = (bf16[192,1536]{1,0:T(8,128)(2,1)S(1)}, bf16[192,1536]{1,0:T(8,128)(2,1)}, u32[]{:S(2)}) copy-start(bf16[192,1536]{1,0:T(8,128)(2,1)} %reshape.26) | copy-start | bytes 1769476
  145.9 8.9 %collective-permute-start.10 = (f32[48,1536]{1,0:T(8,128)S(1)}, f32[48,1536]{1,0:T(8,128)S(1)}, u32[]{:S(2)}, u32[]{:S(2)}) collective-permute-start(f32[48,1536]{1,0:T(8,128)S(1)} %get-tuple-element.60), channel_id=1, source_target_pairs={{0,2},{1,3},{2,6},{3,7},{4,10},{5,11},{6,14},{7,15},{8,18},{9,19},... | collective-permute-start | bytes 884744 | tf_op jit(solution)/shard_map/ppermute | solution.py:116
  147.2 15.5 %collective-permute-start.9 = (f32[48,1536]{1,0:T(8,128)S(1)}, f32[48,1536]{1,0:T(8,128)S(1)}, u32[]{:S(2)}, u32[]{:S(2)}) collective-permute-start(f32[48,1536]{1,0:T(8,128)S(1)} %get-tuple-element.61), channel_id=1, source_target_pairs={{0,0},{1,1},{2,4},{3,5},{4,8},{5,9},{6,12},{7,13},{8,16},{9,17},{1... | collective-permute-start | bytes 884744 | tf_op jit(solution)/shard_map/ppermute | solution.py:116
Sparse Core Ops, SparseCore 0:
  9.6 63.6 all-gather.5
  76.2 73.2 all-gather.3

commit v20 on v19

--- a/solution.py
+++ b/solution.py
@@ -72,7 +72,7 @@
     got = lax.all_to_all(stacked, "inner", split_axis=1, concat_axis=0, tiled=True).reshape(
         head_count * row_count, 3 * head_width
     )
-    early = min(3, len(kv_crossed))
+    early = len(kv_crossed)
     kv_early, got = lax.optimization_barrier((kv_crossed[:early], got))
     kv_crossed = list(kv_early) + kv_crossed[early:]
     query_here = got[:, :head_width]

time: 171 us -> 171 us (level)
    ppermute x8, waiting for transfers between devices: 55.2 us -> 59.3 us  [local(): kv_crossed.append(lax.ppermute(outgoing, ('side', 'inner'), perm))]
    all_to_all x1, waiting for transfers between devices: 12.5 us -> 9.3 us  [a2a(): lax.all_to_all(tensor, 'inner', split_axis=0, concat_axis=0, tiled=True)]
    ppermute x1, waiting for transfers between devices: 4.28 us -> 2.54 us  [local(): kept = kept + lax.ppermute(sent, 'dp', [(0, 1), (1, 0)])]
    unnamed x16 -> x22, local copies, waits for them, and re-layouts: 5.34 us -> 6 us
  transfers between devices with their start and end apart: 15 -> 15, of which waited for: 11 -> 9; matrix products, arithmetic and copies ran while one was open for 23% -> 22% of each run, Pallas kernels for 0% -> 0%
where the time goes in v20:
time: 171 us; the launch traced here: 170 us
  waiting for transfers between devices  80.7 us (47%)
  starting transfers between devices  34.8 us (20%)
  local copies, waits for them, and re-layouts  15.4 us (9%)
  matrix products  15.4 us (9%)
  between operations  14.3 us (8%)
  other arithmetic  9.51 us (6%)
    ppermute x8, waiting for transfers between devices, local(): kv_crossed.append(lax.ppermute(outgoing, ('side', 'inner'), perm))  59.3 us
    ppermute x8, starting transfers between devices, local(): kv_crossed.append(lax.ppermute(outgoing, ('side', 'inner'), perm))  18.6 us
    all_to_all x1, waiting for transfers between devices, a2a(): lax.all_to_all(tensor, 'inner', split_axis=0, concat_axis=0, tiled=True)  9.3 us
    ppermute x2, waiting for transfers between devices, local(): arrived = lax.ppermute(outgoing, ALL, perm)  8.16 us
    unnamed x22, local copies, waits for them, and re-layouts  6 us
    all_to_all x1, starting transfers between devices, local(): lax.all_to_all(stacked, 'inner', split_axis=1, concat_axis=0, tiled=True)  5.31 us
    all_to_all x1, starting transfers between devices, a2a(): lax.all_to_all(tensor, 'inner', split_axis=0, concat_axis=0, tiled=True)  5.14 us
    dot_general x3, matrix products, one_block(): mixed = jnp.dot(weights, value_all, preferred_element_type=jnp.float32)  4.42 us
  transfers between devices with their start and end apart: 15, of which 9 were waited for; matrix products, arithmetic and copies ran while one was open for 22% of the time, Pallas kernels for 0%

profile of v20, /device:TPU:1, one launch (start us, length us, event | category | flops | bytes accessed | tf_op | source)
XLA Modules:
  0.0 170.2 jit_solution(15018882049853274398)
XLA Ops:
  7.2 0.0 all-gather.6.cloned.1.call-start
  7.2 0.7 all-gather.6.cloned.1.call-update
  7.9 1.7 %reshape_squeeze.9 = bf16[192,8,192]{2,1,0:T(8,128)(2,1)S(1)} reshape(bf16[1,192,1536]{2,1,0:T(8,128)(2,1)} %param.8) | data formatting | bytes 1179648 | tf_op jit(solution)/shard_map/reshape;squeeze | solution.py:55
  9.7 0.2 copy.12
  9.8 0.6 reshape_squeeze.10
  10.4 0.2 copy.13
  10.6 0.1 copy-done.2
  10.7 0.6 reshape_squeeze.11
  11.3 0.2 copy.14
  11.5 2.0 %pad_maximum_fusion = bf16[192,8,576]{2,0,1:T(8,128)(2,1)} fusion(bf16[192,8,192]{2,0,1:T(8,128)(2,1)S(1)} %copy.13, bf16[192,8,192]{2,0,1:T(8,128)(2,1)S(1)} %copy.12, bf16[192,8,192]{2,0,1:T(8,128)(2,1)S(1)} %copy.14), kind=kLoop, calls=%fused_computation.20 | loop fusion | flops 5308416 | bytes 3538944 | tf_op jit(solution)/shard_map/concatenate | solution.py:71
  13.5 5.3 %all-to-all-start = ((bf16[192,8,576]{2,0,1:T(8,128)(2,1)}), bf16[192,8,576]{2,0,1:T(8,128)(2,1)S(1)}, u32[]{:S(2)}, u32[]{:S(2)}) async-start(bf16[192,8,576]{2,0,1:T(8,128)(2,1)} %pad_maximum_fusion), calls=%async_computation | async-start | bytes 3932160 | tf_op jit(solution)/shard_map/all_to_all | solution.py:72
  18.8 0.7 all-gather.4.cloned.1.call-update
  19.7 1.2 fusion.41
  20.9 2.3 %collective-permute-start = (bf16[192,384]{1,0:T(8,128)(2,1)}, bf16[192,384]{1,0:T(8,128)(2,1)}, u32[]{:S(2)}, u32[]{:S(2)}) collective-permute-start(bf16[192,384]{1,0:T(8,128)(2,1)} %get-tuple-element.63), channel_id=1, source_target_pairs={{0,16},{2,18},{4,20},{6,22},{8,24},{10,26},{12,28},{14,30},{16,0},... | collective-permute-start | bytes 442376 | tf_op jit(solution)/shard_map/ppermute | solution.py:70
  23.2 1.7 collective-permute-start.1
  24.9 2.3 %collective-permute-start.2 = (bf16[192,384]{1,0:T(8,128)(2,1)}, bf16[192,384]{1,0:T(8,128)(2,1)}, u32[]{:S(2)}, u32[]{:S(2)}) collective-permute-start(bf16[192,384]{1,0:T(8,128)(2,1)} %get-tuple-element.65), channel_id=1, source_target_pairs={{0,20},{2,22},{4,24},{6,26},{8,28},{10,30},{12,16},{14,18},{16,4},... | collective-permute-start | bytes 442376 | tf_op jit(solution)/shard_map/ppermute | solution.py:70
  27.2 1.2 collective-permute-start.3
  28.4 2.1 %collective-permute-start.4 = (bf16[192,384]{1,0:T(8,128)(2,1)}, bf16[192,384]{1,0:T(8,128)(2,1)}, u32[]{:S(2)}, u32[]{:S(2)}) collective-permute-start(bf16[192,384]{1,0:T(8,128)(2,1)} %get-tuple-element.67), channel_id=1, source_target_pairs={{0,24},{2,26},{4,28},{6,30},{8,16},{10,18},{12,20},{14,22},{16,8},... | collective-permute-start | bytes 442376 | tf_op jit(solution)/shard_map/ppermute | solution.py:70
  30.5 0.9 fusion.34
  31.4 30.7 %collective-permute-done = bf16[192,384]{1,0:T(8,128)(2,1)} collective-permute-done((bf16[192,384]{1,0:T(8,128)(2,1)}, bf16[192,384]{1,0:T(8,128)(2,1)}, u32[]{:S(2)}, u32[]{:S(2)}) %collective-permute-start) | collective-permute-done | bytes 147488 | tf_op jit(solution)/shard_map/ppermute | solution.py:70
  62.1 4.1 %collective-permute-start.7 = (bf16[192,384]{1,0:T(8,128)(2,1)}, bf16[192,384]{1,0:T(8,128)(2,1)S(1)}, u32[]{:S(2)}, u32[]{:S(2)}) collective-permute-start(bf16[192,384]{1,0:T(8,128)(2,1)} %get-tuple-element.62), channel_id=1, source_target_pairs={{0,30},{2,16},{4,18},{6,20},{8,22},{10,24},{12,26},{14,28},{16,14}... | collective-permute-start | bytes 442376 | tf_op jit(solution)/shard_map/ppermute | solution.py:70
  66.2 4.9 %collective-permute-start.5 = (bf16[192,384]{1,0:T(8,128)(2,1)}, bf16[192,384]{1,0:T(8,128)(2,1)S(1)}, u32[]{:S(2)}, u32[]{:S(2)}) collective-permute-start(bf16[192,384]{1,0:T(8,128)(2,1)} %get-tuple-element.69), channel_id=1, source_target_pairs={{0,26},{2,28},{4,30},{6,16},{8,18},{10,20},{12,22},{14,24},{16,10}... | collective-permute-start | bytes 442376 | tf_op jit(solution)/shard_map/ppermute | solution.py:70
  71.1 2.7 %collective-permute-done.2 = bf16[192,384]{1,0:T(8,128)(2,1)} collective-permute-done((bf16[192,384]{1,0:T(8,128)(2,1)}, bf16[192,384]{1,0:T(8,128)(2,1)}, u32[]{:S(2)}, u32[]{:S(2)}) %collective-permute-start.2) | collective-permute-done | bytes 147488 | tf_op jit(solution)/shard_map/ppermute | solution.py:70
  73.7 3.9 %collective-permute-done.3 = bf16[192,384]{1,0:T(8,128)(2,1)} collective-permute-done((bf16[192,384]{1,0:T(8,128)(2,1)}, bf16[192,384]{1,0:T(8,128)(2,1)}, u32[]{:S(2)}, u32[]{:S(2)}) %collective-permute-start.3) | collective-permute-done | bytes 147488 | tf_op jit(solution)/shard_map/ppermute | solution.py:70
  77.6 1.6 collective-permute-done.4
  79.2 13.2 %collective-permute-done.7 = bf16[192,384]{1,0:T(8,128)(2,1)S(1)} collective-permute-done((bf16[192,384]{1,0:T(8,128)(2,1)}, bf16[192,384]{1,0:T(8,128)(2,1)S(1)}, u32[]{:S(2)}, u32[]{:S(2)}) %collective-permute-start.7) | collective-permute-done | bytes 147488 | tf_op jit(solution)/shard_map/ppermute | solution.py:70
  92.4 7.3 %collective-permute-done.6 = bf16[192,384]{1,0:T(8,128)(2,1)S(1)} collective-permute-done((bf16[192,384]{1,0:T(8,128)(2,1)}, bf16[192,384]{1,0:T(8,128)(2,1)S(1)}, u32[]{:S(2)}, u32[]{:S(2)}) %collective-permute-start.6) | collective-permute-done | bytes 147488 | tf_op jit(solution)/shard_map/ppermute | solution.py:70
  99.7 0.7 copy-done.6
  100.3 0.1 slice.12
  100.4 0.5 slice_dynamic-update-slice_fusion
  100.9 0.9 constant_dynamic-update-slice_fusion.7
  101.8 0.9 constant_dynamic-update-slice_fusion.6
  102.7 0.9 constant_dynamic-update-slice_fusion.5
  103.7 0.9 constant_dynamic-update-slice_fusion.4
  104.6 0.9 constant_dynamic-update-slice_fusion.3
  105.7 1.9 %fusion.42 = (bf16[3072,192]{1,0:T(8,128)(2,1)}, bf16[3072,192]{1,0:T(8,128)(2,1)S(1)}) fusion(bf16[3072,384]{1,0:T(8,128)(2,1)S(1)} %constant_dynamic-update-slice_fusion), kind=kLoop, calls=%fused_computation.66 | loop fusion | bytes 4718592 | tf_op jit(solution)/shard_map/slice | solution.py:81
  107.6 12.0 %while.10 = (s32[]{:T(128)}, bf16[3,512,192]{1,2,0:T(8,128)(2,1)S(1)}, bf16[3,512,192]{2,1,0:T(8,128)(2,1)S(1)}, bf16[3072,192]{1,0:T(8,128)(2,1)S(1)}, bf16[3072,192]{1,0:T(8,128)(2,1)}, /*index=5*/s32[]{:T(128)}) while((s32[]{:T(128)}, bf16[3,512,192]{1,2,0:T(8,128)(2,1)S(1)}, bf16[3,512,192]{2,1,0:T(8,128)(2,1)S(1)}, ...), condition=%wide.region_3.4_spmd, body=%wide.region_0.3_spmd.sunk | while | flops 1220738048 | bytes 27207784 | solution.py:26
  107.6 1.1 multiply_reduce_fusion.2
  108.7 1.2 fusion.56
  109.8 0.3 copy-done
  110.1 1.5 fusion.57
  111.6 1.1 multiply_reduce_fusion.2
  112.7 1.2 fusion.56
  113.9 0.2 copy-done
  114.1 1.5 fusion.57
  115.6 1.1 multiply_reduce_fusion.2
  116.7 1.2 fusion.56
  117.9 0.2 copy-done
  118.1 1.5 fusion.57
  119.6 1.2 copy.17
  120.8 5.1 %all-to-all-start.1 = ((bf16[8,192,192]{2,1,0:T(8,128)(2,1)}), bf16[8,192,192]{2,1,0:T(8,128)(2,1)S(1)}, u32[]{:S(2)}, u32[]{:S(2)}) async-start(bf16[8,192,192]{2,1,0:T(8,128)(2,1)} %bitcast.14), calls=%async_computation.1 | async-start | bytes 1572864 | tf_op jit(solution)/shard_map/all_to_all | solution.py:48
  126.0 3.4 %fusion.23 = f32[2,2,48,1536]{3,2,1,0:T(8,128)S(1)} fusion(bf16[2,2,48,1536]{3,2,1,0:T(8,128)(2,1)S(1)} %bitcast.73, bf16[1,1536,1536]{2,1,0:T(8,128)(2,1)} %all-gather.6.cloned.1.call-done), kind=kOutput, calls=%fused_computation.16 | convolution fusion | flops 905969664 | bytes 6488064 | tf_op jit(solution)/shard_map/dot_general | solution.py:85
  129.4 1.3 collective-permute-start.8
  130.7 9.3 %all-to-all-done.1 = bf16[8,192,192]{2,1,0:T(8,128)(2,1)S(1)} async-done(((bf16[8,192,192]{2,1,0:T(8,128)(2,1)}), bf16[8,192,192]{2,1,0:T(8,128)(2,1)S(1)}, u32[]{:S(2)}, u32[]{:S(2)}) %all-to-all-start.1) | async-done | bytes 589856 | tf_op jit(solution)/shard_map/all_to_all | solution.py:48
  140.0 0.4 copy.18
  140.5 1.5 reshape.26
  142.0 2.5 %collective-permute-done.8 = f32[2,48,1536]{2,1,0:T(8,128)} collective-permute-done((f32[2,48,1536]{2,1,0:T(8,128)S(1)}, f32[2,48,1536]{2,1,0:T(8,128)}, u32[]{:S(2)}, u32[]{:S(2)}) %collective-permute-start.8) | collective-permute-done | bytes 589856 | tf_op jit(solution)/shard_map/ppermute | solution.py:102
  144.5 1.1 bitcast_add_fusion
  145.7 1.1 collective-permute-start.10
  146.8 3.4 %collective-permute-start.9 = (f32[48,1536]{1,0:T(8,128)S(1)}, f32[48,1536]{1,0:T(8,128)S(1)}, u32[]{:S(2)}, u32[]{:S(2)}) collective-permute-start(f32[48,1536]{1,0:T(8,128)S(1)} %get-tuple-element.71), channel_id=1, source_target_pairs={{0,0},{1,1},{2,4},{3,5},{4,8},{5,9},{6,12},{7,13},{8,16},{9,17},{1... | collective-permute-start | bytes 884744 | tf_op jit(solution)/shard_map/ppermute | solution.py:116
  150.1 0.0 all-gather.4.cloned.1.call-done
  150.2 4.2 %fusion.25 = bf16[1,192,1536]{2,1,0:T(8,128)(2,1)} fusion(bf16[192,1536]{1,0:T(8,128)(2,1)S(1)} %copy-done.3, bf16[1536,1536]{1,0:T(8,128)(2,1)} %all-gather.4.cloned.1.call-done), kind=kOutput, calls=%fused_computation.19 | convolution fusion | flops 906264576 | bytes 5898240 | tf_op jit(solution)/shard_map/dot_general | solution.py:91
  154.4 8.2 %collective-permute-done.9 = f32[48,1536]{1,0:T(8,128)S(1)} collective-permute-done((f32[48,1536]{1,0:T(8,128)S(1)}, f32[48,1536]{1,0:T(8,128)S(1)}, u32[]{:S(2)}, u32[]{:S(2)}) %collective-permute-start.9) | collective-permute-done | bytes 294944 | tf_op jit(solution)/shard_map/ppermute | solution.py:116
  162.6 0.7 add.135
  (29 shorter events, 0.3 us)
Async XLA Ops:
  7.2 2.7 %copy-start.1 = (bf16[1,192,1536]{2,1,0:T(8,128)(2,1)S(1)}, bf16[1,192,1536]{2,1,0:T(8,128)(2,1)}, u32[]{:S(2)}) copy-start(bf16[1,192,1536]{2,1,0:T(8,128)(2,1)} %param.9) | copy-start | bytes 1769476
  7.2 118.8 %all-gather.6.cloned.1.call-start = ((), (), s32[]{:S(2)}) async-start(), calls=%async_computation.3 | async-start | bytes 5308416 | tf_op jit(solution)/shard_map/all_gather | solution.py:45
  9.6 1.1 copy-start.2
  13.5 86.1 %all-to-all-start = ((bf16[192,8,576]{2,0,1:T(8,128)(2,1)}), bf16[192,8,576]{2,0,1:T(8,128)(2,1)S(1)}, u32[]{:S(2)}, u32[]{:S(2)}) async-start(bf16[192,8,576]{2,0,1:T(8,128)(2,1)} %pad_maximum_fusion), calls=%async_computation | async-start | bytes 3932160 | tf_op jit(solution)/shard_map/all_to_all | solution.py:72
  18.8 131.3 %all-gather.4.cloned.1.call-start = ((), (), s32[]{:S(2)}) async-start(), calls=%async_computation.2 | async-start | bytes 4866048 | tf_op jit(solution)/shard_map/all_gather | solution.py:44
  20.9 41.2 %collective-permute-start = (bf16[192,384]{1,0:T(8,128)(2,1)}, bf16[192,384]{1,0:T(8,128)(2,1)}, u32[]{:S(2)}, u32[]{:S(2)}) collective-permute-start(bf16[192,384]{1,0:T(8,128)(2,1)} %get-tuple-element.63), channel_id=1, source_target_pairs={{0,16},{2,18},{4,20},{6,22},{8,24},{10,26},{12,28},{14,30},{16,0},... | collective-permute-start | bytes 442376 | tf_op jit(solution)/shard_map/ppermute | solution.py:70
  23.2 43.0 %collective-permute-start.1 = (bf16[192,384]{1,0:T(8,128)(2,1)}, bf16[192,384]{1,0:T(8,128)(2,1)}, u32[]{:S(2)}, u32[]{:S(2)}) collective-permute-start(bf16[192,384]{1,0:T(8,128)(2,1)} %get-tuple-element.64), channel_id=1, source_target_pairs={{0,18},{2,20},{4,22},{6,24},{8,26},{10,28},{12,30},{14,16},{16,2},... | collective-permute-start | bytes 442376 | tf_op jit(solution)/shard_map/ppermute | solution.py:70
  24.9 48.8 %collective-permute-start.2 = (bf16[192,384]{1,0:T(8,128)(2,1)}, bf16[192,384]{1,0:T(8,128)(2,1)}, u32[]{:S(2)}, u32[]{:S(2)}) collective-permute-start(bf16[192,384]{1,0:T(8,128)(2,1)} %get-tuple-element.65), channel_id=1, source_target_pairs={{0,20},{2,22},{4,24},{6,26},{8,28},{10,30},{12,16},{14,18},{16,4},... | collective-permute-start | bytes 442376 | tf_op jit(solution)/shard_map/ppermute | solution.py:70
  27.2 50.4 %collective-permute-start.3 = (bf16[192,384]{1,0:T(8,128)(2,1)}, bf16[192,384]{1,0:T(8,128)(2,1)}, u32[]{:S(2)}, u32[]{:S(2)}) collective-permute-start(bf16[192,384]{1,0:T(8,128)(2,1)} %get-tuple-element.66), channel_id=1, source_target_pairs={{0,22},{2,24},{4,26},{6,28},{8,30},{10,16},{12,18},{14,20},{16,6},... | collective-permute-start | bytes 442376 | tf_op jit(solution)/shard_map/ppermute | solution.py:70
  28.4 50.8 %collective-permute-start.4 = (bf16[192,384]{1,0:T(8,128)(2,1)}, bf16[192,384]{1,0:T(8,128)(2,1)}, u32[]{:S(2)}, u32[]{:S(2)}) collective-permute-start(bf16[192,384]{1,0:T(8,128)(2,1)} %get-tuple-element.67), channel_id=1, source_target_pairs={{0,24},{2,26},{4,28},{6,30},{8,16},{10,18},{12,20},{14,22},{16,8},... | collective-permute-start | bytes 442376 | tf_op jit(solution)/shard_map/ppermute | solution.py:70
  62.1 30.3 %collective-permute-start.7 = (bf16[192,384]{1,0:T(8,128)(2,1)}, bf16[192,384]{1,0:T(8,128)(2,1)S(1)}, u32[]{:S(2)}, u32[]{:S(2)}) collective-permute-start(bf16[192,384]{1,0:T(8,128)(2,1)} %get-tuple-element.62), channel_id=1, source_target_pairs={{0,30},{2,16},{4,18},{6,20},{8,22},{10,24},{12,26},{14,28},{16,14}... | collective-permute-start | bytes 442376 | tf_op jit(solution)/shard_map/ppermute | solution.py:70
  66.2 26.2 %collective-permute-start.5 = (bf16[192,384]{1,0:T(8,128)(2,1)}, bf16[192,384]{1,0:T(8,128)(2,1)S(1)}, u32[]{:S(2)}, u32[]{:S(2)}) collective-permute-start(bf16[192,384]{1,0:T(8,128)(2,1)} %get-tuple-element.69), channel_id=1, source_target_pairs={{0,26},{2,28},{4,30},{6,16},{8,18},{10,20},{12,22},{14,24},{16,10}... | collective-permute-start | bytes 442376 | tf_op jit(solution)/shard_map/ppermute | solution.py:70
  73.7 25.9 %collective-permute-start.6 = (bf16[192,384]{1,0:T(8,128)(2,1)}, bf16[192,384]{1,0:T(8,128)(2,1)S(1)}, u32[]{:S(2)}, u32[]{:S(2)}) collective-permute-start(bf16[192,384]{1,0:T(8,128)(2,1)} %get-tuple-element.68), channel_id=1, source_target_pairs={{0,28},{2,30},{4,16},{6,18},{8,20},{10,22},{12,24},{14,26},{16,12}... | collective-permute-start | bytes 442376 | tf_op jit(solution)/shard_map/ppermute | solution.py:70
  92.4 7.3 %copy-start.4 = (bf16[192,384]{1,0:T(8,128)(2,1)}, bf16[192,384]{1,0:T(8,128)(2,1)S(1)}, u32[]{:S(2)}) copy-start(bf16[192,384]{1,0:T(8,128)(2,1)S(1)} %collective-permute-done.5) | copy-start | bytes 442372
  99.6 0.7 copy-start.6
  100.3 5.2 %copy-start.5 = (bf16[192,384]{1,0:T(8,128)(2,1)S(1)}, bf16[192,384]{1,0:T(8,128)(2,1)}, u32[]{:S(2)}) copy-start(bf16[192,384]{1,0:T(8,128)(2,1)} %copy-done.4) | copy-start | bytes 442372
  100.4 5.2 %copy-start.7 = (bf16[192,384]{1,0:T(8,128)(2,1)S(1)}, bf16[192,384]{1,0:T(8,128)(2,1)}, u32[]{:S(2)}) copy-start(bf16[192,384]{1,0:T(8,128)(2,1)} %copy-done.6) | copy-start | bytes 442372
  108.7 1.4 copy-start
  112.7 1.4 copy-start
  116.7 1.4 copy-start
  120.8 19.2 %all-to-all-start.1 = ((bf16[8,192,192]{2,1,0:T(8,128)(2,1)}), bf16[8,192,192]{2,1,0:T(8,128)(2,1)S(1)}, u32[]{:S(2)}, u32[]{:S(2)}) async-start(bf16[8,192,192]{2,1,0:T(8,128)(2,1)} %bitcast.14), calls=%async_computation.1 | async-start | bytes 1572864 | tf_op jit(solution)/shard_map/all_to_all | solution.py:48
  129.4 15.1 %collective-permute-start.8 = (f32[2,48,1536]{2,1,0:T(8,128)S(1)}, f32[2,48,1536]{2,1,0:T(8,128)}, u32[]{:S(2)}, u32[]{:S(2)}) collective-permute-start(f32[2,48,1536]{2,1,0:T(8,128)S(1)} %dynamic-slice_bitcast_fusion), channel_id=1, source_target_pairs={{0,1},{1,0},{2,3},{3,2},{4,5},{5,4},{6,7},{7,6},{8,9},{9,8},{10,11... | collective-permute-start | bytes 1769480 | tf_op jit(solution)/shard_map/ppermute | solution.py:102
  142.0 8.2 %copy-start.3 = (bf16[192,1536]{1,0:T(8,128)(2,1)S(1)}, bf16[192,1536]{1,0:T(8,128)(2,1)}, u32[]{:S(2)}) copy-start(bf16[192,1536]{1,0:T(8,128)(2,1)} %reshape.26) | copy-start | bytes 1769476
  145.7 8.7 %collective-permute-start.10 = (f32[48,1536]{1,0:T(8,128)S(1)}, f32[48,1536]{1,0:T(8,128)S(1)}, u32[]{:S(2)}, u32[]{:S(2)}) collective-permute-start(f32[48,1536]{1,0:T(8,128)S(1)} %get-tuple-element.70), channel_id=1, source_target_pairs={{0,2},{1,3},{2,6},{3,7},{4,10},{5,11},{6,14},{7,15},{8,18},{9,19},... | collective-permute-start | bytes 884744 | tf_op jit(solution)/shard_map/ppermute | solution.py:116
  146.8 15.8 %collective-permute-start.9 = (f32[48,1536]{1,0:T(8,128)S(1)}, f32[48,1536]{1,0:T(8,128)S(1)}, u32[]{:S(2)}, u32[]{:S(2)}) collective-permute-start(f32[48,1536]{1,0:T(8,128)S(1)} %get-tuple-element.71), channel_id=1, source_target_pairs={{0,0},{1,1},{2,4},{3,5},{4,8},{5,9},{6,12},{7,13},{8,16},{9,17},{1... | collective-permute-start | bytes 884744 | tf_op jit(solution)/shard_map/ppermute | solution.py:116
Sparse Core Ops, SparseCore 0:
  9.6 63.7 all-gather.5
  76.3 72.7 all-gather.3

commit v21 on v19

--- a/solution.py
+++ b/solution.py
@@ -87,10 +87,6 @@
     )
 
     returned = a2a(attended_here.reshape(head_count, row_count, head_width))
-    attended = returned.transpose(1, 0, 2).reshape(row_count, width)
-    projected = jnp.dot(attended, w_full, preferred_element_type=jnp.float32).astype(
-        jnp.bfloat16
-    )
 
     chunk_count = side_count * dp_count
     chunk = head_width // chunk_count
@@ -113,6 +109,7 @@
             outgoing = lax.dynamic_index_in_dim(
                 kept, (side_index + step) % side_count, axis=0, keepdims=False
             )
+            _, returned = lax.optimization_barrier((outgoing, returned))
             arrived = lax.ppermute(outgoing, ALL, perm)
             grad_w_out = arrived if grad_w_out is None else grad_w_out + arrived
     else:
@@ -133,6 +130,10 @@
             )
             arrived = lax.ppermute(outgoing, ALL, perm)
             grad_w_out = arrived if grad_w_out is None else grad_w_out + arrived
+    attended = returned.transpose(1, 0, 2).reshape(row_count, width)
+    projected = jnp.dot(attended, w_full, preferred_element_type=jnp.float32).astype(
+        jnp.bfloat16
+    )
     return (projected.reshape(1, row_count, width), grad_w_out)
 
 

time: 171 us -> 174 us (1.018)
  the two profiles are of different devices: /device:TPU:1 before, /device:TPU:3 now
where the time goes in v21:
time: 174 us
  waiting for transfers between devices  90.4 us (52%)
  starting transfers between devices  30.2 us (17%)
  matrix products  15.4 us (9%)
  between operations  14.3 us (8%)
  local copies, waits for them, and re-layouts  13.9 us (8%)
  other arithmetic  9.53 us (5%)
    ppermute x8, waiting for transfers between devices, local(): kv_crossed.append(lax.ppermute(outgoing, ('side', 'inner'), perm))  55.3 us
    all_gather x1, waiting for transfers between devices, local(): w_full = lax.all_gather(w_out, ALL, axis=0, tiled=True)  20 us
    ppermute x8, starting transfers between devices, local(): kv_crossed.append(lax.ppermute(outgoing, ('side', 'inner'), perm))  18 us
    ppermute x1, waiting for transfers between devices, local(): kept = kept + lax.ppermute(sent, 'dp', [(0, 1), (1, 0)])  13.7 us
    all_to_all x1, starting transfers between devices, a2a(): lax.all_to_all(tensor, 'inner', split_axis=0, concat_axis=0, tiled=True)  5.38 us
    unnamed x14, local copies, waits for them, and re-layouts  5.33 us
    all_to_all x1, starting transfers between devices, local(): lax.all_to_all(stacked, 'inner', split_axis=1, concat_axis=0, tiled=True)  4.48 us
    dot_general x3, matrix products, one_block(): mixed = jnp.dot(weights, value_all, preferred_element_type=jnp.float32)  4.42 us
  transfers between devices with their start and end apart: 15, of which 10 were waited for; matrix products, arithmetic and copies ran while one was open for 21% of the time, Pallas kernels for 0%

profile of v21, /device:TPU:3, one launch (start us, length us, event | category | flops | bytes accessed | tf_op | source)
XLA Modules:
  0.0 173.8 jit_solution(1887989736130136426)
XLA Ops:
  7.2 0.0 all-gather.6.cloned.1.call-start
  7.2 0.7 all-gather.6.cloned.1.call-update
  7.9 1.7 reshape_squeeze.9
  9.7 0.2 copy.12
  9.8 0.6 reshape_squeeze.10
  10.4 0.2 copy.13
  10.6 0.1 copy-done.3
  10.7 0.6 reshape_squeeze.11
  11.3 0.2 copy.14
  11.5 2.1 %pad_maximum_fusion = bf16[192,8,576]{2,0,1:T(8,128)(2,1)} fusion(bf16[192,8,192]{2,0,1:T(8,128)(2,1)S(1)} %copy.13, bf16[192,8,192]{2,0,1:T(8,128)(2,1)S(1)} %copy.12, bf16[192,8,192]{2,0,1:T(8,128)(2,1)S(1)} %copy.14), kind=kLoop, calls=%fused_computation.20 | loop fusion | flops 5308416 | bytes 3538944 | tf_op jit(solution)/shard_map/concatenate | solution.py:71
  13.5 4.5 %all-to-all-start = ((bf16[192,8,576]{2,0,1:T(8,128)(2,1)}), bf16[192,8,576]{2,0,1:T(8,128)(2,1)S(1)}, u32[]{:S(2)}, u32[]{:S(2)}) async-start(bf16[192,8,576]{2,0,1:T(8,128)(2,1)} %pad_maximum_fusion), calls=%async_computation | async-start | bytes 3932160 | tf_op jit(solution)/shard_map/all_to_all | solution.py:72
  18.0 0.7 all-gather.4.cloned.1.call-update
  18.8 1.3 fusion.41
  20.1 2.3 %collective-permute-start = (bf16[192,384]{1,0:T(8,128)(2,1)}, bf16[192,384]{1,0:T(8,128)(2,1)}, u32[]{:S(2)}, u32[]{:S(2)}) collective-permute-start(bf16[192,384]{1,0:T(8,128)(2,1)} %get-tuple-element.57), channel_id=1, source_target_pairs={{0,16},{2,18},{4,20},{6,22},{8,24},{10,26},{12,28},{14,30},{16,0},... | collective-permute-start | bytes 442376 | tf_op jit(solution)/shard_map/ppermute | solution.py:70
  22.4 1.7 collective-permute-start.1
  24.1 2.3 %collective-permute-start.2 = (bf16[192,384]{1,0:T(8,128)(2,1)}, bf16[192,384]{1,0:T(8,128)(2,1)}, u32[]{:S(2)}, u32[]{:S(2)}) collective-permute-start(bf16[192,384]{1,0:T(8,128)(2,1)} %get-tuple-element.59), channel_id=1, source_target_pairs={{0,20},{2,22},{4,24},{6,26},{8,28},{10,30},{12,16},{14,18},{16,4},... | collective-permute-start | bytes 442376 | tf_op jit(solution)/shard_map/ppermute | solution.py:70
  26.4 1.2 collective-permute-start.3
  27.6 2.1 %collective-permute-start.4 = (bf16[192,384]{1,0:T(8,128)(2,1)}, bf16[192,384]{1,0:T(8,128)(2,1)}, u32[]{:S(2)}, u32[]{:S(2)}) collective-permute-start(bf16[192,384]{1,0:T(8,128)(2,1)} %get-tuple-element.61), channel_id=1, source_target_pairs={{0,24},{2,26},{4,28},{6,30},{8,16},{10,18},{12,20},{14,22},{16,8},... | collective-permute-start | bytes 442376 | tf_op jit(solution)/shard_map/ppermute | solution.py:70
  29.7 0.9 fusion.34
  30.6 30.7 %collective-permute-done = bf16[192,384]{1,0:T(8,128)(2,1)} collective-permute-done((bf16[192,384]{1,0:T(8,128)(2,1)}, bf16[192,384]{1,0:T(8,128)(2,1)}, u32[]{:S(2)}, u32[]{:S(2)}) %collective-permute-start) | collective-permute-done | bytes 147488 | tf_op jit(solution)/shard_map/ppermute | solution.py:70
  61.3 3.2 %collective-permute-start.5 = (bf16[192,384]{1,0:T(8,128)(2,1)}, bf16[192,384]{1,0:T(8,128)(2,1)S(1)}, u32[]{:S(2)}, u32[]{:S(2)}) collective-permute-start(bf16[192,384]{1,0:T(8,128)(2,1)} %get-tuple-element.63), channel_id=1, source_target_pairs={{0,26},{2,28},{4,30},{6,16},{8,18},{10,20},{12,22},{14,24},{16,10}... | collective-permute-start | bytes 442376 | tf_op jit(solution)/shard_map/ppermute | solution.py:70
  64.5 0.5 collective-permute-done.1
  65.0 5.2 %collective-permute-start.6 = (bf16[192,384]{1,0:T(8,128)(2,1)}, bf16[192,384]{1,0:T(8,128)(2,1)S(1)}, u32[]{:S(2)}, u32[]{:S(2)}) collective-permute-start(bf16[192,384]{1,0:T(8,128)(2,1)} %get-tuple-element.62), channel_id=1, source_target_pairs={{0,28},{2,30},{4,16},{6,18},{8,20},{10,22},{12,24},{14,26},{16,12}... | collective-permute-start | bytes 442376 | tf_op jit(solution)/shard_map/ppermute | solution.py:70
  70.2 2.7 %collective-permute-done.2 = bf16[192,384]{1,0:T(8,128)(2,1)} collective-permute-done((bf16[192,384]{1,0:T(8,128)(2,1)}, bf16[192,384]{1,0:T(8,128)(2,1)}, u32[]{:S(2)}, u32[]{:S(2)}) %collective-permute-start.2) | collective-permute-done | bytes 147488 | tf_op jit(solution)/shard_map/ppermute | solution.py:70
  72.9 0.5 slice_dynamic-update-slice_fusion
  73.4 0.9 constant_dynamic-update-slice_fusion.7
  74.4 0.9 constant_dynamic-update-slice_fusion.6
  75.3 0.9 constant_dynamic-update-slice_fusion.5
  76.2 0.5 collective-permute-done.3
  76.7 0.9 constant_dynamic-update-slice_fusion.4
  77.7 0.7 collective-permute-done.4
  78.4 0.9 constant_dynamic-update-slice_fusion.3
  79.3 3.1 %collective-permute-done.5 = bf16[192,384]{1,0:T(8,128)(2,1)S(1)} collective-permute-done((bf16[192,384]{1,0:T(8,128)(2,1)}, bf16[192,384]{1,0:T(8,128)(2,1)S(1)}, u32[]{:S(2)}, u32[]{:S(2)}) %collective-permute-start.5) | collective-permute-done | bytes 147488 | tf_op jit(solution)/shard_map/ppermute | solution.py:70
  82.4 0.1 slice.12
  82.5 13.9 %collective-permute-done.6 = bf16[192,384]{1,0:T(8,128)(2,1)S(1)} collective-permute-done((bf16[192,384]{1,0:T(8,128)(2,1)}, bf16[192,384]{1,0:T(8,128)(2,1)S(1)}, u32[]{:S(2)}, u32[]{:S(2)}) %collective-permute-start.6) | collective-permute-done | bytes 147488 | tf_op jit(solution)/shard_map/ppermute | solution.py:70
  96.4 3.2 %collective-permute-done.7 = bf16[192,384]{1,0:T(8,128)(2,1)S(1)} collective-permute-done((bf16[192,384]{1,0:T(8,128)(2,1)}, bf16[192,384]{1,0:T(8,128)(2,1)S(1)}, u32[]{:S(2)}, u32[]{:S(2)}) %collective-permute-start.7) | collective-permute-done | bytes 147488 | tf_op jit(solution)/shard_map/ppermute | solution.py:70
  99.6 1.9 %fusion.42 = (bf16[3072,192]{1,0:T(8,128)(2,1)}, bf16[3072,192]{1,0:T(8,128)(2,1)S(1)}) fusion(bf16[3072,384]{1,0:T(8,128)(2,1)S(1)} %constant_dynamic-update-slice_fusion), kind=kLoop, calls=%fused_computation.66 | loop fusion | bytes 4718592 | tf_op jit(solution)/shard_map/slice | solution.py:81
  101.5 12.0 %while.10 = (s32[]{:T(128)}, bf16[3,512,192]{1,2,0:T(8,128)(2,1)S(1)}, bf16[3,512,192]{2,1,0:T(8,128)(2,1)S(1)}, bf16[3072,192]{1,0:T(8,128)(2,1)S(1)}, bf16[3072,192]{1,0:T(8,128)(2,1)}, /*index=5*/s32[]{:T(128)}) while((s32[]{:T(128)}, bf16[3,512,192]{1,2,0:T(8,128)(2,1)S(1)}, bf16[3,512,192]{2,1,0:T(8,128)(2,1)S(1)}, ...), condition=%wide.region_3.4_spmd, body=%wide.region_0.3_spmd.sunk | while | flops 1220738048 | bytes 27207784 | solution.py:26
  101.5 1.1 multiply_reduce_fusion.2
  102.6 1.2 fusion.56
  103.8 0.2 copy-done.1
  104.0 1.5 fusion.57
  105.5 1.1 multiply_reduce_fusion.2
  106.6 1.2 fusion.56
  107.8 0.3 copy-done.1
  108.1 1.5 fusion.57
  109.6 1.1 multiply_reduce_fusion.2
  110.7 1.2 fusion.56
  111.8 0.2 copy-done.1
  112.1 1.5 fusion.57
  113.6 0.0 all-gather.6.cloned.1.call-done
  113.6 3.4 %fusion.23 = f32[2,2,48,1536]{3,2,1,0:T(8,128)S(1)} fusion(bf16[2,2,48,1536]{3,2,1,0:T(8,128)(2,1)S(1)} %bitcast.73, bf16[1,1536,1536]{2,1,0:T(8,128)(2,1)} %all-gather.6.cloned.1.call-done), kind=kOutput, calls=%fused_computation.16 | convolution fusion | flops 905969664 | bytes 6488064 | tf_op jit(solution)/shard_map/dot_general | solution.py:85
  117.1 0.3 collective-permute-start.8
  117.4 1.2 copy.18
  118.6 5.4 %all-to-all-start.1 = ((bf16[8,192,192]{2,1,0:T(8,128)(2,1)}), bf16[8,192,192]{2,1,0:T(8,128)(2,1)S(1)}, u32[]{:S(2)}, u32[]{:S(2)}) async-start(bf16[8,192,192]{2,1,0:T(8,128)(2,1)} %bitcast.23), calls=%async_computation.1 | async-start | bytes 1572864 | tf_op jit(solution)/shard_map/all_to_all | solution.py:48
  124.0 13.7 %collective-permute-done.8 = f32[2,48,1536]{2,1,0:T(8,128)} collective-permute-done((f32[2,48,1536]{2,1,0:T(8,128)S(1)}, f32[2,48,1536]{2,1,0:T(8,128)}, u32[]{:S(2)}, u32[]{:S(2)}) %collective-permute-start.8) | collective-permute-done | bytes 589856 | tf_op jit(solution)/shard_map/ppermute | solution.py:98
  137.6 1.1 bitcast_add_fusion
  138.8 0.1 collective-permute-start.10
  138.9 1.9 %collective-permute-start.9 = (f32[48,1536]{1,0:T(8,128)S(1)}, f32[48,1536]{1,0:T(8,128)S(1)}, u32[]{:S(2)}, u32[]{:S(2)}) collective-permute-start(f32[48,1536]{1,0:T(8,128)S(1)} %get-tuple-element.64), channel_id=1, source_target_pairs={{0,0},{1,1},{2,4},{3,5},{4,8},{5,9},{6,12},{7,13},{8,16},{9,17},{1... | collective-permute-start | bytes 884744 | tf_op jit(solution)/shard_map/ppermute | solution.py:113
  140.8 0.4 copy.19
  141.3 0.7 reshape.27
  142.0 20.0 %all-gather.4.cloned.1.call-done = bf16[1536,1536]{1,0:T(8,128)(2,1)} async-done(((bf16[48,1536]{1,0:T(8,128)(2,1)}), bf16[1536,1536]{1,0:T(8,128)(2,1)}) %all-gather.4.cloned.1.call-update) | async-done | bytes 4718608 | tf_op jit(solution)/shard_map/all_gather | solution.py:44
  162.0 4.2 %fusion.25 = bf16[1,192,1536]{2,1,0:T(8,128)(2,1)} fusion(bf16[192,1536]{1,0:T(8,128)(2,1)S(1)} %reshape.27, bf16[1536,1536]{1,0:T(8,128)(2,1)} %all-gather.4.cloned.1.call-done), kind=kOutput, calls=%fused_computation.19 | convolution fusion | flops 906264576 | bytes 5898240 | tf_op jit(solution)/shard_map/dot_general | solution.py:134
  166.3 0.7 add.135
  (21 shorter events, 0.2 us)
Async XLA Ops:
  7.2 2.7 %copy-start.2 = (bf16[1,192,1536]{2,1,0:T(8,128)(2,1)S(1)}, bf16[1,192,1536]{2,1,0:T(8,128)(2,1)}, u32[]{:S(2)}) copy-start(bf16[1,192,1536]{2,1,0:T(8,128)(2,1)} %param.9) | copy-start | bytes 1769476
  7.2 106.5 %all-gather.6.cloned.1.call-start = ((), (), s32[]{:S(2)}) async-start(), calls=%async_computation.3 | async-start | bytes 5308416 | tf_op jit(solution)/shard_map/all_gather | solution.py:45
  9.6 1.1 copy-start.3
  13.5 59.4 %all-to-all-start = ((bf16[192,8,576]{2,0,1:T(8,128)(2,1)}), bf16[192,8,576]{2,0,1:T(8,128)(2,1)S(1)}, u32[]{:S(2)}, u32[]{:S(2)}) async-start(bf16[192,8,576]{2,0,1:T(8,128)(2,1)} %pad_maximum_fusion), calls=%async_computation | async-start | bytes 3932160 | tf_op jit(solution)/shard_map/all_to_all | solution.py:72
  18.0 144.0 %all-gather.4.cloned.1.call-start = ((), (), s32[]{:S(2)}) async-start(), calls=%async_computation.2 | async-start | bytes 4866048 | tf_op jit(solution)/shard_map/all_gather | solution.py:44
  20.1 41.2 %collective-permute-start = (bf16[192,384]{1,0:T(8,128)(2,1)}, bf16[192,384]{1,0:T(8,128)(2,1)}, u32[]{:S(2)}, u32[]{:S(2)}) collective-permute-start(bf16[192,384]{1,0:T(8,128)(2,1)} %get-tuple-element.57), channel_id=1, source_target_pairs={{0,16},{2,18},{4,20},{6,22},{8,24},{10,26},{12,28},{14,30},{16,0},... | collective-permute-start | bytes 442376 | tf_op jit(solution)/shard_map/ppermute | solution.py:70
  22.4 42.6 %collective-permute-start.1 = (bf16[192,384]{1,0:T(8,128)(2,1)}, bf16[192,384]{1,0:T(8,128)(2,1)}, u32[]{:S(2)}, u32[]{:S(2)}) collective-permute-start(bf16[192,384]{1,0:T(8,128)(2,1)} %get-tuple-element.58), channel_id=1, source_target_pairs={{0,18},{2,20},{4,22},{6,24},{8,26},{10,28},{12,30},{14,16},{16,2},... | collective-permute-start | bytes 442376 | tf_op jit(solution)/shard_map/ppermute | solution.py:70
  24.1 48.8 %collective-permute-start.2 = (bf16[192,384]{1,0:T(8,128)(2,1)}, bf16[192,384]{1,0:T(8,128)(2,1)}, u32[]{:S(2)}, u32[]{:S(2)}) collective-permute-start(bf16[192,384]{1,0:T(8,128)(2,1)} %get-tuple-element.59), channel_id=1, source_target_pairs={{0,20},{2,22},{4,24},{6,26},{8,28},{10,30},{12,16},{14,18},{16,4},... | collective-permute-start | bytes 442376 | tf_op jit(solution)/shard_map/ppermute | solution.py:70
  26.4 50.3 %collective-permute-start.3 = (bf16[192,384]{1,0:T(8,128)(2,1)}, bf16[192,384]{1,0:T(8,128)(2,1)}, u32[]{:S(2)}, u32[]{:S(2)}) collective-permute-start(bf16[192,384]{1,0:T(8,128)(2,1)} %get-tuple-element.60), channel_id=1, source_target_pairs={{0,22},{2,24},{4,26},{6,28},{8,30},{10,16},{12,18},{14,20},{16,6},... | collective-permute-start | bytes 442376 | tf_op jit(solution)/shard_map/ppermute | solution.py:70
  27.6 50.8 %collective-permute-start.4 = (bf16[192,384]{1,0:T(8,128)(2,1)}, bf16[192,384]{1,0:T(8,128)(2,1)}, u32[]{:S(2)}, u32[]{:S(2)}) collective-permute-start(bf16[192,384]{1,0:T(8,128)(2,1)} %get-tuple-element.61), channel_id=1, source_target_pairs={{0,24},{2,26},{4,28},{6,30},{8,16},{10,18},{12,20},{14,22},{16,8},... | collective-permute-start | bytes 442376 | tf_op jit(solution)/shard_map/ppermute | solution.py:70
  61.3 21.1 %collective-permute-start.5 = (bf16[192,384]{1,0:T(8,128)(2,1)}, bf16[192,384]{1,0:T(8,128)(2,1)S(1)}, u32[]{:S(2)}, u32[]{:S(2)}) collective-permute-start(bf16[192,384]{1,0:T(8,128)(2,1)} %get-tuple-element.63), channel_id=1, source_target_pairs={{0,26},{2,28},{4,30},{6,16},{8,18},{10,20},{12,22},{14,24},{16,10}... | collective-permute-start | bytes 442376 | tf_op jit(solution)/shard_map/ppermute | solution.py:70
  65.0 31.3 %collective-permute-start.6 = (bf16[192,384]{1,0:T(8,128)(2,1)}, bf16[192,384]{1,0:T(8,128)(2,1)S(1)}, u32[]{:S(2)}, u32[]{:S(2)}) collective-permute-start(bf16[192,384]{1,0:T(8,128)(2,1)} %get-tuple-element.62), channel_id=1, source_target_pairs={{0,28},{2,30},{4,16},{6,18},{8,20},{10,22},{12,24},{14,26},{16,12}... | collective-permute-start | bytes 442376 | tf_op jit(solution)/shard_map/ppermute | solution.py:70
  72.9 26.6 %collective-permute-start.7 = (bf16[192,384]{1,0:T(8,128)(2,1)}, bf16[192,384]{1,0:T(8,128)(2,1)S(1)}, u32[]{:S(2)}, u32[]{:S(2)}) collective-permute-start(bf16[192,384]{1,0:T(8,128)(2,1)} %get-tuple-element.56), channel_id=1, source_target_pairs={{0,30},{2,16},{4,18},{6,20},{8,22},{10,24},{12,26},{14,28},{16,14}... | collective-permute-start | bytes 442376 | tf_op jit(solution)/shard_map/ppermute | solution.py:70
  99.6 1.9 %copy-start = (bf16[3,512,192]{1,2,0:T(8,128)(2,1)S(1)}, bf16[3,512,192]{1,2,0:T(8,128)(2,1)}, u32[]{:S(2)}) copy-start(bf16[3,512,192]{1,2,0:T(8,128)(2,1)} %custom-call.1) | copy-start | bytes 1769476
  102.6 1.4 copy-start.1
  106.6 1.4 copy-start.1
  110.7 1.4 copy-start.1
  117.1 20.5 %collective-permute-start.8 = (f32[2,48,1536]{2,1,0:T(8,128)S(1)}, f32[2,48,1536]{2,1,0:T(8,128)}, u32[]{:S(2)}, u32[]{:S(2)}) collective-permute-start(f32[2,48,1536]{2,1,0:T(8,128)S(1)} %dynamic-slice_bitcast_fusion), channel_id=1, source_target_pairs={{0,1},{1,0},{2,3},{3,2},{4,5},{5,4},{6,7},{7,6},{8,9},{9,8},{10,11... | collective-permute-start | bytes 1769480 | tf_op jit(solution)/shard_map/ppermute | solution.py:98
  118.6 22.2 %all-to-all-start.1 = ((bf16[8,192,192]{2,1,0:T(8,128)(2,1)}), bf16[8,192,192]{2,1,0:T(8,128)(2,1)S(1)}, u32[]{:S(2)}, u32[]{:S(2)}) async-start(bf16[8,192,192]{2,1,0:T(8,128)(2,1)} %bitcast.23), calls=%async_computation.1 | async-start | bytes 1572864 | tf_op jit(solution)/shard_map/all_to_all | solution.py:48
  138.8 27.4 %collective-permute-start.10 = (f32[48,1536]{1,0:T(8,128)S(1)}, f32[48,1536]{1,0:T(8,128)S(1)}, u32[]{:S(2)}, u32[]{:S(2)}) collective-permute-start(f32[48,1536]{1,0:T(8,128)S(1)} %get-tuple-element.65), channel_id=1, source_target_pairs={{0,2},{1,3},{2,6},{3,7},{4,10},{5,11},{6,14},{7,15},{8,18},{9,19},... | collective-permute-start | bytes 884744 | tf_op jit(solution)/shard_map/ppermute | solution.py:113
  138.9 27.4 %collective-permute-start.9 = (f32[48,1536]{1,0:T(8,128)S(1)}, f32[48,1536]{1,0:T(8,128)S(1)}, u32[]{:S(2)}, u32[]{:S(2)}) collective-permute-start(f32[48,1536]{1,0:T(8,128)S(1)} %get-tuple-element.64), channel_id=1, source_target_pairs={{0,0},{1,1},{2,4},{3,5},{4,8},{5,9},{6,12},{7,13},{8,16},{9,17},{1... | collective-permute-start | bytes 884744 | tf_op jit(solution)/shard_map/ppermute | solution.py:113
Sparse Core Ops, SparseCore 0:
  9.6 62.7 all-gather.5
  75.4 86.5 all-gather.3
